TPU v7x, 32 devices: a whole 2x2x4 slice. The times are simulated.
32 devices in a mesh: groups: 2 (over y), chan: 4 (over z), tm: 4 (over x, core).
Axes of the slice: x: 2, y: 2, z: 4, core: 2. Of those that a mesh axis runs over, the one named last changes fastest.
Arguments:
- raw: bfloat16 [8192, 2048], P(('groups', 'chan'), 'tm'), parts along dimension 0, may hold values from -20 to 20
- send_blocks: int32 [4, 4, 4, 1], P('chan', 'tm'), may hold values from 0 to 1, as said below
- pair_count: int32 [4, 4, 4], P('chan', 'tm'), may hold values from 0 to 1, as said below
Outputs:
- xspec: bfloat16 [8, 4, 4, 1, 2, 2, 128, 128], P(('groups', 'chan'), 'tm'), parts along dimension 0
There are 2 independent parts, one for each index of `groups`. A program takes and returns all parts, laid end to end along the dimension named above; an argument that names none is the same for every part. Nothing has to cross between parts.
Inputs may be any that keep to these rules, and one draw needn't show every extreme that they name: Each list send_blocks[p, t, c, :] names 1 distinct local blocks of device (p, t). pair_count[c, t, c] is 0; pair_count[c, t, p] is 1 where p and c differ by one; in every index t of tm some owner has 1 from every other source.
All inputs are finite; a program needn't handle non-finite values.
Results may differ from a plain program's by a relative error of at most 0.0066.
Values may be sent and summed in bfloat16 or wider, within the bound.
No kernel may reach another device: no remote copies, remote signals or barrier semaphores. Data moves between devices by JAX's collectives and lax.ppermute only.
A program may use at most 192 MiB of HBM per device.

v0:
```python
import math

import jax
import jax.numpy as jnp
import numpy as np
from jax import lax
from jax.sharding import PartitionSpec as P

BLOCK = 128
NT = 2048
F0 = 128
NBAND = 512
SUBW = 64
RAD = 15


def sinc_value(arg):
    if arg == 0:
        return 1.0
    return math.sin(math.pi * arg) / (math.pi * arg)


def filter_taps():
    low = F0 / NT
    high = (F0 + NBAND) / NT
    taps = []
    for offset in range(-RAD, RAD + 1):
        value = 2.0 * high * sinc_value(2.0 * high * offset) - 2.0 * low * sinc_value(
            2.0 * low * offset
        )
        value = value * (0.5 + 0.5 * math.cos(math.pi * offset / (RAD + 1)))
        taps.append(value)
    return taps


def dft_table():
    samples = np.arange(NT)[:, None]
    freqs = np.arange(F0, F0 + NBAND)[None, :]
    phase = samples * freqs % NT
    angle = 2.0 * np.pi * phase / NT
    return np.concatenate([np.cos(angle), -np.sin(angle)], axis=1)


def band_filter(slab):
    taps = filter_taps()
    signal = slab.astype(jnp.float32)
    total = jnp.zeros(signal.shape, jnp.float32)
    for index in range(2 * RAD + 1):
        total = total + jnp.float32(taps[index]) * jnp.roll(signal, index - RAD, axis=1)
    return total.astype(jnp.bfloat16)


def whiten(spectrum):
    rows = spectrum.shape[0]
    real_part = spectrum[:, :NBAND].reshape(rows, NBAND // SUBW, SUBW)
    imag_part = spectrum[:, NBAND:].reshape(rows, NBAND // SUBW, SUBW)
    power = jnp.mean(real_part * real_part + imag_part * imag_part, axis=2, keepdims=True)
    level = 1.0 / jnp.sqrt(power + 1e-06)
    out = jnp.concatenate(
        [(real_part * level).reshape(rows, NBAND), (imag_part * level).reshape(rows, NBAND)], axis=1
    )
    return out.astype(jnp.bfloat16)


def local(raw, send_blocks, pair_count):
    rows = lax.all_to_all(raw, "tm", split_axis=0, concat_axis=1, tiled=True)
    table = jnp.asarray(dft_table(), dtype=jnp.bfloat16)
    spectrum = jnp.dot(band_filter(rows), table, preferred_element_type=jnp.float32)
    blocks = rows.shape[0] // BLOCK
    whitened = whiten(spectrum).reshape(blocks, BLOCK, 2 * NBAND)
    peers = lax.axis_size("chan")
    width = send_blocks.shape[3]
    every, lists_all = (
        lax.all_gather(whitened, "chan", axis=0, tiled=True),
        lax.all_gather(send_blocks.astype(jnp.bfloat16), "chan", axis=0, tiled=True),
    )
    mine = lax.axis_index("chan")
    column = lax.dynamic_index_in_dim(lists_all[:, 0], mine, axis=1, keepdims=False)
    flat_ids = jnp.arange(peers, dtype=jnp.int32)[:, None] * blocks + column.astype(jnp.int32)
    picked = every[flat_ids]
    turned = jnp.concatenate([whitened[..., NBAND:], -whitened[..., :NBAND]], axis=-1)
    paired = jnp.stack([whitened, turned], axis=1)
    result = jnp.einsum("lrif,pkjf->pklrij", paired, picked, preferred_element_type=jnp.float32)
    result = result * (1.0 / math.sqrt(NBAND))
    live = jnp.arange(width, dtype=jnp.int32)[None, :] < pair_count[0, 0][:, None]
    result = jnp.where(live[:, :, None, None, None, None], result, 0.0)
    return result.astype(jnp.bfloat16)[None, None]


def solution(mesh):
    return jax.shard_map(
        local,
        mesh=mesh,
        in_specs=(P(("groups", "chan"), "tm"), P("chan", "tm", None, None), P("chan", "tm", None)),
        out_specs=P(("groups", "chan"), "tm", None, None, None, None, None, None),
        check_vma=False,
    )
```

profile of v0, /device:TPU:0, one launch (start us, length us, event | category | flops | bytes accessed | tf_op | source)
XLA Modules:
  0.0 150.9 jit_solution(17581047669316288742)
XLA Ops:
  6.5 0.0 all-gather.2.cloned.1.call-start
  6.5 18.7 %all_to_all.13 = bf16[4,256,512]{2,1,0:T(8,128)(2,1)S(1)} all-to-all(bf16[4,256,512]{2,1,0:T(8,128)(2,1)} %bitcast.81), channel_id=1, replica_groups=mesh['groups'=2,'chan'=4,'tm'=4] {'tm'}, dimensions={0} | all-to-all | bytes 2097152 | tf_op jit(solution)/shard_map/all_to_all | solution.py:66
  25.2 1.6 %convert_bitcast_fusion = f32[256,4,512]{2,0,1:T(8,128)} fusion(bf16[4,256,512]{2,1,0:T(8,128)(2,1)S(1)} %all_to_all.13), kind=kLoop, calls=%fused_computation.62 | loop fusion | flops 524288 | bytes 3145728 | tf_op jit(solution)/shard_map/convert_element_type | solution.py:46
  26.8 1.9 %copy.21 = f32[256,4,512]{0,2,1:T(8,128)S(1)} copy(f32[256,4,512]{2,0,1:T(8,128)} %convert_bitcast_fusion) | data formatting | bytes 4194304 | tf_op jit(solution)/shard_map/convert_element_type | solution.py:46
  28.8 2.3 %fusion.76 = (f32[256,2041]{0,1:T(8,128)}, f32[256,2041]{0,1:T(8,128)}) fusion(f32[256,2048]{0,1:T(8,128)S(1)} %bitcast.46), kind=kLoop, calls=%fused_computation.121 | loop fusion | bytes 8359936 | tf_op jit(solution)/shard_map/jit(_roll_static)/slice | solution.py:49
  31.1 2.3 %fusion.78 = (f32[256,2042]{0,1:T(8,128)}, f32[256,2042]{0,1:T(8,128)}) fusion(f32[256,2048]{0,1:T(8,128)S(1)} %bitcast.47), kind=kLoop, calls=%fused_computation.123 | loop fusion | bytes 8364032 | tf_op jit(solution)/shard_map/jit(_roll_static)/slice | solution.py:49
  33.4 2.3 %fusion.80 = (f32[256,2043]{0,1:T(8,128)}, f32[256,2043]{0,1:T(8,128)}) fusion(f32[256,2048]{0,1:T(8,128)S(1)} %bitcast.48), kind=kLoop, calls=%fused_computation.125 | loop fusion | bytes 8368128 | tf_op jit(solution)/shard_map/jit(_roll_static)/slice | solution.py:49
  35.7 2.3 %fusion.82 = (f32[256,2044]{0,1:T(8,128)}, f32[256,2044]{0,1:T(8,128)}) fusion(f32[256,2048]{0,1:T(8,128)S(1)} %bitcast.49), kind=kLoop, calls=%fused_computation.127 | loop fusion | bytes 8372224 | tf_op jit(solution)/shard_map/jit(_roll_static)/slice | solution.py:49
  38.0 2.3 %fusion.84 = (f32[256,2045]{0,1:T(8,128)}, f32[256,2045]{0,1:T(8,128)}) fusion(f32[256,2048]{0,1:T(8,128)S(1)} %bitcast.50), kind=kLoop, calls=%fused_computation.129 | loop fusion | bytes 8376320 | tf_op jit(solution)/shard_map/jit(_roll_static)/slice | solution.py:49
  40.3 2.3 %fusion.86 = (f32[256,2046]{0,1:T(8,128)}, f32[256,2046]{0,1:T(8,128)}) fusion(f32[256,2048]{0,1:T(8,128)S(1)} %bitcast.51), kind=kLoop, calls=%fused_computation.131 | loop fusion | bytes 8380416 | tf_op jit(solution)/shard_map/jit(_roll_static)/slice | solution.py:49
  42.6 2.3 %fusion.88 = (f32[256,2047]{0,1:T(8,128)}, f32[256,2047]{0,1:T(8,128)}) fusion(f32[256,2048]{0,1:T(8,128)S(1)} %bitcast.52), kind=kLoop, calls=%fused_computation.133 | loop fusion | bytes 8384512 | tf_op jit(solution)/shard_map/jit(_roll_static)/slice | solution.py:49
  44.9 2.3 %fusion.62 = (f32[256,2034]{0,1:T(8,128)}, f32[256,2034]{0,1:T(8,128)}) fusion(f32[256,2048]{0,1:T(8,128)S(1)} %bitcast.53), kind=kLoop, calls=%fused_computation.107 | loop fusion | bytes 8331264 | tf_op jit(solution)/shard_map/jit(_roll_static)/slice | solution.py:49
  47.2 2.3 %fusion.64 = (f32[256,2035]{0,1:T(8,128)}, f32[256,2035]{0,1:T(8,128)}) fusion(f32[256,2048]{0,1:T(8,128)S(1)} %bitcast.54), kind=kLoop, calls=%fused_computation.109 | loop fusion | bytes 8335360 | tf_op jit(solution)/shard_map/jit(_roll_static)/slice | solution.py:49
  49.5 2.3 %fusion.66 = (f32[256,2036]{0,1:T(8,128)}, f32[256,2036]{0,1:T(8,128)}) fusion(f32[256,2048]{0,1:T(8,128)S(1)} %bitcast.55), kind=kLoop, calls=%fused_computation.111 | loop fusion | bytes 8339456 | tf_op jit(solution)/shard_map/jit(_roll_static)/slice | solution.py:49
  51.8 2.3 %fusion.68 = (f32[256,2037]{0,1:T(8,128)}, f32[256,2037]{0,1:T(8,128)}) fusion(f32[256,2048]{0,1:T(8,128)S(1)} %bitcast.56), kind=kLoop, calls=%fused_computation.113 | loop fusion | bytes 8343552 | tf_op jit(solution)/shard_map/jit(_roll_static)/slice | solution.py:49
  54.1 2.3 %fusion.70 = (f32[256,2038]{0,1:T(8,128)}, f32[256,2038]{0,1:T(8,128)}) fusion(f32[256,2048]{0,1:T(8,128)S(1)} %bitcast.57), kind=kLoop, calls=%fused_computation.115 | loop fusion | bytes 8347648 | tf_op jit(solution)/shard_map/jit(_roll_static)/slice | solution.py:49
  56.3 2.3 %fusion.72 = (f32[256,2039]{0,1:T(8,128)}, f32[256,2039]{0,1:T(8,128)}) fusion(f32[256,2048]{0,1:T(8,128)S(1)} %bitcast.58), kind=kLoop, calls=%fused_computation.117 | loop fusion | bytes 8351744 | tf_op jit(solution)/shard_map/jit(_roll_static)/slice | solution.py:49
  58.6 2.2 %fusion.74 = (f32[256,2040]{0,1:T(8,128)}, f32[256,2040]{0,1:T(8,128)}) fusion(f32[256,2048]{0,1:T(8,128)S(1)} %bitcast.59), kind=kLoop, calls=%fused_computation.119 | loop fusion | bytes 8355840 | tf_op jit(solution)/shard_map/jit(_roll_static)/slice | solution.py:49
  60.8 2.3 %fusion.60 = (f32[256,2033]{0,1:T(8,128)}, f32[256,2033]{0,1:T(8,128)}) fusion(f32[256,2048]{0,1:T(8,128)S(1)} %bitcast.60), kind=kLoop, calls=%fused_computation.105 | loop fusion | bytes 8327168 | tf_op jit(solution)/shard_map/jit(_roll_static)/slice | solution.py:49
  63.3 27.8 %fusion.40 = f32[256,1024]{1,0:T(8,128)S(1)} fusion(bf16[2048,1024]{1,0:T(8,128)(2,1)} %constant.58.clone, f32[256,2038]{0,1:T(8,128)} %get-tuple-element.26, f32[256,10]{0,1:T(8,128)S(1)} %get-tuple-element.28, f32[256,2037]{0,1:T(8,128)} %get-tuple-element.22, f32[256,11]{0,1:T(8,128)S(1)} %get-tuple-element.24, f32[256,2036]{0,1:T(8,128)} %get-tuple-element.18, ...), kind=kOutput, calls=%fused_computation.74 | convolution fusion | flops 1121976320 | bytes 70254592 | tf_op jit(solution)/shard_map/dot_general | solution.py:68
  91.1 0.1 multiply_add_fusion
  91.2 0.2 copy.22
  91.6 0.2 copy.23
  91.8 0.0 copy-start
  91.8 0.0 copy-start.1
  91.8 0.2 multiply_convert_fusion
  92.0 0.9 pad_maximum_fusion
  92.9 0.0 all-gather.2.cloned.1.call-update
  93.0 0.0 copy-done
  93.0 11.8 %all_gather.7 = bf16[4,1,4,1]{2,3,1,0:T(2,128)(2,1)S(1)} all-gather(bf16[1,1,4,1]{2,3,1,0:T(2,128)(2,1)S(1)} %convert_element_type.49), channel_id=1, replica_groups=mesh['groups'=2,'chan'=4,'tm'=4] {'chan'}, dimensions={0}, use_global_device_ids=true | all-gather | bytes 40 | tf_op jit(solution)/shard_map/all_gather | solution.py:75
  104.8 0.2 convert_reduce_fusion
  105.1 0.0 copy-done.1
  105.1 35.0 %all-gather.2.cloned.1.call-done = bf16[8,128,1024]{2,1,0:T(8,128)(2,1)} async-done(((bf16[2,128,1024]{2,1,0:T(8,128)(2,1)}), bf16[8,128,1024]{2,1,0:T(8,128)(2,1)}) %all-gather.2.cloned.1.call-update) | async-done | bytes 2097168 | tf_op jit(solution)/shard_map/all_gather | solution.py:74
  140.1 2.2 %gather_fusion = bf16[4,128,1024]{2,1,0:T(8,128)(2,1)S(1)} fusion(bf16[8,128,1024]{2,1,0:T(8,128)(2,1)} %all-gather.2.cloned.1.call-done, s32[1024]{0:T(1024)S(1)} %pad_clamp_fusion), kind=kCustom, calls=%fused_computation | custom fusion | bytes 2097168 | tf_op jit(solution)/shard_map/gather | solution.py:80
  142.3 0.8 fusion.34
  143.1 1.0 copy.27
  (23 shorter events, 0.2 us)
Async XLA Ops:
  6.5 133.6 %all-gather.2.cloned.1.call-start = ((), (), s32[]{:S(2)}) async-start(), calls=%async_computation.1 | async-start | bytes 2621440 | tf_op jit(solution)/shard_map/all_gather | solution.py:74
  91.8 1.2 copy-start
  91.8 13.3 %copy-start.1 = (s32[1,1,4]{2,1,0:T(1,128)S(1)}, s32[1,1,4]{2,1,0:T(1,128)}, u32[]{:S(2)}) copy-start(s32[1,1,4]{2,1,0:T(1,128)} %param.6) | copy-start | bytes 52
Sparse Core Ops, SparseCore 0:
  93.1 46.9 all-gather.1
where the time goes:
time: 151 us
  local copies, waits for them, and re-layouts  40 us (26%)
  waiting for transfers between devices  35 us (23%)
  blocking collectives  30.5 us (20%)
  matrix products  28.6 us (19%)
  between operations  13.7 us (9%)
  other arithmetic  3.18 us (2%)
    all_gather x1, waiting for transfers between devices, local(): lax.all_gather(whitened, 'chan', axis=0, tiled=True)  35 us
    slice x30, local copies, waits for them, and re-layouts, band_filter(): jnp.roll(signal, index - RAD, axis=1)  34.4 us
    dot_general x1, matrix products, local(): jnp.dot(band_filter(rows), table, preferred_element_type=jnp.float32)  27.8 us
    all_to_all x1, blocking collectives, local(): rows = lax.all_to_all(raw, 'tm', split_axis=0, concat_axis=1, tiled=True)  18.7 us
    all_gather x1, blocking collectives, local(): lax.all_gather(send_blocks.astype(jnp.bfloat16), 'chan', axis=0, tiled=True)  11.8 us
  transfers between devices with their start and end apart: 1, of which 1 were waited for; matrix products, arithmetic and copies ran while one was open for 0% of the time, Pallas kernels for 0%

commit v1 on v0

v1 whole, which is shorter than its diff:
```python
import math

import jax
import jax.numpy as jnp
import ml_dtypes
import numpy as np
from jax import lax
from jax.experimental import pallas as pl
from jax.experimental.pallas import tpu as pltpu
from jax.sharding import PartitionSpec as P

BLOCK = 128
NT = 2048
F0 = 128
NBAND = 512
SUBW = 64
RAD = 15
TILE = 128
HALF = NT // 2
BF16 = ml_dtypes.bfloat16


def sinc_value(arg):
    if arg == 0:
        return 1.0
    return math.sin(math.pi * arg) / (math.pi * arg)


def filter_taps():
    low = F0 / NT
    high = (F0 + NBAND) / NT
    taps = []
    for offset in range(-RAD, RAD + 1):
        value = 2.0 * high * sinc_value(2.0 * high * offset) - 2.0 * low * sinc_value(
            2.0 * low * offset
        )
        value = value * (0.5 + 0.5 * math.cos(math.pi * offset / (RAD + 1)))
        taps.append(value)
    return taps


def dft_top():
    samples = np.arange(HALF)[:, None]
    freqs = np.arange(F0, F0 + NBAND)[None, :]
    phase = samples * freqs % NT
    angle = 2.0 * np.pi * phase / NT
    return np.concatenate([np.cos(angle), -np.sin(angle)], axis=1).astype(BF16)


def band_matrix():
    taps = np.asarray(filter_taps(), np.float32)
    band = np.zeros((3 * TILE, TILE), np.float32)
    for v in range(3 * TILE):
        for u in range(TILE):
            k = TILE + u - v
            if abs(k) <= RAD:
                band[v, u] = taps[k + RAD]
    hi = band.astype(BF16)
    lo = (band - hi.astype(np.float32)).astype(BF16)
    return np.concatenate([hi, lo], axis=1)


def group_matrix():
    g = np.arange(NBAND) // SUBW
    return ((g[:, None] == g[None, :]).astype(np.float32) / SUBW).astype(BF16)


def spectra_kernel(x_ref, band_ref, tab_ref, grp_ref, o_ref, filt_ref):
    width = x_ref.shape[2]
    ntile = NT // TILE

    def tile(j):
        chunk, off = divmod((j % ntile) * TILE, width)
        return x_ref[chunk, :, off:off + TILE]

    band = band_ref[...]
    for j in range(ntile):
        win = jnp.concatenate([tile(j - 1), tile(j), tile(j + 1)], axis=1)
        acc = jnp.dot(win, band, preferred_element_type=jnp.float32)
        filt_ref[:, j * TILE:(j + 1) * TILE] = (acc[:, :TILE] + acc[:, TILE:]).astype(jnp.bfloat16)
    tab = tab_ref[...]
    first = jnp.dot(filt_ref[:, :HALF], tab, preferred_element_type=jnp.float32)
    second = jnp.dot(filt_ref[:, HALF:], tab, preferred_element_type=jnp.float32)
    lane = lax.broadcasted_iota(jnp.int32, first.shape, 1)
    spec = jnp.where(lane % 2 == 0, first + second, first - second)
    re = spec[:, :NBAND]
    im = spec[:, NBAND:]
    power = re * re + im * im
    p_hi = power.astype(jnp.bfloat16)
    p_lo = (power - p_hi.astype(jnp.float32)).astype(jnp.bfloat16)
    grp = grp_ref[...]
    mean = jnp.dot(p_hi, grp, preferred_element_type=jnp.float32) + jnp.dot(
        p_lo, grp, preferred_element_type=jnp.float32
    )
    level = 1.0 / jnp.sqrt(mean + 1e-06)
    o_ref[:, :NBAND] = (re * level).astype(jnp.bfloat16)
    o_ref[:, NBAND:] = (im * level).astype(jnp.bfloat16)


def spectra(rows3):
    ntm, nrows, width = rows3.shape
    band = jnp.asarray(band_matrix())
    tab = jnp.asarray(dft_top())
    grp = jnp.asarray(group_matrix())
    return pl.pallas_call(
        spectra_kernel,
        grid=(nrows // BLOCK,),
        in_specs=[
            pl.BlockSpec((ntm, BLOCK, width), lambda r: (0, r, 0)),
            pl.BlockSpec(band.shape, lambda r: (0, 0)),
            pl.BlockSpec(tab.shape, lambda r: (0, 0)),
            pl.BlockSpec(grp.shape, lambda r: (0, 0)),
        ],
        out_specs=pl.BlockSpec((BLOCK, 2 * NBAND), lambda r: (r, 0)),
        out_shape=jax.ShapeDtypeStruct((nrows, 2 * NBAND), jnp.bfloat16),
        scratch_shapes=[pltpu.VMEM((BLOCK, NT), jnp.bfloat16)],
    )(rows3, band, tab, grp)


def local(raw, send_blocks, pair_count):
    ntm = lax.axis_size("tm")
    nch, width = raw.shape
    rows3 = lax.all_to_all(raw.reshape(ntm, nch // ntm, width), "tm", 0, 0, tiled=True)
    whitened = spectra(rows3)
    blocks = whitened.shape[0] // BLOCK
    whitened = whitened.reshape(blocks, BLOCK, 2 * NBAND)

    peers = lax.axis_size("chan")
    mine = lax.axis_index("chan")
    cap = send_blocks.shape[3]
    ids = send_blocks[0, 0]
    recv = []
    for d in range(peers):
        dest = (mine + d) % peers
        row = []
        for k in range(cap):
            blk = lax.dynamic_index_in_dim(whitened, ids[dest, k], axis=0, keepdims=False)
            if d:
                blk = lax.ppermute(blk, "chan", perm=[(i, (i + d) % peers) for i in range(peers)])
            row.append(blk)
        recv.append(jnp.stack(row))
    picked = jnp.stack(recv)
    turned = jnp.concatenate([whitened[..., NBAND:], -whitened[..., :NBAND]], axis=-1)
    paired = jnp.stack([whitened, turned], axis=1)
    result = jnp.einsum("lrif,dkjf->dklrij", paired, picked, preferred_element_type=jnp.float32)
    order = (mine - jnp.arange(peers, dtype=jnp.int32)) % peers
    result = jnp.take(result, order, axis=0)
    result = result * (1.0 / math.sqrt(NBAND))
    live = jnp.arange(cap, dtype=jnp.int32)[None, :] < pair_count[0, 0][:, None]
    result = jnp.where(live[:, :, None, None, None, None], result, 0.0)
    return result.astype(jnp.bfloat16)[None, None]


def solution(mesh):
    return jax.shard_map(
        local,
        mesh=mesh,
        in_specs=(P(("groups", "chan"), "tm"), P("chan", "tm", None, None), P("chan", "tm", None)),
        out_specs=P(("groups", "chan"), "tm", None, None, None, None, None, None),
        check_vma=False,
    )
```

time: 151 us -> 55.1 us (0.36)
  the two profiles are of different devices: /device:TPU:0 before, /device:TPU:17 now
where the time goes in v1:
time: 55.1 us; the launch traced here: 54.8 us
  waiting for transfers between devices  28.9 us (52%)
  between operations  7.48 us (14%)
  starting transfers between devices  6.87 us (12%)
  Pallas kernels  5.91 us (11%)
  local copies, waits for them, and re-layouts  4.57 us (8%)
  matrix products  0.74 us (1%)
    ppermute x3, waiting for transfers between devices, local(): lax.ppermute(blk, 'chan', perm=[(i, (i + d) % peers) for i in range(peers)])  23.4 us
    pallas_call x1, Pallas kernels, spectra(): pl.pallas_call(spectra_kernel, grid=(nrows // BLOCK,), in_specs=[pl.Block...  5.91 us
    all_to_all x1, waiting for transfers between devices, local(): lax.all_to_all(raw.reshape(ntm, nch // ntm, width), 'tm', 0, 0, tiled=True)  5.48 us
    all_to_all x1, starting transfers between devices, local(): lax.all_to_all(raw.reshape(ntm, nch // ntm, width), 'tm', 0, 0, tiled=True)  4.29 us
    ppermute x3, starting transfers between devices, local(): lax.ppermute(blk, 'chan', perm=[(i, (i + d) % peers) for i in range(peers)])  2.59 us
    another operation x1, local copies, waits for them, and re-layouts, local(): picked = jnp.stack(recv)  1.31 us
  transfers between devices with their start and end apart: 4, of which 4 were waited for; matrix products, arithmetic and copies ran while one was open for 1% of the time, Pallas kernels for 0%

profile of v1, /device:TPU:17, one launch (start us, length us, event | category | flops | bytes accessed | tf_op | source)
XLA Modules:
  0.0 54.8 jit_solution(1716554369135168992)
XLA Ops:
  0.0 0.0 copy-start.2
  0.0 0.0 copy-start.3
  0.0 4.3 %all-to-all-start = ((bf16[4,256,512]{2,1,0:T(8,128)(2,1)}), bf16[4,256,512]{2,1,0:T(8,128)(2,1)S(1)}, u32[]{:S(2)}, u32[]{:S(2)}) async-start(bf16[4,256,512]{2,1,0:T(8,128)(2,1)} %bitcast.53), calls=%async_computation | async-start | bytes 2097152 | tf_op jit(solution)/shard_map/all_to_all | solution.py:123
  4.3 0.0 copy-done.2
  4.3 0.6 %constant_dynamic-slice_fusion.3 = (s32[1,1,1,1]{2,3,1,0:T(1,128)}, s32[1,1,1,1]{2,3,1,0:T(1,128)}, s32[1,1,1,1]{2,3,1,0:T(1,128)}, s32[1,1,1,1]{2,3,1,0:T(1,128)}) fusion(s32[1,1,4,1]{2,3,1,0:T(1,128)S(1)} %copy-done.2, s32[]{:T(128)S(6)} %select_n.106, s32[]{:T(128)S(6)} %select_n.109, s32[]{:T(128)S(6)} %select_n.115, s32[]{:T(128)S(6)} %select_n.112), kind=kLoop, calls=%fused_computation.32 | loop fusion | bytes 48 | tf_op jit(solution)/shard_map/dynamic_slice | solution.py:137
  12.4 0.0 copy-done.3
  12.4 5.5 %all-to-all-done.x_ref = bf16[4,256,512]{2,1,0:T(8,128)(2,1)S(1)} async-done(((bf16[4,256,512]{2,1,0:T(8,128)(2,1)}), bf16[4,256,512]{2,1,0:T(8,128)(2,1)S(1)}, u32[]{:S(2)}, u32[]{:S(2)}) %all-to-all-start) | async-done | bytes 1048608 | tf_op jit(solution)/shard_map/all_to_all | solution.py:123
  17.9 0.0 copy-start.1
  17.9 1.0 %copy-done.1 = bf16[4,256,512]{2,1,0:T(8,128)(2,1)} copy-done((bf16[4,256,512]{2,1,0:T(8,128)(2,1)}, bf16[4,256,512]{2,1,0:T(8,128)(2,1)S(1)}, u32[]{:S(2)}) %copy-start.1) | copy-done | bytes 1048600
  18.9 5.9 %shard_map.64 = bf16[256,1024]{1,0:T(8,128)(2,1)} custom-call(bf16[4,256,512]{2,1,0:T(8,128)(2,1)} %copy-done.1, bf16[384,256]{1,0:T(8,128)(2,1)} %constant.84.clone.band_ref, bf16[1024,1024]{1,0:T(8,128)(2,1)} %constant.85.clone.tab_ref, bf16[512,512]{1,0:T(8,128)(2,1)} %constant.86.clone.grp_ref), custom_call_target="tpu_custom_call" | custom-call | tf_op jit(solution)/shard_map/pallas_call | solution.py:105
  24.8 0.0 copy-start
  24.8 1.3 %dynamic-slice_bitcast_fusion.3 = (bf16[1,1,128,1024]{3,2,0,1:T(8,128)(2,1)S(1)}, bf16[128,1024]{1,0:T(8,128)(2,1)S(1)}, bf16[128,1024]{1,0:T(8,128)(2,1)S(1)}, bf16[128,1024]{1,0:T(8,128)(2,1)S(1)}) fusion(bf16[2,128,1024]{2,1,0:T(8,128)(2,1)} %bitcast.50, s32[]{:T(128)S(6)} %select_n.107, s32[]{:T(128)S(6)} %select_n.116, s32[]{:T(128)S(6)} %select_n.113, ...), kind=kLoop, calls=%fused_computation.21 | loop fusion | bytes 2097168 | tf_op jit(solution)/shard_map/stack;stack | solution.py:142
  26.1 0.1 collective-permute-start.1
  26.2 2.5 %collective-permute-start.2 = (bf16[128,1024]{1,0:T(8,128)(2,1)S(1)}, bf16[128,1024]{1,0:T(8,128)(2,1)S(1)}, u32[]{:S(2)}, u32[]{:S(2)}) collective-permute-start(bf16[128,1024]{1,0:T(8,128)(2,1)S(1)} %get-tuple-element.8), channel_id=1, source_target_pairs={{0,12},{4,0},{8,4},{12,8},{1,13},{5,1},{9,5},{13,9},{2,14},{6,2},{... | collective-permute-start | bytes 786440 | tf_op jit(solution)/shard_map/ppermute | solution.py:139
  28.7 0.0 collective-permute-start
  28.7 0.0 copy-done
  28.7 0.1 maximum_bitcast_fusion.4
  28.8 8.1 %collective-permute-done.1 = bf16[128,1024]{1,0:T(8,128)(2,1)S(1)} collective-permute-done((bf16[128,1024]{1,0:T(8,128)(2,1)S(1)}, bf16[128,1024]{1,0:T(8,128)(2,1)S(1)}, u32[]{:S(2)}, u32[]{:S(2)}) %collective-permute-start.1) | collective-permute-done | bytes 262176 | tf_op jit(solution)/shard_map/ppermute | solution.py:139
  36.9 11.2 %collective-permute-done.2 = bf16[128,1024]{1,0:T(8,128)(2,1)S(1)} collective-permute-done((bf16[128,1024]{1,0:T(8,128)(2,1)S(1)}, bf16[128,1024]{1,0:T(8,128)(2,1)S(1)}, u32[]{:S(2)}, u32[]{:S(2)}) %collective-permute-start.2) | collective-permute-done | bytes 262176 | tf_op jit(solution)/shard_map/ppermute | solution.py:139
  48.1 4.1 %collective-permute-done = bf16[128,1024]{1,0:T(8,128)(2,1)S(1)} collective-permute-done((bf16[128,1024]{1,0:T(8,128)(2,1)S(1)}, bf16[128,1024]{1,0:T(8,128)(2,1)S(1)}, u32[]{:S(2)}, u32[]{:S(2)}) %collective-permute-start) | collective-permute-done | bytes 262176 | tf_op jit(solution)/shard_map/ppermute | solution.py:139
  52.2 0.7 %convolution_bitcast_fusion = f32[4,2,2,128,128]{3,4,2,1,0:T(8,128)S(1)} fusion(bf16[1,1,128,1024]{3,2,0,1:T(8,128)(2,1)S(1)} %bitcast.55, bf16[1,1,128,1024]{3,2,0,1:T(8,128)(2,1)S(1)} %bitcast.54, bf16[1,1,128,1024]{3,2,0,1:T(8,128)(2,1)S(1)} %bitcast.56, bf16[1,1,128,1024]{3,2,0,1:T(8,128)(2,1)S(1)} %get-tuple-element.7, ...), kind=kOutput, calls=%fused_computation.1 | convolution fusion | flops 543162368 | bytes 3145728 | tf_op jit(solution)/shard_map/lrif,dkjf->dklrij/dot_general | solution.py:145
  52.9 0.6 %gather_fusion = f32[4,2,2,128,128]{3,4,2,1,0:T(8,128)S(1)} fusion(f32[4,2,2,128,128]{3,4,2,1,0:T(8,128)S(1)} %convolution_bitcast_fusion, s32[1024]{0:T(1024)S(1)} %pad_clamp_fusion), kind=kCustom, calls=%fused_computation | custom fusion | bytes 2097168 | tf_op jit(solution)/shard_map/jit(_take)/gather | solution.py:147
  53.6 0.2 fusion.10
  53.8 1.0 %copy.8 = bf16[1,1,4,1,2,2,128,128]{7,6,5,4,3,2,1,0:T(8,128)(2,1)} copy(bf16[1,1,4,1,2,2,128,128]{6,7,5,4,2,3,1,0:T(8,128)(2,1)S(1)} %fusion.10) | data formatting | bytes 1048576 | tf_op jit(solution)/shard_map/convert_element_type | solution.py:151
  (5 shorter events, 0.1 us)
Async XLA Ops:
  0.0 4.3 %copy-start.2 = (s32[1,1,4,1]{2,3,1,0:T(1,128)S(1)}, s32[1,1,4,1]{2,3,1,0:T(1,128)}, u32[]{:S(2)}) copy-start(s32[1,1,4,1]{2,3,1,0:T(1,128)} %param.7) | copy-start | bytes 52
  0.0 12.4 %copy-start.3 = (s32[1,1,4]{2,1,0:T(1,128)S(1)}, s32[1,1,4]{2,1,0:T(1,128)}, u32[]{:S(2)}) copy-start(s32[1,1,4]{2,1,0:T(1,128)} %param.8) | copy-start | bytes 52
  0.0 17.9 %all-to-all-start = ((bf16[4,256,512]{2,1,0:T(8,128)(2,1)}), bf16[4,256,512]{2,1,0:T(8,128)(2,1)S(1)}, u32[]{:S(2)}, u32[]{:S(2)}) async-start(bf16[4,256,512]{2,1,0:T(8,128)(2,1)} %bitcast.53), calls=%async_computation | async-start | bytes 2097152 | tf_op jit(solution)/shard_map/all_to_all | solution.py:123
  17.9 1.0 %copy-start.1 = (bf16[4,256,512]{2,1,0:T(8,128)(2,1)}, bf16[4,256,512]{2,1,0:T(8,128)(2,1)S(1)}, u32[]{:S(2)}) copy-start(bf16[4,256,512]{2,1,0:T(8,128)(2,1)S(1)} %all-to-all-done.x_ref) | copy-start | bytes 3145732
  24.8 3.9 %copy-start = (bf16[256,1024]{1,0:T(8,128)(2,1)S(1)}, bf16[256,1024]{1,0:T(8,128)(2,1)}, u32[]{:S(2)}) copy-start(bf16[256,1024]{1,0:T(8,128)(2,1)} %shard_map.64) | copy-start | bytes 1572868
  26.1 10.8 %collective-permute-start.1 = (bf16[128,1024]{1,0:T(8,128)(2,1)S(1)}, bf16[128,1024]{1,0:T(8,128)(2,1)S(1)}, u32[]{:S(2)}, u32[]{:S(2)}) collective-permute-start(bf16[128,1024]{1,0:T(8,128)(2,1)S(1)} %get-tuple-element.9), channel_id=1, source_target_pairs={{0,8},{4,12},{8,0},{12,4},{1,9},{5,13},{9,1},{13,5},{2,10},{6,14},... | collective-permute-start | bytes 786440 | tf_op jit(solution)/shard_map/ppermute | solution.py:139
  26.2 22.0 %collective-permute-start.2 = (bf16[128,1024]{1,0:T(8,128)(2,1)S(1)}, bf16[128,1024]{1,0:T(8,128)(2,1)S(1)}, u32[]{:S(2)}, u32[]{:S(2)}) collective-permute-start(bf16[128,1024]{1,0:T(8,128)(2,1)S(1)} %get-tuple-element.8), channel_id=1, source_target_pairs={{0,12},{4,0},{8,4},{12,8},{1,13},{5,1},{9,5},{13,9},{2,14},{6,2},{... | collective-permute-start | bytes 786440 | tf_op jit(solution)/shard_map/ppermute | solution.py:139
  28.7 23.5 %collective-permute-start = (bf16[128,1024]{1,0:T(8,128)(2,1)S(1)}, bf16[128,1024]{1,0:T(8,128)(2,1)S(1)}, u32[]{:S(2)}, u32[]{:S(2)}) collective-permute-start(bf16[128,1024]{1,0:T(8,128)(2,1)S(1)} %get-tuple-element.10), channel_id=1, source_target_pairs={{0,4},{4,8},{8,12},{12,0},{1,5},{5,9},{9,13},{13,1},{2,6},{6,10},{... | collective-permute-start | bytes 786440 | tf_op jit(solution)/shard_map/ppermute | solution.py:139

commit v2 on v1

--- a/solution.py
+++ b/solution.py
@@ -65,13 +65,14 @@
     return ((g[:, None] == g[None, :]).astype(np.float32) / SUBW).astype(BF16)
 
 
-def spectra_kernel(x_ref, band_ref, tab_ref, grp_ref, o_ref, filt_ref):
-    width = x_ref.shape[2]
+def spectra_kernel(pos_ref, x_ref, band_ref, tab_ref, grp_ref, o_ref, filt_ref):
+    nslot, _, width = x_ref.shape
     ntile = NT // TILE
+    pos = pos_ref[0]
 
     def tile(j):
         chunk, off = divmod((j % ntile) * TILE, width)
-        return x_ref[chunk, :, off:off + TILE]
+        return x_ref[(pos - chunk + nslot) % nslot, :, off:off + TILE]
 
     band = band_ref[...]
     for j in range(ntile):
@@ -97,31 +98,41 @@
     o_ref[:, NBAND:] = (im * level).astype(jnp.bfloat16)
 
 
-def spectra(rows3):
+def spectra(pos, rows3):
     ntm, nrows, width = rows3.shape
     band = jnp.asarray(band_matrix())
     tab = jnp.asarray(dft_top())
     grp = jnp.asarray(group_matrix())
+    grid_spec = pltpu.PrefetchScalarGridSpec(
+        num_scalar_prefetch=1,
+        grid=(nrows // BLOCK,),
+        in_specs=[
+            pl.BlockSpec((ntm, BLOCK, width), lambda r, p: (0, r, 0)),
+            pl.BlockSpec(band.shape, lambda r, p: (0, 0)),
+            pl.BlockSpec(tab.shape, lambda r, p: (0, 0)),
+            pl.BlockSpec(grp.shape, lambda r, p: (0, 0)),
+        ],
+        out_specs=pl.BlockSpec((BLOCK, 2 * NBAND), lambda r, p: (r, 0)),
+        scratch_shapes=[pltpu.VMEM((BLOCK, NT), jnp.bfloat16)],
+    )
     return pl.pallas_call(
         spectra_kernel,
-        grid=(nrows // BLOCK,),
-        in_specs=[
-            pl.BlockSpec((ntm, BLOCK, width), lambda r: (0, r, 0)),
-            pl.BlockSpec(band.shape, lambda r: (0, 0)),
-            pl.BlockSpec(tab.shape, lambda r: (0, 0)),
-            pl.BlockSpec(grp.shape, lambda r: (0, 0)),
-        ],
-        out_specs=pl.BlockSpec((BLOCK, 2 * NBAND), lambda r: (r, 0)),
+        grid_spec=grid_spec,
         out_shape=jax.ShapeDtypeStruct((nrows, 2 * NBAND), jnp.bfloat16),
-        scratch_shapes=[pltpu.VMEM((BLOCK, NT), jnp.bfloat16)],
-    )(rows3, band, tab, grp)
+    )(pos, rows3, band, tab, grp)
 
 
 def local(raw, send_blocks, pair_count):
     ntm = lax.axis_size("tm")
     nch, width = raw.shape
-    rows3 = lax.all_to_all(raw.reshape(ntm, nch // ntm, width), "tm", 0, 0, tiled=True)
-    whitened = spectra(rows3)
+    here = lax.axis_index("tm")
+    parts = raw.reshape(ntm, nch // ntm, width)
+    slots = [lax.dynamic_index_in_dim(parts, here, axis=0, keepdims=False)]
+    for d in range(1, ntm):
+        piece = lax.dynamic_index_in_dim(parts, (here + d) % ntm, axis=0, keepdims=False)
+        slots.append(lax.ppermute(piece, "tm", perm=[(i, (i + d) % ntm) for i in range(ntm)]))
+    rows3 = jnp.stack(slots)
+    whitened = spectra(here.astype(jnp.int32).reshape(1), rows3)
     blocks = whitened.shape[0] // BLOCK
     whitened = whitened.reshape(blocks, BLOCK, 2 * NBAND)
 

time: 55.1 us -> 52.9 us (0.960)
  the two profiles are of different devices: /device:TPU:17 before, /device:TPU:9 now
where the time goes in v2:
time: 52.9 us; the launch traced here: 52.6 us
  waiting for transfers between devices  25.9 us (49%)
  between operations  7.56 us (14%)
  starting transfers between devices  6.16 us (12%)
  Pallas kernels  5.9 us (11%)
  local copies, waits for them, and re-layouts  4.86 us (9%)
  other arithmetic  1.48 us (3%)
  matrix products  0.74 us (1%)
    ppermute x3, waiting for transfers between devices, local(): lax.ppermute(blk, 'chan', perm=[(i, (i + d) % peers) for i in range(peers)])  22.1 us
    pallas_call x1, Pallas kernels, spectra(): pl.pallas_call(spectra_kernel, grid_spec=grid_spec, out_shape=jax.ShapeDt...  5.9 us
    ppermute x3, starting transfers between devices, local(): lax.ppermute(blk, 'chan', perm=[(i, (i + d) % peers) for i in range(peers)])  3.87 us
    ppermute x3, waiting for transfers between devices, local(): lax.ppermute(piece, 'tm', perm=[(i, (i + d) % ntm) for i in range(ntm)])  3.77 us
    ppermute x3, starting transfers between devices, local(): lax.ppermute(piece, 'tm', perm=[(i, (i + d) % ntm) for i in range(ntm)])  2.3 us
    another operation x1, local copies, waits for them, and re-layouts, local(): picked = jnp.stack(recv)  1.31 us
    dynamic_slice x1, local copies, waits for them, and re-layouts, local(): slots = [lax.dynamic_index_in_dim(parts, here, axis=0, keepdims=False)]  1.28 us
    another operation x1, other arithmetic, local(): rows3 = jnp.stack(slots)  1.11 us
  transfers between devices with their start and end apart: 6, of which 5 were waited for; matrix products, arithmetic and copies ran while one was open for 1% of the time, Pallas kernels for 0%

profile of v2, /device:TPU:9, one launch (start us, length us, event | category | flops | bytes accessed | tf_op | source)
XLA Modules:
  0.0 52.6 jit_solution(17764416420122669957)
XLA Ops:
  0.0 0.0 copy-start.1
  0.0 0.0 copy-start.2
  0.0 1.3 %constant_dynamic-slice_fusion.4 = (bf16[1,256,512]{2,1,0:T(8,128)(2,1)S(1)}, bf16[256,512]{1,0:T(8,128)(2,1)S(1)}, bf16[256,512]{1,0:T(8,128)(2,1)S(1)}, bf16[256,512]{1,0:T(8,128)(2,1)S(1)}) fusion(bf16[4,256,512]{2,1,0:T(8,128)(2,1)} %bitcast.63, s32[]{:T(128)S(6)} %select_n.130, s32[]{:T(128)S(6)} %select_n.136, s32[]{:T(128)S(6)} %select_n.134, ...), kind=kLoop, calls=%fused_computation.31 | loop fusion | bytes 2097168 | tf_op jit(solution)/shard_map/jit(dynamic_index_in_dim)/dynamic_slice | solution.py:130
  1.3 1.8 %collective-permute-start = (bf16[256,512]{1,0:T(8,128)(2,1)S(1)}, bf16[256,512]{1,0:T(8,128)(2,1)S(1)}, u32[]{:S(2)}, u32[]{:S(2)}) collective-permute-start(bf16[256,512]{1,0:T(8,128)(2,1)S(1)} %get-tuple-element.8), channel_id=1, source_target_pairs={{0,1},{1,2},{2,3},{3,0},{4,5},{5,6},{6,7},{7,4},{8,9},{9,10},{10,1... | collective-permute-start | bytes 786440 | tf_op jit(solution)/shard_map/ppermute | solution.py:133
  3.1 0.3 collective-permute-start.1
  3.4 0.2 collective-permute-start.2
  3.7 0.0 copy-done.1
  3.7 0.6 %constant_dynamic-slice_fusion.3 = (s32[1,1,1,1]{2,3,1,0:T(1,128)}, s32[1,1,1,1]{2,3,1,0:T(1,128)}, s32[1,1,1,1]{2,3,1,0:T(1,128)}, s32[1,1,1,1]{2,3,1,0:T(1,128)}) fusion(s32[1,1,4,1]{2,3,1,0:T(1,128)S(1)} %copy-done.1, s32[]{:T(128)S(6)} %select_n.138, s32[]{:T(128)S(6)} %select_n.141, s32[]{:T(128)S(6)} %select_n.147, s32[]{:T(128)S(6)} %select_n.144), kind=kLoop, calls=%fused_computation.30 | loop fusion | bytes 48 | tf_op jit(solution)/shard_map/dynamic_slice | solution.py:148
  11.7 0.0 copy-done.2
  11.8 0.0 collective-permute-done
  11.8 3.2 %collective-permute-done.1 = bf16[256,512]{1,0:T(8,128)(2,1)S(1)} collective-permute-done((bf16[256,512]{1,0:T(8,128)(2,1)S(1)}, bf16[256,512]{1,0:T(8,128)(2,1)S(1)}, u32[]{:S(2)}, u32[]{:S(2)}) %collective-permute-start.1) | collective-permute-done | bytes 262176 | tf_op jit(solution)/shard_map/ppermute | solution.py:133
  14.9 0.6 %collective-permute-done.2 = bf16[256,512]{1,0:T(8,128)(2,1)S(1)} collective-permute-done((bf16[256,512]{1,0:T(8,128)(2,1)S(1)}, bf16[256,512]{1,0:T(8,128)(2,1)S(1)}, u32[]{:S(2)}, u32[]{:S(2)}) %collective-permute-start.2) | collective-permute-done | bytes 262176 | tf_op jit(solution)/shard_map/ppermute | solution.py:133
  15.6 1.1 %pad_maximum_fusion.x_ref = bf16[4,256,512]{2,1,0:T(8,128)(2,1)} fusion(bf16[1,256,512]{2,1,0:T(8,128)(2,1)S(1)} %bitcast.66, bf16[1,256,512]{2,1,0:T(8,128)(2,1)S(1)} %bitcast.65, bf16[1,256,512]{2,1,0:T(8,128)(2,1)S(1)} %bitcast.64, bf16[1,256,512]{2,1,0:T(8,128)(2,1)S(1)} %get-tuple-element.5), kind=kLoop, calls=%fused_computation.2 | loop fusion | flops 1572864 | bytes 2097152 | tf_op jit(solution)/shard_map/stack | solution.py:134
  16.7 5.9 %shard_map.64 = bf16[256,1024]{1,0:T(8,128)(2,1)} custom-call(s32[1]{0:T(128)} %bitcast.1.pos_ref, bf16[4,256,512]{2,1,0:T(8,128)(2,1)} %pad_maximum_fusion.x_ref, bf16[384,256]{1,0:T(8,128)(2,1)} %constant.108.clone.band_ref, bf16[1024,1024]{1,0:T(8,128)(2,1)} %constant.109.clone.tab_ref, bf16[512,512]{1,0:T(8,128)(2,1)} %constant.110.clone.grp_ref), custom_call_target="tpu_custom_call" | custom-call | tf_op jit(solution)/shard_map/pallas_call | solution.py:118
  22.6 0.0 copy-start
  22.6 1.3 %dynamic-slice_bitcast_fusion.3 = (bf16[1,1,128,1024]{3,2,0,1:T(8,128)(2,1)S(1)}, bf16[128,1024]{1,0:T(8,128)(2,1)S(1)}, bf16[128,1024]{1,0:T(8,128)(2,1)S(1)}, bf16[128,1024]{1,0:T(8,128)(2,1)S(1)}) fusion(bf16[2,128,1024]{2,1,0:T(8,128)(2,1)} %bitcast.60, s32[]{:T(128)S(6)} %select_n.139, s32[]{:T(128)S(6)} %select_n.148, s32[]{:T(128)S(6)} %select_n.145, ...), kind=kLoop, calls=%fused_computation.22 | loop fusion | bytes 2097168 | tf_op jit(solution)/shard_map/stack;stack | solution.py:153
  23.9 1.3 %collective-permute-start.3 = (bf16[128,1024]{1,0:T(8,128)(2,1)S(1)}, bf16[128,1024]{1,0:T(8,128)(2,1)S(1)}, u32[]{:S(2)}, u32[]{:S(2)}) collective-permute-start(bf16[128,1024]{1,0:T(8,128)(2,1)S(1)} %get-tuple-element.14), channel_id=1, source_target_pairs={{0,4},{4,8},{8,12},{12,0},{1,5},{5,9},{9,13},{13,1},{2,6},{6,10},{... | collective-permute-start | bytes 786440 | tf_op jit(solution)/shard_map/ppermute | solution.py:150
  25.2 1.1 %collective-permute-start.4 = (bf16[128,1024]{1,0:T(8,128)(2,1)S(1)}, bf16[128,1024]{1,0:T(8,128)(2,1)S(1)}, u32[]{:S(2)}, u32[]{:S(2)}) collective-permute-start(bf16[128,1024]{1,0:T(8,128)(2,1)S(1)} %get-tuple-element.13), channel_id=1, source_target_pairs={{0,8},{4,12},{8,0},{12,4},{1,9},{5,13},{9,1},{13,5},{2,10},{6,14},... | collective-permute-start | bytes 786440 | tf_op jit(solution)/shard_map/ppermute | solution.py:150
  26.4 1.4 %collective-permute-start.5 = (bf16[128,1024]{1,0:T(8,128)(2,1)S(1)}, bf16[128,1024]{1,0:T(8,128)(2,1)S(1)}, u32[]{:S(2)}, u32[]{:S(2)}) collective-permute-start(bf16[128,1024]{1,0:T(8,128)(2,1)S(1)} %get-tuple-element.12), channel_id=1, source_target_pairs={{0,12},{4,0},{8,4},{12,8},{1,13},{5,1},{9,5},{13,9},{2,14},{6,2},{... | collective-permute-start | bytes 786440 | tf_op jit(solution)/shard_map/ppermute | solution.py:150
  27.7 0.0 copy-done
  27.8 0.1 maximum_bitcast_fusion.4
  27.9 4.2 %collective-permute-done.3 = bf16[128,1024]{1,0:T(8,128)(2,1)S(1)} collective-permute-done((bf16[128,1024]{1,0:T(8,128)(2,1)S(1)}, bf16[128,1024]{1,0:T(8,128)(2,1)S(1)}, u32[]{:S(2)}, u32[]{:S(2)}) %collective-permute-start.3) | collective-permute-done | bytes 262176 | tf_op jit(solution)/shard_map/ppermute | solution.py:150
  32.1 15.9 %collective-permute-done.4 = bf16[128,1024]{1,0:T(8,128)(2,1)S(1)} collective-permute-done((bf16[128,1024]{1,0:T(8,128)(2,1)S(1)}, bf16[128,1024]{1,0:T(8,128)(2,1)S(1)}, u32[]{:S(2)}, u32[]{:S(2)}) %collective-permute-start.4) | collective-permute-done | bytes 262176 | tf_op jit(solution)/shard_map/ppermute | solution.py:150
  48.0 2.0 %collective-permute-done.5 = bf16[128,1024]{1,0:T(8,128)(2,1)S(1)} collective-permute-done((bf16[128,1024]{1,0:T(8,128)(2,1)S(1)}, bf16[128,1024]{1,0:T(8,128)(2,1)S(1)}, u32[]{:S(2)}, u32[]{:S(2)}) %collective-permute-start.5) | collective-permute-done | bytes 262176 | tf_op jit(solution)/shard_map/ppermute | solution.py:150
  50.0 0.7 %convolution_bitcast_fusion = f32[4,2,2,128,128]{3,4,2,1,0:T(8,128)S(1)} fusion(bf16[1,1,128,1024]{3,2,0,1:T(8,128)(2,1)S(1)} %bitcast.69, bf16[1,1,128,1024]{3,2,0,1:T(8,128)(2,1)S(1)} %bitcast.68, bf16[1,1,128,1024]{3,2,0,1:T(8,128)(2,1)S(1)} %bitcast.67, bf16[1,1,128,1024]{3,2,0,1:T(8,128)(2,1)S(1)} %get-tuple-element.11, ...), kind=kOutput, calls=%fused_computation.1 | convolution fusion | flops 543162368 | bytes 3145728 | tf_op jit(solution)/shard_map/lrif,dkjf->dklrij/dot_general | solution.py:156
  50.7 0.6 %gather_fusion = f32[4,2,2,128,128]{3,4,2,1,0:T(8,128)S(1)} fusion(f32[4,2,2,128,128]{3,4,2,1,0:T(8,128)S(1)} %convolution_bitcast_fusion, s32[1024]{0:T(1024)S(1)} %pad_clamp_fusion), kind=kCustom, calls=%fused_computation | custom fusion | bytes 2097168 | tf_op jit(solution)/shard_map/jit(_take)/gather | solution.py:158
  51.4 0.2 fusion.10
  51.6 1.0 %copy.8 = bf16[1,1,4,1,2,2,128,128]{7,6,5,4,3,2,1,0:T(8,128)(2,1)} copy(bf16[1,1,4,1,2,2,128,128]{6,7,5,4,2,3,1,0:T(8,128)(2,1)S(1)} %fusion.10) | data formatting | bytes 1048576 | tf_op jit(solution)/shard_map/convert_element_type | solution.py:162
  (5 shorter events, 0.1 us)
Async XLA Ops:
  0.0 3.7 %copy-start.1 = (s32[1,1,4,1]{2,3,1,0:T(1,128)S(1)}, s32[1,1,4,1]{2,3,1,0:T(1,128)}, u32[]{:S(2)}) copy-start(s32[1,1,4,1]{2,3,1,0:T(1,128)} %param.7) | copy-start | bytes 52
  0.0 11.7 %copy-start.2 = (s32[1,1,4]{2,1,0:T(1,128)S(1)}, s32[1,1,4]{2,1,0:T(1,128)}, u32[]{:S(2)}) copy-start(s32[1,1,4]{2,1,0:T(1,128)} %param.8) | copy-start | bytes 52
  1.3 10.5 %collective-permute-start = (bf16[256,512]{1,0:T(8,128)(2,1)S(1)}, bf16[256,512]{1,0:T(8,128)(2,1)S(1)}, u32[]{:S(2)}, u32[]{:S(2)}) collective-permute-start(bf16[256,512]{1,0:T(8,128)(2,1)S(1)} %get-tuple-element.8), channel_id=1, source_target_pairs={{0,1},{1,2},{2,3},{3,0},{4,5},{5,6},{6,7},{7,4},{8,9},{9,10},{10,1... | collective-permute-start | bytes 786440 | tf_op jit(solution)/shard_map/ppermute | solution.py:133
  3.1 11.8 %collective-permute-start.1 = (bf16[256,512]{1,0:T(8,128)(2,1)S(1)}, bf16[256,512]{1,0:T(8,128)(2,1)S(1)}, u32[]{:S(2)}, u32[]{:S(2)}) collective-permute-start(bf16[256,512]{1,0:T(8,128)(2,1)S(1)} %get-tuple-element.7), channel_id=1, source_target_pairs={{0,2},{1,3},{2,0},{3,1},{4,6},{5,7},{6,4},{7,5},{8,10},{9,11},{10,... | collective-permute-start | bytes 786440 | tf_op jit(solution)/shard_map/ppermute | solution.py:133
  3.4 12.2 %collective-permute-start.2 = (bf16[256,512]{1,0:T(8,128)(2,1)S(1)}, bf16[256,512]{1,0:T(8,128)(2,1)S(1)}, u32[]{:S(2)}, u32[]{:S(2)}) collective-permute-start(bf16[256,512]{1,0:T(8,128)(2,1)S(1)} %get-tuple-element.6), channel_id=1, source_target_pairs={{0,3},{1,0},{2,1},{3,2},{4,7},{5,4},{6,5},{7,6},{8,11},{9,8},{10,9... | collective-permute-start | bytes 786440 | tf_op jit(solution)/shard_map/ppermute | solution.py:133
  22.6 5.2 %copy-start = (bf16[256,1024]{1,0:T(8,128)(2,1)S(1)}, bf16[256,1024]{1,0:T(8,128)(2,1)}, u32[]{:S(2)}) copy-start(bf16[256,1024]{1,0:T(8,128)(2,1)} %shard_map.64) | copy-start | bytes 1572868
  23.9 8.2 %collective-permute-start.3 = (bf16[128,1024]{1,0:T(8,128)(2,1)S(1)}, bf16[128,1024]{1,0:T(8,128)(2,1)S(1)}, u32[]{:S(2)}, u32[]{:S(2)}) collective-permute-start(bf16[128,1024]{1,0:T(8,128)(2,1)S(1)} %get-tuple-element.14), channel_id=1, source_target_pairs={{0,4},{4,8},{8,12},{12,0},{1,5},{5,9},{9,13},{13,1},{2,6},{6,10},{... | collective-permute-start | bytes 786440 | tf_op jit(solution)/shard_map/ppermute | solution.py:150
  25.2 22.8 %collective-permute-start.4 = (bf16[128,1024]{1,0:T(8,128)(2,1)S(1)}, bf16[128,1024]{1,0:T(8,128)(2,1)S(1)}, u32[]{:S(2)}, u32[]{:S(2)}) collective-permute-start(bf16[128,1024]{1,0:T(8,128)(2,1)S(1)} %get-tuple-element.13), channel_id=1, source_target_pairs={{0,8},{4,12},{8,0},{12,4},{1,9},{5,13},{9,1},{13,5},{2,10},{6,14},... | collective-permute-start | bytes 786440 | tf_op jit(solution)/shard_map/ppermute | solution.py:150
  26.4 23.6 %collective-permute-start.5 = (bf16[128,1024]{1,0:T(8,128)(2,1)S(1)}, bf16[128,1024]{1,0:T(8,128)(2,1)S(1)}, u32[]{:S(2)}, u32[]{:S(2)}) collective-permute-start(bf16[128,1024]{1,0:T(8,128)(2,1)S(1)} %get-tuple-element.12), channel_id=1, source_target_pairs={{0,12},{4,0},{8,4},{12,8},{1,13},{5,1},{9,5},{13,9},{2,14},{6,2},{... | collective-permute-start | bytes 786440 | tf_op jit(solution)/shard_map/ppermute | solution.py:150

commit v3 on v2

--- a/solution.py
+++ b/solution.py
@@ -17,6 +17,7 @@
 RAD = 15
 TILE = 128
 HALF = NT // 2
+NSPLIT = 2
 BF16 = ml_dtypes.bfloat16
 
 
@@ -115,9 +116,12 @@
         out_specs=pl.BlockSpec((BLOCK, 2 * NBAND), lambda r, p: (r, 0)),
         scratch_shapes=[pltpu.VMEM((BLOCK, NT), jnp.bfloat16)],
     )
+    flops = 2 * nrows * (3 * TILE * 2 * TILE * (NT // TILE) + NT * 2 * NBAND + 2 * NBAND * NBAND)
+    nbytes = rows3.size * 2 + tab.size * 2 + nrows * 2 * NBAND * 2
     return pl.pallas_call(
         spectra_kernel,
         grid_spec=grid_spec,
+        cost_estimate=pl.CostEstimate(flops=flops, transcendentals=nrows * NBAND, bytes_accessed=nbytes),
         out_shape=jax.ShapeDtypeStruct((nrows, 2 * NBAND), jnp.bfloat16),
     )(pos, rows3, band, tab, grp)
 
@@ -126,31 +130,40 @@
     ntm = lax.axis_size("tm")
     nch, width = raw.shape
     here = lax.axis_index("tm")
-    parts = raw.reshape(ntm, nch // ntm, width)
-    slots = [lax.dynamic_index_in_dim(parts, here, axis=0, keepdims=False)]
-    for d in range(1, ntm):
-        piece = lax.dynamic_index_in_dim(parts, (here + d) % ntm, axis=0, keepdims=False)
-        slots.append(lax.ppermute(piece, "tm", perm=[(i, (i + d) % ntm) for i in range(ntm)]))
-    rows3 = jnp.stack(slots)
-    whitened = spectra(here.astype(jnp.int32).reshape(1), rows3)
-    blocks = whitened.shape[0] // BLOCK
-    whitened = whitened.reshape(blocks, BLOCK, 2 * NBAND)
+    blocks = nch // ntm // BLOCK
+    rows = BLOCK // NSPLIT
+    parts = raw.reshape(ntm, blocks, NSPLIT, rows, width)
+    pos = here.astype(jnp.int32).reshape(1)
 
     peers = lax.axis_size("chan")
     mine = lax.axis_index("chan")
     cap = send_blocks.shape[3]
     ids = send_blocks[0, 0]
-    recv = []
-    for d in range(peers):
-        dest = (mine + d) % peers
-        row = []
-        for k in range(cap):
-            blk = lax.dynamic_index_in_dim(whitened, ids[dest, k], axis=0, keepdims=False)
-            if d:
-                blk = lax.ppermute(blk, "chan", perm=[(i, (i + d) % peers) for i in range(peers)])
-            row.append(blk)
-        recv.append(jnp.stack(row))
-    picked = jnp.stack(recv)
+    own_parts = []
+    picked_parts = []
+    for h in range(NSPLIT):
+        part = parts[:, :, h].reshape(ntm, blocks * rows, width)
+        if own_parts:
+            part, own_parts[-1] = lax.optimization_barrier((part, own_parts[-1]))
+        slots = [lax.dynamic_index_in_dim(part, here, axis=0, keepdims=False)]
+        for d in range(1, ntm):
+            piece = lax.dynamic_index_in_dim(part, (here + d) % ntm, axis=0, keepdims=False)
+            slots.append(lax.ppermute(piece, "tm", perm=[(i, (i + d) % ntm) for i in range(ntm)]))
+        whitened = spectra(pos, jnp.stack(slots)).reshape(blocks, rows, 2 * NBAND)
+        own_parts.append(whitened)
+        recv = []
+        for d in range(peers):
+            dest = (mine + d) % peers
+            row = []
+            for k in range(cap):
+                blk = lax.dynamic_index_in_dim(whitened, ids[dest, k], axis=0, keepdims=False)
+                if d:
+                    blk = lax.ppermute(blk, "chan", perm=[(i, (i + d) % peers) for i in range(peers)])
+                row.append(blk)
+            recv.append(jnp.stack(row))
+        picked_parts.append(jnp.stack(recv))
+    whitened = jnp.concatenate(own_parts, axis=1)
+    picked = jnp.concatenate(picked_parts, axis=2)
     turned = jnp.concatenate([whitened[..., NBAND:], -whitened[..., :NBAND]], axis=-1)
     paired = jnp.stack([whitened, turned], axis=1)
     result = jnp.einsum("lrif,dkjf->dklrij", paired, picked, preferred_element_type=jnp.float32)

time: 52.9 us -> 55.7 us (1.053)
  the two profiles are of different devices: /device:TPU:9 before, /device:TPU:0 now
where the time goes in v3:
time: 55.7 us; the launch traced here: 54.9 us
  starting transfers between devices  16.3 us (29%)
  waiting for transfers between devices  12.3 us (22%)
  Pallas kernels  8.6 us (15%)
  between operations  7.77 us (14%)
  local copies, waits for them, and re-layouts  5.99 us (11%)
  other arithmetic  3.12 us (6%)
  matrix products  0.75 us (1%)
    ppermute x6, starting transfers between devices, local(): lax.ppermute(blk, 'chan', perm=[(i, (i + d) % peers) for i in range(peers)])  9.5 us
    pallas_call x2, Pallas kernels, spectra(): pl.pallas_call(spectra_kernel, grid_spec=grid_spec, cost_estimate=pl.Cost...  8.6 us
    ppermute x6, waiting for transfers between devices, local(): lax.ppermute(blk, 'chan', perm=[(i, (i + d) % peers) for i in range(peers)])  7.71 us
    ppermute x6, starting transfers between devices, local(): lax.ppermute(piece, 'tm', perm=[(i, (i + d) % ntm) for i in range(ntm)])  6.8 us
    ppermute x6, waiting for transfers between devices, local(): lax.ppermute(piece, 'tm', perm=[(i, (i + d) % ntm) for i in range(ntm)])  4.63 us
    another operation x2, local copies, waits for them, and re-layouts, local(): picked_parts.append(jnp.stack(recv))  2.31 us
    another operation x2, other arithmetic, local(): whitened = spectra(pos, jnp.stack(slots)).reshape(blocks, rows, 2 * NBAND)  1.72 us
    slice x1, local copies, waits for them, and re-layouts, local(): part = parts[:, :, h].reshape(ntm, blocks * rows, width)  1.3 us
  transfers between devices with their start and end apart: 12, of which 5 were waited for; matrix products, arithmetic and copies ran while one was open for 9% of the time, Pallas kernels for 8%

profile of v3, /device:TPU:0, one launch (start us, length us, event | category | flops | bytes accessed | tf_op | source)
XLA Modules:
  0.0 54.9 jit_solution(547493219865087967)
XLA Ops:
  0.0 0.0 copy-start.3
  0.0 1.3 %fusion.27 = (bf16[4,2,1,64,512]{4,3,2,1,0:T(8,128)(2,1)S(1)}, bf16[4,2,1,64,512]{4,3,2,1,0:T(8,128)(2,1)S(1)}) fusion(bf16[4,2,2,64,512]{4,3,2,1,0:T(8,128)(2,1)} %bitcast.96), kind=kLoop, calls=%fused_computation.71 | loop fusion | bytes 2097152 | tf_op jit(solution)/shard_map/slice | solution.py:145
  1.4 0.5 collective-permute-start
  1.9 2.6 %collective-permute-start.1 = (bf16[128,512]{1,0:T(8,128)(2,1)S(1)}, bf16[128,512]{1,0:T(8,128)(2,1)S(1)}, u32[]{:S(2)}, u32[]{:S(2)}) collective-permute-start(bf16[128,512]{1,0:T(8,128)(2,1)S(1)} %get-tuple-element.19), channel_id=1, source_target_pairs={{0,2},{1,3},{2,0},{3,1},{4,6},{5,7},{6,4},{7,5},{8,10},{9,11},{10,... | collective-permute-start | bytes 393224 | tf_op jit(solution)/shard_map/ppermute | solution.py:151
  4.5 1.4 %collective-permute-start.2 = (bf16[128,512]{1,0:T(8,128)(2,1)S(1)}, bf16[128,512]{1,0:T(8,128)(2,1)S(1)}, u32[]{:S(2)}, u32[]{:S(2)}) collective-permute-start(bf16[128,512]{1,0:T(8,128)(2,1)S(1)} %get-tuple-element.18), channel_id=1, source_target_pairs={{0,3},{1,0},{2,1},{3,2},{4,7},{5,4},{6,5},{7,6},{8,11},{9,8},{10,9... | collective-permute-start | bytes 393224 | tf_op jit(solution)/shard_map/ppermute | solution.py:151
  5.8 0.0 copy-done.3
  5.9 1.1 %collective-permute-done = bf16[128,512]{1,0:T(8,128)(2,1)S(1)} collective-permute-done((bf16[128,512]{1,0:T(8,128)(2,1)S(1)}, bf16[128,512]{1,0:T(8,128)(2,1)S(1)}, u32[]{:S(2)}, u32[]{:S(2)}) %collective-permute-start) | collective-permute-done | bytes 131104 | tf_op jit(solution)/shard_map/ppermute | solution.py:151
  6.9 1.7 %collective-permute-done.1 = bf16[128,512]{1,0:T(8,128)(2,1)S(1)} collective-permute-done((bf16[128,512]{1,0:T(8,128)(2,1)S(1)}, bf16[128,512]{1,0:T(8,128)(2,1)S(1)}, u32[]{:S(2)}, u32[]{:S(2)}) %collective-permute-start.1) | collective-permute-done | bytes 131104 | tf_op jit(solution)/shard_map/ppermute | solution.py:151
  8.6 1.9 %collective-permute-done.2 = bf16[128,512]{1,0:T(8,128)(2,1)S(1)} collective-permute-done((bf16[128,512]{1,0:T(8,128)(2,1)S(1)}, bf16[128,512]{1,0:T(8,128)(2,1)S(1)}, u32[]{:S(2)}, u32[]{:S(2)}) %collective-permute-start.2) | collective-permute-done | bytes 131104 | tf_op jit(solution)/shard_map/ppermute | solution.py:151
  10.5 0.9 %pad_maximum_fusion.1.x_ref = bf16[4,128,512]{2,1,0:T(8,128)(2,1)} fusion(bf16[1,128,512]{2,1,0:T(8,128)(2,1)S(1)} %bitcast.102, bf16[1,128,512]{2,1,0:T(8,128)(2,1)S(1)} %bitcast.101, bf16[1,128,512]{2,1,0:T(8,128)(2,1)S(1)} %bitcast.100, bf16[1,128,512]{2,1,0:T(8,128)(2,1)S(1)} %get-tuple-element.17), kind=kLoop, calls=%fused_computation.30 | loop fusion | flops 786432 | bytes 1048576 | tf_op jit(solution)/shard_map/stack | solution.py:152
  11.4 0.0 copy-start.2
  11.4 4.3 %shard_map.91 = bf16[128,1024]{1,0:T(8,128)(2,1)} custom-call(s32[1]{0:T(128)} %bitcast.1.pos_ref, bf16[4,128,512]{2,1,0:T(8,128)(2,1)} %pad_maximum_fusion.1.x_ref, bf16[384,256]{1,0:T(8,128)(2,1)} %constant.138.clone.band_ref, bf16[1024,1024]{1,0:T(8,128)(2,1)} %constant.139.clone.tab_ref, bf16[512,512]{1,0:T(8,128)(2,1)} %constant.140.clone.grp_ref), custom_call_target="tpu_custom_call" | custom-call | flops 1073741824 | bytes 2883584 | tf_op jit(solution)/shard_map/pallas_call | solution.py:121
  15.7 0.1 collective-permute-start.6
  15.7 2.3 %collective-permute-start.7 = (bf16[128,512]{1,0:T(8,128)(2,1)S(1)}, bf16[128,512]{1,0:T(8,128)(2,1)S(1)}, u32[]{:S(2)}, u32[]{:S(2)}) collective-permute-start(bf16[128,512]{1,0:T(8,128)(2,1)S(1)} %get-tuple-element.15), channel_id=1, source_target_pairs={{0,2},{1,3},{2,0},{3,1},{4,6},{5,7},{6,4},{7,5},{8,10},{9,11},{10,... | collective-permute-start | bytes 393224 | tf_op jit(solution)/shard_map/ppermute | solution.py:151
  18.0 0.0 collective-permute-start.8
  18.1 0.0 copy-done.2
  18.1 0.7 %constant_dynamic-slice_fusion.4 = (s32[1,1,1,1]{2,3,1,0:T(1,128)}, s32[1,1,1,1]{2,3,1,0:T(1,128)}, s32[1,1,1,1]{2,3,1,0:T(1,128)}, s32[1,1,1,1]{2,3,1,0:T(1,128)}) fusion(s32[1,1,4,1]{2,3,1,0:T(1,128)S(1)} %copy-done.2, s32[]{:T(128)S(6)} %select_n.164, s32[]{:T(128)S(6)} %select_n.167, s32[]{:T(128)S(6)} %select_n.173, s32[]{:T(128)S(6)} %select_n.170), kind=kLoop, calls=%fused_computation.54 | loop fusion | bytes 48 | tf_op jit(solution)/shard_map/dynamic_slice | solution.py:159
  26.3 1.1 %dynamic-slice_bitcast_fusion.10 = (bf16[1,1,64,1024]{3,2,0,1:T(8,128)(2,1)S(1)}, bf16[64,1024]{1,0:T(8,128)(2,1)S(1)}, bf16[64,1024]{1,0:T(8,128)(2,1)S(1)}, bf16[64,1024]{1,0:T(8,128)(2,1)S(1)}) fusion(bf16[2,64,1024]{2,1,0:T(8,128)(2,1)} %bitcast.88, s32[]{:T(128)S(6)} %select_n.165, s32[]{:T(128)S(6)} %select_n.174, s32[]{:T(128)S(6)} %select_n.171, ...), kind=kLoop, calls=%fused_computation.46 | loop fusion | bytes 1048592 | tf_op jit(solution)/shard_map/stack;stack | solution.py:164
  27.5 1.6 %collective-permute-start.3 = (bf16[64,1024]{1,0:T(8,128)(2,1)S(1)}, bf16[64,1024]{1,0:T(8,128)(2,1)S(1)}, u32[]{:S(2)}, u32[]{:S(2)}) collective-permute-start(bf16[64,1024]{1,0:T(8,128)(2,1)S(1)} %get-tuple-element.24), channel_id=1, source_target_pairs={{0,4},{4,8},{8,12},{12,0},{1,5},{5,9},{9,13},{13,1},{2,6},{6,10},{... | collective-permute-start | bytes 393224 | tf_op jit(solution)/shard_map/ppermute | solution.py:161
  29.1 2.6 %collective-permute-start.4 = (bf16[64,1024]{1,0:T(8,128)(2,1)S(1)}, bf16[64,1024]{1,0:T(8,128)(2,1)S(1)}, u32[]{:S(2)}, u32[]{:S(2)}) collective-permute-start(bf16[64,1024]{1,0:T(8,128)(2,1)S(1)} %get-tuple-element.23), channel_id=1, source_target_pairs={{0,8},{4,12},{8,0},{12,4},{1,9},{5,13},{9,1},{13,5},{2,10},{6,14},... | collective-permute-start | bytes 393224 | tf_op jit(solution)/shard_map/ppermute | solution.py:161
  31.7 0.0 collective-permute-done.6
  31.7 1.3 %collective-permute-start.5 = (bf16[64,1024]{1,0:T(8,128)(2,1)S(1)}, bf16[64,1024]{1,0:T(8,128)(2,1)S(1)}, u32[]{:S(2)}, u32[]{:S(2)}) collective-permute-start(bf16[64,1024]{1,0:T(8,128)(2,1)S(1)} %get-tuple-element.22), channel_id=1, source_target_pairs={{0,12},{4,0},{8,4},{12,8},{1,13},{5,1},{9,5},{13,9},{2,14},{6,2},{... | collective-permute-start | bytes 393224 | tf_op jit(solution)/shard_map/ppermute | solution.py:161
  33.1 0.0 collective-permute-done.7
  33.1 0.0 collective-permute-done.8
  33.1 0.9 %pad_maximum_fusion.2.x_ref = bf16[4,128,512]{2,1,0:T(8,128)(2,1)} fusion(bf16[1,128,512]{2,1,0:T(8,128)(2,1)S(1)} %bitcast.99, bf16[1,128,512]{2,1,0:T(8,128)(2,1)S(1)} %bitcast.98, bf16[1,128,512]{2,1,0:T(8,128)(2,1)S(1)} %bitcast.97, bf16[1,128,512]{2,1,0:T(8,128)(2,1)S(1)} %get-tuple-element.13), kind=kLoop, calls=%fused_computation.31 | loop fusion | flops 786432 | bytes 1048576 | tf_op jit(solution)/shard_map/stack | solution.py:152
  33.9 0.0 copy-start
  33.9 4.3 %shard_map.92 = bf16[128,1024]{1,0:T(8,128)(2,1)} custom-call(s32[1]{0:T(128)} %bitcast.1.pos_ref, bf16[4,128,512]{2,1,0:T(8,128)(2,1)} %pad_maximum_fusion.2.x_ref, bf16[384,256]{1,0:T(8,128)(2,1)} %constant.138.clone.band_ref, bf16[1024,1024]{1,0:T(8,128)(2,1)} %constant.139.clone.tab_ref, bf16[512,512]{1,0:T(8,128)(2,1)} %constant.140.clone.grp_ref), custom_call_target="tpu_custom_call" | custom-call | flops 1073741824 | bytes 2883584 | tf_op jit(solution)/shard_map/pallas_call | solution.py:121
  38.2 0.0 copy-start.1
  38.3 1.2 %dynamic-slice_bitcast_fusion.3 = (bf16[1,1,64,1024]{3,2,0,1:T(8,128)(2,1)S(1)}, bf16[64,1024]{1,0:T(8,128)(2,1)S(1)}, bf16[64,1024]{1,0:T(8,128)(2,1)S(1)}, bf16[64,1024]{1,0:T(8,128)(2,1)S(1)}) fusion(bf16[2,64,1024]{2,1,0:T(8,128)(2,1)} %bitcast.91, s32[]{:T(128)S(6)} %select_n.165, s32[]{:T(128)S(6)} %select_n.174, s32[]{:T(128)S(6)} %select_n.171, ...), kind=kLoop, calls=%fused_computation.39 | loop fusion | bytes 1048592 | tf_op jit(solution)/shard_map/stack;stack | solution.py:164
  39.4 0.7 %collective-permute-start.9 = (bf16[64,1024]{1,0:T(8,128)(2,1)S(1)}, bf16[64,1024]{1,0:T(8,128)(2,1)S(1)}, u32[]{:S(2)}, u32[]{:S(2)}) collective-permute-start(bf16[64,1024]{1,0:T(8,128)(2,1)S(1)} %get-tuple-element.28), channel_id=1, source_target_pairs={{0,4},{4,8},{8,12},{12,0},{1,5},{5,9},{9,13},{13,1},{2,6},{6,10},{... | collective-permute-start | bytes 393224 | tf_op jit(solution)/shard_map/ppermute | solution.py:161
  40.1 0.3 collective-permute-start.10
  40.5 0.0 copy-done
  40.5 1.0 %fusion.20 = (bf16[2,128,512]{2,1,0:T(8,128)(2,1)S(1)}, bf16[2,128,512]{2,1,0:T(8,128)(2,1)S(1)}) fusion(bf16[2,64,1024]{2,1,0:T(8,128)(2,1)S(1)} %bitcast.89, bf16[2,64,1024]{2,1,0:T(8,128)(2,1)} %bitcast.92), kind=kLoop, calls=%fused_computation.33 | loop fusion | flops 1179648 | bytes 1048576 | tf_op jit(solution)/shard_map/concatenate | solution.py:165
  41.5 0.0 collective-permute-done.3
  41.5 2.9 %collective-permute-start.11 = (bf16[64,1024]{1,0:T(8,128)(2,1)S(1)}, bf16[64,1024]{1,0:T(8,128)(2,1)S(1)}, u32[]{:S(2)}, u32[]{:S(2)}) collective-permute-start(bf16[64,1024]{1,0:T(8,128)(2,1)S(1)} %get-tuple-element.26), channel_id=1, source_target_pairs={{0,12},{4,0},{8,4},{12,8},{1,13},{5,1},{9,5},{13,9},{2,14},{6,2},{... | collective-permute-start | bytes 393224 | tf_op jit(solution)/shard_map/ppermute | solution.py:161
  44.4 0.0 copy-done.1
  44.4 0.1 fusion.19
  44.5 0.0 collective-permute-done.4
  44.5 0.0 collective-permute-done.5
  44.5 3.2 %collective-permute-done.9 = bf16[64,1024]{1,0:T(8,128)(2,1)S(1)} collective-permute-done((bf16[64,1024]{1,0:T(8,128)(2,1)S(1)}, bf16[64,1024]{1,0:T(8,128)(2,1)S(1)}, u32[]{:S(2)}, u32[]{:S(2)}) %collective-permute-start.9) | collective-permute-done | bytes 131104 | tf_op jit(solution)/shard_map/ppermute | solution.py:161
  47.7 4.5 %collective-permute-done.10 = bf16[64,1024]{1,0:T(8,128)(2,1)S(1)} collective-permute-done((bf16[64,1024]{1,0:T(8,128)(2,1)S(1)}, bf16[64,1024]{1,0:T(8,128)(2,1)S(1)}, u32[]{:S(2)}, u32[]{:S(2)}) %collective-permute-start.10) | collective-permute-done | bytes 131104 | tf_op jit(solution)/shard_map/ppermute | solution.py:161
  52.2 0.0 collective-permute-done.11
  52.2 0.7 %convolution_bitcast_fusion = f32[4,2,2,128,128]{3,4,2,1,0:T(8,128)S(1)} fusion(bf16[1,1,64,1024]{3,2,0,1:T(8,128)(2,1)S(1)} %bitcast.108, bf16[1,1,64,1024]{3,2,0,1:T(8,128)(2,1)S(1)} %bitcast.107, bf16[1,1,64,1024]{3,2,0,1:T(8,128)(2,1)S(1)} %bitcast.106, bf16[1,1,64,1024]{3,2,0,1:T(8,128)(2,1)S(1)} %get-tuple-element.25, ...), kind=kOutput, calls=%fused_computation.1 | convolution fusion | flops 547356672 | bytes 3145728 | tf_op jit(solution)/shard_map/lrif,dkjf->dklrij/dot_general | solution.py:169
  53.0 0.6 %gather_fusion = f32[4,2,2,128,128]{3,4,2,1,0:T(8,128)S(1)} fusion(f32[4,2,2,128,128]{3,4,2,1,0:T(8,128)S(1)} %convolution_bitcast_fusion, s32[1024]{0:T(1024)S(1)} %pad_clamp_fusion), kind=kCustom, calls=%fused_computation | custom fusion | bytes 2097168 | tf_op jit(solution)/shard_map/jit(_take)/gather | solution.py:171
  53.6 0.2 fusion.18
  53.9 1.0 %copy.13 = bf16[1,1,4,1,2,2,128,128]{7,6,5,4,3,2,1,0:T(8,128)(2,1)} copy(bf16[1,1,4,1,2,2,128,128]{6,7,5,4,2,3,1,0:T(8,128)(2,1)S(1)} %fusion.18) | data formatting | bytes 1048576 | tf_op jit(solution)/shard_map/convert_element_type | solution.py:175
  (6 shorter events, 0.1 us)
Async XLA Ops:
  0.0 5.8 %copy-start.3 = (s32[1,1,4]{2,1,0:T(1,128)S(1)}, s32[1,1,4]{2,1,0:T(1,128)}, u32[]{:S(2)}) copy-start(s32[1,1,4]{2,1,0:T(1,128)} %param.11) | copy-start | bytes 52
  1.4 5.6 %collective-permute-start = (bf16[128,512]{1,0:T(8,128)(2,1)S(1)}, bf16[128,512]{1,0:T(8,128)(2,1)S(1)}, u32[]{:S(2)}, u32[]{:S(2)}) collective-permute-start(bf16[128,512]{1,0:T(8,128)(2,1)S(1)} %get-tuple-element.20), channel_id=1, source_target_pairs={{0,1},{1,2},{2,3},{3,0},{4,5},{5,6},{6,7},{7,4},{8,9},{9,10},{10,1... | collective-permute-start | bytes 393224 | tf_op jit(solution)/shard_map/ppermute | solution.py:151
  1.9 6.8 %collective-permute-start.1 = (bf16[128,512]{1,0:T(8,128)(2,1)S(1)}, bf16[128,512]{1,0:T(8,128)(2,1)S(1)}, u32[]{:S(2)}, u32[]{:S(2)}) collective-permute-start(bf16[128,512]{1,0:T(8,128)(2,1)S(1)} %get-tuple-element.19), channel_id=1, source_target_pairs={{0,2},{1,3},{2,0},{3,1},{4,6},{5,7},{6,4},{7,5},{8,10},{9,11},{10,... | collective-permute-start | bytes 393224 | tf_op jit(solution)/shard_map/ppermute | solution.py:151
  4.5 6.0 %collective-permute-start.2 = (bf16[128,512]{1,0:T(8,128)(2,1)S(1)}, bf16[128,512]{1,0:T(8,128)(2,1)S(1)}, u32[]{:S(2)}, u32[]{:S(2)}) collective-permute-start(bf16[128,512]{1,0:T(8,128)(2,1)S(1)} %get-tuple-element.18), channel_id=1, source_target_pairs={{0,3},{1,0},{2,1},{3,2},{4,7},{5,4},{6,5},{7,6},{8,11},{9,8},{10,9... | collective-permute-start | bytes 393224 | tf_op jit(solution)/shard_map/ppermute | solution.py:151
  11.4 6.7 %copy-start.2 = (s32[1,1,4,1]{2,3,1,0:T(1,128)S(1)}, s32[1,1,4,1]{2,3,1,0:T(1,128)}, u32[]{:S(2)}) copy-start(s32[1,1,4,1]{2,3,1,0:T(1,128)} %param.10) | copy-start | bytes 52
  15.7 16.0 %collective-permute-start.6 = (bf16[128,512]{1,0:T(8,128)(2,1)S(1)}, bf16[128,512]{1,0:T(8,128)(2,1)S(1)}, u32[]{:S(2)}, u32[]{:S(2)}) collective-permute-start(bf16[128,512]{1,0:T(8,128)(2,1)S(1)} %get-tuple-element.16), channel_id=1, source_target_pairs={{0,1},{1,2},{2,3},{3,0},{4,5},{5,6},{6,7},{7,4},{8,9},{9,10},{10,1... | collective-permute-start | bytes 393224 | tf_op jit(solution)/shard_map/ppermute | solution.py:151
  15.7 17.3 %collective-permute-start.7 = (bf16[128,512]{1,0:T(8,128)(2,1)S(1)}, bf16[128,512]{1,0:T(8,128)(2,1)S(1)}, u32[]{:S(2)}, u32[]{:S(2)}) collective-permute-start(bf16[128,512]{1,0:T(8,128)(2,1)S(1)} %get-tuple-element.15), channel_id=1, source_target_pairs={{0,2},{1,3},{2,0},{3,1},{4,6},{5,7},{6,4},{7,5},{8,10},{9,11},{10,... | collective-permute-start | bytes 393224 | tf_op jit(solution)/shard_map/ppermute | solution.py:151
  18.0 15.0 %collective-permute-start.8 = (bf16[128,512]{1,0:T(8,128)(2,1)S(1)}, bf16[128,512]{1,0:T(8,128)(2,1)S(1)}, u32[]{:S(2)}, u32[]{:S(2)}) collective-permute-start(bf16[128,512]{1,0:T(8,128)(2,1)S(1)} %get-tuple-element.14), channel_id=1, source_target_pairs={{0,3},{1,0},{2,1},{3,2},{4,7},{5,4},{6,5},{7,6},{8,11},{9,8},{10,9... | collective-permute-start | bytes 393224 | tf_op jit(solution)/shard_map/ppermute | solution.py:151
  27.5 14.0 %collective-permute-start.3 = (bf16[64,1024]{1,0:T(8,128)(2,1)S(1)}, bf16[64,1024]{1,0:T(8,128)(2,1)S(1)}, u32[]{:S(2)}, u32[]{:S(2)}) collective-permute-start(bf16[64,1024]{1,0:T(8,128)(2,1)S(1)} %get-tuple-element.24), channel_id=1, source_target_pairs={{0,4},{4,8},{8,12},{12,0},{1,5},{5,9},{9,13},{13,1},{2,6},{6,10},{... | collective-permute-start | bytes 393224 | tf_op jit(solution)/shard_map/ppermute | solution.py:161
  29.1 15.4 %collective-permute-start.4 = (bf16[64,1024]{1,0:T(8,128)(2,1)S(1)}, bf16[64,1024]{1,0:T(8,128)(2,1)S(1)}, u32[]{:S(2)}, u32[]{:S(2)}) collective-permute-start(bf16[64,1024]{1,0:T(8,128)(2,1)S(1)} %get-tuple-element.23), channel_id=1, source_target_pairs={{0,8},{4,12},{8,0},{12,4},{1,9},{5,13},{9,1},{13,5},{2,10},{6,14},... | collective-permute-start | bytes 393224 | tf_op jit(solution)/shard_map/ppermute | solution.py:161
  31.7 12.8 %collective-permute-start.5 = (bf16[64,1024]{1,0:T(8,128)(2,1)S(1)}, bf16[64,1024]{1,0:T(8,128)(2,1)S(1)}, u32[]{:S(2)}, u32[]{:S(2)}) collective-permute-start(bf16[64,1024]{1,0:T(8,128)(2,1)S(1)} %get-tuple-element.22), channel_id=1, source_target_pairs={{0,12},{4,0},{8,4},{12,8},{1,13},{5,1},{9,5},{13,9},{2,14},{6,2},{... | collective-permute-start | bytes 393224 | tf_op jit(solution)/shard_map/ppermute | solution.py:161
  33.9 6.6 %copy-start = (bf16[128,1024]{1,0:T(8,128)(2,1)S(1)}, bf16[128,1024]{1,0:T(8,128)(2,1)}, u32[]{:S(2)}) copy-start(bf16[128,1024]{1,0:T(8,128)(2,1)} %shard_map.91) | copy-start | bytes 786436
  38.2 6.2 %copy-start.1 = (bf16[128,1024]{1,0:T(8,128)(2,1)S(1)}, bf16[128,1024]{1,0:T(8,128)(2,1)}, u32[]{:S(2)}) copy-start(bf16[128,1024]{1,0:T(8,128)(2,1)} %shard_map.92) | copy-start | bytes 786436
  39.4 8.3 %collective-permute-start.9 = (bf16[64,1024]{1,0:T(8,128)(2,1)S(1)}, bf16[64,1024]{1,0:T(8,128)(2,1)S(1)}, u32[]{:S(2)}, u32[]{:S(2)}) collective-permute-start(bf16[64,1024]{1,0:T(8,128)(2,1)S(1)} %get-tuple-element.28), channel_id=1, source_target_pairs={{0,4},{4,8},{8,12},{12,0},{1,5},{5,9},{9,13},{13,1},{2,6},{6,10},{... | collective-permute-start | bytes 393224 | tf_op jit(solution)/shard_map/ppermute | solution.py:161
  40.1 12.1 %collective-permute-start.10 = (bf16[64,1024]{1,0:T(8,128)(2,1)S(1)}, bf16[64,1024]{1,0:T(8,128)(2,1)S(1)}, u32[]{:S(2)}, u32[]{:S(2)}) collective-permute-start(bf16[64,1024]{1,0:T(8,128)(2,1)S(1)} %get-tuple-element.27), channel_id=1, source_target_pairs={{0,8},{4,12},{8,0},{12,4},{1,9},{5,13},{9,1},{13,5},{2,10},{6,14},... | collective-permute-start | bytes 393224 | tf_op jit(solution)/shard_map/ppermute | solution.py:161
  41.5 10.7 %collective-permute-start.11 = (bf16[64,1024]{1,0:T(8,128)(2,1)S(1)}, bf16[64,1024]{1,0:T(8,128)(2,1)S(1)}, u32[]{:S(2)}, u32[]{:S(2)}) collective-permute-start(bf16[64,1024]{1,0:T(8,128)(2,1)S(1)} %get-tuple-element.26), channel_id=1, source_target_pairs={{0,12},{4,0},{8,4},{12,8},{1,13},{5,1},{9,5},{13,9},{2,14},{6,2},{... | collective-permute-start | bytes 393224 | tf_op jit(solution)/shard_map/ppermute | solution.py:161

commit v4 on v3

--- a/solution.py
+++ b/solution.py
@@ -156,7 +156,10 @@
             dest = (mine + d) % peers
             row = []
             for k in range(cap):
-                blk = lax.dynamic_index_in_dim(whitened, ids[dest, k], axis=0, keepdims=False)
+                want = lax.dynamic_index_in_dim(ids[:, k], dest, keepdims=False)
+                blk = whitened[0]
+                for b in range(1, blocks):
+                    blk = jnp.where(want == b, whitened[b], blk)
                 if d:
                     blk = lax.ppermute(blk, "chan", perm=[(i, (i + d) % peers) for i in range(peers)])
                 row.append(blk)

time: 55.7 us -> 48.1 us (0.86)
  between operations: 7.77 us -> 2.75 us
  waiting for transfers between devices: 12.3 us -> 9.1 us
  other arithmetic: 3.12 us -> 6.08 us
  local copies, waits for them, and re-layouts: 5.99 us -> 3.7 us
    another operation x2 -> x0, local copies, waits for them, and re-layouts: 2.31 us -> none  [local(): picked_parts.append(jnp.stack(recv))]
    ppermute x6, waiting for transfers between devices: 4.63 us -> 2.45 us  [local(): lax.ppermute(piece, 'tm', perm=[(i, (i + d) % ntm) for i in range(ntm)])]
    another operation x0 -> x2, other arithmetic: none -> 2.01 us  [local(): picked_parts.append(jnp.stack(recv))]
    ppermute x6, waiting for transfers between devices: 7.71 us -> 6.64 us  [local(): lax.ppermute(blk, 'chan', perm=[(i, (i + d) % peers) for i in range(peers)])]
    another operation x1, other arithmetic: 0.09 us -> 1.05 us  [local(): paired = jnp.stack([whitened, turned], axis=1)]
  transfers between devices with their start and end apart: 12 -> 12, of which waited for: 5 -> 5; matrix products, arithmetic and copies ran while one was open for 9% -> 12% of each run, Pallas kernels for 8% -> 9%
where the time goes in v4:
time: 48.1 us; the launch traced here: 47.7 us
  starting transfers between devices  16.8 us (35%)
  waiting for transfers between devices  9.1 us (19%)
  Pallas kernels  8.58 us (18%)
  other arithmetic  6.08 us (13%)
  local copies, waits for them, and re-layouts  3.7 us (8%)
  between operations  2.75 us (6%)
  matrix products  0.74 us (2%)
    ppermute x6, starting transfers between devices, local(): lax.ppermute(blk, 'chan', perm=[(i, (i + d) % peers) for i in range(peers)])  9.52 us
    pallas_call x2, Pallas kernels, spectra(): pl.pallas_call(spectra_kernel, grid_spec=grid_spec, cost_estimate=pl.Cost...  8.58 us
    ppermute x6, starting transfers between devices, local(): lax.ppermute(piece, 'tm', perm=[(i, (i + d) % ntm) for i in range(ntm)])  7.3 us
    ppermute x6, waiting for transfers between devices, local(): lax.ppermute(blk, 'chan', perm=[(i, (i + d) % peers) for i in range(peers)])  6.64 us
    ppermute x6, waiting for transfers between devices, local(): lax.ppermute(piece, 'tm', perm=[(i, (i + d) % ntm) for i in range(ntm)])  2.45 us
    another operation x2, other arithmetic, local(): picked_parts.append(jnp.stack(recv))  2.01 us
    another operation x2, other arithmetic, local(): whitened = spectra(pos, jnp.stack(slots)).reshape(blocks, rows, 2 * NBAND)  1.72 us
    slice x1, local copies, waits for them, and re-layouts, local(): part = parts[:, :, h].reshape(ntm, blocks * rows, width)  1.32 us
  transfers between devices with their start and end apart: 12, of which 5 were waited for; matrix products, arithmetic and copies ran while one was open for 12% of the time, Pallas kernels for 9%

profile of v4, /device:TPU:0, one launch (start us, length us, event | category | flops | bytes accessed | tf_op | source)
XLA Modules:
  0.0 47.7 jit_solution(18144836937175557771)
XLA Ops:
  0.0 0.0 copy-start.2
  0.0 0.0 copy-start.1
  0.0 1.3 %fusion.27 = (bf16[4,2,1,64,512]{4,3,2,1,0:T(8,128)(2,1)S(1)}, bf16[4,2,1,64,512]{4,3,2,1,0:T(8,128)(2,1)S(1)}) fusion(bf16[4,2,2,64,512]{4,3,2,1,0:T(8,128)(2,1)} %bitcast.82), kind=kLoop, calls=%fused_computation.71 | loop fusion | bytes 2097152 | tf_op jit(solution)/shard_map/slice | solution.py:145
  1.4 2.4 %collective-permute-start.2 = (bf16[128,512]{1,0:T(8,128)(2,1)S(1)}, bf16[128,512]{1,0:T(8,128)(2,1)S(1)}, u32[]{:S(2)}, u32[]{:S(2)}) collective-permute-start(bf16[128,512]{1,0:T(8,128)(2,1)S(1)} %get-tuple-element.18), channel_id=1, source_target_pairs={{0,3},{1,0},{2,1},{3,2},{4,7},{5,4},{6,5},{7,6},{8,11},{9,8},{10,9... | collective-permute-start | bytes 393224 | tf_op jit(solution)/shard_map/ppermute | solution.py:151
  3.8 0.0 collective-permute-start
  3.8 1.1 %collective-permute-start.1 = (bf16[128,512]{1,0:T(8,128)(2,1)S(1)}, bf16[128,512]{1,0:T(8,128)(2,1)S(1)}, u32[]{:S(2)}, u32[]{:S(2)}) collective-permute-start(bf16[128,512]{1,0:T(8,128)(2,1)S(1)} %get-tuple-element.19), channel_id=1, source_target_pairs={{0,2},{1,3},{2,0},{3,1},{4,6},{5,7},{6,4},{7,5},{8,10},{9,11},{10,... | collective-permute-start | bytes 393224 | tf_op jit(solution)/shard_map/ppermute | solution.py:151
  4.9 0.0 copy-done.2
  5.0 0.0 copy-done.1
  5.0 0.7 %constant_dynamic-slice_fusion.5 = (s32[1,1,1,1]{2,3,1,0:T(1,128)}, s32[1,1,1,1]{2,3,1,0:T(1,128)}, s32[1,1,1,1]{2,3,1,0:T(1,128)}, s32[1,1,1,1]{2,3,1,0:T(1,128)}) fusion(s32[1,1,4,1]{2,3,1,0:T(1,128)S(1)} %copy-done.1, s32[]{:T(128)S(6)} %select_n.183, s32[]{:T(128)S(6)} %select_n.194, s32[]{:T(128)S(6)} %select_n.202, s32[]{:T(128)S(6)} %select_n.198), kind=kLoop, calls=%fused_computation.56 | loop fusion | bytes 48 | tf_op jit(solution)/shard_map/jit(dynamic_index_in_dim)/dynamic_slice | solution.py:159
  8.2 0.0 collective-permute-done.2
  8.2 1.4 %collective-permute-done = bf16[128,512]{1,0:T(8,128)(2,1)S(1)} collective-permute-done((bf16[128,512]{1,0:T(8,128)(2,1)S(1)}, bf16[128,512]{1,0:T(8,128)(2,1)S(1)}, u32[]{:S(2)}, u32[]{:S(2)}) %collective-permute-start) | collective-permute-done | bytes 131104 | tf_op jit(solution)/shard_map/ppermute | solution.py:151
  9.6 1.1 %collective-permute-done.1 = bf16[128,512]{1,0:T(8,128)(2,1)S(1)} collective-permute-done((bf16[128,512]{1,0:T(8,128)(2,1)S(1)}, bf16[128,512]{1,0:T(8,128)(2,1)S(1)}, u32[]{:S(2)}, u32[]{:S(2)}) %collective-permute-start.1) | collective-permute-done | bytes 131104 | tf_op jit(solution)/shard_map/ppermute | solution.py:151
  10.7 0.9 %pad_maximum_fusion.1.x_ref = bf16[4,128,512]{2,1,0:T(8,128)(2,1)} fusion(bf16[1,128,512]{2,1,0:T(8,128)(2,1)S(1)} %bitcast.83, bf16[1,128,512]{2,1,0:T(8,128)(2,1)S(1)} %bitcast.85, bf16[1,128,512]{2,1,0:T(8,128)(2,1)S(1)} %bitcast.84, bf16[1,128,512]{2,1,0:T(8,128)(2,1)S(1)} %get-tuple-element.17), kind=kLoop, calls=%fused_computation.30 | loop fusion | flops 786432 | bytes 1048576 | tf_op jit(solution)/shard_map/stack | solution.py:152
  11.5 4.3 %shard_map.91 = bf16[128,1024]{1,0:T(8,128)(2,1)} custom-call(s32[1]{0:T(128)} %bitcast.2.pos_ref, bf16[4,128,512]{2,1,0:T(8,128)(2,1)} %pad_maximum_fusion.1.x_ref, bf16[384,256]{1,0:T(8,128)(2,1)} %constant.142.clone.band_ref, bf16[1024,1024]{1,0:T(8,128)(2,1)} %constant.143.clone.tab_ref, bf16[512,512]{1,0:T(8,128)(2,1)} %constant.144.clone.grp_ref), custom_call_target="tpu_custom_call" | custom-call | flops 1073741824 | bytes 2883584 | tf_op jit(solution)/shard_map/pallas_call | solution.py:121
  15.9 0.7 %collective-permute-start.6 = (bf16[128,512]{1,0:T(8,128)(2,1)S(1)}, bf16[128,512]{1,0:T(8,128)(2,1)S(1)}, u32[]{:S(2)}, u32[]{:S(2)}) collective-permute-start(bf16[128,512]{1,0:T(8,128)(2,1)S(1)} %get-tuple-element.16), channel_id=1, source_target_pairs={{0,1},{1,2},{2,3},{3,0},{4,5},{5,6},{6,7},{7,4},{8,9},{9,10},{10,1... | collective-permute-start | bytes 393224 | tf_op jit(solution)/shard_map/ppermute | solution.py:151
  16.6 1.7 %collective-permute-start.7 = (bf16[128,512]{1,0:T(8,128)(2,1)S(1)}, bf16[128,512]{1,0:T(8,128)(2,1)S(1)}, u32[]{:S(2)}, u32[]{:S(2)}) collective-permute-start(bf16[128,512]{1,0:T(8,128)(2,1)S(1)} %get-tuple-element.15), channel_id=1, source_target_pairs={{0,2},{1,3},{2,0},{3,1},{4,6},{5,7},{6,4},{7,5},{8,10},{9,11},{10,... | collective-permute-start | bytes 393224 | tf_op jit(solution)/shard_map/ppermute | solution.py:151
  18.3 1.4 %collective-permute-start.8 = (bf16[128,512]{1,0:T(8,128)(2,1)S(1)}, bf16[128,512]{1,0:T(8,128)(2,1)S(1)}, u32[]{:S(2)}, u32[]{:S(2)}) collective-permute-start(bf16[128,512]{1,0:T(8,128)(2,1)S(1)} %get-tuple-element.14), channel_id=1, source_target_pairs={{0,3},{1,0},{2,1},{3,2},{4,7},{5,4},{6,5},{7,6},{8,11},{9,8},{10,9... | collective-permute-start | bytes 393224 | tf_op jit(solution)/shard_map/ppermute | solution.py:151
  19.7 1.0 %select_bitcast_fusion.1 = (bf16[1,1,64,1024]{3,2,1,0:T(8,128)(2,1)S(1)}, bf16[64,1024]{1,0:T(8,128)(2,1)S(1)}, bf16[64,1024]{1,0:T(8,128)(2,1)S(1)}, bf16[64,1024]{1,0:T(8,128)(2,1)S(1)}) fusion(pred[]{:T(512)} %bitcast.1, bf16[128,1024]{1,0:T(8,128)(2,1)} %shard_map.91, pred[]{:T(512)} %bitcast.14, pred[]{:T(512)} %bitcast.16, pred[]{:T(512)} %bitcast.12), kind=kLoop, calls=%fused_computation.40 | loop fusion | flops 262144 | bytes 786436 | tf_op jit(solution)/shard_map/stack;stack | solution.py:167
  20.7 1.6 %collective-permute-start.3 = (bf16[64,1024]{1,0:T(8,128)(2,1)S(1)}, bf16[64,1024]{1,0:T(8,128)(2,1)S(1)}, u32[]{:S(2)}, u32[]{:S(2)}) collective-permute-start(bf16[64,1024]{1,0:T(8,128)(2,1)S(1)} %get-tuple-element.24), channel_id=1, source_target_pairs={{0,4},{4,8},{8,12},{12,0},{1,5},{5,9},{9,13},{13,1},{2,6},{6,10},{... | collective-permute-start | bytes 393224 | tf_op jit(solution)/shard_map/ppermute | solution.py:164
  22.3 2.6 %collective-permute-start.4 = (bf16[64,1024]{1,0:T(8,128)(2,1)S(1)}, bf16[64,1024]{1,0:T(8,128)(2,1)S(1)}, u32[]{:S(2)}, u32[]{:S(2)}) collective-permute-start(bf16[64,1024]{1,0:T(8,128)(2,1)S(1)} %get-tuple-element.22), channel_id=1, source_target_pairs={{0,8},{4,12},{8,0},{12,4},{1,9},{5,13},{9,1},{13,5},{2,10},{6,14},... | collective-permute-start | bytes 393224 | tf_op jit(solution)/shard_map/ppermute | solution.py:164
  24.9 0.0 collective-permute-done.6
  24.9 1.4 %collective-permute-start.5 = (bf16[64,1024]{1,0:T(8,128)(2,1)S(1)}, bf16[64,1024]{1,0:T(8,128)(2,1)S(1)}, u32[]{:S(2)}, u32[]{:S(2)}) collective-permute-start(bf16[64,1024]{1,0:T(8,128)(2,1)S(1)} %get-tuple-element.23), channel_id=1, source_target_pairs={{0,12},{4,0},{8,4},{12,8},{1,13},{5,1},{9,5},{13,9},{2,14},{6,2},{... | collective-permute-start | bytes 393224 | tf_op jit(solution)/shard_map/ppermute | solution.py:164
  26.2 0.0 collective-permute-done.7
  26.3 0.0 collective-permute-done.8
  26.3 0.9 %pad_maximum_fusion.2.x_ref = bf16[4,128,512]{2,1,0:T(8,128)(2,1)} fusion(bf16[1,128,512]{2,1,0:T(8,128)(2,1)S(1)} %bitcast.88, bf16[1,128,512]{2,1,0:T(8,128)(2,1)S(1)} %bitcast.87, bf16[1,128,512]{2,1,0:T(8,128)(2,1)S(1)} %bitcast.86, bf16[1,128,512]{2,1,0:T(8,128)(2,1)S(1)} %get-tuple-element.13), kind=kLoop, calls=%fused_computation.31 | loop fusion | flops 786432 | bytes 1048576 | tf_op jit(solution)/shard_map/stack | solution.py:152
  27.1 0.0 copy-start
  27.1 4.3 %shard_map.92 = bf16[128,1024]{1,0:T(8,128)(2,1)} custom-call(s32[1]{0:T(128)} %bitcast.2.pos_ref, bf16[4,128,512]{2,1,0:T(8,128)(2,1)} %pad_maximum_fusion.2.x_ref, bf16[384,256]{1,0:T(8,128)(2,1)} %constant.142.clone.band_ref, bf16[1024,1024]{1,0:T(8,128)(2,1)} %constant.143.clone.tab_ref, bf16[512,512]{1,0:T(8,128)(2,1)} %constant.144.clone.grp_ref), custom_call_target="tpu_custom_call" | custom-call | flops 1073741824 | bytes 2883584 | tf_op jit(solution)/shard_map/pallas_call | solution.py:121
  31.4 1.0 %select_bitcast_fusion = (bf16[1,1,64,1024]{3,2,1,0:T(8,128)(2,1)S(1)}, bf16[64,1024]{1,0:T(8,128)(2,1)S(1)}, bf16[64,1024]{1,0:T(8,128)(2,1)S(1)}, bf16[64,1024]{1,0:T(8,128)(2,1)S(1)}) fusion(pred[]{:T(512)} %bitcast.1, bf16[128,1024]{1,0:T(8,128)(2,1)} %shard_map.92, pred[]{:T(512)} %bitcast.14, pred[]{:T(512)} %bitcast.16, pred[]{:T(512)} %bitcast.12), kind=kLoop, calls=%fused_computation.36 | loop fusion | flops 262144 | bytes 786436 | tf_op jit(solution)/shard_map/stack;stack | solution.py:167
  32.4 0.7 %collective-permute-start.9 = (bf16[64,1024]{1,0:T(8,128)(2,1)S(1)}, bf16[64,1024]{1,0:T(8,128)(2,1)S(1)}, u32[]{:S(2)}, u32[]{:S(2)}) collective-permute-start(bf16[64,1024]{1,0:T(8,128)(2,1)S(1)} %get-tuple-element.28), channel_id=1, source_target_pairs={{0,4},{4,8},{8,12},{12,0},{1,5},{5,9},{9,13},{13,1},{2,6},{6,10},{... | collective-permute-start | bytes 393224 | tf_op jit(solution)/shard_map/ppermute | solution.py:164
  33.2 1.6 %collective-permute-start.10 = (bf16[64,1024]{1,0:T(8,128)(2,1)S(1)}, bf16[64,1024]{1,0:T(8,128)(2,1)S(1)}, u32[]{:S(2)}, u32[]{:S(2)}) collective-permute-start(bf16[64,1024]{1,0:T(8,128)(2,1)S(1)} %get-tuple-element.26), channel_id=1, source_target_pairs={{0,8},{4,12},{8,0},{12,4},{1,9},{5,13},{9,1},{13,5},{2,10},{6,14},... | collective-permute-start | bytes 393224 | tf_op jit(solution)/shard_map/ppermute | solution.py:164
  34.7 0.0 copy-done
  34.7 1.0 %fusion.20 = (bf16[2,128,512]{2,1,0:T(8,128)(2,1)S(1)}, bf16[2,128,512]{2,1,0:T(8,128)(2,1)S(1)}) fusion(bf16[2,64,1024]{2,1,0:T(8,128)(2,1)S(1)} %bitcast.76, bf16[2,64,1024]{2,1,0:T(8,128)(2,1)} %bitcast.78), kind=kLoop, calls=%fused_computation.33 | loop fusion | flops 1179648 | bytes 1048576 | tf_op jit(solution)/shard_map/concatenate | solution.py:168
  35.7 0.0 collective-permute-done.3
  35.8 1.7 %collective-permute-start.11 = (bf16[64,1024]{1,0:T(8,128)(2,1)S(1)}, bf16[64,1024]{1,0:T(8,128)(2,1)S(1)}, u32[]{:S(2)}, u32[]{:S(2)}) collective-permute-start(bf16[64,1024]{1,0:T(8,128)(2,1)S(1)} %get-tuple-element.27), channel_id=1, source_target_pairs={{0,12},{4,0},{8,4},{12,8},{1,13},{5,1},{9,5},{13,9},{2,14},{6,2},{... | collective-permute-start | bytes 393224 | tf_op jit(solution)/shard_map/ppermute | solution.py:164
  37.4 1.0 %fusion.19 = (bf16[2,1,128,1024]{3,2,1,0:T(8,128)(2,1)S(1)}, bf16[2,1,128,1024]{3,2,1,0:T(8,128)(2,1)S(1)}) fusion(bf16[2,64,1024]{2,1,0:T(8,128)(2,1)} %bitcast.79, bf16[2,64,1024]{2,1,0:T(8,128)(2,1)S(1)} %bitcast.77, bf16[2,128,512]{2,1,0:T(8,128)(2,1)S(1)} %get-tuple-element.12, bf16[2,128,512]{2,1,0:T(8,128)(2,1)S(1)} %get-tuple-element.11), kind=kLoop, calls=%fused_computation.29 | loop fusion | flops 2097152 | bytes 2097152 | tf_op jit(solution)/shard_map/stack | solution.py:171
  38.5 0.0 collective-permute-done.4
  38.5 0.0 collective-permute-done.5
  38.5 2.3 %collective-permute-done.9 = bf16[64,1024]{1,0:T(8,128)(2,1)S(1)} collective-permute-done((bf16[64,1024]{1,0:T(8,128)(2,1)S(1)}, bf16[64,1024]{1,0:T(8,128)(2,1)S(1)}, u32[]{:S(2)}, u32[]{:S(2)}) %collective-permute-start.9) | collective-permute-done | bytes 131104 | tf_op jit(solution)/shard_map/ppermute | solution.py:164
  40.8 3.4 %collective-permute-done.10 = bf16[64,1024]{1,0:T(8,128)(2,1)S(1)} collective-permute-done((bf16[64,1024]{1,0:T(8,128)(2,1)S(1)}, bf16[64,1024]{1,0:T(8,128)(2,1)S(1)}, u32[]{:S(2)}, u32[]{:S(2)}) %collective-permute-start.10) | collective-permute-done | bytes 131104 | tf_op jit(solution)/shard_map/ppermute | solution.py:164
  44.2 0.9 %collective-permute-done.11 = bf16[64,1024]{1,0:T(8,128)(2,1)S(1)} collective-permute-done((bf16[64,1024]{1,0:T(8,128)(2,1)S(1)}, bf16[64,1024]{1,0:T(8,128)(2,1)S(1)}, u32[]{:S(2)}, u32[]{:S(2)}) %collective-permute-start.11) | collective-permute-done | bytes 131104 | tf_op jit(solution)/shard_map/ppermute | solution.py:164
  45.1 0.7 %convolution_bitcast_fusion = f32[4,2,2,128,128]{3,4,2,1,0:T(8,128)S(1)} fusion(bf16[1,1,64,1024]{3,2,1,0:T(8,128)(2,1)S(1)} %bitcast.94, bf16[1,1,64,1024]{3,2,1,0:T(8,128)(2,1)S(1)} %bitcast.93, bf16[1,1,64,1024]{3,2,1,0:T(8,128)(2,1)S(1)} %bitcast.92, bf16[1,1,64,1024]{3,2,1,0:T(8,128)(2,1)S(1)} %get-tuple-element.25, ...), kind=kOutput, calls=%fused_computation.1 | convolution fusion | flops 547356672 | bytes 3145728 | tf_op jit(solution)/shard_map/lrif,dkjf->dklrij/dot_general | solution.py:172
  45.9 0.6 %gather_fusion = f32[4,2,2,128,128]{3,4,2,1,0:T(8,128)S(1)} fusion(f32[4,2,2,128,128]{3,4,2,1,0:T(8,128)S(1)} %convolution_bitcast_fusion, s32[1024]{0:T(1024)S(1)} %pad_clamp_fusion), kind=kCustom, calls=%fused_computation | custom fusion | bytes 2097168 | tf_op jit(solution)/shard_map/jit(_take)/gather | solution.py:174
  46.5 0.2 fusion.18
  46.7 1.0 %copy.13 = bf16[1,1,4,1,2,2,128,128]{7,6,5,4,3,2,1,0:T(8,128)(2,1)} copy(bf16[1,1,4,1,2,2,128,128]{6,7,5,4,2,3,1,0:T(8,128)(2,1)S(1)} %fusion.18) | data formatting | bytes 1048576 | tf_op jit(solution)/shard_map/convert_element_type | solution.py:178
  (6 shorter events, 0.1 us)
Async XLA Ops:
  0.0 4.9 %copy-start.2 = (s32[1,1,4]{2,1,0:T(1,128)S(1)}, s32[1,1,4]{2,1,0:T(1,128)}, u32[]{:S(2)}) copy-start(s32[1,1,4]{2,1,0:T(1,128)} %param.11) | copy-start | bytes 52
  0.0 5.0 %copy-start.1 = (s32[1,1,4,1]{2,3,1,0:T(1,128)S(1)}, s32[1,1,4,1]{2,3,1,0:T(1,128)}, u32[]{:S(2)}) copy-start(s32[1,1,4,1]{2,3,1,0:T(1,128)} %param.10) | copy-start | bytes 52
  1.4 6.8 %collective-permute-start.2 = (bf16[128,512]{1,0:T(8,128)(2,1)S(1)}, bf16[128,512]{1,0:T(8,128)(2,1)S(1)}, u32[]{:S(2)}, u32[]{:S(2)}) collective-permute-start(bf16[128,512]{1,0:T(8,128)(2,1)S(1)} %get-tuple-element.18), channel_id=1, source_target_pairs={{0,3},{1,0},{2,1},{3,2},{4,7},{5,4},{6,5},{7,6},{8,11},{9,8},{10,9... | collective-permute-start | bytes 393224 | tf_op jit(solution)/shard_map/ppermute | solution.py:151
  3.8 5.8 %collective-permute-start = (bf16[128,512]{1,0:T(8,128)(2,1)S(1)}, bf16[128,512]{1,0:T(8,128)(2,1)S(1)}, u32[]{:S(2)}, u32[]{:S(2)}) collective-permute-start(bf16[128,512]{1,0:T(8,128)(2,1)S(1)} %get-tuple-element.20), channel_id=1, source_target_pairs={{0,1},{1,2},{2,3},{3,0},{4,5},{5,6},{6,7},{7,4},{8,9},{9,10},{10,1... | collective-permute-start | bytes 393224 | tf_op jit(solution)/shard_map/ppermute | solution.py:151
  3.8 6.8 %collective-permute-start.1 = (bf16[128,512]{1,0:T(8,128)(2,1)S(1)}, bf16[128,512]{1,0:T(8,128)(2,1)S(1)}, u32[]{:S(2)}, u32[]{:S(2)}) collective-permute-start(bf16[128,512]{1,0:T(8,128)(2,1)S(1)} %get-tuple-element.19), channel_id=1, source_target_pairs={{0,2},{1,3},{2,0},{3,1},{4,6},{5,7},{6,4},{7,5},{8,10},{9,11},{10,... | collective-permute-start | bytes 393224 | tf_op jit(solution)/shard_map/ppermute | solution.py:151
  15.9 9.0 %collective-permute-start.6 = (bf16[128,512]{1,0:T(8,128)(2,1)S(1)}, bf16[128,512]{1,0:T(8,128)(2,1)S(1)}, u32[]{:S(2)}, u32[]{:S(2)}) collective-permute-start(bf16[128,512]{1,0:T(8,128)(2,1)S(1)} %get-tuple-element.16), channel_id=1, source_target_pairs={{0,1},{1,2},{2,3},{3,0},{4,5},{5,6},{6,7},{7,4},{8,9},{9,10},{10,1... | collective-permute-start | bytes 393224 | tf_op jit(solution)/shard_map/ppermute | solution.py:151
  16.6 9.7 %collective-permute-start.7 = (bf16[128,512]{1,0:T(8,128)(2,1)S(1)}, bf16[128,512]{1,0:T(8,128)(2,1)S(1)}, u32[]{:S(2)}, u32[]{:S(2)}) collective-permute-start(bf16[128,512]{1,0:T(8,128)(2,1)S(1)} %get-tuple-element.15), channel_id=1, source_target_pairs={{0,2},{1,3},{2,0},{3,1},{4,6},{5,7},{6,4},{7,5},{8,10},{9,11},{10,... | collective-permute-start | bytes 393224 | tf_op jit(solution)/shard_map/ppermute | solution.py:151
  18.3 8.0 %collective-permute-start.8 = (bf16[128,512]{1,0:T(8,128)(2,1)S(1)}, bf16[128,512]{1,0:T(8,128)(2,1)S(1)}, u32[]{:S(2)}, u32[]{:S(2)}) collective-permute-start(bf16[128,512]{1,0:T(8,128)(2,1)S(1)} %get-tuple-element.14), channel_id=1, source_target_pairs={{0,3},{1,0},{2,1},{3,2},{4,7},{5,4},{6,5},{7,6},{8,11},{9,8},{10,9... | collective-permute-start | bytes 393224 | tf_op jit(solution)/shard_map/ppermute | solution.py:151
  20.7 15.1 %collective-permute-start.3 = (bf16[64,1024]{1,0:T(8,128)(2,1)S(1)}, bf16[64,1024]{1,0:T(8,128)(2,1)S(1)}, u32[]{:S(2)}, u32[]{:S(2)}) collective-permute-start(bf16[64,1024]{1,0:T(8,128)(2,1)S(1)} %get-tuple-element.24), channel_id=1, source_target_pairs={{0,4},{4,8},{8,12},{12,0},{1,5},{5,9},{9,13},{13,1},{2,6},{6,10},{... | collective-permute-start | bytes 393224 | tf_op jit(solution)/shard_map/ppermute | solution.py:164
  22.3 16.2 %collective-permute-start.4 = (bf16[64,1024]{1,0:T(8,128)(2,1)S(1)}, bf16[64,1024]{1,0:T(8,128)(2,1)S(1)}, u32[]{:S(2)}, u32[]{:S(2)}) collective-permute-start(bf16[64,1024]{1,0:T(8,128)(2,1)S(1)} %get-tuple-element.22), channel_id=1, source_target_pairs={{0,8},{4,12},{8,0},{12,4},{1,9},{5,13},{9,1},{13,5},{2,10},{6,14},... | collective-permute-start | bytes 393224 | tf_op jit(solution)/shard_map/ppermute | solution.py:164
  24.9 13.6 %collective-permute-start.5 = (bf16[64,1024]{1,0:T(8,128)(2,1)S(1)}, bf16[64,1024]{1,0:T(8,128)(2,1)S(1)}, u32[]{:S(2)}, u32[]{:S(2)}) collective-permute-start(bf16[64,1024]{1,0:T(8,128)(2,1)S(1)} %get-tuple-element.23), channel_id=1, source_target_pairs={{0,12},{4,0},{8,4},{12,8},{1,13},{5,1},{9,5},{13,9},{2,14},{6,2},{... | collective-permute-start | bytes 393224 | tf_op jit(solution)/shard_map/ppermute | solution.py:164
  27.1 7.6 %copy-start = (bf16[128,1024]{1,0:T(8,128)(2,1)S(1)}, bf16[128,1024]{1,0:T(8,128)(2,1)}, u32[]{:S(2)}) copy-start(bf16[128,1024]{1,0:T(8,128)(2,1)} %shard_map.91) | copy-start | bytes 786436
  32.4 8.3 %collective-permute-start.9 = (bf16[64,1024]{1,0:T(8,128)(2,1)S(1)}, bf16[64,1024]{1,0:T(8,128)(2,1)S(1)}, u32[]{:S(2)}, u32[]{:S(2)}) collective-permute-start(bf16[64,1024]{1,0:T(8,128)(2,1)S(1)} %get-tuple-element.28), channel_id=1, source_target_pairs={{0,4},{4,8},{8,12},{12,0},{1,5},{5,9},{9,13},{13,1},{2,6},{6,10},{... | collective-permute-start | bytes 393224 | tf_op jit(solution)/shard_map/ppermute | solution.py:164
  33.2 11.0 %collective-permute-start.10 = (bf16[64,1024]{1,0:T(8,128)(2,1)S(1)}, bf16[64,1024]{1,0:T(8,128)(2,1)S(1)}, u32[]{:S(2)}, u32[]{:S(2)}) collective-permute-start(bf16[64,1024]{1,0:T(8,128)(2,1)S(1)} %get-tuple-element.26), channel_id=1, source_target_pairs={{0,8},{4,12},{8,0},{12,4},{1,9},{5,13},{9,1},{13,5},{2,10},{6,14},... | collective-permute-start | bytes 393224 | tf_op jit(solution)/shard_map/ppermute | solution.py:164
  35.8 9.4 %collective-permute-start.11 = (bf16[64,1024]{1,0:T(8,128)(2,1)S(1)}, bf16[64,1024]{1,0:T(8,128)(2,1)S(1)}, u32[]{:S(2)}, u32[]{:S(2)}) collective-permute-start(bf16[64,1024]{1,0:T(8,128)(2,1)S(1)} %get-tuple-element.27), channel_id=1, source_target_pairs={{0,12},{4,0},{8,4},{12,8},{1,13},{5,1},{9,5},{13,9},{2,14},{6,2},{... | collective-permute-start | bytes 393224 | tf_op jit(solution)/shard_map/ppermute | solution.py:164

commit v5 on v3

--- a/solution.py
+++ b/solution.py
@@ -151,24 +151,20 @@
             slots.append(lax.ppermute(piece, "tm", perm=[(i, (i + d) % ntm) for i in range(ntm)]))
         whitened = spectra(pos, jnp.stack(slots)).reshape(blocks, rows, 2 * NBAND)
         own_parts.append(whitened)
-        recv = []
-        for d in range(peers):
-            dest = (mine + d) % peers
-            row = []
-            for k in range(cap):
-                blk = lax.dynamic_index_in_dim(whitened, ids[dest, k], axis=0, keepdims=False)
-                if d:
-                    blk = lax.ppermute(blk, "chan", perm=[(i, (i + d) % peers) for i in range(peers)])
-                row.append(blk)
-            recv.append(jnp.stack(row))
-        picked_parts.append(jnp.stack(recv))
+        outgoing = []
+        for k in range(cap):
+            want = ids[:, k][:, None, None]
+            sel = jnp.broadcast_to(whitened[0], (peers, rows, 2 * NBAND))
+            for b in range(1, blocks):
+                sel = jnp.where(want == b, whitened[b][None], sel)
+            outgoing.append(sel)
+        outgoing = jnp.stack(outgoing, axis=1)
+        picked_parts.append(lax.all_to_all(outgoing, "chan", 0, 0, tiled=True))
     whitened = jnp.concatenate(own_parts, axis=1)
     picked = jnp.concatenate(picked_parts, axis=2)
     turned = jnp.concatenate([whitened[..., NBAND:], -whitened[..., :NBAND]], axis=-1)
     paired = jnp.stack([whitened, turned], axis=1)
     result = jnp.einsum("lrif,dkjf->dklrij", paired, picked, preferred_element_type=jnp.float32)
-    order = (mine - jnp.arange(peers, dtype=jnp.int32)) % peers
-    result = jnp.take(result, order, axis=0)
     result = result * (1.0 / math.sqrt(NBAND))
     live = jnp.arange(cap, dtype=jnp.int32)[None, :] < pair_count[0, 0][:, None]
     result = jnp.where(live[:, :, None, None, None, None], result, 0.0)

time: 55.7 us -> 70.6 us (1.27)
  blocking collectives: 0 us -> 19.6 us
  waiting for transfers between devices: 12.3 us -> 24.3 us
  between operations: 7.77 us -> 0.12 us
  starting transfers between devices: 16.3 us -> 10.8 us
  local copies, waits for them, and re-layouts: 5.99 us -> 3.4 us
    all_to_all x0 -> x1, blocking collectives: none -> 19.6 us  [local(): picked_parts.append(lax.all_to_all(outgoing, 'chan', 0, 0, tiled=True))]
    all_to_all x0 -> x1, waiting for transfers between devices: none -> 13.8 us  [local(): picked_parts.append(lax.all_to_all(outgoing, 'chan', 0, 0, tiled=True))]
    ppermute x6 -> x0, starting transfers between devices: 9.5 us -> none  [local(): lax.ppermute(blk, 'chan', perm=[(i, (i + d) % peers) for i in range(peers)])]
    ppermute x6 -> x0, waiting for transfers between devices: 7.71 us -> none  [local(): lax.ppermute(blk, 'chan', perm=[(i, (i + d) % peers) for i in range(peers)])]
    ppermute x6, waiting for transfers between devices: 4.63 us -> 10.4 us  [local(): lax.ppermute(piece, 'tm', perm=[(i, (i + d) % ntm) for i in range(ntm)])]
    all_to_all x0 -> x1, starting transfers between devices: none -> 3.47 us  [local(): picked_parts.append(lax.all_to_all(outgoing, 'chan', 0, 0, tiled=True))]
    another operation x2 -> x0, local copies, waits for them, and re-layouts: 2.31 us -> none  [local(): picked_parts.append(jnp.stack(recv))]
    broadcast_in_dim x0 -> x1, local copies, waits for them, and re-layouts: none -> 1.01 us  [local(): return result.astype(jnp.bfloat16)[None, None]]
  transfers between devices with their start and end apart: 12 -> 7, of which waited for: 5 -> 7; matrix products, arithmetic and copies ran while one was open for 9% -> 0% of each run, Pallas kernels for 8% -> 0%
where the time goes in v5:
time: 70.6 us; the launch traced here: 70.3 us
  waiting for transfers between devices  24.3 us (34%)
  blocking collectives  19.6 us (28%)
  starting transfers between devices  10.8 us (15%)
  Pallas kernels  8.59 us (12%)
  local copies, waits for them, and re-layouts  3.4 us (5%)
  other arithmetic  2.86 us (4%)
  matrix products  0.74 us (1%)
    all_to_all x1, blocking collectives, local(): picked_parts.append(lax.all_to_all(outgoing, 'chan', 0, 0, tiled=True))  19.6 us
    all_to_all x1, waiting for transfers between devices, local(): picked_parts.append(lax.all_to_all(outgoing, 'chan', 0, 0, tiled=True))  13.8 us
    ppermute x6, waiting for transfers between devices, local(): lax.ppermute(piece, 'tm', perm=[(i, (i + d) % ntm) for i in range(ntm)])  10.4 us
    pallas_call x2, Pallas kernels, spectra(): pl.pallas_call(spectra_kernel, grid_spec=grid_spec, cost_estimate=pl.Cost...  8.59 us
    ppermute x6, starting transfers between devices, local(): lax.ppermute(piece, 'tm', perm=[(i, (i + d) % ntm) for i in range(ntm)])  7.29 us
    all_to_all x1, starting transfers between devices, local(): picked_parts.append(lax.all_to_all(outgoing, 'chan', 0, 0, tiled=True))  3.47 us
    another operation x2, other arithmetic, local(): whitened = spectra(pos, jnp.stack(slots)).reshape(blocks, rows, 2 * NBAND)  1.72 us
  transfers between devices with their start and end apart: 7, of which 7 were waited for; matrix products, arithmetic and copies ran while one was open for 0% of the time, Pallas kernels for 0%

profile of v5, /device:TPU:0, one launch (start us, length us, event | category | flops | bytes accessed | tf_op | source)
XLA Modules:
  0.0 70.3 jit_solution(4157554892318790957)
XLA Ops:
  0.0 1.3 %fusion.13 = (bf16[4,2,1,64,512]{4,3,2,1,0:T(8,128)(2,1)S(1)}, bf16[4,2,1,64,512]{4,3,2,1,0:T(8,128)(2,1)S(1)}) fusion(bf16[4,2,2,64,512]{4,3,2,1,0:T(8,128)(2,1)} %bitcast.68), kind=kLoop, calls=%fused_computation.36 | loop fusion | bytes 2097152 | tf_op jit(solution)/shard_map/slice | solution.py:145
  1.4 2.4 %collective-permute-start.2 = (bf16[128,512]{1,0:T(8,128)(2,1)S(1)}, bf16[128,512]{1,0:T(8,128)(2,1)S(1)}, u32[]{:S(2)}, u32[]{:S(2)}) collective-permute-start(bf16[128,512]{1,0:T(8,128)(2,1)S(1)} %get-tuple-element.18), channel_id=1, source_target_pairs={{0,3},{1,0},{2,1},{3,2},{4,7},{5,4},{6,5},{7,6},{8,11},{9,8},{10,9... | collective-permute-start | bytes 393224 | tf_op jit(solution)/shard_map/ppermute | solution.py:151
  3.8 0.0 collective-permute-start
  3.8 1.1 %collective-permute-start.1 = (bf16[128,512]{1,0:T(8,128)(2,1)S(1)}, bf16[128,512]{1,0:T(8,128)(2,1)S(1)}, u32[]{:S(2)}, u32[]{:S(2)}) collective-permute-start(bf16[128,512]{1,0:T(8,128)(2,1)S(1)} %get-tuple-element.19), channel_id=1, source_target_pairs={{0,2},{1,3},{2,0},{3,1},{4,6},{5,7},{6,4},{7,5},{8,10},{9,11},{10,... | collective-permute-start | bytes 393224 | tf_op jit(solution)/shard_map/ppermute | solution.py:151
  4.9 2.8 %collective-permute-done.2 = bf16[128,512]{1,0:T(8,128)(2,1)S(1)} collective-permute-done((bf16[128,512]{1,0:T(8,128)(2,1)S(1)}, bf16[128,512]{1,0:T(8,128)(2,1)S(1)}, u32[]{:S(2)}, u32[]{:S(2)}) %collective-permute-start.2) | collective-permute-done | bytes 131104 | tf_op jit(solution)/shard_map/ppermute | solution.py:151
  7.6 1.9 %collective-permute-done = bf16[128,512]{1,0:T(8,128)(2,1)S(1)} collective-permute-done((bf16[128,512]{1,0:T(8,128)(2,1)S(1)}, bf16[128,512]{1,0:T(8,128)(2,1)S(1)}, u32[]{:S(2)}, u32[]{:S(2)}) %collective-permute-start) | collective-permute-done | bytes 131104 | tf_op jit(solution)/shard_map/ppermute | solution.py:151
  9.6 1.1 %collective-permute-done.1 = bf16[128,512]{1,0:T(8,128)(2,1)S(1)} collective-permute-done((bf16[128,512]{1,0:T(8,128)(2,1)S(1)}, bf16[128,512]{1,0:T(8,128)(2,1)S(1)}, u32[]{:S(2)}, u32[]{:S(2)}) %collective-permute-start.1) | collective-permute-done | bytes 131104 | tf_op jit(solution)/shard_map/ppermute | solution.py:151
  10.6 0.9 %pad_maximum_fusion.1.x_ref = bf16[4,128,512]{2,1,0:T(8,128)(2,1)} fusion(bf16[1,128,512]{2,1,0:T(8,128)(2,1)S(1)} %bitcast.72, bf16[1,128,512]{2,1,0:T(8,128)(2,1)S(1)} %bitcast.76, bf16[1,128,512]{2,1,0:T(8,128)(2,1)S(1)} %bitcast.74, bf16[1,128,512]{2,1,0:T(8,128)(2,1)S(1)} %get-tuple-element.17), kind=kLoop, calls=%fused_computation.17 | loop fusion | flops 786432 | bytes 1048576 | tf_op jit(solution)/shard_map/stack | solution.py:152
  11.5 0.0 copy-start.2
  11.5 4.3 %shard_map.91 = bf16[128,1024]{1,0:T(8,128)(2,1)} custom-call(s32[1]{0:T(128)} %bitcast.2.pos_ref, bf16[4,128,512]{2,1,0:T(8,128)(2,1)} %pad_maximum_fusion.1.x_ref, bf16[384,256]{1,0:T(8,128)(2,1)} %constant.66.clone.band_ref, bf16[1024,1024]{1,0:T(8,128)(2,1)} %constant.67.clone.tab_ref, bf16[512,512]{1,0:T(8,128)(2,1)} %constant.68.clone.grp_ref), custom_call_target="tpu_custom_call" | custom-call | flops 1073741824 | bytes 2883584 | tf_op jit(solution)/shard_map/pallas_call | solution.py:121
  15.8 0.7 %collective-permute-start.3 = (bf16[128,512]{1,0:T(8,128)(2,1)S(1)}, bf16[128,512]{1,0:T(8,128)(2,1)S(1)}, u32[]{:S(2)}, u32[]{:S(2)}) collective-permute-start(bf16[128,512]{1,0:T(8,128)(2,1)S(1)} %get-tuple-element.16), channel_id=1, source_target_pairs={{0,1},{1,2},{2,3},{3,0},{4,5},{5,6},{6,7},{7,4},{8,9},{9,10},{10,1... | collective-permute-start | bytes 393224 | tf_op jit(solution)/shard_map/ppermute | solution.py:151
  16.6 1.7 %collective-permute-start.4 = (bf16[128,512]{1,0:T(8,128)(2,1)S(1)}, bf16[128,512]{1,0:T(8,128)(2,1)S(1)}, u32[]{:S(2)}, u32[]{:S(2)}) collective-permute-start(bf16[128,512]{1,0:T(8,128)(2,1)S(1)} %get-tuple-element.15), channel_id=1, source_target_pairs={{0,2},{1,3},{2,0},{3,1},{4,6},{5,7},{6,4},{7,5},{8,10},{9,11},{10,... | collective-permute-start | bytes 393224 | tf_op jit(solution)/shard_map/ppermute | solution.py:151
  18.3 1.3 %collective-permute-start.5 = (bf16[128,512]{1,0:T(8,128)(2,1)S(1)}, bf16[128,512]{1,0:T(8,128)(2,1)S(1)}, u32[]{:S(2)}, u32[]{:S(2)}) collective-permute-start(bf16[128,512]{1,0:T(8,128)(2,1)S(1)} %get-tuple-element.14), channel_id=1, source_target_pairs={{0,3},{1,0},{2,1},{3,2},{4,7},{5,4},{6,5},{7,6},{8,11},{9,8},{10,9... | collective-permute-start | bytes 393224 | tf_op jit(solution)/shard_map/ppermute | solution.py:151
  19.6 0.0 copy-done.2
  19.6 1.3 %collective-permute-done.3 = bf16[128,512]{1,0:T(8,128)(2,1)S(1)} collective-permute-done((bf16[128,512]{1,0:T(8,128)(2,1)S(1)}, bf16[128,512]{1,0:T(8,128)(2,1)S(1)}, u32[]{:S(2)}, u32[]{:S(2)}) %collective-permute-start.3) | collective-permute-done | bytes 131104 | tf_op jit(solution)/shard_map/ppermute | solution.py:151
  20.9 2.0 %collective-permute-done.4 = bf16[128,512]{1,0:T(8,128)(2,1)S(1)} collective-permute-done((bf16[128,512]{1,0:T(8,128)(2,1)S(1)}, bf16[128,512]{1,0:T(8,128)(2,1)S(1)}, u32[]{:S(2)}, u32[]{:S(2)}) %collective-permute-start.4) | collective-permute-done | bytes 131104 | tf_op jit(solution)/shard_map/ppermute | solution.py:151
  23.0 1.3 %collective-permute-done.5 = bf16[128,512]{1,0:T(8,128)(2,1)S(1)} collective-permute-done((bf16[128,512]{1,0:T(8,128)(2,1)S(1)}, bf16[128,512]{1,0:T(8,128)(2,1)S(1)}, u32[]{:S(2)}, u32[]{:S(2)}) %collective-permute-start.5) | collective-permute-done | bytes 131104 | tf_op jit(solution)/shard_map/ppermute | solution.py:151
  24.3 0.9 %pad_maximum_fusion.2.x_ref = bf16[4,128,512]{2,1,0:T(8,128)(2,1)} fusion(bf16[1,128,512]{2,1,0:T(8,128)(2,1)S(1)} %bitcast.75, bf16[1,128,512]{2,1,0:T(8,128)(2,1)S(1)} %bitcast.73, bf16[1,128,512]{2,1,0:T(8,128)(2,1)S(1)} %bitcast.71, bf16[1,128,512]{2,1,0:T(8,128)(2,1)S(1)} %get-tuple-element.13), kind=kLoop, calls=%fused_computation.18 | loop fusion | flops 786432 | bytes 1048576 | tf_op jit(solution)/shard_map/stack | solution.py:152
  25.2 0.0 copy-start
  25.2 4.3 %shard_map.92 = bf16[128,1024]{1,0:T(8,128)(2,1)} custom-call(s32[1]{0:T(128)} %bitcast.2.pos_ref, bf16[4,128,512]{2,1,0:T(8,128)(2,1)} %pad_maximum_fusion.2.x_ref, bf16[384,256]{1,0:T(8,128)(2,1)} %constant.66.clone.band_ref, bf16[1024,1024]{1,0:T(8,128)(2,1)} %constant.67.clone.tab_ref, bf16[512,512]{1,0:T(8,128)(2,1)} %constant.68.clone.grp_ref), custom_call_target="tpu_custom_call" | custom-call | flops 1073741824 | bytes 2883584 | tf_op jit(solution)/shard_map/pallas_call | solution.py:121
  29.5 0.0 copy-done
  29.5 1.0 %fusion.14 = (bf16[64,1024]{1,0:T(8,128)(2,1)S(1)}, bf16[64,1024]{1,0:T(8,128)(2,1)S(1)}, bf16[64,1024]{1,0:T(8,128)(2,1)S(1)}, bf16[64,1024]{1,0:T(8,128)(2,1)S(1)}) fusion(bf16[128,1024]{1,0:T(8,128)(2,1)S(1)} %copy-done, bf16[128,1024]{1,0:T(8,128)(2,1)} %shard_map.92), kind=kLoop, calls=%fused_computation.37 | loop fusion | bytes 1048576 | tf_op jit(solution)/shard_map/slice | solution.py:159
  30.5 0.0 copy-start.3
  30.5 0.0 copy-start.1
  30.5 1.0 %broadcast_select_fusion.1 = (bf16[4,1,64,1024]{3,2,1,0:T(8,128)(2,1)S(1)}, bf16[4,1,64,1024]{3,2,1,0:T(8,128)(2,1)}) fusion(pred[4]{0:T(512)(128)(4,1)S(1)} %compare_bitcast_fusion, bf16[64,1024]{1,0:T(8,128)(2,1)S(1)} %get-tuple-element.22, bf16[64,1024]{1,0:T(8,128)(2,1)S(1)} %get-tuple-element.21, bf16[64,1024]{1,0:T(8,128)(2,1)S(1)} %get-tuple-element.27, ...), kind=kLoop, calls=%fused_computation.21 | loop fusion | flops 524288 | bytes 1572868 | tf_op jit(solution)/shard_map/jit(_where)/select_n | solution.py:159
  31.4 19.6 %all_to_all.10 = bf16[4,1,64,1024]{3,2,1,0:T(8,128)(2,1)S(1)} all-to-all(bf16[4,1,64,1024]{3,2,1,0:T(8,128)(2,1)S(1)} %get-tuple-element.25), channel_id=1, replica_groups=mesh['groups'=2,'chan'=4,'tm'=4] {'chan'}, dimensions={0} | all-to-all | bytes 1048576 | tf_op jit(solution)/shard_map/all_to_all | solution.py:162
  51.0 3.5 %all-to-all-start.1 = ((bf16[4,1,64,1024]{3,2,1,0:T(8,128)(2,1)}), bf16[4,1,64,1024]{3,2,1,0:T(8,128)(2,1)S(1)}, u32[]{:S(2)}, u32[]{:S(2)}) async-start(bf16[4,1,64,1024]{3,2,1,0:T(8,128)(2,1)} %get-tuple-element.26), calls=%async_computation.1 | async-start | bytes 1048576 | tf_op jit(solution)/shard_map/all_to_all | solution.py:162
  54.5 0.0 copy-done.3
  54.5 0.0 copy-done.1
  54.6 0.1 fusion.9
  54.6 0.1 fusion.8
  54.7 13.8 %all-to-all-done.1 = bf16[4,1,64,1024]{3,2,1,0:T(8,128)(2,1)S(1)} async-done(((bf16[4,1,64,1024]{3,2,1,0:T(8,128)(2,1)}), bf16[4,1,64,1024]{3,2,1,0:T(8,128)(2,1)S(1)}, u32[]{:S(2)}, u32[]{:S(2)}) %all-to-all-start.1) | async-done | bytes 524320 | tf_op jit(solution)/shard_map/all_to_all | solution.py:162
  68.6 0.7 %fusion.3 = bf16[1,1,4,1,2,2,128,128]{6,7,5,4,2,3,1,0:T(8,128)(2,1)S(1)} fusion(bf16[4,1,64,1024]{3,2,0,1:T(8,128)(2,1)S(1)} %bitcast.70, bf16[4,1,64,1024]{3,2,0,1:T(8,128)(2,1)S(1)} %bitcast.69, bf16[2,1,128,1024]{3,2,1,0:T(8,128)(2,1)S(1)} %get-tuple-element.30, bf16[2,1,128,1024]{3,2,1,0:T(8,128)(2,1)S(1)} %get-tuple-element.29, ...), kind=kOutput, calls=%fused_computation.4 | convolution fusion | flops 541851648 | bytes 2621444 | tf_op jit(solution)/shard_map/lrif,dkjf->dklrij/dot_general | solution.py:167
  69.3 1.0 %copy.19 = bf16[1,1,4,1,2,2,128,128]{7,6,5,4,3,2,1,0:T(8,128)(2,1)} copy(bf16[1,1,4,1,2,2,128,128]{6,7,5,4,2,3,1,0:T(8,128)(2,1)S(1)} %fusion.3) | data formatting | bytes 1048576 | tf_op jit(solution)/shard_map/broadcast_in_dim | solution.py:171
  (4 shorter events, 0.1 us)
Async XLA Ops:
  1.4 6.3 %collective-permute-start.2 = (bf16[128,512]{1,0:T(8,128)(2,1)S(1)}, bf16[128,512]{1,0:T(8,128)(2,1)S(1)}, u32[]{:S(2)}, u32[]{:S(2)}) collective-permute-start(bf16[128,512]{1,0:T(8,128)(2,1)S(1)} %get-tuple-element.18), channel_id=1, source_target_pairs={{0,3},{1,0},{2,1},{3,2},{4,7},{5,4},{6,5},{7,6},{8,11},{9,8},{10,9... | collective-permute-start | bytes 393224 | tf_op jit(solution)/shard_map/ppermute | solution.py:151
  3.8 5.8 %collective-permute-start = (bf16[128,512]{1,0:T(8,128)(2,1)S(1)}, bf16[128,512]{1,0:T(8,128)(2,1)S(1)}, u32[]{:S(2)}, u32[]{:S(2)}) collective-permute-start(bf16[128,512]{1,0:T(8,128)(2,1)S(1)} %get-tuple-element.20), channel_id=1, source_target_pairs={{0,1},{1,2},{2,3},{3,0},{4,5},{5,6},{6,7},{7,4},{8,9},{9,10},{10,1... | collective-permute-start | bytes 393224 | tf_op jit(solution)/shard_map/ppermute | solution.py:151
  3.8 6.8 %collective-permute-start.1 = (bf16[128,512]{1,0:T(8,128)(2,1)S(1)}, bf16[128,512]{1,0:T(8,128)(2,1)S(1)}, u32[]{:S(2)}, u32[]{:S(2)}) collective-permute-start(bf16[128,512]{1,0:T(8,128)(2,1)S(1)} %get-tuple-element.19), channel_id=1, source_target_pairs={{0,2},{1,3},{2,0},{3,1},{4,6},{5,7},{6,4},{7,5},{8,10},{9,11},{10,... | collective-permute-start | bytes 393224 | tf_op jit(solution)/shard_map/ppermute | solution.py:151
  11.5 8.1 %copy-start.2 = (s32[1,1,4,1]{2,3,1,0:T(1,128)S(1)}, s32[1,1,4,1]{2,3,1,0:T(1,128)}, u32[]{:S(2)}) copy-start(s32[1,1,4,1]{2,3,1,0:T(1,128)} %param.10) | copy-start | bytes 52
  15.8 5.1 %collective-permute-start.3 = (bf16[128,512]{1,0:T(8,128)(2,1)S(1)}, bf16[128,512]{1,0:T(8,128)(2,1)S(1)}, u32[]{:S(2)}, u32[]{:S(2)}) collective-permute-start(bf16[128,512]{1,0:T(8,128)(2,1)S(1)} %get-tuple-element.16), channel_id=1, source_target_pairs={{0,1},{1,2},{2,3},{3,0},{4,5},{5,6},{6,7},{7,4},{8,9},{9,10},{10,1... | collective-permute-start | bytes 393224 | tf_op jit(solution)/shard_map/ppermute | solution.py:151
  16.6 6.4 %collective-permute-start.4 = (bf16[128,512]{1,0:T(8,128)(2,1)S(1)}, bf16[128,512]{1,0:T(8,128)(2,1)S(1)}, u32[]{:S(2)}, u32[]{:S(2)}) collective-permute-start(bf16[128,512]{1,0:T(8,128)(2,1)S(1)} %get-tuple-element.15), channel_id=1, source_target_pairs={{0,2},{1,3},{2,0},{3,1},{4,6},{5,7},{6,4},{7,5},{8,10},{9,11},{10,... | collective-permute-start | bytes 393224 | tf_op jit(solution)/shard_map/ppermute | solution.py:151
  18.3 6.0 %collective-permute-start.5 = (bf16[128,512]{1,0:T(8,128)(2,1)S(1)}, bf16[128,512]{1,0:T(8,128)(2,1)S(1)}, u32[]{:S(2)}, u32[]{:S(2)}) collective-permute-start(bf16[128,512]{1,0:T(8,128)(2,1)S(1)} %get-tuple-element.14), channel_id=1, source_target_pairs={{0,3},{1,0},{2,1},{3,2},{4,7},{5,4},{6,5},{7,6},{8,11},{9,8},{10,9... | collective-permute-start | bytes 393224 | tf_op jit(solution)/shard_map/ppermute | solution.py:151
  25.2 4.3 %copy-start = (bf16[128,1024]{1,0:T(8,128)(2,1)S(1)}, bf16[128,1024]{1,0:T(8,128)(2,1)}, u32[]{:S(2)}) copy-start(bf16[128,1024]{1,0:T(8,128)(2,1)} %shard_map.91) | copy-start | bytes 786436
  30.5 24.1 %copy-start.3 = (s32[1,1,4]{2,1,0:T(1,128)S(1)}, s32[1,1,4]{2,1,0:T(1,128)}, u32[]{:S(2)}) copy-start(s32[1,1,4]{2,1,0:T(1,128)} %param.11) | copy-start | bytes 52
  30.5 24.1 %copy-start.1 = (bf16[128,1024]{1,0:T(8,128)(2,1)S(1)}, bf16[128,1024]{1,0:T(8,128)(2,1)}, u32[]{:S(2)}) copy-start(bf16[128,1024]{1,0:T(8,128)(2,1)} %shard_map.92) | copy-start | bytes 786436
  51.0 17.5 %all-to-all-start.1 = ((bf16[4,1,64,1024]{3,2,1,0:T(8,128)(2,1)}), bf16[4,1,64,1024]{3,2,1,0:T(8,128)(2,1)S(1)}, u32[]{:S(2)}, u32[]{:S(2)}) async-start(bf16[4,1,64,1024]{3,2,1,0:T(8,128)(2,1)} %get-tuple-element.26), calls=%async_computation.1 | async-start | bytes 1048576 | tf_op jit(solution)/shard_map/all_to_all | solution.py:162

commit v6 on v4

--- a/solution.py
+++ b/solution.py
@@ -17,7 +17,7 @@
 RAD = 15
 TILE = 128
 HALF = NT // 2
-NSPLIT = 2
+NSPLIT = 1
 BF16 = ml_dtypes.bfloat16
 
 

time: 48.1 us -> 52.6 us (1.094)
  the two profiles are of different devices: /device:TPU:0 before, /device:TPU:9 now
where the time goes in v6:
time: 52.6 us; the launch traced here: 52.4 us
  waiting for transfers between devices  29.8 us (57%)
  starting transfers between devices  6.12 us (12%)
  Pallas kernels  5.9 us (11%)
  other arithmetic  3.67 us (7%)
  local copies, waits for them, and re-layouts  3.54 us (7%)
  between operations  2.62 us (5%)
  matrix products  0.74 us (1%)
    ppermute x3, waiting for transfers between devices, local(): lax.ppermute(blk, 'chan', perm=[(i, (i + d) % peers) for i in range(peers)])  21.1 us
    ppermute x3, waiting for transfers between devices, local(): lax.ppermute(piece, 'tm', perm=[(i, (i + d) % ntm) for i in range(ntm)])  8.72 us
    pallas_call x1, Pallas kernels, spectra(): pl.pallas_call(spectra_kernel, grid_spec=grid_spec, cost_estimate=pl.Cost...  5.9 us
    ppermute x3, starting transfers between devices, local(): lax.ppermute(blk, 'chan', perm=[(i, (i + d) % peers) for i in range(peers)])  3.82 us
    ppermute x3, starting transfers between devices, local(): lax.ppermute(piece, 'tm', perm=[(i, (i + d) % ntm) for i in range(ntm)])  2.3 us
    dynamic_slice x1, local copies, waits for them, and re-layouts, local(): slots = [lax.dynamic_index_in_dim(part, here, axis=0, keepdims=False)]  1.28 us
    another operation x1, other arithmetic, local(): picked_parts.append(jnp.stack(recv))  1.16 us
    another operation x1, other arithmetic, local(): whitened = spectra(pos, jnp.stack(slots)).reshape(blocks, rows, 2 * NBAND)  1.11 us
  transfers between devices with their start and end apart: 6, of which 6 were waited for; matrix products, arithmetic and copies ran while one was open for 3% of the time, Pallas kernels for 0%

profile of v6, /device:TPU:9, one launch (start us, length us, event | category | flops | bytes accessed | tf_op | source)
XLA Modules:
  0.0 52.4 jit_solution(17805139358236644541)
XLA Ops:
  0.0 0.0 copy-start.1
  0.0 0.0 copy-start.2
  0.0 1.3 %constant_dynamic-slice_fusion.3 = (bf16[1,256,512]{2,1,0:T(8,128)(2,1)S(1)}, bf16[256,512]{1,0:T(8,128)(2,1)S(1)}, bf16[256,512]{1,0:T(8,128)(2,1)S(1)}, bf16[256,512]{1,0:T(8,128)(2,1)S(1)}) fusion(bf16[4,256,512]{2,1,0:T(8,128)(2,1)} %bitcast.56, s32[]{:T(128)S(6)} %select_n.147, s32[]{:T(128)S(6)} %select_n.153, s32[]{:T(128)S(6)} %select_n.151, ...), kind=kLoop, calls=%fused_computation.36 | loop fusion | bytes 2097168 | tf_op jit(solution)/shard_map/jit(dynamic_index_in_dim)/dynamic_slice | solution.py:148
  1.3 1.8 %collective-permute-start = (bf16[256,512]{1,0:T(8,128)(2,1)S(1)}, bf16[256,512]{1,0:T(8,128)(2,1)S(1)}, u32[]{:S(2)}, u32[]{:S(2)}) collective-permute-start(bf16[256,512]{1,0:T(8,128)(2,1)S(1)} %get-tuple-element.8), channel_id=1, source_target_pairs={{0,1},{1,2},{2,3},{3,0},{4,5},{5,6},{6,7},{7,4},{8,9},{9,10},{10,1... | collective-permute-start | bytes 786440 | tf_op jit(solution)/shard_map/ppermute | solution.py:151
  3.1 0.3 collective-permute-start.1
  3.4 0.2 collective-permute-start.2
  3.7 0.0 copy-done.1
  3.7 0.6 %constant_dynamic-slice_fusion.4 = (s32[1,1,1,1]{2,3,1,0:T(1,128)}, s32[1,1,1,1]{2,3,1,0:T(1,128)}, s32[1,1,1,1]{2,3,1,0:T(1,128)}, s32[1,1,1,1]{2,3,1,0:T(1,128)}) fusion(s32[1,1,4,1]{2,3,1,0:T(1,128)S(1)} %copy-done.1, s32[]{:T(128)S(6)} %select_n.145, s32[]{:T(128)S(6)} %select_n.156, s32[]{:T(128)S(6)} %select_n.164, s32[]{:T(128)S(6)} %select_n.160), kind=kLoop, calls=%fused_computation.37 | loop fusion | bytes 48 | tf_op jit(solution)/shard_map/jit(dynamic_index_in_dim)/dynamic_slice | solution.py:159
  6.8 0.0 copy-done.2
  6.8 1.8 %collective-permute-done = bf16[256,512]{1,0:T(8,128)(2,1)S(1)} collective-permute-done((bf16[256,512]{1,0:T(8,128)(2,1)S(1)}, bf16[256,512]{1,0:T(8,128)(2,1)S(1)}, u32[]{:S(2)}, u32[]{:S(2)}) %collective-permute-start) | collective-permute-done | bytes 262176 | tf_op jit(solution)/shard_map/ppermute | solution.py:151
  8.6 6.3 %collective-permute-done.1 = bf16[256,512]{1,0:T(8,128)(2,1)S(1)} collective-permute-done((bf16[256,512]{1,0:T(8,128)(2,1)S(1)}, bf16[256,512]{1,0:T(8,128)(2,1)S(1)}, u32[]{:S(2)}, u32[]{:S(2)}) %collective-permute-start.1) | collective-permute-done | bytes 262176 | tf_op jit(solution)/shard_map/ppermute | solution.py:151
  14.9 0.6 %collective-permute-done.2 = bf16[256,512]{1,0:T(8,128)(2,1)S(1)} collective-permute-done((bf16[256,512]{1,0:T(8,128)(2,1)S(1)}, bf16[256,512]{1,0:T(8,128)(2,1)S(1)}, u32[]{:S(2)}, u32[]{:S(2)}) %collective-permute-start.2) | collective-permute-done | bytes 262176 | tf_op jit(solution)/shard_map/ppermute | solution.py:151
  15.6 1.1 %pad_maximum_fusion.x_ref = bf16[4,256,512]{2,1,0:T(8,128)(2,1)} fusion(bf16[1,256,512]{2,1,0:T(8,128)(2,1)S(1)} %bitcast.59, bf16[1,256,512]{2,1,0:T(8,128)(2,1)S(1)} %bitcast.58, bf16[1,256,512]{2,1,0:T(8,128)(2,1)S(1)} %bitcast.57, bf16[1,256,512]{2,1,0:T(8,128)(2,1)S(1)} %get-tuple-element.5), kind=kLoop, calls=%fused_computation.2 | loop fusion | flops 1572864 | bytes 2097152 | tf_op jit(solution)/shard_map/stack | solution.py:152
  16.7 5.9 %shard_map.64 = bf16[256,1024]{1,0:T(8,128)(2,1)} custom-call(s32[1]{0:T(128)} %bitcast.2.pos_ref, bf16[4,256,512]{2,1,0:T(8,128)(2,1)} %pad_maximum_fusion.x_ref, bf16[384,256]{1,0:T(8,128)(2,1)} %constant.112.clone.band_ref, bf16[1024,1024]{1,0:T(8,128)(2,1)} %constant.113.clone.tab_ref, bf16[512,512]{1,0:T(8,128)(2,1)} %constant.114.clone.grp_ref), custom_call_target="tpu_custom_call" | custom-call | flops 2147483648 | bytes 3670016 | tf_op jit(solution)/shard_map/pallas_call | solution.py:121
  22.6 0.0 copy-start
  22.6 1.2 %select_bitcast_fusion = (bf16[1,1,128,1024]{3,2,1,0:T(8,128)(2,1)S(1)}, bf16[128,1024]{1,0:T(8,128)(2,1)S(1)}, bf16[128,1024]{1,0:T(8,128)(2,1)S(1)}, bf16[128,1024]{1,0:T(8,128)(2,1)S(1)}) fusion(pred[]{:T(512)} %bitcast.1, bf16[256,1024]{1,0:T(8,128)(2,1)} %shard_map.64, pred[]{:T(512)} %bitcast.13, pred[]{:T(512)} %bitcast.15, pred[]{:T(512)} %bitcast.11), kind=kLoop, calls=%fused_computation.19 | loop fusion | flops 524288 | bytes 1572868 | tf_op jit(solution)/shard_map/stack;stack | solution.py:167
  23.7 1.3 %collective-permute-start.3 = (bf16[128,1024]{1,0:T(8,128)(2,1)S(1)}, bf16[128,1024]{1,0:T(8,128)(2,1)S(1)}, u32[]{:S(2)}, u32[]{:S(2)}) collective-permute-start(bf16[128,1024]{1,0:T(8,128)(2,1)S(1)} %get-tuple-element.14), channel_id=1, source_target_pairs={{0,4},{4,8},{8,12},{12,0},{1,5},{5,9},{9,13},{13,1},{2,6},{6,10},{... | collective-permute-start | bytes 786440 | tf_op jit(solution)/shard_map/ppermute | solution.py:164
  25.1 1.1 %collective-permute-start.4 = (bf16[128,1024]{1,0:T(8,128)(2,1)S(1)}, bf16[128,1024]{1,0:T(8,128)(2,1)S(1)}, u32[]{:S(2)}, u32[]{:S(2)}) collective-permute-start(bf16[128,1024]{1,0:T(8,128)(2,1)S(1)} %get-tuple-element.12), channel_id=1, source_target_pairs={{0,8},{4,12},{8,0},{12,4},{1,9},{5,13},{9,1},{13,5},{2,10},{6,14},... | collective-permute-start | bytes 786440 | tf_op jit(solution)/shard_map/ppermute | solution.py:164
  26.2 1.4 %collective-permute-start.5 = (bf16[128,1024]{1,0:T(8,128)(2,1)S(1)}, bf16[128,1024]{1,0:T(8,128)(2,1)S(1)}, u32[]{:S(2)}, u32[]{:S(2)}) collective-permute-start(bf16[128,1024]{1,0:T(8,128)(2,1)S(1)} %get-tuple-element.13), channel_id=1, source_target_pairs={{0,12},{4,0},{8,4},{12,8},{1,13},{5,1},{9,5},{13,9},{2,14},{6,2},{... | collective-permute-start | bytes 786440 | tf_op jit(solution)/shard_map/ppermute | solution.py:164
  27.5 1.1 %fusion.15 = (bf16[2,128,512]{2,1,0:T(8,128)(2,1)S(1)}, bf16[2,128,512]{2,1,0:T(8,128)(2,1)S(1)}) fusion(bf16[2,128,1024]{2,1,0:T(8,128)(2,1)} %bitcast.54), kind=kLoop, calls=%fused_computation.46 | loop fusion | flops 131072 | bytes 1048576 | tf_op jit(solution)/shard_map/slice | solution.py:170
  28.6 0.1 maximum_bitcast_fusion.4
  28.7 3.3 %collective-permute-done.3 = bf16[128,1024]{1,0:T(8,128)(2,1)S(1)} collective-permute-done((bf16[128,1024]{1,0:T(8,128)(2,1)S(1)}, bf16[128,1024]{1,0:T(8,128)(2,1)S(1)}, u32[]{:S(2)}, u32[]{:S(2)}) %collective-permute-start.3) | collective-permute-done | bytes 262176 | tf_op jit(solution)/shard_map/ppermute | solution.py:164
  31.9 15.9 %collective-permute-done.4 = bf16[128,1024]{1,0:T(8,128)(2,1)S(1)} collective-permute-done((bf16[128,1024]{1,0:T(8,128)(2,1)S(1)}, bf16[128,1024]{1,0:T(8,128)(2,1)S(1)}, u32[]{:S(2)}, u32[]{:S(2)}) %collective-permute-start.4) | collective-permute-done | bytes 262176 | tf_op jit(solution)/shard_map/ppermute | solution.py:164
  47.9 1.9 %collective-permute-done.5 = bf16[128,1024]{1,0:T(8,128)(2,1)S(1)} collective-permute-done((bf16[128,1024]{1,0:T(8,128)(2,1)S(1)}, bf16[128,1024]{1,0:T(8,128)(2,1)S(1)}, u32[]{:S(2)}, u32[]{:S(2)}) %collective-permute-start.5) | collective-permute-done | bytes 262176 | tf_op jit(solution)/shard_map/ppermute | solution.py:164
  49.8 0.0 copy-done
  49.8 0.7 %convolution_bitcast_fusion = f32[4,2,2,128,128]{3,4,2,1,0:T(8,128)S(1)} fusion(bf16[1,1,128,1024]{3,2,1,0:T(8,128)(2,1)S(1)} %bitcast.62, bf16[1,1,128,1024]{3,2,1,0:T(8,128)(2,1)S(1)} %bitcast.61, bf16[1,1,128,1024]{3,2,1,0:T(8,128)(2,1)S(1)} %bitcast.60, bf16[1,1,128,1024]{3,2,1,0:T(8,128)(2,1)S(1)} %get-tuple-element.11, ...), kind=kOutput, calls=%fused_computation.1 | convolution fusion | flops 543162368 | bytes 3145728 | tf_op jit(solution)/shard_map/lrif,dkjf->dklrij/dot_general | solution.py:172
  50.5 0.6 %gather_fusion = f32[4,2,2,128,128]{3,4,2,1,0:T(8,128)S(1)} fusion(f32[4,2,2,128,128]{3,4,2,1,0:T(8,128)S(1)} %convolution_bitcast_fusion, s32[1024]{0:T(1024)S(1)} %pad_clamp_fusion), kind=kCustom, calls=%fused_computation | custom fusion | bytes 2097168 | tf_op jit(solution)/shard_map/jit(_take)/gather | solution.py:174
  51.2 0.2 fusion.10
  51.4 1.0 %copy.8 = bf16[1,1,4,1,2,2,128,128]{7,6,5,4,3,2,1,0:T(8,128)(2,1)} copy(bf16[1,1,4,1,2,2,128,128]{6,7,5,4,2,3,1,0:T(8,128)(2,1)S(1)} %fusion.10) | data formatting | bytes 1048576 | tf_op jit(solution)/shard_map/convert_element_type | solution.py:178
  (4 shorter events, 0.0 us)
Async XLA Ops:
  0.0 3.7 %copy-start.1 = (s32[1,1,4,1]{2,3,1,0:T(1,128)S(1)}, s32[1,1,4,1]{2,3,1,0:T(1,128)}, u32[]{:S(2)}) copy-start(s32[1,1,4,1]{2,3,1,0:T(1,128)} %param.7) | copy-start | bytes 52
  0.0 6.8 %copy-start.2 = (s32[1,1,4]{2,1,0:T(1,128)S(1)}, s32[1,1,4]{2,1,0:T(1,128)}, u32[]{:S(2)}) copy-start(s32[1,1,4]{2,1,0:T(1,128)} %param.8) | copy-start | bytes 52
  1.3 7.3 %collective-permute-start = (bf16[256,512]{1,0:T(8,128)(2,1)S(1)}, bf16[256,512]{1,0:T(8,128)(2,1)S(1)}, u32[]{:S(2)}, u32[]{:S(2)}) collective-permute-start(bf16[256,512]{1,0:T(8,128)(2,1)S(1)} %get-tuple-element.8), channel_id=1, source_target_pairs={{0,1},{1,2},{2,3},{3,0},{4,5},{5,6},{6,7},{7,4},{8,9},{9,10},{10,1... | collective-permute-start | bytes 786440 | tf_op jit(solution)/shard_map/ppermute | solution.py:151
  3.1 11.8 %collective-permute-start.1 = (bf16[256,512]{1,0:T(8,128)(2,1)S(1)}, bf16[256,512]{1,0:T(8,128)(2,1)S(1)}, u32[]{:S(2)}, u32[]{:S(2)}) collective-permute-start(bf16[256,512]{1,0:T(8,128)(2,1)S(1)} %get-tuple-element.7), channel_id=1, source_target_pairs={{0,2},{1,3},{2,0},{3,1},{4,6},{5,7},{6,4},{7,5},{8,10},{9,11},{10,... | collective-permute-start | bytes 786440 | tf_op jit(solution)/shard_map/ppermute | solution.py:151
  3.4 12.2 %collective-permute-start.2 = (bf16[256,512]{1,0:T(8,128)(2,1)S(1)}, bf16[256,512]{1,0:T(8,128)(2,1)S(1)}, u32[]{:S(2)}, u32[]{:S(2)}) collective-permute-start(bf16[256,512]{1,0:T(8,128)(2,1)S(1)} %get-tuple-element.6), channel_id=1, source_target_pairs={{0,3},{1,0},{2,1},{3,2},{4,7},{5,4},{6,5},{7,6},{8,11},{9,8},{10,9... | collective-permute-start | bytes 786440 | tf_op jit(solution)/shard_map/ppermute | solution.py:151
  22.6 27.2 %copy-start = (bf16[256,1024]{1,0:T(8,128)(2,1)S(1)}, bf16[256,1024]{1,0:T(8,128)(2,1)}, u32[]{:S(2)}) copy-start(bf16[256,1024]{1,0:T(8,128)(2,1)} %shard_map.64) | copy-start | bytes 1572868
  23.7 8.2 %collective-permute-start.3 = (bf16[128,1024]{1,0:T(8,128)(2,1)S(1)}, bf16[128,1024]{1,0:T(8,128)(2,1)S(1)}, u32[]{:S(2)}, u32[]{:S(2)}) collective-permute-start(bf16[128,1024]{1,0:T(8,128)(2,1)S(1)} %get-tuple-element.14), channel_id=1, source_target_pairs={{0,4},{4,8},{8,12},{12,0},{1,5},{5,9},{9,13},{13,1},{2,6},{6,10},{... | collective-permute-start | bytes 786440 | tf_op jit(solution)/shard_map/ppermute | solution.py:164
  25.1 22.8 %collective-permute-start.4 = (bf16[128,1024]{1,0:T(8,128)(2,1)S(1)}, bf16[128,1024]{1,0:T(8,128)(2,1)S(1)}, u32[]{:S(2)}, u32[]{:S(2)}) collective-permute-start(bf16[128,1024]{1,0:T(8,128)(2,1)S(1)} %get-tuple-element.12), channel_id=1, source_target_pairs={{0,8},{4,12},{8,0},{12,4},{1,9},{5,13},{9,1},{13,5},{2,10},{6,14},... | collective-permute-start | bytes 786440 | tf_op jit(solution)/shard_map/ppermute | solution.py:164
  26.2 23.6 %collective-permute-start.5 = (bf16[128,1024]{1,0:T(8,128)(2,1)S(1)}, bf16[128,1024]{1,0:T(8,128)(2,1)S(1)}, u32[]{:S(2)}, u32[]{:S(2)}) collective-permute-start(bf16[128,1024]{1,0:T(8,128)(2,1)S(1)} %get-tuple-element.13), channel_id=1, source_target_pairs={{0,12},{4,0},{8,4},{12,8},{1,13},{5,1},{9,5},{13,9},{2,14},{6,2},{... | collective-permute-start | bytes 786440 | tf_op jit(solution)/shard_map/ppermute | solution.py:164

commit v7 on v4

--- a/solution.py
+++ b/solution.py
@@ -144,12 +144,13 @@
     for h in range(NSPLIT):
         part = parts[:, :, h].reshape(ntm, blocks * rows, width)
         if own_parts:
-            part, own_parts[-1] = lax.optimization_barrier((part, own_parts[-1]))
+            part, prev_slots = lax.optimization_barrier((part, prev_slots))
         slots = [lax.dynamic_index_in_dim(part, here, axis=0, keepdims=False)]
         for d in range(1, ntm):
             piece = lax.dynamic_index_in_dim(part, (here + d) % ntm, axis=0, keepdims=False)
             slots.append(lax.ppermute(piece, "tm", perm=[(i, (i + d) % ntm) for i in range(ntm)]))
-        whitened = spectra(pos, jnp.stack(slots)).reshape(blocks, rows, 2 * NBAND)
+        prev_slots = jnp.stack(slots)
+        whitened = spectra(pos, prev_slots).reshape(blocks, rows, 2 * NBAND)
         own_parts.append(whitened)
         recv = []
         for d in range(peers):

time: 48.1 us -> 47.4 us (0.985)
  waiting for transfers between devices: 9.1 us -> 8.07 us
    ppermute x6, waiting for transfers between devices: 6.64 us -> 5.61 us  [local(): lax.ppermute(blk, 'chan', perm=[(i, (i + d) % peers) for i in range(peers)])]
  transfers between devices with their start and end apart: 12 -> 12, of which waited for: 5 -> 4; matrix products, arithmetic and copies ran while one was open for 12% -> 12% of each run, Pallas kernels for 9% -> 18%
where the time goes in v7:
time: 47.4 us; the launch traced here: 46.7 us
  starting transfers between devices  16.8 us (35%)
  Pallas kernels  8.6 us (18%)
  waiting for transfers between devices  8.07 us (17%)
  other arithmetic  6.08 us (13%)
  local copies, waits for them, and re-layouts  3.7 us (8%)
  between operations  2.75 us (6%)
  matrix products  0.74 us (2%)
    ppermute x6, starting transfers between devices, local(): lax.ppermute(blk, 'chan', perm=[(i, (i + d) % peers) for i in range(peers)])  9.49 us
    pallas_call x2, Pallas kernels, spectra(): pl.pallas_call(spectra_kernel, grid_spec=grid_spec, cost_estimate=pl.Cost...  8.6 us
    ppermute x6, starting transfers between devices, local(): lax.ppermute(piece, 'tm', perm=[(i, (i + d) % ntm) for i in range(ntm)])  7.29 us
    ppermute x6, waiting for transfers between devices, local(): lax.ppermute(blk, 'chan', perm=[(i, (i + d) % peers) for i in range(peers)])  5.61 us
    ppermute x6, waiting for transfers between devices, local(): lax.ppermute(piece, 'tm', perm=[(i, (i + d) % ntm) for i in range(ntm)])  2.45 us
    another operation x2, other arithmetic, local(): picked_parts.append(jnp.stack(recv))  2.01 us
    another operation x2, other arithmetic, local(): prev_slots = jnp.stack(slots)  1.72 us
    slice x1, local copies, waits for them, and re-layouts, local(): part = parts[:, :, h].reshape(ntm, blocks * rows, width)  1.32 us
  transfers between devices with their start and end apart: 12, of which 4 were waited for; matrix products, arithmetic and copies ran while one was open for 12% of the time, Pallas kernels for 18%

profile of v7, /device:TPU:0, one launch (start us, length us, event | category | flops | bytes accessed | tf_op | source)
XLA Modules:
  0.0 46.7 jit_solution(17033787568968071483)
XLA Ops:
  0.0 0.0 copy-start.2
  0.0 0.0 copy-start.1
  0.0 1.3 %fusion.27 = (bf16[4,2,1,64,512]{4,3,2,1,0:T(8,128)(2,1)S(1)}, bf16[4,2,1,64,512]{4,3,2,1,0:T(8,128)(2,1)S(1)}) fusion(bf16[4,2,2,64,512]{4,3,2,1,0:T(8,128)(2,1)} %bitcast.82), kind=kLoop, calls=%fused_computation.71 | loop fusion | bytes 2097152 | tf_op jit(solution)/shard_map/slice | solution.py:145
  1.4 2.4 %collective-permute-start.2 = (bf16[128,512]{1,0:T(8,128)(2,1)S(1)}, bf16[128,512]{1,0:T(8,128)(2,1)S(1)}, u32[]{:S(2)}, u32[]{:S(2)}) collective-permute-start(bf16[128,512]{1,0:T(8,128)(2,1)S(1)} %get-tuple-element.16), channel_id=1, source_target_pairs={{0,3},{1,0},{2,1},{3,2},{4,7},{5,4},{6,5},{7,6},{8,11},{9,8},{10,9... | collective-permute-start | bytes 393224 | tf_op jit(solution)/shard_map/ppermute | solution.py:151
  3.8 0.0 collective-permute-start
  3.8 1.1 %collective-permute-start.1 = (bf16[128,512]{1,0:T(8,128)(2,1)S(1)}, bf16[128,512]{1,0:T(8,128)(2,1)S(1)}, u32[]{:S(2)}, u32[]{:S(2)}) collective-permute-start(bf16[128,512]{1,0:T(8,128)(2,1)S(1)} %get-tuple-element.17), channel_id=1, source_target_pairs={{0,2},{1,3},{2,0},{3,1},{4,6},{5,7},{6,4},{7,5},{8,10},{9,11},{10,... | collective-permute-start | bytes 393224 | tf_op jit(solution)/shard_map/ppermute | solution.py:151
  4.9 0.0 copy-done.2
  5.0 0.0 copy-done.1
  5.0 0.7 %constant_dynamic-slice_fusion.5 = (s32[1,1,1,1]{2,3,1,0:T(1,128)}, s32[1,1,1,1]{2,3,1,0:T(1,128)}, s32[1,1,1,1]{2,3,1,0:T(1,128)}, s32[1,1,1,1]{2,3,1,0:T(1,128)}) fusion(s32[1,1,4,1]{2,3,1,0:T(1,128)S(1)} %copy-done.1, s32[]{:T(128)S(6)} %select_n.183, s32[]{:T(128)S(6)} %select_n.194, s32[]{:T(128)S(6)} %select_n.202, s32[]{:T(128)S(6)} %select_n.198), kind=kLoop, calls=%fused_computation.56 | loop fusion | bytes 48 | tf_op jit(solution)/shard_map/jit(dynamic_index_in_dim)/dynamic_slice | solution.py:160
  8.2 0.0 collective-permute-done.2
  8.2 1.4 %collective-permute-done = bf16[128,512]{1,0:T(8,128)(2,1)S(1)} collective-permute-done((bf16[128,512]{1,0:T(8,128)(2,1)S(1)}, bf16[128,512]{1,0:T(8,128)(2,1)S(1)}, u32[]{:S(2)}, u32[]{:S(2)}) %collective-permute-start) | collective-permute-done | bytes 131104 | tf_op jit(solution)/shard_map/ppermute | solution.py:151
  9.6 1.1 %collective-permute-done.1 = bf16[128,512]{1,0:T(8,128)(2,1)S(1)} collective-permute-done((bf16[128,512]{1,0:T(8,128)(2,1)S(1)}, bf16[128,512]{1,0:T(8,128)(2,1)S(1)}, u32[]{:S(2)}, u32[]{:S(2)}) %collective-permute-start.1) | collective-permute-done | bytes 131104 | tf_op jit(solution)/shard_map/ppermute | solution.py:151
  10.7 0.9 %pad_maximum_fusion.1.x_ref = bf16[4,128,512]{2,1,0:T(8,128)(2,1)} fusion(bf16[1,128,512]{2,1,0:T(8,128)(2,1)S(1)} %bitcast.83, bf16[1,128,512]{2,1,0:T(8,128)(2,1)S(1)} %bitcast.85, bf16[1,128,512]{2,1,0:T(8,128)(2,1)S(1)} %bitcast.84, bf16[1,128,512]{2,1,0:T(8,128)(2,1)S(1)} %get-tuple-element.15), kind=kLoop, calls=%fused_computation.30 | loop fusion | flops 786432 | bytes 1048576 | tf_op jit(solution)/shard_map/stack | solution.py:152
  11.6 0.7 %collective-permute-start.6 = (bf16[128,512]{1,0:T(8,128)(2,1)S(1)}, bf16[128,512]{1,0:T(8,128)(2,1)S(1)}, u32[]{:S(2)}, u32[]{:S(2)}) collective-permute-start(bf16[128,512]{1,0:T(8,128)(2,1)S(1)} %get-tuple-element.14), channel_id=1, source_target_pairs={{0,1},{1,2},{2,3},{3,0},{4,5},{5,6},{6,7},{7,4},{8,9},{9,10},{10,1... | collective-permute-start | bytes 393224 | tf_op jit(solution)/shard_map/ppermute | solution.py:151
  12.3 1.7 %collective-permute-start.7 = (bf16[128,512]{1,0:T(8,128)(2,1)S(1)}, bf16[128,512]{1,0:T(8,128)(2,1)S(1)}, u32[]{:S(2)}, u32[]{:S(2)}) collective-permute-start(bf16[128,512]{1,0:T(8,128)(2,1)S(1)} %get-tuple-element.13), channel_id=1, source_target_pairs={{0,2},{1,3},{2,0},{3,1},{4,6},{5,7},{6,4},{7,5},{8,10},{9,11},{10,... | collective-permute-start | bytes 393224 | tf_op jit(solution)/shard_map/ppermute | solution.py:151
  14.0 1.4 %collective-permute-start.8 = (bf16[128,512]{1,0:T(8,128)(2,1)S(1)}, bf16[128,512]{1,0:T(8,128)(2,1)S(1)}, u32[]{:S(2)}, u32[]{:S(2)}) collective-permute-start(bf16[128,512]{1,0:T(8,128)(2,1)S(1)} %get-tuple-element.12), channel_id=1, source_target_pairs={{0,3},{1,0},{2,1},{3,2},{4,7},{5,4},{6,5},{7,6},{8,11},{9,8},{10,9... | collective-permute-start | bytes 393224 | tf_op jit(solution)/shard_map/ppermute | solution.py:151
  15.4 4.3 %shard_map.91 = bf16[128,1024]{1,0:T(8,128)(2,1)} custom-call(s32[1]{0:T(128)} %bitcast.2.pos_ref, bf16[4,128,512]{2,1,0:T(8,128)(2,1)} %pad_maximum_fusion.1.x_ref, bf16[384,256]{1,0:T(8,128)(2,1)} %constant.142.clone.band_ref, bf16[1024,1024]{1,0:T(8,128)(2,1)} %constant.143.clone.tab_ref, bf16[512,512]{1,0:T(8,128)(2,1)} %constant.144.clone.grp_ref), custom_call_target="tpu_custom_call" | custom-call | flops 1073741824 | bytes 2883584 | tf_op jit(solution)/shard_map/pallas_call | solution.py:121
  19.7 1.0 %select_bitcast_fusion.1 = (bf16[1,1,64,1024]{3,2,1,0:T(8,128)(2,1)S(1)}, bf16[64,1024]{1,0:T(8,128)(2,1)S(1)}, bf16[64,1024]{1,0:T(8,128)(2,1)S(1)}, bf16[64,1024]{1,0:T(8,128)(2,1)S(1)}) fusion(pred[]{:T(512)} %bitcast.1, bf16[128,1024]{1,0:T(8,128)(2,1)} %shard_map.91, pred[]{:T(512)} %bitcast.14, pred[]{:T(512)} %bitcast.16, pred[]{:T(512)} %bitcast.12), kind=kLoop, calls=%fused_computation.40 | loop fusion | flops 262144 | bytes 786436 | tf_op jit(solution)/shard_map/stack;stack | solution.py:168
  20.7 1.6 %collective-permute-start.3 = (bf16[64,1024]{1,0:T(8,128)(2,1)S(1)}, bf16[64,1024]{1,0:T(8,128)(2,1)S(1)}, u32[]{:S(2)}, u32[]{:S(2)}) collective-permute-start(bf16[64,1024]{1,0:T(8,128)(2,1)S(1)} %get-tuple-element.22), channel_id=1, source_target_pairs={{0,4},{4,8},{8,12},{12,0},{1,5},{5,9},{9,13},{13,1},{2,6},{6,10},{... | collective-permute-start | bytes 393224 | tf_op jit(solution)/shard_map/ppermute | solution.py:165
  22.3 2.6 %collective-permute-start.4 = (bf16[64,1024]{1,0:T(8,128)(2,1)S(1)}, bf16[64,1024]{1,0:T(8,128)(2,1)S(1)}, u32[]{:S(2)}, u32[]{:S(2)}) collective-permute-start(bf16[64,1024]{1,0:T(8,128)(2,1)S(1)} %get-tuple-element.20), channel_id=1, source_target_pairs={{0,8},{4,12},{8,0},{12,4},{1,9},{5,13},{9,1},{13,5},{2,10},{6,14},... | collective-permute-start | bytes 393224 | tf_op jit(solution)/shard_map/ppermute | solution.py:165
  24.9 0.0 collective-permute-done.6
  24.9 1.3 %collective-permute-start.5 = (bf16[64,1024]{1,0:T(8,128)(2,1)S(1)}, bf16[64,1024]{1,0:T(8,128)(2,1)S(1)}, u32[]{:S(2)}, u32[]{:S(2)}) collective-permute-start(bf16[64,1024]{1,0:T(8,128)(2,1)S(1)} %get-tuple-element.21), channel_id=1, source_target_pairs={{0,12},{4,0},{8,4},{12,8},{1,13},{5,1},{9,5},{13,9},{2,14},{6,2},{... | collective-permute-start | bytes 393224 | tf_op jit(solution)/shard_map/ppermute | solution.py:165
  26.2 0.0 collective-permute-done.7
  26.2 0.0 collective-permute-done.8
  26.2 0.9 %pad_maximum_fusion.2.x_ref = bf16[4,128,512]{2,1,0:T(8,128)(2,1)} fusion(bf16[1,128,512]{2,1,0:T(8,128)(2,1)S(1)} %bitcast.88, bf16[1,128,512]{2,1,0:T(8,128)(2,1)S(1)} %bitcast.87, bf16[1,128,512]{2,1,0:T(8,128)(2,1)S(1)} %bitcast.86, bf16[1,128,512]{2,1,0:T(8,128)(2,1)S(1)} %get-tuple-element.11), kind=kLoop, calls=%fused_computation.31 | loop fusion | flops 786432 | bytes 1048576 | tf_op jit(solution)/shard_map/stack | solution.py:152
  27.1 0.0 copy-start
  27.1 4.3 %shard_map.92 = bf16[128,1024]{1,0:T(8,128)(2,1)} custom-call(s32[1]{0:T(128)} %bitcast.2.pos_ref, bf16[4,128,512]{2,1,0:T(8,128)(2,1)} %pad_maximum_fusion.2.x_ref, bf16[384,256]{1,0:T(8,128)(2,1)} %constant.142.clone.band_ref, bf16[1024,1024]{1,0:T(8,128)(2,1)} %constant.143.clone.tab_ref, bf16[512,512]{1,0:T(8,128)(2,1)} %constant.144.clone.grp_ref), custom_call_target="tpu_custom_call" | custom-call | flops 1073741824 | bytes 2883584 | tf_op jit(solution)/shard_map/pallas_call | solution.py:121
  31.4 1.0 %select_bitcast_fusion = (bf16[1,1,64,1024]{3,2,1,0:T(8,128)(2,1)S(1)}, bf16[64,1024]{1,0:T(8,128)(2,1)S(1)}, bf16[64,1024]{1,0:T(8,128)(2,1)S(1)}, bf16[64,1024]{1,0:T(8,128)(2,1)S(1)}) fusion(pred[]{:T(512)} %bitcast.1, bf16[128,1024]{1,0:T(8,128)(2,1)} %shard_map.92, pred[]{:T(512)} %bitcast.14, pred[]{:T(512)} %bitcast.16, pred[]{:T(512)} %bitcast.12), kind=kLoop, calls=%fused_computation.36 | loop fusion | flops 262144 | bytes 786436 | tf_op jit(solution)/shard_map/stack;stack | solution.py:168
  32.4 0.7 %collective-permute-start.9 = (bf16[64,1024]{1,0:T(8,128)(2,1)S(1)}, bf16[64,1024]{1,0:T(8,128)(2,1)S(1)}, u32[]{:S(2)}, u32[]{:S(2)}) collective-permute-start(bf16[64,1024]{1,0:T(8,128)(2,1)S(1)} %get-tuple-element.26), channel_id=1, source_target_pairs={{0,4},{4,8},{8,12},{12,0},{1,5},{5,9},{9,13},{13,1},{2,6},{6,10},{... | collective-permute-start | bytes 393224 | tf_op jit(solution)/shard_map/ppermute | solution.py:165
  33.2 0.3 collective-permute-start.10
  33.5 0.0 copy-done
  33.5 1.0 %fusion.20 = (bf16[2,128,512]{2,1,0:T(8,128)(2,1)S(1)}, bf16[2,128,512]{2,1,0:T(8,128)(2,1)S(1)}) fusion(bf16[2,64,1024]{2,1,0:T(8,128)(2,1)S(1)} %bitcast.76, bf16[2,64,1024]{2,1,0:T(8,128)(2,1)} %bitcast.78), kind=kLoop, calls=%fused_computation.33 | loop fusion | flops 1179648 | bytes 1048576 | tf_op jit(solution)/shard_map/concatenate | solution.py:169
  34.5 0.0 collective-permute-done.3
  34.5 2.9 %collective-permute-start.11 = (bf16[64,1024]{1,0:T(8,128)(2,1)S(1)}, bf16[64,1024]{1,0:T(8,128)(2,1)S(1)}, u32[]{:S(2)}, u32[]{:S(2)}) collective-permute-start(bf16[64,1024]{1,0:T(8,128)(2,1)S(1)} %get-tuple-element.25), channel_id=1, source_target_pairs={{0,12},{4,0},{8,4},{12,8},{1,13},{5,1},{9,5},{13,9},{2,14},{6,2},{... | collective-permute-start | bytes 393224 | tf_op jit(solution)/shard_map/ppermute | solution.py:165
  37.4 1.0 %fusion.19 = (bf16[2,1,128,1024]{3,2,1,0:T(8,128)(2,1)S(1)}, bf16[2,1,128,1024]{3,2,1,0:T(8,128)(2,1)S(1)}) fusion(bf16[2,64,1024]{2,1,0:T(8,128)(2,1)} %bitcast.79, bf16[2,64,1024]{2,1,0:T(8,128)(2,1)S(1)} %bitcast.77, bf16[2,128,512]{2,1,0:T(8,128)(2,1)S(1)} %get-tuple-element.10, bf16[2,128,512]{2,1,0:T(8,128)(2,1)S(1)} %get-tuple-element.9), kind=kLoop, calls=%fused_computation.29 | loop fusion | flops 2097152 | bytes 2097152 | tf_op jit(solution)/shard_map/stack | solution.py:172
  38.5 0.0 collective-permute-done.4
  38.5 0.0 collective-permute-done.5
  38.5 2.3 %collective-permute-done.9 = bf16[64,1024]{1,0:T(8,128)(2,1)S(1)} collective-permute-done((bf16[64,1024]{1,0:T(8,128)(2,1)S(1)}, bf16[64,1024]{1,0:T(8,128)(2,1)S(1)}, u32[]{:S(2)}, u32[]{:S(2)}) %collective-permute-start.9) | collective-permute-done | bytes 131104 | tf_op jit(solution)/shard_map/ppermute | solution.py:165
  40.8 3.3 %collective-permute-done.10 = bf16[64,1024]{1,0:T(8,128)(2,1)S(1)} collective-permute-done((bf16[64,1024]{1,0:T(8,128)(2,1)S(1)}, bf16[64,1024]{1,0:T(8,128)(2,1)S(1)}, u32[]{:S(2)}, u32[]{:S(2)}) %collective-permute-start.10) | collective-permute-done | bytes 131104 | tf_op jit(solution)/shard_map/ppermute | solution.py:165
  44.1 0.0 collective-permute-done.11
  44.1 0.7 %convolution_bitcast_fusion = f32[4,2,2,128,128]{3,4,2,1,0:T(8,128)S(1)} fusion(bf16[1,1,64,1024]{3,2,1,0:T(8,128)(2,1)S(1)} %bitcast.94, bf16[1,1,64,1024]{3,2,1,0:T(8,128)(2,1)S(1)} %bitcast.93, bf16[1,1,64,1024]{3,2,1,0:T(8,128)(2,1)S(1)} %bitcast.92, bf16[1,1,64,1024]{3,2,1,0:T(8,128)(2,1)S(1)} %get-tuple-element.23, ...), kind=kOutput, calls=%fused_computation.1 | convolution fusion | flops 547356672 | bytes 3145728 | tf_op jit(solution)/shard_map/lrif,dkjf->dklrij/dot_general | solution.py:173
  44.8 0.6 %gather_fusion = f32[4,2,2,128,128]{3,4,2,1,0:T(8,128)S(1)} fusion(f32[4,2,2,128,128]{3,4,2,1,0:T(8,128)S(1)} %convolution_bitcast_fusion, s32[1024]{0:T(1024)S(1)} %pad_clamp_fusion), kind=kCustom, calls=%fused_computation | custom fusion | bytes 2097168 | tf_op jit(solution)/shard_map/jit(_take)/gather | solution.py:175
  45.5 0.2 fusion.18
  45.7 1.0 %copy.13 = bf16[1,1,4,1,2,2,128,128]{7,6,5,4,3,2,1,0:T(8,128)(2,1)} copy(bf16[1,1,4,1,2,2,128,128]{6,7,5,4,2,3,1,0:T(8,128)(2,1)S(1)} %fusion.18) | data formatting | bytes 1048576 | tf_op jit(solution)/shard_map/convert_element_type | solution.py:179
  (6 shorter events, 0.1 us)
Async XLA Ops:
  0.0 4.9 %copy-start.2 = (s32[1,1,4]{2,1,0:T(1,128)S(1)}, s32[1,1,4]{2,1,0:T(1,128)}, u32[]{:S(2)}) copy-start(s32[1,1,4]{2,1,0:T(1,128)} %param.11) | copy-start | bytes 52
  0.0 5.0 %copy-start.1 = (s32[1,1,4,1]{2,3,1,0:T(1,128)S(1)}, s32[1,1,4,1]{2,3,1,0:T(1,128)}, u32[]{:S(2)}) copy-start(s32[1,1,4,1]{2,3,1,0:T(1,128)} %param.10) | copy-start | bytes 52
  1.4 6.8 %collective-permute-start.2 = (bf16[128,512]{1,0:T(8,128)(2,1)S(1)}, bf16[128,512]{1,0:T(8,128)(2,1)S(1)}, u32[]{:S(2)}, u32[]{:S(2)}) collective-permute-start(bf16[128,512]{1,0:T(8,128)(2,1)S(1)} %get-tuple-element.16), channel_id=1, source_target_pairs={{0,3},{1,0},{2,1},{3,2},{4,7},{5,4},{6,5},{7,6},{8,11},{9,8},{10,9... | collective-permute-start | bytes 393224 | tf_op jit(solution)/shard_map/ppermute | solution.py:151
  3.8 5.8 %collective-permute-start = (bf16[128,512]{1,0:T(8,128)(2,1)S(1)}, bf16[128,512]{1,0:T(8,128)(2,1)S(1)}, u32[]{:S(2)}, u32[]{:S(2)}) collective-permute-start(bf16[128,512]{1,0:T(8,128)(2,1)S(1)} %get-tuple-element.18), channel_id=1, source_target_pairs={{0,1},{1,2},{2,3},{3,0},{4,5},{5,6},{6,7},{7,4},{8,9},{9,10},{10,1... | collective-permute-start | bytes 393224 | tf_op jit(solution)/shard_map/ppermute | solution.py:151
  3.8 6.8 %collective-permute-start.1 = (bf16[128,512]{1,0:T(8,128)(2,1)S(1)}, bf16[128,512]{1,0:T(8,128)(2,1)S(1)}, u32[]{:S(2)}, u32[]{:S(2)}) collective-permute-start(bf16[128,512]{1,0:T(8,128)(2,1)S(1)} %get-tuple-element.17), channel_id=1, source_target_pairs={{0,2},{1,3},{2,0},{3,1},{4,6},{5,7},{6,4},{7,5},{8,10},{9,11},{10,... | collective-permute-start | bytes 393224 | tf_op jit(solution)/shard_map/ppermute | solution.py:151
  11.6 13.3 %collective-permute-start.6 = (bf16[128,512]{1,0:T(8,128)(2,1)S(1)}, bf16[128,512]{1,0:T(8,128)(2,1)S(1)}, u32[]{:S(2)}, u32[]{:S(2)}) collective-permute-start(bf16[128,512]{1,0:T(8,128)(2,1)S(1)} %get-tuple-element.14), channel_id=1, source_target_pairs={{0,1},{1,2},{2,3},{3,0},{4,5},{5,6},{6,7},{7,4},{8,9},{9,10},{10,1... | collective-permute-start | bytes 393224 | tf_op jit(solution)/shard_map/ppermute | solution.py:151
  12.3 13.9 %collective-permute-start.7 = (bf16[128,512]{1,0:T(8,128)(2,1)S(1)}, bf16[128,512]{1,0:T(8,128)(2,1)S(1)}, u32[]{:S(2)}, u32[]{:S(2)}) collective-permute-start(bf16[128,512]{1,0:T(8,128)(2,1)S(1)} %get-tuple-element.13), channel_id=1, source_target_pairs={{0,2},{1,3},{2,0},{3,1},{4,6},{5,7},{6,4},{7,5},{8,10},{9,11},{10,... | collective-permute-start | bytes 393224 | tf_op jit(solution)/shard_map/ppermute | solution.py:151
  14.0 12.2 %collective-permute-start.8 = (bf16[128,512]{1,0:T(8,128)(2,1)S(1)}, bf16[128,512]{1,0:T(8,128)(2,1)S(1)}, u32[]{:S(2)}, u32[]{:S(2)}) collective-permute-start(bf16[128,512]{1,0:T(8,128)(2,1)S(1)} %get-tuple-element.12), channel_id=1, source_target_pairs={{0,3},{1,0},{2,1},{3,2},{4,7},{5,4},{6,5},{7,6},{8,11},{9,8},{10,9... | collective-permute-start | bytes 393224 | tf_op jit(solution)/shard_map/ppermute | solution.py:151
  20.7 13.8 %collective-permute-start.3 = (bf16[64,1024]{1,0:T(8,128)(2,1)S(1)}, bf16[64,1024]{1,0:T(8,128)(2,1)S(1)}, u32[]{:S(2)}, u32[]{:S(2)}) collective-permute-start(bf16[64,1024]{1,0:T(8,128)(2,1)S(1)} %get-tuple-element.22), channel_id=1, source_target_pairs={{0,4},{4,8},{8,12},{12,0},{1,5},{5,9},{9,13},{13,1},{2,6},{6,10},{... | collective-permute-start | bytes 393224 | tf_op jit(solution)/shard_map/ppermute | solution.py:165
  22.3 16.2 %collective-permute-start.4 = (bf16[64,1024]{1,0:T(8,128)(2,1)S(1)}, bf16[64,1024]{1,0:T(8,128)(2,1)S(1)}, u32[]{:S(2)}, u32[]{:S(2)}) collective-permute-start(bf16[64,1024]{1,0:T(8,128)(2,1)S(1)} %get-tuple-element.20), channel_id=1, source_target_pairs={{0,8},{4,12},{8,0},{12,4},{1,9},{5,13},{9,1},{13,5},{2,10},{6,14},... | collective-permute-start | bytes 393224 | tf_op jit(solution)/shard_map/ppermute | solution.py:165
  24.9 13.6 %collective-permute-start.5 = (bf16[64,1024]{1,0:T(8,128)(2,1)S(1)}, bf16[64,1024]{1,0:T(8,128)(2,1)S(1)}, u32[]{:S(2)}, u32[]{:S(2)}) collective-permute-start(bf16[64,1024]{1,0:T(8,128)(2,1)S(1)} %get-tuple-element.21), channel_id=1, source_target_pairs={{0,12},{4,0},{8,4},{12,8},{1,13},{5,1},{9,5},{13,9},{2,14},{6,2},{... | collective-permute-start | bytes 393224 | tf_op jit(solution)/shard_map/ppermute | solution.py:165
  27.1 6.4 %copy-start = (bf16[128,1024]{1,0:T(8,128)(2,1)S(1)}, bf16[128,1024]{1,0:T(8,128)(2,1)}, u32[]{:S(2)}) copy-start(bf16[128,1024]{1,0:T(8,128)(2,1)} %shard_map.91) | copy-start | bytes 786436
  32.4 8.4 %collective-permute-start.9 = (bf16[64,1024]{1,0:T(8,128)(2,1)S(1)}, bf16[64,1024]{1,0:T(8,128)(2,1)S(1)}, u32[]{:S(2)}, u32[]{:S(2)}) collective-permute-start(bf16[64,1024]{1,0:T(8,128)(2,1)S(1)} %get-tuple-element.26), channel_id=1, source_target_pairs={{0,4},{4,8},{8,12},{12,0},{1,5},{5,9},{9,13},{13,1},{2,6},{6,10},{... | collective-permute-start | bytes 393224 | tf_op jit(solution)/shard_map/ppermute | solution.py:165
  33.2 10.9 %collective-permute-start.10 = (bf16[64,1024]{1,0:T(8,128)(2,1)S(1)}, bf16[64,1024]{1,0:T(8,128)(2,1)S(1)}, u32[]{:S(2)}, u32[]{:S(2)}) collective-permute-start(bf16[64,1024]{1,0:T(8,128)(2,1)S(1)} %get-tuple-element.24), channel_id=1, source_target_pairs={{0,8},{4,12},{8,0},{12,4},{1,9},{5,13},{9,1},{13,5},{2,10},{6,14},... | collective-permute-start | bytes 393224 | tf_op jit(solution)/shard_map/ppermute | solution.py:165
  34.5 9.6 %collective-permute-start.11 = (bf16[64,1024]{1,0:T(8,128)(2,1)S(1)}, bf16[64,1024]{1,0:T(8,128)(2,1)S(1)}, u32[]{:S(2)}, u32[]{:S(2)}) collective-permute-start(bf16[64,1024]{1,0:T(8,128)(2,1)S(1)} %get-tuple-element.25), channel_id=1, source_target_pairs={{0,12},{4,0},{8,4},{12,8},{1,13},{5,1},{9,5},{13,9},{2,14},{6,2},{... | collective-permute-start | bytes 393224 | tf_op jit(solution)/shard_map/ppermute | solution.py:165

commit v8 on v3

--- a/solution.py
+++ b/solution.py
@@ -66,20 +66,27 @@
     return ((g[:, None] == g[None, :]).astype(np.float32) / SUBW).astype(BF16)
 
 
-def spectra_kernel(pos_ref, x_ref, band_ref, tab_ref, grp_ref, o_ref, filt_ref):
-    nslot, _, width = x_ref.shape
+def spectra_kernel(pos_ref, want_ref, *refs):
+    nsend = want_ref.shape[0]
+    nslot = len(refs) - 5 - nsend
+    x_refs = refs[:nslot]
+    band_ref, tab_ref, grp_ref, o_ref = refs[nslot:nslot + 4]
+    send_refs = refs[nslot + 4:nslot + 4 + nsend]
+    filt_ref = refs[-1]
+    width = x_refs[0].shape[1]
     ntile = NT // TILE
     pos = pos_ref[0]
 
     def tile(j):
-        chunk, off = divmod((j % ntile) * TILE, width)
-        return x_ref[(pos - chunk + nslot) % nslot, :, off:off + TILE]
+        slot, off = divmod((j % ntile) * TILE, width)
+        return x_refs[slot][:, off:off + TILE]
 
     band = band_ref[...]
     for j in range(ntile):
         win = jnp.concatenate([tile(j - 1), tile(j), tile(j + 1)], axis=1)
         acc = jnp.dot(win, band, preferred_element_type=jnp.float32)
-        filt_ref[:, j * TILE:(j + 1) * TILE] = (acc[:, :TILE] + acc[:, TILE:]).astype(jnp.bfloat16)
+        col = pl.multiple_of((j * TILE + pos * width) % NT, TILE)
+        filt_ref[:, pl.ds(col, TILE)] = (acc[:, :TILE] + acc[:, TILE:]).astype(jnp.bfloat16)
     tab = tab_ref[...]
     first = jnp.dot(filt_ref[:, :HALF], tab, preferred_element_type=jnp.float32)
     second = jnp.dot(filt_ref[:, HALF:], tab, preferred_element_type=jnp.float32)
@@ -97,33 +104,35 @@
     level = 1.0 / jnp.sqrt(mean + 1e-06)
     o_ref[:, :NBAND] = (re * level).astype(jnp.bfloat16)
     o_ref[:, NBAND:] = (im * level).astype(jnp.bfloat16)
+    rpb = send_refs[0].shape[0]
+    for e in range(nsend):
+        start = pl.multiple_of(want_ref[e] * rpb, rpb)
+        send_refs[e][...] = o_ref[pl.ds(start, rpb), :]
 
 
-def spectra(pos, rows3):
-    ntm, nrows, width = rows3.shape
+def spectra(pos, want, slots, peers, cap, blocks):
+    nrows, width = slots[0].shape
     band = jnp.asarray(band_matrix())
     tab = jnp.asarray(dft_top())
     grp = jnp.asarray(group_matrix())
+    rpb = nrows // blocks
+    full = lambda shape: pl.BlockSpec(shape, lambda i, p, w: (0,) * len(shape))
     grid_spec = pltpu.PrefetchScalarGridSpec(
-        num_scalar_prefetch=1,
-        grid=(nrows // BLOCK,),
-        in_specs=[
-            pl.BlockSpec((ntm, BLOCK, width), lambda r, p: (0, r, 0)),
-            pl.BlockSpec(band.shape, lambda r, p: (0, 0)),
-            pl.BlockSpec(tab.shape, lambda r, p: (0, 0)),
-            pl.BlockSpec(grp.shape, lambda r, p: (0, 0)),
-        ],
-        out_specs=pl.BlockSpec((BLOCK, 2 * NBAND), lambda r, p: (r, 0)),
-        scratch_shapes=[pltpu.VMEM((BLOCK, NT), jnp.bfloat16)],
+        num_scalar_prefetch=2,
+        grid=(1,),
+        in_specs=[full(x.shape) for x in slots] + [full(band.shape), full(tab.shape), full(grp.shape)],
+        out_specs=[full((nrows, 2 * NBAND))] + [full((rpb, 2 * NBAND))] * (peers * cap),
+        scratch_shapes=[pltpu.VMEM((nrows, NT), jnp.bfloat16)],
     )
     flops = 2 * nrows * (3 * TILE * 2 * TILE * (NT // TILE) + NT * 2 * NBAND + 2 * NBAND * NBAND)
-    nbytes = rows3.size * 2 + tab.size * 2 + nrows * 2 * NBAND * 2
+    nbytes = nrows * NT * 2 + tab.size * 2 + (nrows + peers * cap * rpb) * 2 * NBAND * 2
     return pl.pallas_call(
         spectra_kernel,
         grid_spec=grid_spec,
         cost_estimate=pl.CostEstimate(flops=flops, transcendentals=nrows * NBAND, bytes_accessed=nbytes),
-        out_shape=jax.ShapeDtypeStruct((nrows, 2 * NBAND), jnp.bfloat16),
-    )(pos, rows3, band, tab, grp)
+        out_shape=[jax.ShapeDtypeStruct((nrows, 2 * NBAND), jnp.bfloat16)]
+        + [jax.ShapeDtypeStruct((rpb, 2 * NBAND), jnp.bfloat16)] * (peers * cap),
+    )(pos, want, *slots, band, tab, grp)
 
 
 def local(raw, send_blocks, pair_count):
@@ -138,25 +147,26 @@
     peers = lax.axis_size("chan")
     mine = lax.axis_index("chan")
     cap = send_blocks.shape[3]
-    ids = send_blocks[0, 0]
+    owners = (mine + jnp.arange(peers, dtype=jnp.int32)) % peers
+    want = jnp.take(send_blocks[0, 0], owners, axis=0).reshape(peers * cap)
     own_parts = []
     picked_parts = []
     for h in range(NSPLIT):
         part = parts[:, :, h].reshape(ntm, blocks * rows, width)
         if own_parts:
-            part, own_parts[-1] = lax.optimization_barrier((part, own_parts[-1]))
+            part, prev_slots = lax.optimization_barrier((part, prev_slots))
         slots = [lax.dynamic_index_in_dim(part, here, axis=0, keepdims=False)]
         for d in range(1, ntm):
-            piece = lax.dynamic_index_in_dim(part, (here + d) % ntm, axis=0, keepdims=False)
-            slots.append(lax.ppermute(piece, "tm", perm=[(i, (i + d) % ntm) for i in range(ntm)]))
-        whitened = spectra(pos, jnp.stack(slots)).reshape(blocks, rows, 2 * NBAND)
-        own_parts.append(whitened)
+            piece = lax.dynamic_index_in_dim(part, (here - d) % ntm, axis=0, keepdims=False)
+            slots.append(lax.ppermute(piece, "tm", perm=[(i, (i - d) % ntm) for i in range(ntm)]))
+        prev_slots = tuple(slots)
+        whitened, *outgoing = spectra(pos, want, slots, peers, cap, blocks)
+        own_parts.append(whitened.reshape(blocks, rows, 2 * NBAND))
         recv = []
         for d in range(peers):
-            dest = (mine + d) % peers
             row = []
             for k in range(cap):
-                blk = lax.dynamic_index_in_dim(whitened, ids[dest, k], axis=0, keepdims=False)
+                blk = outgoing[d * cap + k]
                 if d:
                     blk = lax.ppermute(blk, "chan", perm=[(i, (i + d) % peers) for i in range(peers)])
                 row.append(blk)

time: 55.7 us -> 49.9 us (0.90); the launches traced: 54.9 us -> 49.7 us
  between operations: 7.77 us -> 0.17 us
  waiting for transfers between devices: 12.3 us -> 15.9 us
  starting transfers between devices: 16.3 us -> 13.7 us
  Pallas kernels: 8.6 us -> 10.6 us
    ppermute x6, waiting for transfers between devices: 7.71 us -> 10.4 us  [local(): lax.ppermute(blk, 'chan', perm=[(i, (i + d) % peers) for i in range(peers)])]
    another operation x2 -> x0, local copies, waits for them, and re-layouts: 2.31 us -> none  [local(): picked_parts.append(jnp.stack(recv))]
    pallas_call x2, Pallas kernels: 8.6 us -> 10.6 us  [spectra(): pl.pallas_call(spectra_kernel, grid_spec=grid_spec, cost_estimate=pl.Cost...]
    ppermute x6, starting transfers between devices: 6.8 us -> 4.99 us  [local(): lax.ppermute(piece, 'tm', perm=[(i, (i - d) % ntm) for i in range(ntm)])]
    another operation x2 -> x0, other arithmetic: 1.72 us -> none  [local(): whitened = spectra(pos, jnp.stack(slots)).reshape(blocks, rows, 2 * NBAND)]
    squeeze x0 -> x2, local copies, waits for them, and re-layouts: none -> 1.44 us  [local(): lax.dynamic_index_in_dim(part, (here - d) % ntm, axis=0, keepdims=False)]
    another operation x1, other arithmetic: 0.09 us -> 1.03 us  [local(): paired = jnp.stack([whitened, turned], axis=1)]
    ppermute x6, waiting for transfers between devices: 4.63 us -> 5.49 us  [local(): lax.ppermute(piece, 'tm', perm=[(i, (i - d) % ntm) for i in range(ntm)])]
  transfers between devices with their start and end apart: 12 -> 12, of which waited for: 5 -> 4; matrix products, arithmetic and copies ran while one was open for 9% -> 7% of each run, Pallas kernels for 8% -> 21%
where the time goes in v8:
time: 49.9 us; the launch traced here: 49.7 us
  waiting for transfers between devices  15.9 us (32%)
  starting transfers between devices  13.7 us (27%)
  Pallas kernels  10.6 us (21%)
  local copies, waits for them, and re-layouts  5.74 us (12%)
  other arithmetic  2.91 us (6%)
  matrix products  0.76 us (2%)
    pallas_call x2, Pallas kernels, spectra(): pl.pallas_call(spectra_kernel, grid_spec=grid_spec, cost_estimate=pl.Cost...  10.6 us
    ppermute x6, waiting for transfers between devices, local(): lax.ppermute(blk, 'chan', perm=[(i, (i + d) % peers) for i in range(peers)])  10.4 us
    ppermute x6, starting transfers between devices, local(): lax.ppermute(blk, 'chan', perm=[(i, (i + d) % peers) for i in range(peers)])  8.68 us
    ppermute x6, waiting for transfers between devices, local(): lax.ppermute(piece, 'tm', perm=[(i, (i - d) % ntm) for i in range(ntm)])  5.49 us
    ppermute x6, starting transfers between devices, local(): lax.ppermute(piece, 'tm', perm=[(i, (i - d) % ntm) for i in range(ntm)])  4.99 us
    squeeze x2, local copies, waits for them, and re-layouts, local(): lax.dynamic_index_in_dim(part, (here - d) % ntm, axis=0, keepdims=False)  1.44 us
    slice x1, local copies, waits for them, and re-layouts, local(): part = parts[:, :, h].reshape(ntm, blocks * rows, width)  1.3 us
    another operation x1, other arithmetic, local(): paired = jnp.stack([whitened, turned], axis=1)  1.03 us
  transfers between devices with their start and end apart: 12, of which 4 were waited for; matrix products, arithmetic and copies ran while one was open for 7% of the time, Pallas kernels for 21%

profile of v8, /device:TPU:0, one launch (start us, length us, event | category | flops | bytes accessed | tf_op | source)
XLA Modules:
  0.0 49.7 jit_solution(2220809262298623098)
XLA Ops:
  0.0 0.0 copy-start
  0.0 1.3 %fusion.30 = (bf16[4,2,1,64,512]{4,3,2,1,0:T(8,128)(2,1)S(1)}, bf16[4,2,1,64,512]{4,3,2,1,0:T(8,128)(2,1)S(1)}) fusion(bf16[4,2,2,64,512]{4,3,2,1,0:T(8,128)(2,1)} %bitcast.70), kind=kLoop, calls=%fused_computation.71 | loop fusion | bytes 2097152 | tf_op jit(solution)/shard_map/slice | solution.py:155
  1.3 0.7 %dynamic-slice_bitcast_fusion.4 = (bf16[128,512]{1,0:T(8,128)(2,1)S(1)}, bf16[128,512]{1,0:T(8,128)(2,1)S(1)}, bf16[128,512]{1,0:T(8,128)(2,1)S(1)}, bf16[128,512]{1,0:T(8,128)(2,1)}) fusion(bf16[4,128,512]{2,1,0:T(8,128)(2,1)S(1)} %bitcast.69, s32[]{:T(128)S(6)} %select_n.151, s32[]{:T(128)S(6)} %select_n.149, s32[]{:T(128)S(6)} %select_n.147, s32[]{:T(128)S(6)} %select_n.145), kind=kLoop, calls=%fused_computation.39 | loop fusion | bytes 1048592 | tf_op jit(solution)/shard_map/jit(dynamic_index_in_dim)/squeeze | solution.py:160
  2.0 2.4 %collective-permute-start = (bf16[128,512]{1,0:T(8,128)(2,1)S(1)}, bf16[128,512]{1,0:T(8,128)(2,1)S(1)}, u32[]{:S(2)}, u32[]{:S(2)}) collective-permute-start(bf16[128,512]{1,0:T(8,128)(2,1)S(1)} %get-tuple-element.37), channel_id=1, source_target_pairs={{0,3},{1,0},{2,1},{3,2},{4,7},{5,4},{6,5},{7,6},{8,11},{9,8},{10,9... | collective-permute-start | bytes 393224 | tf_op jit(solution)/shard_map/ppermute | solution.py:161
  4.4 0.6 %collective-permute-start.1 = (bf16[128,512]{1,0:T(8,128)(2,1)S(1)}, bf16[128,512]{1,0:T(8,128)(2,1)S(1)}, u32[]{:S(2)}, u32[]{:S(2)}) collective-permute-start(bf16[128,512]{1,0:T(8,128)(2,1)S(1)} %get-tuple-element.36), channel_id=1, source_target_pairs={{0,2},{1,3},{2,0},{3,1},{4,6},{5,7},{6,4},{7,5},{8,10},{9,11},{10,... | collective-permute-start | bytes 393224 | tf_op jit(solution)/shard_map/ppermute | solution.py:161
  5.0 0.2 collective-permute-start.2
  5.2 0.0 copy-done
  5.2 0.6 %gather_fusion = s32[4]{0:T(128)S(1)} fusion(s32[4]{0:T(128)S(1)} %bitcast.67, s32[1024]{0:T(1024)S(1)} %pad_clamp_fusion.1), kind=kCustom, calls=%fused_computation | custom fusion | bytes 48 | tf_op jit(solution)/shard_map/jit(_take)/gather | solution.py:151
  5.9 0.6 %and_select_fusion.2.want_ref = s32[4]{0:T(128)} fusion(s32[4]{0:T(128)S(1)} %gather_fusion, s32[]{:T(128)S(6)} %axis_index.23), kind=kLoop, calls=%fused_computation.59 | loop fusion | flops 76 | bytes 36 | tf_op jit(solution)/shard_map/jit(_take)/select_n | solution.py:151
  6.4 0.0 copy-done.8
  6.5 1.7 %collective-permute-done.refs_1_ = bf16[128,512]{1,0:T(8,128)(2,1)S(1)} collective-permute-done((bf16[128,512]{1,0:T(8,128)(2,1)S(1)}, bf16[128,512]{1,0:T(8,128)(2,1)S(1)}, u32[]{:S(2)}, u32[]{:S(2)}) %collective-permute-start) | collective-permute-done | bytes 131104 | tf_op jit(solution)/shard_map/ppermute | solution.py:161
  8.2 3.7 %collective-permute-done.1.refs_2_ = bf16[128,512]{1,0:T(8,128)(2,1)S(1)} collective-permute-done((bf16[128,512]{1,0:T(8,128)(2,1)S(1)}, bf16[128,512]{1,0:T(8,128)(2,1)S(1)}, u32[]{:S(2)}, u32[]{:S(2)}) %collective-permute-start.1) | collective-permute-done | bytes 131104 | tf_op jit(solution)/shard_map/ppermute | solution.py:161
  11.9 0.0 collective-permute-done.2.refs_3_
  11.9 0.7 %dynamic-slice_bitcast_fusion = (bf16[128,512]{1,0:T(8,128)(2,1)S(1)}, bf16[128,512]{1,0:T(8,128)(2,1)S(1)}, bf16[128,512]{1,0:T(8,128)(2,1)S(1)}, bf16[128,512]{1,0:T(8,128)(2,1)}) fusion(bf16[4,128,512]{2,1,0:T(8,128)(2,1)S(1)} %bitcast.68, s32[]{:T(128)S(6)} %select_n.151, s32[]{:T(128)S(6)} %select_n.149, s32[]{:T(128)S(6)} %select_n.147, s32[]{:T(128)S(6)} %select_n.145), kind=kLoop, calls=%fused_computation.35 | loop fusion | bytes 1048592 | tf_op jit(solution)/shard_map/jit(dynamic_index_in_dim)/squeeze | solution.py:160
  12.7 0.0 collective-permute-start.6
  12.7 1.6 %collective-permute-start.7 = (bf16[128,512]{1,0:T(8,128)(2,1)S(1)}, bf16[128,512]{1,0:T(8,128)(2,1)S(1)}, u32[]{:S(2)}, u32[]{:S(2)}) collective-permute-start(bf16[128,512]{1,0:T(8,128)(2,1)S(1)} %get-tuple-element.32), channel_id=1, source_target_pairs={{0,2},{1,3},{2,0},{3,1},{4,6},{5,7},{6,4},{7,5},{8,10},{9,11},{10,... | collective-permute-start | bytes 393224 | tf_op jit(solution)/shard_map/ppermute | solution.py:161
  14.3 0.2 collective-permute-start.8
  14.5 0.0 copy-done.2
  14.5 0.0 copy-done.3
  14.5 0.0 copy-done.4
  14.6 5.3 %shard_map.91 = (bf16[128,1024]{1,0:T(8,128)(2,1)}, bf16[64,1024]{1,0:T(8,128)(2,1)}, bf16[64,1024]{1,0:T(8,128)(2,1)}, bf16[64,1024]{1,0:T(8,128)(2,1)}, bf16[64,1024]{1,0:T(8,128)(2,1)}) custom-call(s32[1]{0:T(128)} %bitcast.1.pos_ref, s32[4]{0:T(128)} %and_select_fusion.2.want_ref, bf16[128,512]{1,0:T(8,128)(2,1)} %get-tuple-element.38.refs_0_, ...), custom_call_target="tpu_custom_call" | custom-call | flops 1073741824 | bytes 3407872 | tf_op jit(solution)/shard_map/pallas_call | solution.py:129
  19.9 3.6 %collective-permute-start.5 = (bf16[64,1024]{1,0:T(8,128)(2,1)}, bf16[64,1024]{1,0:T(8,128)(2,1)S(1)}, u32[]{:S(2)}, u32[]{:S(2)}) collective-permute-start(bf16[64,1024]{1,0:T(8,128)(2,1)} %get-tuple-element.19), channel_id=1, source_target_pairs={{0,12},{4,0},{8,4},{12,8},{1,13},{5,1},{9,5},{13,9},{2,14},{6,2},{... | collective-permute-start | bytes 393224 | tf_op jit(solution)/shard_map/ppermute | solution.py:171
  23.5 0.0 collective-permute-start.4
  23.5 0.0 collective-permute-done.6.refs_1_
  23.5 1.0 %collective-permute-start.3 = (bf16[64,1024]{1,0:T(8,128)(2,1)}, bf16[64,1024]{1,0:T(8,128)(2,1)S(1)}, u32[]{:S(2)}, u32[]{:S(2)}) collective-permute-start(bf16[64,1024]{1,0:T(8,128)(2,1)} %get-tuple-element.17), channel_id=1, source_target_pairs={{0,4},{4,8},{8,12},{12,0},{1,5},{5,9},{9,13},{13,1},{2,6},{6,10},{... | collective-permute-start | bytes 393224 | tf_op jit(solution)/shard_map/ppermute | solution.py:171
  24.5 0.0 collective-permute-done.7.refs_2_
  24.5 0.0 collective-permute-done.8.refs_3_
  24.5 0.0 copy-start.7
  24.5 0.6 %copy-done.6 = bf16[128,512]{1,0:T(8,128)(2,1)} copy-done((bf16[128,512]{1,0:T(8,128)(2,1)}, bf16[128,512]{1,0:T(8,128)(2,1)S(1)}, u32[]{:S(2)}) %copy-start.6) | copy-done | bytes 131096
  25.1 0.1 copy-done.7
  25.2 5.3 %shard_map.92 = (bf16[128,1024]{1,0:T(8,128)(2,1)}, bf16[64,1024]{1,0:T(8,128)(2,1)}, bf16[64,1024]{1,0:T(8,128)(2,1)}, bf16[64,1024]{1,0:T(8,128)(2,1)}, bf16[64,1024]{1,0:T(8,128)(2,1)}) custom-call(s32[1]{0:T(128)} %bitcast.1.pos_ref, s32[4]{0:T(128)} %and_select_fusion.2.want_ref, bf16[128,512]{1,0:T(8,128)(2,1)} %get-tuple-element.34.refs_0_, ...), custom_call_target="tpu_custom_call" | custom-call | flops 1073741824 | bytes 3407872 | tf_op jit(solution)/shard_map/pallas_call | solution.py:129
  30.5 2.9 %collective-permute-start.11 = (bf16[64,1024]{1,0:T(8,128)(2,1)}, bf16[64,1024]{1,0:T(8,128)(2,1)S(1)}, u32[]{:S(2)}, u32[]{:S(2)}) collective-permute-start(bf16[64,1024]{1,0:T(8,128)(2,1)} %get-tuple-element.24), channel_id=1, source_target_pairs={{0,12},{4,0},{8,4},{12,8},{1,13},{5,1},{9,5},{13,9},{2,14},{6,2},{... | collective-permute-start | bytes 393224 | tf_op jit(solution)/shard_map/ppermute | solution.py:171
  33.4 1.1 %collective-permute-start.10 = (bf16[64,1024]{1,0:T(8,128)(2,1)}, bf16[64,1024]{1,0:T(8,128)(2,1)S(1)}, u32[]{:S(2)}, u32[]{:S(2)}) collective-permute-start(bf16[64,1024]{1,0:T(8,128)(2,1)} %get-tuple-element.23), channel_id=1, source_target_pairs={{0,8},{4,12},{8,0},{12,4},{1,9},{5,13},{9,1},{13,5},{2,10},{6,14},... | collective-permute-start | bytes 393224 | tf_op jit(solution)/shard_map/ppermute | solution.py:171
  34.5 0.0 copy-done.1
  34.5 1.0 %fusion.20 = (bf16[2,128,512]{2,1,0:T(8,128)(2,1)S(1)}, bf16[2,128,512]{2,1,0:T(8,128)(2,1)S(1)}) fusion(bf16[2,64,1024]{2,1,0:T(8,128)(2,1)S(1)} %bitcast.71, bf16[2,64,1024]{2,1,0:T(8,128)(2,1)} %bitcast.73), kind=kLoop, calls=%fused_computation.32 | loop fusion | flops 1179648 | bytes 1048576 | tf_op jit(solution)/shard_map/concatenate | solution.py:175
  35.5 0.0 collective-permute-done.5
  35.5 0.1 collective-permute-start.9
  35.6 1.0 %fusion.19 = (bf16[2,1,128,1024]{3,2,1,0:T(8,128)(2,1)S(1)}, bf16[2,1,128,1024]{3,2,1,0:T(8,128)(2,1)S(1)}) fusion(bf16[2,64,1024]{2,1,0:T(8,128)(2,1)} %bitcast.74, bf16[2,64,1024]{2,1,0:T(8,128)(2,1)S(1)} %bitcast.72, bf16[2,128,512]{2,1,0:T(8,128)(2,1)S(1)} %get-tuple-element.30, bf16[2,128,512]{2,1,0:T(8,128)(2,1)S(1)} %get-tuple-element.29), kind=kLoop, calls=%fused_computation.30 | loop fusion | flops 2097152 | bytes 2097152 | tf_op jit(solution)/shard_map/stack | solution.py:178
  36.7 0.0 collective-permute-done.4
  36.7 0.0 collective-permute-done.3
  36.7 1.9 %collective-permute-done.11 = bf16[64,1024]{1,0:T(8,128)(2,1)S(1)} collective-permute-done((bf16[64,1024]{1,0:T(8,128)(2,1)}, bf16[64,1024]{1,0:T(8,128)(2,1)S(1)}, u32[]{:S(2)}, u32[]{:S(2)}) %collective-permute-start.11) | collective-permute-done | bytes 131104 | tf_op jit(solution)/shard_map/ppermute | solution.py:171
  38.6 8.4 %collective-permute-done.10 = bf16[64,1024]{1,0:T(8,128)(2,1)S(1)} collective-permute-done((bf16[64,1024]{1,0:T(8,128)(2,1)}, bf16[64,1024]{1,0:T(8,128)(2,1)S(1)}, u32[]{:S(2)}, u32[]{:S(2)}) %collective-permute-start.10) | collective-permute-done | bytes 131104 | tf_op jit(solution)/shard_map/ppermute | solution.py:171
  47.0 0.0 collective-permute-done.9
  47.0 0.0 copy-done.9
  47.1 0.8 %convolution_bitcast_fusion = f32[4,2,2,128,128]{3,4,2,1,0:T(8,128)S(1)} fusion(bf16[1,1,64,1024]{3,2,1,0:T(8,128)(2,1)S(1)} %bitcast.78, bf16[1,1,64,1024]{3,2,1,0:T(8,128)(2,1)S(1)} %bitcast.79, bf16[1,1,64,1024]{3,2,1,0:T(8,128)(2,1)S(1)} %bitcast.80, bf16[1,1,64,1024]{3,2,1,0:T(8,128)(2,1)S(1)} %bitcast.82, bf16[1,1,64,1024]{3,2,1,0:T(8,128)(2,1)S(1)} %bitcast.75, ...), kind=kOutput, calls=%fused_computation.2 | convolution fusion | flops 547356672 | bytes 3145728 | tf_op jit(solution)/shard_map/lrif,dkjf->dklrij/dot_general | solution.py:179
  47.8 0.6 %gather_fusion.1 = f32[4,2,2,128,128]{3,4,2,1,0:T(8,128)S(1)} fusion(f32[4,2,2,128,128]{3,4,2,1,0:T(8,128)S(1)} %convolution_bitcast_fusion, s32[1024]{0:T(1024)S(1)} %pad_clamp_fusion), kind=kCustom, calls=%fused_computation.1 | custom fusion | bytes 2097168 | tf_op jit(solution)/shard_map/jit(_take)/gather | solution.py:181
  48.4 0.2 fusion.18
  48.7 1.0 %copy.13 = bf16[1,1,4,1,2,2,128,128]{7,6,5,4,3,2,1,0:T(8,128)(2,1)} copy(bf16[1,1,4,1,2,2,128,128]{6,7,5,4,2,3,1,0:T(8,128)(2,1)S(1)} %fusion.18) | data formatting | bytes 1048576 | tf_op jit(solution)/shard_map/convert_element_type | solution.py:185
  (17 shorter events, 0.1 us)
Async XLA Ops:
  0.0 5.2 %copy-start = (s32[1,1,4,1]{2,3,1,0:T(1,128)S(1)}, s32[1,1,4,1]{2,3,1,0:T(1,128)}, u32[]{:S(2)}) copy-start(s32[1,1,4,1]{2,3,1,0:T(1,128)} %param.10) | copy-start | bytes 52
  0.0 6.4 %copy-start.8 = (s32[1,1,4]{2,1,0:T(1,128)S(1)}, s32[1,1,4]{2,1,0:T(1,128)}, u32[]{:S(2)}) copy-start(s32[1,1,4]{2,1,0:T(1,128)} %param.11) | copy-start | bytes 52
  2.0 6.2 %collective-permute-start = (bf16[128,512]{1,0:T(8,128)(2,1)S(1)}, bf16[128,512]{1,0:T(8,128)(2,1)S(1)}, u32[]{:S(2)}, u32[]{:S(2)}) collective-permute-start(bf16[128,512]{1,0:T(8,128)(2,1)S(1)} %get-tuple-element.37), channel_id=1, source_target_pairs={{0,3},{1,0},{2,1},{3,2},{4,7},{5,4},{6,5},{7,6},{8,11},{9,8},{10,9... | collective-permute-start | bytes 393224 | tf_op jit(solution)/shard_map/ppermute | solution.py:161
  4.4 7.5 %collective-permute-start.1 = (bf16[128,512]{1,0:T(8,128)(2,1)S(1)}, bf16[128,512]{1,0:T(8,128)(2,1)S(1)}, u32[]{:S(2)}, u32[]{:S(2)}) collective-permute-start(bf16[128,512]{1,0:T(8,128)(2,1)S(1)} %get-tuple-element.36), channel_id=1, source_target_pairs={{0,2},{1,3},{2,0},{3,1},{4,6},{5,7},{6,4},{7,5},{8,10},{9,11},{10,... | collective-permute-start | bytes 393224 | tf_op jit(solution)/shard_map/ppermute | solution.py:161
  5.0 7.0 %collective-permute-start.2 = (bf16[128,512]{1,0:T(8,128)(2,1)S(1)}, bf16[128,512]{1,0:T(8,128)(2,1)S(1)}, u32[]{:S(2)}, u32[]{:S(2)}) collective-permute-start(bf16[128,512]{1,0:T(8,128)(2,1)S(1)} %get-tuple-element.35), channel_id=1, source_target_pairs={{0,1},{1,2},{2,3},{3,0},{4,5},{5,6},{6,7},{7,4},{8,9},{9,10},{10,1... | collective-permute-start | bytes 393224 | tf_op jit(solution)/shard_map/ppermute | solution.py:161
  8.2 6.3 %copy-start.2 = (bf16[128,512]{1,0:T(8,128)(2,1)}, bf16[128,512]{1,0:T(8,128)(2,1)S(1)}, u32[]{:S(2)}) copy-start(bf16[128,512]{1,0:T(8,128)(2,1)S(1)} %collective-permute-done.refs_1_) | copy-start | bytes 393220
  11.9 2.6 %copy-start.3 = (bf16[128,512]{1,0:T(8,128)(2,1)}, bf16[128,512]{1,0:T(8,128)(2,1)S(1)}, u32[]{:S(2)}) copy-start(bf16[128,512]{1,0:T(8,128)(2,1)S(1)} %collective-permute-done.1.refs_2_) | copy-start | bytes 393220
  11.9 2.6 %copy-start.4 = (bf16[128,512]{1,0:T(8,128)(2,1)}, bf16[128,512]{1,0:T(8,128)(2,1)S(1)}, u32[]{:S(2)}) copy-start(bf16[128,512]{1,0:T(8,128)(2,1)S(1)} %collective-permute-done.2.refs_3_) | copy-start | bytes 393220
  12.7 10.8 %collective-permute-start.6 = (bf16[128,512]{1,0:T(8,128)(2,1)S(1)}, bf16[128,512]{1,0:T(8,128)(2,1)S(1)}, u32[]{:S(2)}, u32[]{:S(2)}) collective-permute-start(bf16[128,512]{1,0:T(8,128)(2,1)S(1)} %get-tuple-element.33), channel_id=1, source_target_pairs={{0,3},{1,0},{2,1},{3,2},{4,7},{5,4},{6,5},{7,6},{8,11},{9,8},{10,9... | collective-permute-start | bytes 393224 | tf_op jit(solution)/shard_map/ppermute | solution.py:161
  12.7 11.8 %collective-permute-start.7 = (bf16[128,512]{1,0:T(8,128)(2,1)S(1)}, bf16[128,512]{1,0:T(8,128)(2,1)S(1)}, u32[]{:S(2)}, u32[]{:S(2)}) collective-permute-start(bf16[128,512]{1,0:T(8,128)(2,1)S(1)} %get-tuple-element.32), channel_id=1, source_target_pairs={{0,2},{1,3},{2,0},{3,1},{4,6},{5,7},{6,4},{7,5},{8,10},{9,11},{10,... | collective-permute-start | bytes 393224 | tf_op jit(solution)/shard_map/ppermute | solution.py:161
  14.3 10.2 %collective-permute-start.8 = (bf16[128,512]{1,0:T(8,128)(2,1)S(1)}, bf16[128,512]{1,0:T(8,128)(2,1)S(1)}, u32[]{:S(2)}, u32[]{:S(2)}) collective-permute-start(bf16[128,512]{1,0:T(8,128)(2,1)S(1)} %get-tuple-element.31), channel_id=1, source_target_pairs={{0,1},{1,2},{2,3},{3,0},{4,5},{5,6},{6,7},{7,4},{8,9},{9,10},{10,1... | collective-permute-start | bytes 393224 | tf_op jit(solution)/shard_map/ppermute | solution.py:161
  19.9 14.6 %copy-start.1 = (bf16[128,1024]{1,0:T(8,128)(2,1)S(1)}, bf16[128,1024]{1,0:T(8,128)(2,1)}, u32[]{:S(2)}) copy-start(bf16[128,1024]{1,0:T(8,128)(2,1)} %get-tuple-element.25) | copy-start | bytes 786436
  19.9 15.7 %collective-permute-start.5 = (bf16[64,1024]{1,0:T(8,128)(2,1)}, bf16[64,1024]{1,0:T(8,128)(2,1)S(1)}, u32[]{:S(2)}, u32[]{:S(2)}) collective-permute-start(bf16[64,1024]{1,0:T(8,128)(2,1)} %get-tuple-element.19), channel_id=1, source_target_pairs={{0,12},{4,0},{8,4},{12,8},{1,13},{5,1},{9,5},{13,9},{2,14},{6,2},{... | collective-permute-start | bytes 393224 | tf_op jit(solution)/shard_map/ppermute | solution.py:171
  23.5 13.2 %collective-permute-start.4 = (bf16[64,1024]{1,0:T(8,128)(2,1)}, bf16[64,1024]{1,0:T(8,128)(2,1)S(1)}, u32[]{:S(2)}, u32[]{:S(2)}) collective-permute-start(bf16[64,1024]{1,0:T(8,128)(2,1)} %get-tuple-element.18), channel_id=1, source_target_pairs={{0,8},{4,12},{8,0},{12,4},{1,9},{5,13},{9,1},{13,5},{2,10},{6,14},... | collective-permute-start | bytes 393224 | tf_op jit(solution)/shard_map/ppermute | solution.py:171
  23.5 1.0 %copy-start.5 = (bf16[128,512]{1,0:T(8,128)(2,1)}, bf16[128,512]{1,0:T(8,128)(2,1)S(1)}, u32[]{:S(2)}) copy-start(bf16[128,512]{1,0:T(8,128)(2,1)S(1)} %collective-permute-done.6.refs_1_) | copy-start | bytes 393220
  23.5 13.2 %collective-permute-start.3 = (bf16[64,1024]{1,0:T(8,128)(2,1)}, bf16[64,1024]{1,0:T(8,128)(2,1)S(1)}, u32[]{:S(2)}, u32[]{:S(2)}) collective-permute-start(bf16[64,1024]{1,0:T(8,128)(2,1)} %get-tuple-element.17), channel_id=1, source_target_pairs={{0,4},{4,8},{8,12},{12,0},{1,5},{5,9},{9,13},{13,1},{2,6},{6,10},{... | collective-permute-start | bytes 393224 | tf_op jit(solution)/shard_map/ppermute | solution.py:171
  24.5 0.7 %copy-start.6 = (bf16[128,512]{1,0:T(8,128)(2,1)}, bf16[128,512]{1,0:T(8,128)(2,1)S(1)}, u32[]{:S(2)}) copy-start(bf16[128,512]{1,0:T(8,128)(2,1)S(1)} %collective-permute-done.7.refs_2_) | copy-start | bytes 393220
  24.5 0.7 %copy-start.7 = (bf16[128,512]{1,0:T(8,128)(2,1)}, bf16[128,512]{1,0:T(8,128)(2,1)S(1)}, u32[]{:S(2)}) copy-start(bf16[128,512]{1,0:T(8,128)(2,1)S(1)} %collective-permute-done.8.refs_3_) | copy-start | bytes 393220
  30.5 16.6 %copy-start.9 = (bf16[64,1024]{1,0:T(8,128)(2,1)S(1)}, bf16[64,1024]{1,0:T(8,128)(2,1)}, u32[]{:S(2)}) copy-start(bf16[64,1024]{1,0:T(8,128)(2,1)} %get-tuple-element.16) | copy-start | bytes 393220
  30.5 16.6 %copy-start.10 = (bf16[64,1024]{1,0:T(8,128)(2,1)S(1)}, bf16[64,1024]{1,0:T(8,128)(2,1)}, u32[]{:S(2)}) copy-start(bf16[64,1024]{1,0:T(8,128)(2,1)} %get-tuple-element.21) | copy-start | bytes 393220
  30.5 8.1 %collective-permute-start.11 = (bf16[64,1024]{1,0:T(8,128)(2,1)}, bf16[64,1024]{1,0:T(8,128)(2,1)S(1)}, u32[]{:S(2)}, u32[]{:S(2)}) collective-permute-start(bf16[64,1024]{1,0:T(8,128)(2,1)} %get-tuple-element.24), channel_id=1, source_target_pairs={{0,12},{4,0},{8,4},{12,8},{1,13},{5,1},{9,5},{13,9},{2,14},{6,2},{... | collective-permute-start | bytes 393224 | tf_op jit(solution)/shard_map/ppermute | solution.py:171
  33.4 13.6 %collective-permute-start.10 = (bf16[64,1024]{1,0:T(8,128)(2,1)}, bf16[64,1024]{1,0:T(8,128)(2,1)S(1)}, u32[]{:S(2)}, u32[]{:S(2)}) collective-permute-start(bf16[64,1024]{1,0:T(8,128)(2,1)} %get-tuple-element.23), channel_id=1, source_target_pairs={{0,8},{4,12},{8,0},{12,4},{1,9},{5,13},{9,1},{13,5},{2,10},{6,14},... | collective-permute-start | bytes 393224 | tf_op jit(solution)/shard_map/ppermute | solution.py:171
  35.5 11.5 %collective-permute-start.9 = (bf16[64,1024]{1,0:T(8,128)(2,1)}, bf16[64,1024]{1,0:T(8,128)(2,1)S(1)}, u32[]{:S(2)}, u32[]{:S(2)}) collective-permute-start(bf16[64,1024]{1,0:T(8,128)(2,1)} %get-tuple-element.22), channel_id=1, source_target_pairs={{0,4},{4,8},{8,12},{12,0},{1,5},{5,9},{9,13},{13,1},{2,6},{6,10},{... | collective-permute-start | bytes 393224 | tf_op jit(solution)/shard_map/ppermute | solution.py:171

commit v9 on v7

--- a/solution.py
+++ b/solution.py
@@ -150,8 +150,9 @@
             piece = lax.dynamic_index_in_dim(part, (here + d) % ntm, axis=0, keepdims=False)
             slots.append(lax.ppermute(piece, "tm", perm=[(i, (i + d) % ntm) for i in range(ntm)]))
         prev_slots = jnp.stack(slots)
-        whitened = spectra(pos, prev_slots).reshape(blocks, rows, 2 * NBAND)
-        own_parts.append(whitened)
+        flat = spectra(pos, prev_slots)
+        whitened = flat.reshape(blocks, rows, 2 * NBAND)
+        own_parts.append(flat)
         recv = []
         for d in range(peers):
             dest = (mine + d) % peers
@@ -164,19 +165,59 @@
                 if d:
                     blk = lax.ppermute(blk, "chan", perm=[(i, (i + d) % peers) for i in range(peers)])
                 row.append(blk)
-            recv.append(jnp.stack(row))
-        picked_parts.append(jnp.stack(recv))
-    whitened = jnp.concatenate(own_parts, axis=1)
-    picked = jnp.concatenate(picked_parts, axis=2)
-    turned = jnp.concatenate([whitened[..., NBAND:], -whitened[..., :NBAND]], axis=-1)
-    paired = jnp.stack([whitened, turned], axis=1)
-    result = jnp.einsum("lrif,dkjf->dklrij", paired, picked, preferred_element_type=jnp.float32)
-    order = (mine - jnp.arange(peers, dtype=jnp.int32)) % peers
-    result = jnp.take(result, order, axis=0)
-    result = result * (1.0 / math.sqrt(NBAND))
-    live = jnp.arange(cap, dtype=jnp.int32)[None, :] < pair_count[0, 0][:, None]
-    result = jnp.where(live[:, :, None, None, None, None], result, 0.0)
-    return result.astype(jnp.bfloat16)[None, None]
+            recv.append(row)
+        picked_parts.append(recv)
+    return xspec(mine.astype(jnp.int32).reshape(1), pair_count[0, 0], own_parts, picked_parts)[None, None]
+
+
+def xspec_kernel(mine_ref, count_ref, *refs):
+    o_ref = refs[-1]
+    npeer, cap, blocks = o_ref.shape[:3]
+    own_refs = refs[:NSPLIT]
+    recv_refs = refs[NSPLIT:-1]
+    rows = own_refs[0].shape[0] // blocks
+    mine = mine_ref[0]
+    scale = 1.0 / math.sqrt(NBAND)
+    dims = (((1,), (1,)), ((), ()))
+    pairs = []
+    for l in range(blocks):
+        own = jnp.concatenate([r[l * rows:(l + 1) * rows, :] for r in own_refs], axis=0)
+        turned = jnp.concatenate([own[:, NBAND:], -own[:, :NBAND]], axis=1)
+        pairs.append((own, turned))
+    for d in range(npeer):
+        src = (mine - d + npeer) % npeer
+        for k in range(cap):
+            picked = jnp.concatenate(
+                [recv_refs[(h * npeer + d) * cap + k][...] for h in range(NSPLIT)], axis=0
+            )
+            live = k < count_ref[src]
+            for l in range(blocks):
+                for r in range(2):
+                    val = lax.dot_general(pairs[l][r], picked, dims, preferred_element_type=jnp.float32)
+                    val = jnp.where(live, val * scale, 0.0)
+                    o_ref[src, k, l, r] = val.astype(jnp.bfloat16)
+
+
+def xspec(mine, count, own_parts, picked_parts):
+    peers, cap = len(picked_parts[0]), len(picked_parts[0][0])
+    blocks = own_parts[0].shape[0] // picked_parts[0][0][0].shape[0]
+    ins = list(own_parts) + [blk for part in picked_parts for row in part for blk in row]
+    full = lambda shape: pl.BlockSpec(shape, lambda i, m, c: (0,) * len(shape))
+    out_shape = (peers, cap, blocks, 2, BLOCK, BLOCK)
+    grid_spec = pltpu.PrefetchScalarGridSpec(
+        num_scalar_prefetch=2,
+        grid=(1,),
+        in_specs=[full(x.shape) for x in ins],
+        out_specs=full(out_shape),
+    )
+    flops = 2 * peers * cap * blocks * 2 * BLOCK * BLOCK * 2 * NBAND
+    nbytes = sum(x.size for x in ins) * 2 + math.prod(out_shape) * 2
+    return pl.pallas_call(
+        xspec_kernel,
+        grid_spec=grid_spec,
+        cost_estimate=pl.CostEstimate(flops=flops, transcendentals=0, bytes_accessed=nbytes),
+        out_shape=jax.ShapeDtypeStruct(out_shape, jnp.bfloat16),
+    )(mine, count, *ins)
 
 
 def solution(mesh):

time: 47.4 us -> 52.2 us (1.10)
  waiting for transfers between devices: 8.07 us -> 15.2 us
  Pallas kernels: 8.6 us -> 12.7 us
  starting transfers between devices: 16.8 us -> 13.7 us
  other arithmetic: 6.08 us -> 5.04 us
  local copies, waits for them, and re-layouts: 3.7 us -> 2.71 us
  matrix products: 0.74 us -> 0 us
    ppermute x6, waiting for transfers between devices: 5.61 us -> 11.6 us  [local(): lax.ppermute(blk, 'chan', perm=[(i, (i + d) % peers) for i in range(peers)])]
    pallas_call x0 -> x1, Pallas kernels: none -> 4.1 us  [xspec(): pl.pallas_call(xspec_kernel, grid_spec=grid_spec, cost_estimate=pl.CostEs...]
    select_n x1 -> x2, other arithmetic: 0.01 us -> 3.32 us  [local(): blk = jnp.where(want == b, whitened[b], blk)]
    another operation x3 -> x0, other arithmetic: 3.06 us -> none  [the longest x2 2.01 us: local(): picked_parts.append(jnp.stack(recv))]
    ppermute x6, starting transfers between devices: 7.29 us -> 5.16 us  [local(): lax.ppermute(piece, 'tm', perm=[(i, (i + d) % ntm) for i in range(ntm)])]
    ppermute x6, waiting for transfers between devices: 2.45 us -> 3.59 us  [local(): lax.ppermute(piece, 'tm', perm=[(i, (i + d) % ntm) for i in range(ntm)])]
    concatenate x1 -> x0, other arithmetic: 1.02 us -> none  [local(): whitened = jnp.concatenate(own_parts, axis=1)]
    convert_element_type x1 -> x0, local copies, waits for them, and re-layouts: 1.01 us -> none  [local(): return result.astype(jnp.bfloat16)[None, None]]
  transfers between devices with their start and end apart: 12 -> 12, of which waited for: 4 -> 4; matrix products, arithmetic and copies ran while one was open for 12% -> 9% of each run, Pallas kernels for 18% -> 17%
where the time goes in v9:
time: 52.2 us; the launch traced here: 51.9 us
  waiting for transfers between devices  15.2 us (29%)
  starting transfers between devices  13.7 us (26%)
  Pallas kernels  12.7 us (24%)
  other arithmetic  5.04 us (10%)
  local copies, waits for them, and re-layouts  2.71 us (5%)
  between operations  2.59 us (5%)
    ppermute x6, waiting for transfers between devices, local(): lax.ppermute(blk, 'chan', perm=[(i, (i + d) % peers) for i in range(peers)])  11.6 us
    ppermute x6, starting transfers between devices, local(): lax.ppermute(blk, 'chan', perm=[(i, (i + d) % peers) for i in range(peers)])  8.57 us
    pallas_call x2, Pallas kernels, spectra(): pl.pallas_call(spectra_kernel, grid_spec=grid_spec, cost_estimate=pl.Cost...  8.57 us
    ppermute x6, starting transfers between devices, local(): lax.ppermute(piece, 'tm', perm=[(i, (i + d) % ntm) for i in range(ntm)])  5.16 us
    pallas_call x1, Pallas kernels, xspec(): pl.pallas_call(xspec_kernel, grid_spec=grid_spec, cost_estimate=pl.CostEs...  4.1 us
    ppermute x6, waiting for transfers between devices, local(): lax.ppermute(piece, 'tm', perm=[(i, (i + d) % ntm) for i in range(ntm)])  3.59 us
    select_n x2, other arithmetic, local(): blk = jnp.where(want == b, whitened[b], blk)  3.32 us
    another operation x2, other arithmetic, local(): prev_slots = jnp.stack(slots)  1.72 us
  transfers between devices with their start and end apart: 12, of which 4 were waited for; matrix products, arithmetic and copies ran while one was open for 9% of the time, Pallas kernels for 17%

profile of v9, /device:TPU:0, one launch (start us, length us, event | category | flops | bytes accessed | tf_op | source)
XLA Modules:
  0.0 51.9 jit_solution(1608160023065283173)
XLA Ops:
  0.0 0.0 copy-start.6
  0.0 1.3 %fusion = (bf16[4,2,1,64,512]{4,3,2,1,0:T(8,128)(2,1)S(1)}, bf16[4,2,1,64,512]{4,3,2,1,0:T(8,128)(2,1)S(1)}) fusion(bf16[4,2,2,64,512]{4,3,2,1,0:T(8,128)(2,1)} %bitcast.37), kind=kLoop, calls=%fused_computation.22 | loop fusion | bytes 2097152 | tf_op jit(solution)/shard_map/slice | solution.py:145
  1.4 2.4 %collective-permute-start.2 = (bf16[128,512]{1,0:T(8,128)(2,1)S(1)}, bf16[128,512]{1,0:T(8,128)(2,1)S(1)}, u32[]{:S(2)}, u32[]{:S(2)}) collective-permute-start(bf16[128,512]{1,0:T(8,128)(2,1)S(1)} %get-tuple-element.14), channel_id=1, source_target_pairs={{0,3},{1,0},{2,1},{3,2},{4,7},{5,4},{6,5},{7,6},{8,11},{9,8},{10,9... | collective-permute-start | bytes 393224 | tf_op jit(solution)/shard_map/ppermute | solution.py:151
  3.8 0.6 %collective-permute-start.1 = (bf16[128,512]{1,0:T(8,128)(2,1)S(1)}, bf16[128,512]{1,0:T(8,128)(2,1)S(1)}, u32[]{:S(2)}, u32[]{:S(2)}) collective-permute-start(bf16[128,512]{1,0:T(8,128)(2,1)S(1)} %get-tuple-element.15), channel_id=1, source_target_pairs={{0,2},{1,3},{2,0},{3,1},{4,6},{5,7},{6,4},{7,5},{8,10},{9,11},{10,... | collective-permute-start | bytes 393224 | tf_op jit(solution)/shard_map/ppermute | solution.py:151
  4.5 0.2 collective-permute-start
  4.6 0.0 copy-done.6
  4.6 0.7 %constant_dynamic-slice_fusion = (s32[1,1,1,1]{2,3,1,0:T(1,128)}, s32[1,1,1,1]{2,3,1,0:T(1,128)}, s32[1,1,1,1]{2,3,1,0:T(1,128)}, s32[1,1,1,1]{2,3,1,0:T(1,128)}) fusion(s32[1,1,4,1]{2,3,1,0:T(1,128)S(1)} %copy-done.6, s32[]{:T(128)S(6)} %select_n.141, s32[]{:T(128)S(6)} %select_n.133, s32[]{:T(128)S(6)} %select_n.129, s32[]{:T(128)S(6)} %select_n.137), kind=kLoop, calls=%fused_computation.16 | loop fusion | bytes 48 | tf_op jit(solution)/shard_map/jit(dynamic_index_in_dim)/dynamic_slice | solution.py:161
  7.8 0.0 collective-permute-done.2
  7.8 3.6 %collective-permute-done.1 = bf16[128,512]{1,0:T(8,128)(2,1)S(1)} collective-permute-done((bf16[128,512]{1,0:T(8,128)(2,1)S(1)}, bf16[128,512]{1,0:T(8,128)(2,1)S(1)}, u32[]{:S(2)}, u32[]{:S(2)}) %collective-permute-start.1) | collective-permute-done | bytes 131104 | tf_op jit(solution)/shard_map/ppermute | solution.py:151
  11.4 0.0 collective-permute-done
  11.4 0.9 %pad_maximum_fusion.x_ref = bf16[4,128,512]{2,1,0:T(8,128)(2,1)} fusion(bf16[1,128,512]{2,1,0:T(8,128)(2,1)S(1)} %bitcast.38, bf16[1,128,512]{2,1,0:T(8,128)(2,1)S(1)} %bitcast.39, bf16[1,128,512]{2,1,0:T(8,128)(2,1)S(1)} %bitcast.40, bf16[1,128,512]{2,1,0:T(8,128)(2,1)S(1)} %get-tuple-element.13), kind=kLoop, calls=%fused_computation | loop fusion | flops 786432 | bytes 1048576 | tf_op jit(solution)/shard_map/stack | solution.py:152
  12.3 0.1 collective-permute-start.5
  12.3 1.7 %collective-permute-start.4 = (bf16[128,512]{1,0:T(8,128)(2,1)S(1)}, bf16[128,512]{1,0:T(8,128)(2,1)S(1)}, u32[]{:S(2)}, u32[]{:S(2)}) collective-permute-start(bf16[128,512]{1,0:T(8,128)(2,1)S(1)} %get-tuple-element.11), channel_id=1, source_target_pairs={{0,2},{1,3},{2,0},{3,1},{4,6},{5,7},{6,4},{7,5},{8,10},{9,11},{10,... | collective-permute-start | bytes 393224 | tf_op jit(solution)/shard_map/ppermute | solution.py:151
  14.0 0.2 collective-permute-start.3
  14.2 4.3 %shard_map.91.refs_0_ = bf16[128,1024]{1,0:T(8,128)(2,1)} custom-call(s32[1]{0:T(128)} %bitcast.2.pos_ref, bf16[4,128,512]{2,1,0:T(8,128)(2,1)} %pad_maximum_fusion.x_ref, bf16[384,256]{1,0:T(8,128)(2,1)} %constant.114.clone.band_ref, bf16[1024,1024]{1,0:T(8,128)(2,1)} %constant.115.clone.tab_ref, bf16[512,512]{1,0:T(8,128)(2,1)} %constant.116.clone.grp_ref), custom_call_target="tpu_custom_call" | custom-call | flops 1073741824 | bytes 2883584 | tf_op jit(solution)/shard_map/pallas_call | solution.py:121
  18.5 1.7 %broadcast_select_fusion.1 = (bf16[64,1024]{1,0:T(8,128)(2,1)S(1)}, bf16[64,1024]{1,0:T(8,128)(2,1)S(1)}, bf16[64,1024]{1,0:T(8,128)(2,1)}, bf16[64,1024]{1,0:T(8,128)(2,1)S(1)}) fusion(pred[]{:T(512)} %bitcast.21, bf16[128,1024]{1,0:T(8,128)(2,1)} %shard_map.91.refs_0_, pred[]{:T(512)} %bitcast.20, pred[]{:T(512)} %bitcast.18, pred[]{:T(512)} %bitcast.19), kind=kLoop, calls=%fused_computation.9 | loop fusion | flops 262144 | bytes 786436 | tf_op jit(solution)/shard_map/jit(_where)/select_n | solution.py:164
  20.1 3.6 %collective-permute-start.8 = (bf16[64,1024]{1,0:T(8,128)(2,1)S(1)}, bf16[64,1024]{1,0:T(8,128)(2,1)S(1)}, u32[]{:S(2)}, u32[]{:S(2)}) collective-permute-start(bf16[64,1024]{1,0:T(8,128)(2,1)S(1)} %get-tuple-element.21), channel_id=1, source_target_pairs={{0,12},{4,0},{8,4},{12,8},{1,13},{5,1},{9,5},{13,9},{2,14},{6,2},{... | collective-permute-start | bytes 393224 | tf_op jit(solution)/shard_map/ppermute | solution.py:166
  23.7 0.0 collective-permute-start.7
  23.8 0.0 collective-permute-done.5
  23.8 1.0 %collective-permute-start.6 = (bf16[64,1024]{1,0:T(8,128)(2,1)S(1)}, bf16[64,1024]{1,0:T(8,128)(2,1)S(1)}, u32[]{:S(2)}, u32[]{:S(2)}) collective-permute-start(bf16[64,1024]{1,0:T(8,128)(2,1)S(1)} %get-tuple-element.24), channel_id=1, source_target_pairs={{0,4},{4,8},{8,12},{12,0},{1,5},{5,9},{9,13},{13,1},{2,6},{6,10},{... | collective-permute-start | bytes 393224 | tf_op jit(solution)/shard_map/ppermute | solution.py:166
  24.8 0.0 collective-permute-done.4
  24.8 0.0 collective-permute-done.3
  24.8 0.9 %pad_maximum_fusion.1.x_ref = bf16[4,128,512]{2,1,0:T(8,128)(2,1)} fusion(bf16[1,128,512]{2,1,0:T(8,128)(2,1)S(1)} %bitcast.41, bf16[1,128,512]{2,1,0:T(8,128)(2,1)S(1)} %bitcast.42, bf16[1,128,512]{2,1,0:T(8,128)(2,1)S(1)} %bitcast.43, bf16[1,128,512]{2,1,0:T(8,128)(2,1)S(1)} %get-tuple-element.9), kind=kLoop, calls=%fused_computation.1 | loop fusion | flops 786432 | bytes 1048576 | tf_op jit(solution)/shard_map/stack | solution.py:152
  25.6 4.3 %shard_map.92.refs_1_ = bf16[128,1024]{1,0:T(8,128)(2,1)} custom-call(s32[1]{0:T(128)} %bitcast.2.pos_ref, bf16[4,128,512]{2,1,0:T(8,128)(2,1)} %pad_maximum_fusion.1.x_ref, bf16[384,256]{1,0:T(8,128)(2,1)} %constant.114.clone.band_ref, bf16[1024,1024]{1,0:T(8,128)(2,1)} %constant.115.clone.tab_ref, bf16[512,512]{1,0:T(8,128)(2,1)} %constant.116.clone.grp_ref), custom_call_target="tpu_custom_call" | custom-call | flops 1073741824 | bytes 2883584 | tf_op jit(solution)/shard_map/pallas_call | solution.py:121
  29.9 1.7 %broadcast_select_fusion = (bf16[64,1024]{1,0:T(8,128)(2,1)S(1)}, bf16[64,1024]{1,0:T(8,128)(2,1)S(1)}, bf16[64,1024]{1,0:T(8,128)(2,1)}, bf16[64,1024]{1,0:T(8,128)(2,1)S(1)}) fusion(pred[]{:T(512)} %bitcast.21, bf16[128,1024]{1,0:T(8,128)(2,1)} %shard_map.92.refs_1_, pred[]{:T(512)} %bitcast.20, pred[]{:T(512)} %bitcast.18, pred[]{:T(512)} %bitcast.19), kind=kLoop, calls=%fused_computation.8 | loop fusion | flops 262144 | bytes 786436 | tf_op jit(solution)/shard_map/jit(_where)/select_n | solution.py:164
  31.6 2.8 %collective-permute-start.11 = (bf16[64,1024]{1,0:T(8,128)(2,1)S(1)}, bf16[64,1024]{1,0:T(8,128)(2,1)S(1)}, u32[]{:S(2)}, u32[]{:S(2)}) collective-permute-start(bf16[64,1024]{1,0:T(8,128)(2,1)S(1)} %get-tuple-element.17), channel_id=1, source_target_pairs={{0,12},{4,0},{8,4},{12,8},{1,13},{5,1},{9,5},{13,9},{2,14},{6,2},{... | collective-permute-start | bytes 393224 | tf_op jit(solution)/shard_map/ppermute | solution.py:166
  34.4 1.1 %collective-permute-start.10 = (bf16[64,1024]{1,0:T(8,128)(2,1)S(1)}, bf16[64,1024]{1,0:T(8,128)(2,1)S(1)}, u32[]{:S(2)}, u32[]{:S(2)}) collective-permute-start(bf16[64,1024]{1,0:T(8,128)(2,1)S(1)} %get-tuple-element.18), channel_id=1, source_target_pairs={{0,8},{4,12},{8,0},{12,4},{1,9},{5,13},{9,1},{13,5},{2,10},{6,14},... | collective-permute-start | bytes 393224 | tf_op jit(solution)/shard_map/ppermute | solution.py:166
  35.5 0.0 collective-permute-done.8.refs_5_
  35.5 0.0 copy-start
  35.5 0.0 collective-permute-start.9
  35.5 0.5 collective-permute-done.7.refs_4_
  36.0 0.0 copy-start.1
  36.0 0.0 collective-permute-done.6.refs_3_
  36.0 0.0 copy-start.2
  36.0 3.0 %collective-permute-done.11.refs_9_ = bf16[64,1024]{1,0:T(8,128)(2,1)S(1)} collective-permute-done((bf16[64,1024]{1,0:T(8,128)(2,1)S(1)}, bf16[64,1024]{1,0:T(8,128)(2,1)S(1)}, u32[]{:S(2)}, u32[]{:S(2)}) %collective-permute-start.11) | collective-permute-done | bytes 131104 | tf_op jit(solution)/shard_map/ppermute | solution.py:166
  39.0 0.0 copy-start.3
  39.0 8.1 %collective-permute-done.10.refs_8_ = bf16[64,1024]{1,0:T(8,128)(2,1)S(1)} collective-permute-done((bf16[64,1024]{1,0:T(8,128)(2,1)S(1)}, bf16[64,1024]{1,0:T(8,128)(2,1)S(1)}, u32[]{:S(2)}, u32[]{:S(2)}) %collective-permute-start.10) | collective-permute-done | bytes 131104 | tf_op jit(solution)/shard_map/ppermute | solution.py:166
  47.1 0.0 copy-start.4
  47.1 0.0 collective-permute-done.9.refs_7_
  47.1 0.0 copy-start.5
  47.1 0.0 copy-done
  47.2 0.0 copy-done.1
  47.2 0.0 copy-done.2
  47.2 0.0 copy-done.3
  47.2 0.6 %copy-done.4 = bf16[64,1024]{1,0:T(8,128)(2,1)} copy-done((bf16[64,1024]{1,0:T(8,128)(2,1)}, bf16[64,1024]{1,0:T(8,128)(2,1)S(1)}, u32[]{:S(2)}) %copy-start.4) | copy-done | bytes 131096
  47.8 0.0 copy-done.5
  47.8 4.1 %shard_map.93 = bf16[4,1,2,2,128,128]{5,4,3,2,1,0:T(8,128)(2,1)} custom-call(s32[1]{0:T(128)} %bitcast.mine_ref, s32[4]{0:T(128)} %bitcast.44, bf16[128,1024]{1,0:T(8,128)(2,1)} %shard_map.91.refs_0_, bf16[128,1024]{1,0:T(8,128)(2,1)} %shard_map.92.refs_1_, bf16[64,1024]{1,0:T(8,128)(2,1)} %get-tuple-element.23.refs_2_, bf16[64,1024]{1,0:T(8,128)(2,1)} %copy-done.2, ...), custom_call_target="tpu_custom_call" | custom-call | flops 536870912 | bytes 2097152 | tf_op jit(solution)/shard_map/pallas_call | solution.py:215
  (2 shorter events, 0.1 us)
Async XLA Ops:
  0.0 4.6 %copy-start.6 = (s32[1,1,4,1]{2,3,1,0:T(1,128)S(1)}, s32[1,1,4,1]{2,3,1,0:T(1,128)}, u32[]{:S(2)}) copy-start(s32[1,1,4,1]{2,3,1,0:T(1,128)} %param.10) | copy-start | bytes 52
  1.4 6.4 %collective-permute-start.2 = (bf16[128,512]{1,0:T(8,128)(2,1)S(1)}, bf16[128,512]{1,0:T(8,128)(2,1)S(1)}, u32[]{:S(2)}, u32[]{:S(2)}) collective-permute-start(bf16[128,512]{1,0:T(8,128)(2,1)S(1)} %get-tuple-element.14), channel_id=1, source_target_pairs={{0,3},{1,0},{2,1},{3,2},{4,7},{5,4},{6,5},{7,6},{8,11},{9,8},{10,9... | collective-permute-start | bytes 393224 | tf_op jit(solution)/shard_map/ppermute | solution.py:151
  3.8 7.5 %collective-permute-start.1 = (bf16[128,512]{1,0:T(8,128)(2,1)S(1)}, bf16[128,512]{1,0:T(8,128)(2,1)S(1)}, u32[]{:S(2)}, u32[]{:S(2)}) collective-permute-start(bf16[128,512]{1,0:T(8,128)(2,1)S(1)} %get-tuple-element.15), channel_id=1, source_target_pairs={{0,2},{1,3},{2,0},{3,1},{4,6},{5,7},{6,4},{7,5},{8,10},{9,11},{10,... | collective-permute-start | bytes 393224 | tf_op jit(solution)/shard_map/ppermute | solution.py:151
  4.5 6.9 %collective-permute-start = (bf16[128,512]{1,0:T(8,128)(2,1)S(1)}, bf16[128,512]{1,0:T(8,128)(2,1)S(1)}, u32[]{:S(2)}, u32[]{:S(2)}) collective-permute-start(bf16[128,512]{1,0:T(8,128)(2,1)S(1)} %get-tuple-element.16), channel_id=1, source_target_pairs={{0,1},{1,2},{2,3},{3,0},{4,5},{5,6},{6,7},{7,4},{8,9},{9,10},{10,1... | collective-permute-start | bytes 393224 | tf_op jit(solution)/shard_map/ppermute | solution.py:151
  12.3 11.5 %collective-permute-start.5 = (bf16[128,512]{1,0:T(8,128)(2,1)S(1)}, bf16[128,512]{1,0:T(8,128)(2,1)S(1)}, u32[]{:S(2)}, u32[]{:S(2)}) collective-permute-start(bf16[128,512]{1,0:T(8,128)(2,1)S(1)} %get-tuple-element.10), channel_id=1, source_target_pairs={{0,3},{1,0},{2,1},{3,2},{4,7},{5,4},{6,5},{7,6},{8,11},{9,8},{10,9... | collective-permute-start | bytes 393224 | tf_op jit(solution)/shard_map/ppermute | solution.py:151
  12.3 12.4 %collective-permute-start.4 = (bf16[128,512]{1,0:T(8,128)(2,1)S(1)}, bf16[128,512]{1,0:T(8,128)(2,1)S(1)}, u32[]{:S(2)}, u32[]{:S(2)}) collective-permute-start(bf16[128,512]{1,0:T(8,128)(2,1)S(1)} %get-tuple-element.11), channel_id=1, source_target_pairs={{0,2},{1,3},{2,0},{3,1},{4,6},{5,7},{6,4},{7,5},{8,10},{9,11},{10,... | collective-permute-start | bytes 393224 | tf_op jit(solution)/shard_map/ppermute | solution.py:151
  14.0 10.7 %collective-permute-start.3 = (bf16[128,512]{1,0:T(8,128)(2,1)S(1)}, bf16[128,512]{1,0:T(8,128)(2,1)S(1)}, u32[]{:S(2)}, u32[]{:S(2)}) collective-permute-start(bf16[128,512]{1,0:T(8,128)(2,1)S(1)} %get-tuple-element.12), channel_id=1, source_target_pairs={{0,1},{1,2},{2,3},{3,0},{4,5},{5,6},{6,7},{7,4},{8,9},{9,10},{10,1... | collective-permute-start | bytes 393224 | tf_op jit(solution)/shard_map/ppermute | solution.py:151
  20.1 15.4 %collective-permute-start.8 = (bf16[64,1024]{1,0:T(8,128)(2,1)S(1)}, bf16[64,1024]{1,0:T(8,128)(2,1)S(1)}, u32[]{:S(2)}, u32[]{:S(2)}) collective-permute-start(bf16[64,1024]{1,0:T(8,128)(2,1)S(1)} %get-tuple-element.21), channel_id=1, source_target_pairs={{0,12},{4,0},{8,4},{12,8},{1,13},{5,1},{9,5},{13,9},{2,14},{6,2},{... | collective-permute-start | bytes 393224 | tf_op jit(solution)/shard_map/ppermute | solution.py:166
  23.7 12.3 %collective-permute-start.7 = (bf16[64,1024]{1,0:T(8,128)(2,1)S(1)}, bf16[64,1024]{1,0:T(8,128)(2,1)S(1)}, u32[]{:S(2)}, u32[]{:S(2)}) collective-permute-start(bf16[64,1024]{1,0:T(8,128)(2,1)S(1)} %get-tuple-element.22), channel_id=1, source_target_pairs={{0,8},{4,12},{8,0},{12,4},{1,9},{5,13},{9,1},{13,5},{2,10},{6,14},... | collective-permute-start | bytes 393224 | tf_op jit(solution)/shard_map/ppermute | solution.py:166
  23.8 12.3 %collective-permute-start.6 = (bf16[64,1024]{1,0:T(8,128)(2,1)S(1)}, bf16[64,1024]{1,0:T(8,128)(2,1)S(1)}, u32[]{:S(2)}, u32[]{:S(2)}) collective-permute-start(bf16[64,1024]{1,0:T(8,128)(2,1)S(1)} %get-tuple-element.24), channel_id=1, source_target_pairs={{0,4},{4,8},{8,12},{12,0},{1,5},{5,9},{9,13},{13,1},{2,6},{6,10},{... | collective-permute-start | bytes 393224 | tf_op jit(solution)/shard_map/ppermute | solution.py:166
  31.6 7.5 %collective-permute-start.11 = (bf16[64,1024]{1,0:T(8,128)(2,1)S(1)}, bf16[64,1024]{1,0:T(8,128)(2,1)S(1)}, u32[]{:S(2)}, u32[]{:S(2)}) collective-permute-start(bf16[64,1024]{1,0:T(8,128)(2,1)S(1)} %get-tuple-element.17), channel_id=1, source_target_pairs={{0,12},{4,0},{8,4},{12,8},{1,13},{5,1},{9,5},{13,9},{2,14},{6,2},{... | collective-permute-start | bytes 393224 | tf_op jit(solution)/shard_map/ppermute | solution.py:166
  34.4 12.8 %collective-permute-start.10 = (bf16[64,1024]{1,0:T(8,128)(2,1)S(1)}, bf16[64,1024]{1,0:T(8,128)(2,1)S(1)}, u32[]{:S(2)}, u32[]{:S(2)}) collective-permute-start(bf16[64,1024]{1,0:T(8,128)(2,1)S(1)} %get-tuple-element.18), channel_id=1, source_target_pairs={{0,8},{4,12},{8,0},{12,4},{1,9},{5,13},{9,1},{13,5},{2,10},{6,14},... | collective-permute-start | bytes 393224 | tf_op jit(solution)/shard_map/ppermute | solution.py:166
  35.5 11.6 %copy-start = (bf16[64,1024]{1,0:T(8,128)(2,1)}, bf16[64,1024]{1,0:T(8,128)(2,1)S(1)}, u32[]{:S(2)}) copy-start(bf16[64,1024]{1,0:T(8,128)(2,1)S(1)} %collective-permute-done.8.refs_5_) | copy-start | bytes 393220
  35.5 11.6 %collective-permute-start.9 = (bf16[64,1024]{1,0:T(8,128)(2,1)S(1)}, bf16[64,1024]{1,0:T(8,128)(2,1)S(1)}, u32[]{:S(2)}, u32[]{:S(2)}) collective-permute-start(bf16[64,1024]{1,0:T(8,128)(2,1)S(1)} %get-tuple-element.20), channel_id=1, source_target_pairs={{0,4},{4,8},{8,12},{12,0},{1,5},{5,9},{9,13},{13,1},{2,6},{6,10},{... | collective-permute-start | bytes 393224 | tf_op jit(solution)/shard_map/ppermute | solution.py:166
  36.0 11.1 %copy-start.1 = (bf16[64,1024]{1,0:T(8,128)(2,1)}, bf16[64,1024]{1,0:T(8,128)(2,1)S(1)}, u32[]{:S(2)}) copy-start(bf16[64,1024]{1,0:T(8,128)(2,1)S(1)} %collective-permute-done.7.refs_4_) | copy-start | bytes 393220
  36.0 11.2 %copy-start.2 = (bf16[64,1024]{1,0:T(8,128)(2,1)}, bf16[64,1024]{1,0:T(8,128)(2,1)S(1)}, u32[]{:S(2)}) copy-start(bf16[64,1024]{1,0:T(8,128)(2,1)S(1)} %collective-permute-done.6.refs_3_) | copy-start | bytes 393220
  39.0 8.1 %copy-start.3 = (bf16[64,1024]{1,0:T(8,128)(2,1)}, bf16[64,1024]{1,0:T(8,128)(2,1)S(1)}, u32[]{:S(2)}) copy-start(bf16[64,1024]{1,0:T(8,128)(2,1)S(1)} %collective-permute-done.11.refs_9_) | copy-start | bytes 393220
  47.1 0.7 %copy-start.4 = (bf16[64,1024]{1,0:T(8,128)(2,1)}, bf16[64,1024]{1,0:T(8,128)(2,1)S(1)}, u32[]{:S(2)}) copy-start(bf16[64,1024]{1,0:T(8,128)(2,1)S(1)} %collective-permute-done.10.refs_8_) | copy-start | bytes 393220
  47.1 0.7 %copy-start.5 = (bf16[64,1024]{1,0:T(8,128)(2,1)}, bf16[64,1024]{1,0:T(8,128)(2,1)S(1)}, u32[]{:S(2)}) copy-start(bf16[64,1024]{1,0:T(8,128)(2,1)S(1)} %collective-permute-done.9.refs_7_) | copy-start | bytes 393220

commit v10 on v7

--- a/solution.py
+++ b/solution.py
@@ -66,7 +66,11 @@
     return ((g[:, None] == g[None, :]).astype(np.float32) / SUBW).astype(BF16)
 
 
-def spectra_kernel(pos_ref, x_ref, band_ref, tab_ref, grp_ref, o_ref, filt_ref):
+def spectra_kernel(pos_ref, x_ref, band_ref, tab_hbm, grp_hbm, o_ref, filt_ref, tab_ref, grp_ref, sem):
+    tab_copy = pltpu.make_async_copy(tab_hbm, tab_ref, sem.at[0])
+    grp_copy = pltpu.make_async_copy(grp_hbm, grp_ref, sem.at[1])
+    tab_copy.start()
+    grp_copy.start()
     nslot, _, width = x_ref.shape
     ntile = NT // TILE
     pos = pos_ref[0]
@@ -80,6 +84,7 @@
         win = jnp.concatenate([tile(j - 1), tile(j), tile(j + 1)], axis=1)
         acc = jnp.dot(win, band, preferred_element_type=jnp.float32)
         filt_ref[:, j * TILE:(j + 1) * TILE] = (acc[:, :TILE] + acc[:, TILE:]).astype(jnp.bfloat16)
+    tab_copy.wait()
     tab = tab_ref[...]
     first = jnp.dot(filt_ref[:, :HALF], tab, preferred_element_type=jnp.float32)
     second = jnp.dot(filt_ref[:, HALF:], tab, preferred_element_type=jnp.float32)
@@ -90,6 +95,7 @@
     power = re * re + im * im
     p_hi = power.astype(jnp.bfloat16)
     p_lo = (power - p_hi.astype(jnp.float32)).astype(jnp.bfloat16)
+    grp_copy.wait()
     grp = grp_ref[...]
     mean = jnp.dot(p_hi, grp, preferred_element_type=jnp.float32) + jnp.dot(
         p_lo, grp, preferred_element_type=jnp.float32
@@ -110,11 +116,16 @@
         in_specs=[
             pl.BlockSpec((ntm, BLOCK, width), lambda r, p: (0, r, 0)),
             pl.BlockSpec(band.shape, lambda r, p: (0, 0)),
-            pl.BlockSpec(tab.shape, lambda r, p: (0, 0)),
-            pl.BlockSpec(grp.shape, lambda r, p: (0, 0)),
+            pl.BlockSpec(memory_space=pl.ANY),
+            pl.BlockSpec(memory_space=pl.ANY),
         ],
         out_specs=pl.BlockSpec((BLOCK, 2 * NBAND), lambda r, p: (r, 0)),
-        scratch_shapes=[pltpu.VMEM((BLOCK, NT), jnp.bfloat16)],
+        scratch_shapes=[
+            pltpu.VMEM((BLOCK, NT), jnp.bfloat16),
+            pltpu.VMEM(tab.shape, jnp.bfloat16),
+            pltpu.VMEM(grp.shape, jnp.bfloat16),
+            pltpu.SemaphoreType.DMA((2,)),
+        ],
     )
     flops = 2 * nrows * (3 * TILE * 2 * TILE * (NT // TILE) + NT * 2 * NBAND + 2 * NBAND * NBAND)
     nbytes = rows3.size * 2 + tab.size * 2 + nrows * 2 * NBAND * 2
@@ -142,9 +153,9 @@
     own_parts = []
     picked_parts = []
     for h in range(NSPLIT):
+        if own_parts:
+            parts, prev_slots = lax.optimization_barrier((parts, prev_slots))
         part = parts[:, :, h].reshape(ntm, blocks * rows, width)
-        if own_parts:
-            part, prev_slots = lax.optimization_barrier((part, prev_slots))
         slots = [lax.dynamic_index_in_dim(part, here, axis=0, keepdims=False)]
         for d in range(1, ntm):
             piece = lax.dynamic_index_in_dim(part, (here + d) % ntm, axis=0, keepdims=False)

time: 47.4 us -> 47.9 us (1.011)
  Pallas kernels: 8.6 us -> 9.21 us
    pallas_call x2, Pallas kernels: 8.6 us -> 9.21 us  [spectra(): pl.pallas_call(spectra_kernel, grid_spec=grid_spec, cost_estimate=pl.Cost...]
    slice x1 -> x2, local copies, waits for them, and re-layouts: 1.32 us -> 1.22 us  [local(): part = parts[:, :, h].reshape(ntm, blocks * rows, width)]
  transfers between devices with their start and end apart: 12 -> 12, of which waited for: 4 -> 4; matrix products, arithmetic and copies ran while one was open for 12% -> 12% of each run, Pallas kernels for 18% -> 20%
where the time goes in v10:
time: 47.9 us; the launch traced here: 47.1 us
  starting transfers between devices  16.8 us (35%)
  Pallas kernels  9.21 us (19%)
  waiting for transfers between devices  7.74 us (16%)
  other arithmetic  6.09 us (13%)
  local copies, waits for them, and re-layouts  3.7 us (8%)
  between operations  2.78 us (6%)
  matrix products  0.74 us (2%)
    ppermute x6, starting transfers between devices, local(): lax.ppermute(blk, 'chan', perm=[(i, (i + d) % peers) for i in range(peers)])  9.5 us
    pallas_call x2, Pallas kernels, spectra(): pl.pallas_call(spectra_kernel, grid_spec=grid_spec, cost_estimate=pl.Cost...  9.21 us
    ppermute x6, starting transfers between devices, local(): lax.ppermute(piece, 'tm', perm=[(i, (i + d) % ntm) for i in range(ntm)])  7.33 us
    ppermute x6, waiting for transfers between devices, local(): lax.ppermute(blk, 'chan', perm=[(i, (i + d) % peers) for i in range(peers)])  5.29 us
    ppermute x6, waiting for transfers between devices, local(): lax.ppermute(piece, 'tm', perm=[(i, (i + d) % ntm) for i in range(ntm)])  2.45 us
    another operation x2, other arithmetic, local(): picked_parts.append(jnp.stack(recv))  2.02 us
    another operation x2, other arithmetic, local(): prev_slots = jnp.stack(slots)  1.72 us
    slice x2, local copies, waits for them, and re-layouts, local(): part = parts[:, :, h].reshape(ntm, blocks * rows, width)  1.22 us
  transfers between devices with their start and end apart: 12, of which 4 were waited for; matrix products, arithmetic and copies ran while one was open for 12% of the time, Pallas kernels for 20%

profile of v10, /device:TPU:0, one launch (start us, length us, event | category | flops | bytes accessed | tf_op | source)
XLA Modules:
  0.0 47.1 jit_solution(1458507419365316113)
XLA Ops:
  0.0 0.0 copy-start
  0.0 0.0 copy-start.3
  0.0 0.0 copy-start.2
  0.0 1.2 %slice.50 = bf16[4,2,1,64,512]{4,3,2,1,0:T(8,128)(2,1)S(1)} slice(bf16[4,2,2,64,512]{4,3,2,1,0:T(8,128)(2,1)} %bitcast.74), slice={[0:4], [0:2], [0:1], [0:64], [0:512]} | slice | bytes 1048576 | tf_op jit(solution)/shard_map/slice | solution.py:158
  1.3 2.5 %collective-permute-start.2 = (bf16[128,512]{1,0:T(8,128)(2,1)S(1)}, bf16[128,512]{1,0:T(8,128)(2,1)S(1)}, u32[]{:S(2)}, u32[]{:S(2)}) collective-permute-start(bf16[128,512]{1,0:T(8,128)(2,1)S(1)} %get-tuple-element.14), channel_id=1, source_target_pairs={{0,3},{1,0},{2,1},{3,2},{4,7},{5,4},{6,5},{7,6},{8,11},{9,8},{10,9... | collective-permute-start | bytes 393224 | tf_op jit(solution)/shard_map/ppermute | solution.py:162
  3.7 0.0 collective-permute-start
  3.7 1.1 %collective-permute-start.1 = (bf16[128,512]{1,0:T(8,128)(2,1)S(1)}, bf16[128,512]{1,0:T(8,128)(2,1)S(1)}, u32[]{:S(2)}, u32[]{:S(2)}) collective-permute-start(bf16[128,512]{1,0:T(8,128)(2,1)S(1)} %get-tuple-element.15), channel_id=1, source_target_pairs={{0,2},{1,3},{2,0},{3,1},{4,6},{5,7},{6,4},{7,5},{8,10},{9,11},{10,... | collective-permute-start | bytes 393224 | tf_op jit(solution)/shard_map/ppermute | solution.py:162
  4.8 0.0 copy-done.3
  4.9 0.0 copy-done.2
  4.9 0.7 %constant_dynamic-slice_fusion.5 = (s32[1,1,1,1]{2,3,1,0:T(1,128)}, s32[1,1,1,1]{2,3,1,0:T(1,128)}, s32[1,1,1,1]{2,3,1,0:T(1,128)}, s32[1,1,1,1]{2,3,1,0:T(1,128)}) fusion(s32[1,1,4,1]{2,3,1,0:T(1,128)S(1)} %copy-done.2, s32[]{:T(128)S(6)} %select_n.183, s32[]{:T(128)S(6)} %select_n.194, s32[]{:T(128)S(6)} %select_n.202, s32[]{:T(128)S(6)} %select_n.198), kind=kLoop, calls=%fused_computation.56 | loop fusion | bytes 48 | tf_op jit(solution)/shard_map/jit(dynamic_index_in_dim)/dynamic_slice | solution.py:171
  8.1 0.0 collective-permute-done.2
  8.1 1.4 %collective-permute-done = bf16[128,512]{1,0:T(8,128)(2,1)S(1)} collective-permute-done((bf16[128,512]{1,0:T(8,128)(2,1)S(1)}, bf16[128,512]{1,0:T(8,128)(2,1)S(1)}, u32[]{:S(2)}, u32[]{:S(2)}) %collective-permute-start) | collective-permute-done | bytes 131104 | tf_op jit(solution)/shard_map/ppermute | solution.py:162
  9.5 1.1 %collective-permute-done.1 = bf16[128,512]{1,0:T(8,128)(2,1)S(1)} collective-permute-done((bf16[128,512]{1,0:T(8,128)(2,1)S(1)}, bf16[128,512]{1,0:T(8,128)(2,1)S(1)}, u32[]{:S(2)}, u32[]{:S(2)}) %collective-permute-start.1) | collective-permute-done | bytes 131104 | tf_op jit(solution)/shard_map/ppermute | solution.py:162
  10.6 0.9 %pad_maximum_fusion.1.x_ref = bf16[4,128,512]{2,1,0:T(8,128)(2,1)} fusion(bf16[1,128,512]{2,1,0:T(8,128)(2,1)S(1)} %bitcast.82, bf16[1,128,512]{2,1,0:T(8,128)(2,1)S(1)} %bitcast.84, bf16[1,128,512]{2,1,0:T(8,128)(2,1)S(1)} %bitcast.83, bf16[1,128,512]{2,1,0:T(8,128)(2,1)S(1)} %get-tuple-element.13), kind=kLoop, calls=%fused_computation.30 | loop fusion | flops 786432 | bytes 1048576 | tf_op jit(solution)/shard_map/stack | solution.py:163
  11.4 0.0 copy-done
  11.4 0.1 copy.11
  11.6 0.7 %collective-permute-start.6 = (bf16[128,512]{1,0:T(8,128)(2,1)S(1)}, bf16[128,512]{1,0:T(8,128)(2,1)S(1)}, u32[]{:S(2)}, u32[]{:S(2)}) collective-permute-start(bf16[128,512]{1,0:T(8,128)(2,1)S(1)} %get-tuple-element.12), channel_id=1, source_target_pairs={{0,1},{1,2},{2,3},{3,0},{4,5},{5,6},{6,7},{7,4},{8,9},{9,10},{10,1... | collective-permute-start | bytes 393224 | tf_op jit(solution)/shard_map/ppermute | solution.py:162
  12.4 1.7 %collective-permute-start.7 = (bf16[128,512]{1,0:T(8,128)(2,1)S(1)}, bf16[128,512]{1,0:T(8,128)(2,1)S(1)}, u32[]{:S(2)}, u32[]{:S(2)}) collective-permute-start(bf16[128,512]{1,0:T(8,128)(2,1)S(1)} %get-tuple-element.11), channel_id=1, source_target_pairs={{0,2},{1,3},{2,0},{3,1},{4,6},{5,7},{6,4},{7,5},{8,10},{9,11},{10,... | collective-permute-start | bytes 393224 | tf_op jit(solution)/shard_map/ppermute | solution.py:162
  14.1 1.4 %collective-permute-start.8 = (bf16[128,512]{1,0:T(8,128)(2,1)S(1)}, bf16[128,512]{1,0:T(8,128)(2,1)S(1)}, u32[]{:S(2)}, u32[]{:S(2)}) collective-permute-start(bf16[128,512]{1,0:T(8,128)(2,1)S(1)} %get-tuple-element.10), channel_id=1, source_target_pairs={{0,3},{1,0},{2,1},{3,2},{4,7},{5,4},{6,5},{7,6},{8,11},{9,8},{10,9... | collective-permute-start | bytes 393224 | tf_op jit(solution)/shard_map/ppermute | solution.py:162
  15.4 4.6 %shard_map.91 = bf16[128,1024]{1,0:T(8,128)(2,1)} custom-call(s32[1]{0:T(128)} %bitcast.2.pos_ref, bf16[4,128,512]{2,1,0:T(8,128)(2,1)} %pad_maximum_fusion.1.x_ref, bf16[384,256]{1,0:T(8,128)(2,1)} %constant.142.clone.band_ref, bf16[1024,1024]{1,0:T(8,128)(2,1)} %constant.143.clone.tab_hbm, bf16[512,512]{1,0:T(8,128)(2,1)} %constant.144.clone.grp_hbm), custom_call_target="tpu_custom_call" | custom-call | flops 1073741824 | bytes 2883584 | tf_op jit(solution)/shard_map/pallas_call | solution.py:132
  20.0 1.0 %select_bitcast_fusion.1 = (bf16[1,1,64,1024]{3,2,1,0:T(8,128)(2,1)S(1)}, bf16[64,1024]{1,0:T(8,128)(2,1)S(1)}, bf16[64,1024]{1,0:T(8,128)(2,1)S(1)}, bf16[64,1024]{1,0:T(8,128)(2,1)S(1)}) fusion(pred[]{:T(512)} %bitcast.1, bf16[128,1024]{1,0:T(8,128)(2,1)} %shard_map.91, pred[]{:T(512)} %bitcast.14, pred[]{:T(512)} %bitcast.16, pred[]{:T(512)} %bitcast.12), kind=kLoop, calls=%fused_computation.40 | loop fusion | flops 262144 | bytes 786436 | tf_op jit(solution)/shard_map/stack;stack | solution.py:179
  21.1 1.6 %collective-permute-start.3 = (bf16[64,1024]{1,0:T(8,128)(2,1)S(1)}, bf16[64,1024]{1,0:T(8,128)(2,1)S(1)}, u32[]{:S(2)}, u32[]{:S(2)}) collective-permute-start(bf16[64,1024]{1,0:T(8,128)(2,1)S(1)} %get-tuple-element.20), channel_id=1, source_target_pairs={{0,4},{4,8},{8,12},{12,0},{1,5},{5,9},{9,13},{13,1},{2,6},{6,10},{... | collective-permute-start | bytes 393224 | tf_op jit(solution)/shard_map/ppermute | solution.py:176
  22.7 2.6 %collective-permute-start.4 = (bf16[64,1024]{1,0:T(8,128)(2,1)S(1)}, bf16[64,1024]{1,0:T(8,128)(2,1)S(1)}, u32[]{:S(2)}, u32[]{:S(2)}) collective-permute-start(bf16[64,1024]{1,0:T(8,128)(2,1)S(1)} %get-tuple-element.18), channel_id=1, source_target_pairs={{0,8},{4,12},{8,0},{12,4},{1,9},{5,13},{9,1},{13,5},{2,10},{6,14},... | collective-permute-start | bytes 393224 | tf_op jit(solution)/shard_map/ppermute | solution.py:176
  25.3 0.0 collective-permute-done.6
  25.3 1.3 %collective-permute-start.5 = (bf16[64,1024]{1,0:T(8,128)(2,1)S(1)}, bf16[64,1024]{1,0:T(8,128)(2,1)S(1)}, u32[]{:S(2)}, u32[]{:S(2)}) collective-permute-start(bf16[64,1024]{1,0:T(8,128)(2,1)S(1)} %get-tuple-element.19), channel_id=1, source_target_pairs={{0,12},{4,0},{8,4},{12,8},{1,13},{5,1},{9,5},{13,9},{2,14},{6,2},{... | collective-permute-start | bytes 393224 | tf_op jit(solution)/shard_map/ppermute | solution.py:176
  26.6 0.0 collective-permute-done.7
  26.6 0.0 collective-permute-done.8
  26.6 0.9 %pad_maximum_fusion.2.x_ref = bf16[4,128,512]{2,1,0:T(8,128)(2,1)} fusion(bf16[1,128,512]{2,1,0:T(8,128)(2,1)S(1)} %bitcast.87, bf16[1,128,512]{2,1,0:T(8,128)(2,1)S(1)} %bitcast.86, bf16[1,128,512]{2,1,0:T(8,128)(2,1)S(1)} %bitcast.85, bf16[1,128,512]{2,1,0:T(8,128)(2,1)S(1)} %get-tuple-element.9), kind=kLoop, calls=%fused_computation.31 | loop fusion | flops 786432 | bytes 1048576 | tf_op jit(solution)/shard_map/stack | solution.py:163
  27.5 0.0 copy-start.1
  27.5 4.6 %shard_map.92 = bf16[128,1024]{1,0:T(8,128)(2,1)} custom-call(s32[1]{0:T(128)} %bitcast.2.pos_ref, bf16[4,128,512]{2,1,0:T(8,128)(2,1)} %pad_maximum_fusion.2.x_ref, bf16[384,256]{1,0:T(8,128)(2,1)} %constant.142.clone.band_ref, bf16[1024,1024]{1,0:T(8,128)(2,1)} %constant.143.clone.tab_hbm, bf16[512,512]{1,0:T(8,128)(2,1)} %constant.144.clone.grp_hbm), custom_call_target="tpu_custom_call" | custom-call | flops 1073741824 | bytes 2883584 | tf_op jit(solution)/shard_map/pallas_call | solution.py:132
  32.1 1.0 %select_bitcast_fusion = (bf16[1,1,64,1024]{3,2,1,0:T(8,128)(2,1)S(1)}, bf16[64,1024]{1,0:T(8,128)(2,1)S(1)}, bf16[64,1024]{1,0:T(8,128)(2,1)S(1)}, bf16[64,1024]{1,0:T(8,128)(2,1)S(1)}) fusion(pred[]{:T(512)} %bitcast.1, bf16[128,1024]{1,0:T(8,128)(2,1)} %shard_map.92, pred[]{:T(512)} %bitcast.14, pred[]{:T(512)} %bitcast.16, pred[]{:T(512)} %bitcast.12), kind=kLoop, calls=%fused_computation.36 | loop fusion | flops 262144 | bytes 786436 | tf_op jit(solution)/shard_map/stack;stack | solution.py:179
  33.1 0.7 %collective-permute-start.9 = (bf16[64,1024]{1,0:T(8,128)(2,1)S(1)}, bf16[64,1024]{1,0:T(8,128)(2,1)S(1)}, u32[]{:S(2)}, u32[]{:S(2)}) collective-permute-start(bf16[64,1024]{1,0:T(8,128)(2,1)S(1)} %get-tuple-element.24), channel_id=1, source_target_pairs={{0,4},{4,8},{8,12},{12,0},{1,5},{5,9},{9,13},{13,1},{2,6},{6,10},{... | collective-permute-start | bytes 393224 | tf_op jit(solution)/shard_map/ppermute | solution.py:176
  33.9 0.3 collective-permute-start.10
  34.2 0.0 copy-done.1
  34.2 1.0 %fusion.20 = (bf16[2,128,512]{2,1,0:T(8,128)(2,1)S(1)}, bf16[2,128,512]{2,1,0:T(8,128)(2,1)S(1)}) fusion(bf16[2,64,1024]{2,1,0:T(8,128)(2,1)S(1)} %bitcast.76, bf16[2,64,1024]{2,1,0:T(8,128)(2,1)} %bitcast.78), kind=kLoop, calls=%fused_computation.33 | loop fusion | flops 1179648 | bytes 1048576 | tf_op jit(solution)/shard_map/concatenate | solution.py:180
  35.2 0.0 collective-permute-done.3
  35.2 2.9 %collective-permute-start.11 = (bf16[64,1024]{1,0:T(8,128)(2,1)S(1)}, bf16[64,1024]{1,0:T(8,128)(2,1)S(1)}, u32[]{:S(2)}, u32[]{:S(2)}) collective-permute-start(bf16[64,1024]{1,0:T(8,128)(2,1)S(1)} %get-tuple-element.23), channel_id=1, source_target_pairs={{0,12},{4,0},{8,4},{12,8},{1,13},{5,1},{9,5},{13,9},{2,14},{6,2},{... | collective-permute-start | bytes 393224 | tf_op jit(solution)/shard_map/ppermute | solution.py:176
  38.1 1.0 %fusion.19 = (bf16[2,1,128,1024]{3,2,1,0:T(8,128)(2,1)S(1)}, bf16[2,1,128,1024]{3,2,1,0:T(8,128)(2,1)S(1)}) fusion(bf16[2,64,1024]{2,1,0:T(8,128)(2,1)} %bitcast.79, bf16[2,64,1024]{2,1,0:T(8,128)(2,1)S(1)} %bitcast.77, bf16[2,128,512]{2,1,0:T(8,128)(2,1)S(1)} %get-tuple-element.8, bf16[2,128,512]{2,1,0:T(8,128)(2,1)S(1)} %get-tuple-element.7), kind=kLoop, calls=%fused_computation.29 | loop fusion | flops 2097152 | bytes 2097152 | tf_op jit(solution)/shard_map/stack | solution.py:183
  39.2 0.0 collective-permute-done.4
  39.2 0.0 collective-permute-done.5
  39.2 2.3 %collective-permute-done.9 = bf16[64,1024]{1,0:T(8,128)(2,1)S(1)} collective-permute-done((bf16[64,1024]{1,0:T(8,128)(2,1)S(1)}, bf16[64,1024]{1,0:T(8,128)(2,1)S(1)}, u32[]{:S(2)}, u32[]{:S(2)}) %collective-permute-start.9) | collective-permute-done | bytes 131104 | tf_op jit(solution)/shard_map/ppermute | solution.py:176
  41.5 3.0 %collective-permute-done.10 = bf16[64,1024]{1,0:T(8,128)(2,1)S(1)} collective-permute-done((bf16[64,1024]{1,0:T(8,128)(2,1)S(1)}, bf16[64,1024]{1,0:T(8,128)(2,1)S(1)}, u32[]{:S(2)}, u32[]{:S(2)}) %collective-permute-start.10) | collective-permute-done | bytes 131104 | tf_op jit(solution)/shard_map/ppermute | solution.py:176
  44.5 0.0 collective-permute-done.11
  44.5 0.7 %convolution_bitcast_fusion = f32[4,2,2,128,128]{3,4,2,1,0:T(8,128)S(1)} fusion(bf16[1,1,64,1024]{3,2,1,0:T(8,128)(2,1)S(1)} %bitcast.93, bf16[1,1,64,1024]{3,2,1,0:T(8,128)(2,1)S(1)} %bitcast.92, bf16[1,1,64,1024]{3,2,1,0:T(8,128)(2,1)S(1)} %bitcast.91, bf16[1,1,64,1024]{3,2,1,0:T(8,128)(2,1)S(1)} %get-tuple-element.21, ...), kind=kOutput, calls=%fused_computation.1 | convolution fusion | flops 547356672 | bytes 3145728 | tf_op jit(solution)/shard_map/lrif,dkjf->dklrij/dot_general | solution.py:184
  45.2 0.6 %gather_fusion = f32[4,2,2,128,128]{3,4,2,1,0:T(8,128)S(1)} fusion(f32[4,2,2,128,128]{3,4,2,1,0:T(8,128)S(1)} %convolution_bitcast_fusion, s32[1024]{0:T(1024)S(1)} %pad_clamp_fusion), kind=kCustom, calls=%fused_computation | custom fusion | bytes 2097168 | tf_op jit(solution)/shard_map/jit(_take)/gather | solution.py:186
  45.8 0.2 fusion.18
  46.1 1.0 %copy.13 = bf16[1,1,4,1,2,2,128,128]{7,6,5,4,3,2,1,0:T(8,128)(2,1)} copy(bf16[1,1,4,1,2,2,128,128]{6,7,5,4,2,3,1,0:T(8,128)(2,1)S(1)} %fusion.18) | data formatting | bytes 1048576 | tf_op jit(solution)/shard_map/convert_element_type | solution.py:190
  (7 shorter events, 0.2 us)
Async XLA Ops:
  0.0 11.4 %copy-start = (bf16[1024,512]{1,0:T(8,128)(2,1)S(1)}, bf16[1024,512]{1,0:T(8,128)(2,1)}, u32[]{:S(2)}) copy-start(bf16[1024,512]{1,0:T(8,128)(2,1)} %param.9) | copy-start | bytes 3145732
  0.0 4.8 %copy-start.3 = (s32[1,1,4]{2,1,0:T(1,128)S(1)}, s32[1,1,4]{2,1,0:T(1,128)}, u32[]{:S(2)}) copy-start(s32[1,1,4]{2,1,0:T(1,128)} %param.11) | copy-start | bytes 52
  0.0 4.9 %copy-start.2 = (s32[1,1,4,1]{2,3,1,0:T(1,128)S(1)}, s32[1,1,4,1]{2,3,1,0:T(1,128)}, u32[]{:S(2)}) copy-start(s32[1,1,4,1]{2,3,1,0:T(1,128)} %param.10) | copy-start | bytes 52
  1.3 6.9 %collective-permute-start.2 = (bf16[128,512]{1,0:T(8,128)(2,1)S(1)}, bf16[128,512]{1,0:T(8,128)(2,1)S(1)}, u32[]{:S(2)}, u32[]{:S(2)}) collective-permute-start(bf16[128,512]{1,0:T(8,128)(2,1)S(1)} %get-tuple-element.14), channel_id=1, source_target_pairs={{0,3},{1,0},{2,1},{3,2},{4,7},{5,4},{6,5},{7,6},{8,11},{9,8},{10,9... | collective-permute-start | bytes 393224 | tf_op jit(solution)/shard_map/ppermute | solution.py:162
  3.7 5.8 %collective-permute-start = (bf16[128,512]{1,0:T(8,128)(2,1)S(1)}, bf16[128,512]{1,0:T(8,128)(2,1)S(1)}, u32[]{:S(2)}, u32[]{:S(2)}) collective-permute-start(bf16[128,512]{1,0:T(8,128)(2,1)S(1)} %get-tuple-element.16), channel_id=1, source_target_pairs={{0,1},{1,2},{2,3},{3,0},{4,5},{5,6},{6,7},{7,4},{8,9},{9,10},{10,1... | collective-permute-start | bytes 393224 | tf_op jit(solution)/shard_map/ppermute | solution.py:162
  3.7 6.8 %collective-permute-start.1 = (bf16[128,512]{1,0:T(8,128)(2,1)S(1)}, bf16[128,512]{1,0:T(8,128)(2,1)S(1)}, u32[]{:S(2)}, u32[]{:S(2)}) collective-permute-start(bf16[128,512]{1,0:T(8,128)(2,1)S(1)} %get-tuple-element.15), channel_id=1, source_target_pairs={{0,2},{1,3},{2,0},{3,1},{4,6},{5,7},{6,4},{7,5},{8,10},{9,11},{10,... | collective-permute-start | bytes 393224 | tf_op jit(solution)/shard_map/ppermute | solution.py:162
  11.6 13.6 %collective-permute-start.6 = (bf16[128,512]{1,0:T(8,128)(2,1)S(1)}, bf16[128,512]{1,0:T(8,128)(2,1)S(1)}, u32[]{:S(2)}, u32[]{:S(2)}) collective-permute-start(bf16[128,512]{1,0:T(8,128)(2,1)S(1)} %get-tuple-element.12), channel_id=1, source_target_pairs={{0,1},{1,2},{2,3},{3,0},{4,5},{5,6},{6,7},{7,4},{8,9},{9,10},{10,1... | collective-permute-start | bytes 393224 | tf_op jit(solution)/shard_map/ppermute | solution.py:162
  12.4 14.2 %collective-permute-start.7 = (bf16[128,512]{1,0:T(8,128)(2,1)S(1)}, bf16[128,512]{1,0:T(8,128)(2,1)S(1)}, u32[]{:S(2)}, u32[]{:S(2)}) collective-permute-start(bf16[128,512]{1,0:T(8,128)(2,1)S(1)} %get-tuple-element.11), channel_id=1, source_target_pairs={{0,2},{1,3},{2,0},{3,1},{4,6},{5,7},{6,4},{7,5},{8,10},{9,11},{10,... | collective-permute-start | bytes 393224 | tf_op jit(solution)/shard_map/ppermute | solution.py:162
  14.1 12.5 %collective-permute-start.8 = (bf16[128,512]{1,0:T(8,128)(2,1)S(1)}, bf16[128,512]{1,0:T(8,128)(2,1)S(1)}, u32[]{:S(2)}, u32[]{:S(2)}) collective-permute-start(bf16[128,512]{1,0:T(8,128)(2,1)S(1)} %get-tuple-element.10), channel_id=1, source_target_pairs={{0,3},{1,0},{2,1},{3,2},{4,7},{5,4},{6,5},{7,6},{8,11},{9,8},{10,9... | collective-permute-start | bytes 393224 | tf_op jit(solution)/shard_map/ppermute | solution.py:162
  21.1 14.2 %collective-permute-start.3 = (bf16[64,1024]{1,0:T(8,128)(2,1)S(1)}, bf16[64,1024]{1,0:T(8,128)(2,1)S(1)}, u32[]{:S(2)}, u32[]{:S(2)}) collective-permute-start(bf16[64,1024]{1,0:T(8,128)(2,1)S(1)} %get-tuple-element.20), channel_id=1, source_target_pairs={{0,4},{4,8},{8,12},{12,0},{1,5},{5,9},{9,13},{13,1},{2,6},{6,10},{... | collective-permute-start | bytes 393224 | tf_op jit(solution)/shard_map/ppermute | solution.py:176
  22.7 16.5 %collective-permute-start.4 = (bf16[64,1024]{1,0:T(8,128)(2,1)S(1)}, bf16[64,1024]{1,0:T(8,128)(2,1)S(1)}, u32[]{:S(2)}, u32[]{:S(2)}) collective-permute-start(bf16[64,1024]{1,0:T(8,128)(2,1)S(1)} %get-tuple-element.18), channel_id=1, source_target_pairs={{0,8},{4,12},{8,0},{12,4},{1,9},{5,13},{9,1},{13,5},{2,10},{6,14},... | collective-permute-start | bytes 393224 | tf_op jit(solution)/shard_map/ppermute | solution.py:176
  25.3 13.9 %collective-permute-start.5 = (bf16[64,1024]{1,0:T(8,128)(2,1)S(1)}, bf16[64,1024]{1,0:T(8,128)(2,1)S(1)}, u32[]{:S(2)}, u32[]{:S(2)}) collective-permute-start(bf16[64,1024]{1,0:T(8,128)(2,1)S(1)} %get-tuple-element.19), channel_id=1, source_target_pairs={{0,12},{4,0},{8,4},{12,8},{1,13},{5,1},{9,5},{13,9},{2,14},{6,2},{... | collective-permute-start | bytes 393224 | tf_op jit(solution)/shard_map/ppermute | solution.py:176
  27.5 6.7 %copy-start.1 = (bf16[128,1024]{1,0:T(8,128)(2,1)S(1)}, bf16[128,1024]{1,0:T(8,128)(2,1)}, u32[]{:S(2)}) copy-start(bf16[128,1024]{1,0:T(8,128)(2,1)} %shard_map.91) | copy-start | bytes 786436
  33.1 8.4 %collective-permute-start.9 = (bf16[64,1024]{1,0:T(8,128)(2,1)S(1)}, bf16[64,1024]{1,0:T(8,128)(2,1)S(1)}, u32[]{:S(2)}, u32[]{:S(2)}) collective-permute-start(bf16[64,1024]{1,0:T(8,128)(2,1)S(1)} %get-tuple-element.24), channel_id=1, source_target_pairs={{0,4},{4,8},{8,12},{12,0},{1,5},{5,9},{9,13},{13,1},{2,6},{6,10},{... | collective-permute-start | bytes 393224 | tf_op jit(solution)/shard_map/ppermute | solution.py:176
  33.9 10.6 %collective-permute-start.10 = (bf16[64,1024]{1,0:T(8,128)(2,1)S(1)}, bf16[64,1024]{1,0:T(8,128)(2,1)S(1)}, u32[]{:S(2)}, u32[]{:S(2)}) collective-permute-start(bf16[64,1024]{1,0:T(8,128)(2,1)S(1)} %get-tuple-element.22), channel_id=1, source_target_pairs={{0,8},{4,12},{8,0},{12,4},{1,9},{5,13},{9,1},{13,5},{2,10},{6,14},... | collective-permute-start | bytes 393224 | tf_op jit(solution)/shard_map/ppermute | solution.py:176
  35.2 9.2 %collective-permute-start.11 = (bf16[64,1024]{1,0:T(8,128)(2,1)S(1)}, bf16[64,1024]{1,0:T(8,128)(2,1)S(1)}, u32[]{:S(2)}, u32[]{:S(2)}) collective-permute-start(bf16[64,1024]{1,0:T(8,128)(2,1)S(1)} %get-tuple-element.23), channel_id=1, source_target_pairs={{0,12},{4,0},{8,4},{12,8},{1,13},{5,1},{9,5},{13,9},{2,14},{6,2},{... | collective-permute-start | bytes 393224 | tf_op jit(solution)/shard_map/ppermute | solution.py:176

commit v11 on v7

--- a/solution.py
+++ b/solution.py
@@ -1,3 +1,4 @@
+import functools
 import math
 
 import jax
@@ -66,7 +67,8 @@
     return ((g[:, None] == g[None, :]).astype(np.float32) / SUBW).astype(BF16)
 
 
-def spectra_kernel(pos_ref, x_ref, band_ref, tab_ref, grp_ref, o_ref, filt_ref):
+def spectra_kernel(cap, pos_ref, mine_ref, ids_ref, x_ref, band_ref, tab_ref, grp_ref, o_ref, *rest):
+    send_refs, filt_ref = rest[:-1], rest[-1]
     nslot, _, width = x_ref.shape
     ntile = NT // TILE
     pos = pos_ref[0]
@@ -97,33 +99,44 @@
     level = 1.0 / jnp.sqrt(mean + 1e-06)
     o_ref[:, :NBAND] = (re * level).astype(jnp.bfloat16)
     o_ref[:, NBAND:] = (im * level).astype(jnp.bfloat16)
+    npeer = len(send_refs) // cap
+    rpb = send_refs[0].shape[0]
+    mine = mine_ref[0]
+    for e in range(npeer * cap):
+        d, k = divmod(e, cap)
+        owner = (mine + d) % npeer
+        start = pl.multiple_of(ids_ref[owner * cap + k] * rpb, rpb)
+        send_refs[e][...] = o_ref[pl.ds(start, rpb), :]
 
 
-def spectra(pos, rows3):
+def spectra(pos, mine, ids, rows3, peers, cap, blocks):
     ntm, nrows, width = rows3.shape
+    rpb = nrows // blocks
     band = jnp.asarray(band_matrix())
     tab = jnp.asarray(dft_top())
     grp = jnp.asarray(group_matrix())
     grid_spec = pltpu.PrefetchScalarGridSpec(
-        num_scalar_prefetch=1,
-        grid=(nrows // BLOCK,),
+        num_scalar_prefetch=3,
+        grid=(1,),
         in_specs=[
-            pl.BlockSpec((ntm, BLOCK, width), lambda r, p: (0, r, 0)),
-            pl.BlockSpec(band.shape, lambda r, p: (0, 0)),
-            pl.BlockSpec(tab.shape, lambda r, p: (0, 0)),
-            pl.BlockSpec(grp.shape, lambda r, p: (0, 0)),
+            pl.BlockSpec((ntm, nrows, width), lambda r, p, m, i: (0, 0, 0)),
+            pl.BlockSpec(band.shape, lambda r, p, m, i: (0, 0)),
+            pl.BlockSpec(tab.shape, lambda r, p, m, i: (0, 0)),
+            pl.BlockSpec(grp.shape, lambda r, p, m, i: (0, 0)),
         ],
-        out_specs=pl.BlockSpec((BLOCK, 2 * NBAND), lambda r, p: (r, 0)),
-        scratch_shapes=[pltpu.VMEM((BLOCK, NT), jnp.bfloat16)],
+        out_specs=[pl.BlockSpec((nrows, 2 * NBAND), lambda r, p, m, i: (0, 0))]
+        + [pl.BlockSpec((rpb, 2 * NBAND), lambda r, p, m, i: (0, 0))] * (peers * cap),
+        scratch_shapes=[pltpu.VMEM((nrows, NT), jnp.bfloat16)],
     )
     flops = 2 * nrows * (3 * TILE * 2 * TILE * (NT // TILE) + NT * 2 * NBAND + 2 * NBAND * NBAND)
     nbytes = rows3.size * 2 + tab.size * 2 + nrows * 2 * NBAND * 2
     return pl.pallas_call(
-        spectra_kernel,
+        functools.partial(spectra_kernel, cap),
         grid_spec=grid_spec,
         cost_estimate=pl.CostEstimate(flops=flops, transcendentals=nrows * NBAND, bytes_accessed=nbytes),
-        out_shape=jax.ShapeDtypeStruct((nrows, 2 * NBAND), jnp.bfloat16),
-    )(pos, rows3, band, tab, grp)
+        out_shape=[jax.ShapeDtypeStruct((nrows, 2 * NBAND), jnp.bfloat16)]
+        + [jax.ShapeDtypeStruct((rpb, 2 * NBAND), jnp.bfloat16)] * (peers * cap),
+    )(pos, mine, ids, rows3, band, tab, grp)
 
 
 def local(raw, send_blocks, pair_count):
@@ -138,7 +151,8 @@
     peers = lax.axis_size("chan")
     mine = lax.axis_index("chan")
     cap = send_blocks.shape[3]
-    ids = send_blocks[0, 0]
+    ids_flat = send_blocks[0, 0].reshape(peers * cap)
+    chan_pos = mine.astype(jnp.int32).reshape(1)
     own_parts = []
     picked_parts = []
     for h in range(NSPLIT):
@@ -150,17 +164,13 @@
             piece = lax.dynamic_index_in_dim(part, (here + d) % ntm, axis=0, keepdims=False)
             slots.append(lax.ppermute(piece, "tm", perm=[(i, (i + d) % ntm) for i in range(ntm)]))
         prev_slots = jnp.stack(slots)
-        whitened = spectra(pos, prev_slots).reshape(blocks, rows, 2 * NBAND)
-        own_parts.append(whitened)
+        whitened, *outgoing = spectra(pos, chan_pos, ids_flat, prev_slots, peers, cap, blocks)
+        own_parts.append(whitened.reshape(blocks, rows, 2 * NBAND))
         recv = []
         for d in range(peers):
-            dest = (mine + d) % peers
             row = []
             for k in range(cap):
-                want = lax.dynamic_index_in_dim(ids[:, k], dest, keepdims=False)
-                blk = whitened[0]
-                for b in range(1, blocks):
-                    blk = jnp.where(want == b, whitened[b], blk)
+                blk = outgoing[d * cap + k]
                 if d:
                     blk = lax.ppermute(blk, "chan", perm=[(i, (i + d) % peers) for i in range(peers)])
                 row.append(blk)

time: 47.4 us -> 49.4 us (1.042)
  waiting for transfers between devices: 8.07 us -> 17 us
  starting transfers between devices: 16.8 us -> 13.8 us
  between operations: 2.75 us -> 0.13 us
  other arithmetic: 6.08 us -> 4.08 us
  Pallas kernels: 8.6 us -> 10.4 us
  local copies, waits for them, and re-layouts: 3.7 us -> 3.02 us
    ppermute x6, waiting for transfers between devices: 5.61 us -> 10.3 us  [local(): lax.ppermute(blk, 'chan', perm=[(i, (i + d) % peers) for i in range(peers)])]
    ppermute x6, waiting for transfers between devices: 2.45 us -> 6.71 us  [local(): lax.ppermute(piece, 'tm', perm=[(i, (i + d) % ntm) for i in range(ntm)])]
    ppermute x6, starting transfers between devices: 7.29 us -> 5.16 us  [local(): lax.ppermute(piece, 'tm', perm=[(i, (i + d) % ntm) for i in range(ntm)])]
    another operation x2 -> x0, other arithmetic: 2.01 us -> none  [local(): picked_parts.append(jnp.stack(recv))]
    pallas_call x2, Pallas kernels: 8.6 us -> 10.4 us  [spectra(): pl.pallas_call(functools.partial(spectra_kernel, cap), grid_spec=grid_spe...]
    ppermute x6, starting transfers between devices: 9.49 us -> 8.64 us  [local(): lax.ppermute(blk, 'chan', perm=[(i, (i + d) % peers) for i in range(peers)])]
    dynamic_slice x1 -> x0, local copies, waits for them, and re-layouts: 0.66 us -> none  [local(): want = lax.dynamic_index_in_dim(ids[:, k], dest, keepdims=False)]
  transfers between devices with their start and end apart: 12 -> 12, of which waited for: 4 -> 4; matrix products, arithmetic and copies ran while one was open for 12% -> 6% of each run, Pallas kernels for 18% -> 21%
where the time goes in v11:
time: 49.4 us; the launch traced here: 49.2 us
  waiting for transfers between devices  17 us (34%)
  starting transfers between devices  13.8 us (28%)
  Pallas kernels  10.4 us (21%)
  other arithmetic  4.08 us (8%)
  local copies, waits for them, and re-layouts  3.02 us (6%)
  matrix products  0.76 us (2%)
    pallas_call x2, Pallas kernels, spectra(): pl.pallas_call(functools.partial(spectra_kernel, cap), grid_spec=grid_spe...  10.4 us
    ppermute x6, waiting for transfers between devices, local(): lax.ppermute(blk, 'chan', perm=[(i, (i + d) % peers) for i in range(peers)])  10.3 us
    ppermute x6, starting transfers between devices, local(): lax.ppermute(blk, 'chan', perm=[(i, (i + d) % peers) for i in range(peers)])  8.64 us
    ppermute x6, waiting for transfers between devices, local(): lax.ppermute(piece, 'tm', perm=[(i, (i + d) % ntm) for i in range(ntm)])  6.71 us
    ppermute x6, starting transfers between devices, local(): lax.ppermute(piece, 'tm', perm=[(i, (i + d) % ntm) for i in range(ntm)])  5.16 us
    another operation x2, other arithmetic, local(): prev_slots = jnp.stack(slots)  1.72 us
    slice x1, local copies, waits for them, and re-layouts, local(): part = parts[:, :, h].reshape(ntm, blocks * rows, width)  1.3 us
    another operation x1, other arithmetic, local(): paired = jnp.stack([whitened, turned], axis=1)  1.05 us
  transfers between devices with their start and end apart: 12, of which 4 were waited for; matrix products, arithmetic and copies ran while one was open for 6% of the time, Pallas kernels for 21%

profile of v11, /device:TPU:0, one launch (start us, length us, event | category | flops | bytes accessed | tf_op | source)
XLA Modules:
  0.0 49.2 jit_solution(11300406558243182875)
XLA Ops:
  0.0 0.0 copy-start.1
  0.0 1.3 %fusion.27 = (bf16[4,2,1,64,512]{4,3,2,1,0:T(8,128)(2,1)S(1)}, bf16[4,2,1,64,512]{4,3,2,1,0:T(8,128)(2,1)S(1)}) fusion(bf16[4,2,2,64,512]{4,3,2,1,0:T(8,128)(2,1)} %bitcast.74), kind=kLoop, calls=%fused_computation.59 | loop fusion | bytes 2097152 | tf_op jit(solution)/shard_map/slice | solution.py:159
  1.4 2.4 %collective-permute-start.2 = (bf16[128,512]{1,0:T(8,128)(2,1)S(1)}, bf16[128,512]{1,0:T(8,128)(2,1)S(1)}, u32[]{:S(2)}, u32[]{:S(2)}) collective-permute-start(bf16[128,512]{1,0:T(8,128)(2,1)S(1)} %get-tuple-element.36), channel_id=1, source_target_pairs={{0,3},{1,0},{2,1},{3,2},{4,7},{5,4},{6,5},{7,6},{8,11},{9,8},{10,9... | collective-permute-start | bytes 393224 | tf_op jit(solution)/shard_map/ppermute | solution.py:165
  3.8 0.6 %collective-permute-start.1 = (bf16[128,512]{1,0:T(8,128)(2,1)S(1)}, bf16[128,512]{1,0:T(8,128)(2,1)S(1)}, u32[]{:S(2)}, u32[]{:S(2)}) collective-permute-start(bf16[128,512]{1,0:T(8,128)(2,1)S(1)} %get-tuple-element.37), channel_id=1, source_target_pairs={{0,2},{1,3},{2,0},{3,1},{4,6},{5,7},{6,4},{7,5},{8,10},{9,11},{10,... | collective-permute-start | bytes 393224 | tf_op jit(solution)/shard_map/ppermute | solution.py:165
  4.5 0.2 collective-permute-start
  4.6 0.0 copy-done.1
  4.7 2.9 %collective-permute-done.2 = bf16[128,512]{1,0:T(8,128)(2,1)S(1)} collective-permute-done((bf16[128,512]{1,0:T(8,128)(2,1)S(1)}, bf16[128,512]{1,0:T(8,128)(2,1)S(1)}, u32[]{:S(2)}, u32[]{:S(2)}) %collective-permute-start.2) | collective-permute-done | bytes 131104 | tf_op jit(solution)/shard_map/ppermute | solution.py:165
  7.6 3.8 %collective-permute-done.1 = bf16[128,512]{1,0:T(8,128)(2,1)S(1)} collective-permute-done((bf16[128,512]{1,0:T(8,128)(2,1)S(1)}, bf16[128,512]{1,0:T(8,128)(2,1)S(1)}, u32[]{:S(2)}, u32[]{:S(2)}) %collective-permute-start.1) | collective-permute-done | bytes 131104 | tf_op jit(solution)/shard_map/ppermute | solution.py:165
  11.4 0.0 collective-permute-done
  11.4 0.9 %pad_maximum_fusion.1.x_ref = bf16[4,128,512]{2,1,0:T(8,128)(2,1)} fusion(bf16[1,128,512]{2,1,0:T(8,128)(2,1)S(1)} %bitcast.82, bf16[1,128,512]{2,1,0:T(8,128)(2,1)S(1)} %bitcast.83, bf16[1,128,512]{2,1,0:T(8,128)(2,1)S(1)} %bitcast.84, bf16[1,128,512]{2,1,0:T(8,128)(2,1)S(1)} %get-tuple-element.35), kind=kLoop, calls=%fused_computation.30 | loop fusion | flops 786432 | bytes 1048576 | tf_op jit(solution)/shard_map/stack | solution.py:166
  12.3 0.1 collective-permute-start.8
  12.3 1.7 %collective-permute-start.7 = (bf16[128,512]{1,0:T(8,128)(2,1)S(1)}, bf16[128,512]{1,0:T(8,128)(2,1)S(1)}, u32[]{:S(2)}, u32[]{:S(2)}) collective-permute-start(bf16[128,512]{1,0:T(8,128)(2,1)S(1)} %get-tuple-element.33), channel_id=1, source_target_pairs={{0,2},{1,3},{2,0},{3,1},{4,6},{5,7},{6,4},{7,5},{8,10},{9,11},{10,... | collective-permute-start | bytes 393224 | tf_op jit(solution)/shard_map/ppermute | solution.py:165
  14.0 0.2 collective-permute-start.6
  14.2 5.1 %shard_map.91 = (bf16[128,1024]{1,0:T(8,128)(2,1)}, bf16[64,1024]{1,0:T(8,128)(2,1)}, bf16[64,1024]{1,0:T(8,128)(2,1)}, bf16[64,1024]{1,0:T(8,128)(2,1)}, bf16[64,1024]{1,0:T(8,128)(2,1)}) custom-call(s32[1]{0:T(128)} %bitcast.1.pos_ref, s32[1]{0:T(128)} %bitcast.2.mine_ref, s32[4]{0:T(128)} %bitcast.91, bf16[4,128,512]{2,1,0:T(8,128)(2,1)} %pad_maximum_fusion.1.x_ref, ...), custom_call_target="tpu_custom_call" | custom-call | flops 1073741824 | bytes 2883584 | tf_op jit(solution)/shard_map/pallas_call | solution.py:133
  19.3 3.6 %collective-permute-start.5 = (bf16[64,1024]{1,0:T(8,128)(2,1)}, bf16[64,1024]{1,0:T(8,128)(2,1)S(1)}, u32[]{:S(2)}, u32[]{:S(2)}) collective-permute-start(bf16[64,1024]{1,0:T(8,128)(2,1)} %get-tuple-element.19), channel_id=1, source_target_pairs={{0,12},{4,0},{8,4},{12,8},{1,13},{5,1},{9,5},{13,9},{2,14},{6,2},{... | collective-permute-start | bytes 393224 | tf_op jit(solution)/shard_map/ppermute | solution.py:175
  22.9 0.0 collective-permute-start.4
  22.9 0.0 collective-permute-done.8
  22.9 1.0 %collective-permute-start.3 = (bf16[64,1024]{1,0:T(8,128)(2,1)}, bf16[64,1024]{1,0:T(8,128)(2,1)S(1)}, u32[]{:S(2)}, u32[]{:S(2)}) collective-permute-start(bf16[64,1024]{1,0:T(8,128)(2,1)} %get-tuple-element.17), channel_id=1, source_target_pairs={{0,4},{4,8},{8,12},{12,0},{1,5},{5,9},{9,13},{13,1},{2,6},{6,10},{... | collective-permute-start | bytes 393224 | tf_op jit(solution)/shard_map/ppermute | solution.py:175
  23.9 0.0 collective-permute-done.7
  24.0 0.0 collective-permute-done.6
  24.0 0.9 %pad_maximum_fusion.2.x_ref = bf16[4,128,512]{2,1,0:T(8,128)(2,1)} fusion(bf16[1,128,512]{2,1,0:T(8,128)(2,1)S(1)} %bitcast.79, bf16[1,128,512]{2,1,0:T(8,128)(2,1)S(1)} %bitcast.80, bf16[1,128,512]{2,1,0:T(8,128)(2,1)S(1)} %bitcast.81, bf16[1,128,512]{2,1,0:T(8,128)(2,1)S(1)} %get-tuple-element.31), kind=kLoop, calls=%fused_computation.31 | loop fusion | flops 786432 | bytes 1048576 | tf_op jit(solution)/shard_map/stack | solution.py:166
  24.8 0.0 copy-start
  24.8 5.3 %shard_map.92 = (bf16[128,1024]{1,0:T(8,128)(2,1)}, bf16[64,1024]{1,0:T(8,128)(2,1)}, bf16[64,1024]{1,0:T(8,128)(2,1)}, bf16[64,1024]{1,0:T(8,128)(2,1)}, bf16[64,1024]{1,0:T(8,128)(2,1)}) custom-call(s32[1]{0:T(128)} %bitcast.1.pos_ref, s32[1]{0:T(128)} %bitcast.2.mine_ref, s32[4]{0:T(128)} %bitcast.92, bf16[4,128,512]{2,1,0:T(8,128)(2,1)} %pad_maximum_fusion.2.x_ref, ...), custom_call_target="tpu_custom_call" | custom-call | flops 1073741824 | bytes 2883584 | tf_op jit(solution)/shard_map/pallas_call | solution.py:133
  30.1 0.0 copy-start.2
  30.1 0.0 copy-start.3
  30.1 2.8 %collective-permute-start.11 = (bf16[64,1024]{1,0:T(8,128)(2,1)}, bf16[64,1024]{1,0:T(8,128)(2,1)S(1)}, u32[]{:S(2)}, u32[]{:S(2)}) collective-permute-start(bf16[64,1024]{1,0:T(8,128)(2,1)} %get-tuple-element.24), channel_id=1, source_target_pairs={{0,12},{4,0},{8,4},{12,8},{1,13},{5,1},{9,5},{13,9},{2,14},{6,2},{... | collective-permute-start | bytes 393224 | tf_op jit(solution)/shard_map/ppermute | solution.py:175
  32.9 1.1 %collective-permute-start.10 = (bf16[64,1024]{1,0:T(8,128)(2,1)}, bf16[64,1024]{1,0:T(8,128)(2,1)S(1)}, u32[]{:S(2)}, u32[]{:S(2)}) collective-permute-start(bf16[64,1024]{1,0:T(8,128)(2,1)} %get-tuple-element.23), channel_id=1, source_target_pairs={{0,8},{4,12},{8,0},{12,4},{1,9},{5,13},{9,1},{13,5},{2,10},{6,14},... | collective-permute-start | bytes 393224 | tf_op jit(solution)/shard_map/ppermute | solution.py:175
  34.1 0.0 copy-done
  34.1 1.0 %fusion.20 = (bf16[2,128,512]{2,1,0:T(8,128)(2,1)S(1)}, bf16[2,128,512]{2,1,0:T(8,128)(2,1)S(1)}) fusion(bf16[2,64,1024]{2,1,0:T(8,128)(2,1)S(1)} %bitcast.75, bf16[2,64,1024]{2,1,0:T(8,128)(2,1)} %bitcast.77), kind=kLoop, calls=%fused_computation.33 | loop fusion | flops 1179648 | bytes 1048576 | tf_op jit(solution)/shard_map/concatenate | solution.py:179
  35.1 0.0 collective-permute-done.5
  35.1 0.1 collective-permute-start.9
  35.2 1.1 %fusion.19 = (bf16[2,1,128,1024]{3,2,1,0:T(8,128)(2,1)S(1)}, bf16[2,1,128,1024]{3,2,1,0:T(8,128)(2,1)S(1)}) fusion(bf16[2,64,1024]{2,1,0:T(8,128)(2,1)} %bitcast.78, bf16[2,64,1024]{2,1,0:T(8,128)(2,1)S(1)} %bitcast.76, bf16[2,128,512]{2,1,0:T(8,128)(2,1)S(1)} %get-tuple-element.30, bf16[2,128,512]{2,1,0:T(8,128)(2,1)S(1)} %get-tuple-element.29), kind=kLoop, calls=%fused_computation.29 | loop fusion | flops 2097152 | bytes 2097152 | tf_op jit(solution)/shard_map/stack | solution.py:182
  36.2 0.0 collective-permute-done.4
  36.2 0.0 collective-permute-done.3
  36.2 1.9 %collective-permute-done.11 = bf16[64,1024]{1,0:T(8,128)(2,1)S(1)} collective-permute-done((bf16[64,1024]{1,0:T(8,128)(2,1)}, bf16[64,1024]{1,0:T(8,128)(2,1)S(1)}, u32[]{:S(2)}, u32[]{:S(2)}) %collective-permute-start.11) | collective-permute-done | bytes 131104 | tf_op jit(solution)/shard_map/ppermute | solution.py:175
  38.1 8.4 %collective-permute-done.10 = bf16[64,1024]{1,0:T(8,128)(2,1)S(1)} collective-permute-done((bf16[64,1024]{1,0:T(8,128)(2,1)}, bf16[64,1024]{1,0:T(8,128)(2,1)S(1)}, u32[]{:S(2)}, u32[]{:S(2)}) %collective-permute-start.10) | collective-permute-done | bytes 131104 | tf_op jit(solution)/shard_map/ppermute | solution.py:175
  46.5 0.0 collective-permute-done.9
  46.5 0.0 copy-done.2
  46.5 0.0 copy-done.3
  46.5 0.8 %convolution_bitcast_fusion = f32[4,2,2,128,128]{3,4,2,1,0:T(8,128)S(1)} fusion(bf16[1,1,64,1024]{3,2,1,0:T(8,128)(2,1)S(1)} %bitcast.88, bf16[1,1,64,1024]{3,2,1,0:T(8,128)(2,1)S(1)} %bitcast.89, bf16[1,1,64,1024]{3,2,1,0:T(8,128)(2,1)S(1)} %bitcast.90, bf16[1,1,64,1024]{3,2,1,0:T(8,128)(2,1)S(1)} %bitcast.94, bf16[1,1,64,1024]{3,2,1,0:T(8,128)(2,1)S(1)} %bitcast.85, ...), kind=kOutput, calls=%fused_computation.1 | convolution fusion | flops 547356672 | bytes 3145728 | tf_op jit(solution)/shard_map/lrif,dkjf->dklrij/dot_general | solution.py:183
  47.3 0.6 %gather_fusion = f32[4,2,2,128,128]{3,4,2,1,0:T(8,128)S(1)} fusion(f32[4,2,2,128,128]{3,4,2,1,0:T(8,128)S(1)} %convolution_bitcast_fusion, s32[1024]{0:T(1024)S(1)} %pad_clamp_fusion), kind=kCustom, calls=%fused_computation | custom fusion | bytes 2097168 | tf_op jit(solution)/shard_map/jit(_take)/gather | solution.py:185
  47.9 0.2 fusion.18
  48.2 1.0 %copy.13 = bf16[1,1,4,1,2,2,128,128]{7,6,5,4,3,2,1,0:T(8,128)(2,1)} copy(bf16[1,1,4,1,2,2,128,128]{6,7,5,4,2,3,1,0:T(8,128)(2,1)S(1)} %fusion.18) | data formatting | bytes 1048576 | tf_op jit(solution)/shard_map/convert_element_type | solution.py:189
  (6 shorter events, 0.1 us)
Async XLA Ops:
  0.0 4.6 %copy-start.1 = (s32[1,1,4]{2,1,0:T(1,128)S(1)}, s32[1,1,4]{2,1,0:T(1,128)}, u32[]{:S(2)}) copy-start(s32[1,1,4]{2,1,0:T(1,128)} %param.11) | copy-start | bytes 52
  1.4 6.2 %collective-permute-start.2 = (bf16[128,512]{1,0:T(8,128)(2,1)S(1)}, bf16[128,512]{1,0:T(8,128)(2,1)S(1)}, u32[]{:S(2)}, u32[]{:S(2)}) collective-permute-start(bf16[128,512]{1,0:T(8,128)(2,1)S(1)} %get-tuple-element.36), channel_id=1, source_target_pairs={{0,3},{1,0},{2,1},{3,2},{4,7},{5,4},{6,5},{7,6},{8,11},{9,8},{10,9... | collective-permute-start | bytes 393224 | tf_op jit(solution)/shard_map/ppermute | solution.py:165
  3.8 7.5 %collective-permute-start.1 = (bf16[128,512]{1,0:T(8,128)(2,1)S(1)}, bf16[128,512]{1,0:T(8,128)(2,1)S(1)}, u32[]{:S(2)}, u32[]{:S(2)}) collective-permute-start(bf16[128,512]{1,0:T(8,128)(2,1)S(1)} %get-tuple-element.37), channel_id=1, source_target_pairs={{0,2},{1,3},{2,0},{3,1},{4,6},{5,7},{6,4},{7,5},{8,10},{9,11},{10,... | collective-permute-start | bytes 393224 | tf_op jit(solution)/shard_map/ppermute | solution.py:165
  4.5 6.9 %collective-permute-start = (bf16[128,512]{1,0:T(8,128)(2,1)S(1)}, bf16[128,512]{1,0:T(8,128)(2,1)S(1)}, u32[]{:S(2)}, u32[]{:S(2)}) collective-permute-start(bf16[128,512]{1,0:T(8,128)(2,1)S(1)} %get-tuple-element.38), channel_id=1, source_target_pairs={{0,1},{1,2},{2,3},{3,0},{4,5},{5,6},{6,7},{7,4},{8,9},{9,10},{10,1... | collective-permute-start | bytes 393224 | tf_op jit(solution)/shard_map/ppermute | solution.py:165
  12.3 10.7 %collective-permute-start.8 = (bf16[128,512]{1,0:T(8,128)(2,1)S(1)}, bf16[128,512]{1,0:T(8,128)(2,1)S(1)}, u32[]{:S(2)}, u32[]{:S(2)}) collective-permute-start(bf16[128,512]{1,0:T(8,128)(2,1)S(1)} %get-tuple-element.32), channel_id=1, source_target_pairs={{0,3},{1,0},{2,1},{3,2},{4,7},{5,4},{6,5},{7,6},{8,11},{9,8},{10,9... | collective-permute-start | bytes 393224 | tf_op jit(solution)/shard_map/ppermute | solution.py:165
  12.3 11.6 %collective-permute-start.7 = (bf16[128,512]{1,0:T(8,128)(2,1)S(1)}, bf16[128,512]{1,0:T(8,128)(2,1)S(1)}, u32[]{:S(2)}, u32[]{:S(2)}) collective-permute-start(bf16[128,512]{1,0:T(8,128)(2,1)S(1)} %get-tuple-element.33), channel_id=1, source_target_pairs={{0,2},{1,3},{2,0},{3,1},{4,6},{5,7},{6,4},{7,5},{8,10},{9,11},{10,... | collective-permute-start | bytes 393224 | tf_op jit(solution)/shard_map/ppermute | solution.py:165
  14.0 9.9 %collective-permute-start.6 = (bf16[128,512]{1,0:T(8,128)(2,1)S(1)}, bf16[128,512]{1,0:T(8,128)(2,1)S(1)}, u32[]{:S(2)}, u32[]{:S(2)}) collective-permute-start(bf16[128,512]{1,0:T(8,128)(2,1)S(1)} %get-tuple-element.34), channel_id=1, source_target_pairs={{0,1},{1,2},{2,3},{3,0},{4,5},{5,6},{6,7},{7,4},{8,9},{9,10},{10,1... | collective-permute-start | bytes 393224 | tf_op jit(solution)/shard_map/ppermute | solution.py:165
  19.3 15.8 %collective-permute-start.5 = (bf16[64,1024]{1,0:T(8,128)(2,1)}, bf16[64,1024]{1,0:T(8,128)(2,1)S(1)}, u32[]{:S(2)}, u32[]{:S(2)}) collective-permute-start(bf16[64,1024]{1,0:T(8,128)(2,1)} %get-tuple-element.19), channel_id=1, source_target_pairs={{0,12},{4,0},{8,4},{12,8},{1,13},{5,1},{9,5},{13,9},{2,14},{6,2},{... | collective-permute-start | bytes 393224 | tf_op jit(solution)/shard_map/ppermute | solution.py:175
  22.9 13.3 %collective-permute-start.4 = (bf16[64,1024]{1,0:T(8,128)(2,1)}, bf16[64,1024]{1,0:T(8,128)(2,1)S(1)}, u32[]{:S(2)}, u32[]{:S(2)}) collective-permute-start(bf16[64,1024]{1,0:T(8,128)(2,1)} %get-tuple-element.18), channel_id=1, source_target_pairs={{0,8},{4,12},{8,0},{12,4},{1,9},{5,13},{9,1},{13,5},{2,10},{6,14},... | collective-permute-start | bytes 393224 | tf_op jit(solution)/shard_map/ppermute | solution.py:175
  22.9 13.3 %collective-permute-start.3 = (bf16[64,1024]{1,0:T(8,128)(2,1)}, bf16[64,1024]{1,0:T(8,128)(2,1)S(1)}, u32[]{:S(2)}, u32[]{:S(2)}) collective-permute-start(bf16[64,1024]{1,0:T(8,128)(2,1)} %get-tuple-element.17), channel_id=1, source_target_pairs={{0,4},{4,8},{8,12},{12,0},{1,5},{5,9},{9,13},{13,1},{2,6},{6,10},{... | collective-permute-start | bytes 393224 | tf_op jit(solution)/shard_map/ppermute | solution.py:175
  24.8 9.2 %copy-start = (bf16[128,1024]{1,0:T(8,128)(2,1)S(1)}, bf16[128,1024]{1,0:T(8,128)(2,1)}, u32[]{:S(2)}) copy-start(bf16[128,1024]{1,0:T(8,128)(2,1)} %get-tuple-element.25) | copy-start | bytes 786436
  30.1 16.4 %copy-start.2 = (bf16[64,1024]{1,0:T(8,128)(2,1)S(1)}, bf16[64,1024]{1,0:T(8,128)(2,1)}, u32[]{:S(2)}) copy-start(bf16[64,1024]{1,0:T(8,128)(2,1)} %get-tuple-element.16) | copy-start | bytes 393220
  30.1 16.4 %copy-start.3 = (bf16[64,1024]{1,0:T(8,128)(2,1)S(1)}, bf16[64,1024]{1,0:T(8,128)(2,1)}, u32[]{:S(2)}) copy-start(bf16[64,1024]{1,0:T(8,128)(2,1)} %get-tuple-element.21) | copy-start | bytes 393220
  30.1 8.0 %collective-permute-start.11 = (bf16[64,1024]{1,0:T(8,128)(2,1)}, bf16[64,1024]{1,0:T(8,128)(2,1)S(1)}, u32[]{:S(2)}, u32[]{:S(2)}) collective-permute-start(bf16[64,1024]{1,0:T(8,128)(2,1)} %get-tuple-element.24), channel_id=1, source_target_pairs={{0,12},{4,0},{8,4},{12,8},{1,13},{5,1},{9,5},{13,9},{2,14},{6,2},{... | collective-permute-start | bytes 393224 | tf_op jit(solution)/shard_map/ppermute | solution.py:175
  32.9 13.6 %collective-permute-start.10 = (bf16[64,1024]{1,0:T(8,128)(2,1)}, bf16[64,1024]{1,0:T(8,128)(2,1)S(1)}, u32[]{:S(2)}, u32[]{:S(2)}) collective-permute-start(bf16[64,1024]{1,0:T(8,128)(2,1)} %get-tuple-element.23), channel_id=1, source_target_pairs={{0,8},{4,12},{8,0},{12,4},{1,9},{5,13},{9,1},{13,5},{2,10},{6,14},... | collective-permute-start | bytes 393224 | tf_op jit(solution)/shard_map/ppermute | solution.py:175
  35.1 11.4 %collective-permute-start.9 = (bf16[64,1024]{1,0:T(8,128)(2,1)}, bf16[64,1024]{1,0:T(8,128)(2,1)S(1)}, u32[]{:S(2)}, u32[]{:S(2)}) collective-permute-start(bf16[64,1024]{1,0:T(8,128)(2,1)} %get-tuple-element.22), channel_id=1, source_target_pairs={{0,4},{4,8},{8,12},{12,0},{1,5},{5,9},{9,13},{13,1},{2,6},{6,10},{... | collective-permute-start | bytes 393224 | tf_op jit(solution)/shard_map/ppermute | solution.py:175

commit v12 on v7

--- a/solution.py
+++ b/solution.py
@@ -17,7 +17,7 @@
 RAD = 15
 TILE = 128
 HALF = NT // 2
-NSPLIT = 2
+SPLITS = (3, 1)
 BF16 = ml_dtypes.bfloat16
 
 
@@ -106,15 +106,15 @@
     grp = jnp.asarray(group_matrix())
     grid_spec = pltpu.PrefetchScalarGridSpec(
         num_scalar_prefetch=1,
-        grid=(nrows // BLOCK,),
+        grid=(1,),
         in_specs=[
-            pl.BlockSpec((ntm, BLOCK, width), lambda r, p: (0, r, 0)),
+            pl.BlockSpec((ntm, nrows, width), lambda r, p: (0, 0, 0)),
             pl.BlockSpec(band.shape, lambda r, p: (0, 0)),
             pl.BlockSpec(tab.shape, lambda r, p: (0, 0)),
             pl.BlockSpec(grp.shape, lambda r, p: (0, 0)),
         ],
-        out_specs=pl.BlockSpec((BLOCK, 2 * NBAND), lambda r, p: (r, 0)),
-        scratch_shapes=[pltpu.VMEM((BLOCK, NT), jnp.bfloat16)],
+        out_specs=pl.BlockSpec((nrows, 2 * NBAND), lambda r, p: (0, 0)),
+        scratch_shapes=[pltpu.VMEM((nrows, NT), jnp.bfloat16)],
     )
     flops = 2 * nrows * (3 * TILE * 2 * TILE * (NT // TILE) + NT * 2 * NBAND + 2 * NBAND * NBAND)
     nbytes = rows3.size * 2 + tab.size * 2 + nrows * 2 * NBAND * 2
@@ -131,8 +131,9 @@
     nch, width = raw.shape
     here = lax.axis_index("tm")
     blocks = nch // ntm // BLOCK
-    rows = BLOCK // NSPLIT
-    parts = raw.reshape(ntm, blocks, NSPLIT, rows, width)
+    parts = raw.reshape(ntm, blocks, BLOCK, width)
+    unit = BLOCK // sum(SPLITS)
+    bounds = [unit * sum(SPLITS[:h]) for h in range(len(SPLITS) + 1)]
     pos = here.astype(jnp.int32).reshape(1)
 
     peers = lax.axis_size("chan")
@@ -141,8 +142,9 @@
     ids = send_blocks[0, 0]
     own_parts = []
     picked_parts = []
-    for h in range(NSPLIT):
-        part = parts[:, :, h].reshape(ntm, blocks * rows, width)
+    for h in range(len(SPLITS)):
+        rows = bounds[h + 1] - bounds[h]
+        part = parts[:, :, bounds[h]:bounds[h + 1]].reshape(ntm, blocks * rows, width)
         if own_parts:
             part, prev_slots = lax.optimization_barrier((part, prev_slots))
         slots = [lax.dynamic_index_in_dim(part, here, axis=0, keepdims=False)]

time: 47.4 us -> 53.8 us (1.14)
  waiting for transfers between devices: 8.07 us -> 16.3 us
  starting transfers between devices: 16.8 us -> 13.9 us
  local copies, waits for them, and re-layouts: 3.7 us -> 4.58 us
  Pallas kernels: 8.6 us -> 9.25 us
    ppermute x6, waiting for transfers between devices: 5.61 us -> 12.1 us  [local(): lax.ppermute(blk, 'chan', perm=[(i, (i + d) % peers) for i in range(peers)])]
    ppermute x6, starting transfers between devices: 9.49 us -> 6.63 us  [local(): lax.ppermute(blk, 'chan', perm=[(i, (i + d) % peers) for i in range(peers)])]
    ppermute x6, waiting for transfers between devices: 2.45 us -> 4.27 us  [local(): lax.ppermute(piece, 'tm', perm=[(i, (i + d) % ntm) for i in range(ntm)])]
    slice x1 -> x2, local copies, waits for them, and re-layouts: 1.32 us -> 2.2 us  [local(): parts[:, :, bounds[h]:bounds[h + 1]].reshape(ntm, blocks * rows, width)]
    pallas_call x2, Pallas kernels: 8.6 us -> 9.25 us  [spectra(): pl.pallas_call(spectra_kernel, grid_spec=grid_spec, cost_estimate=pl.Cost...]
  transfers between devices with their start and end apart: 12 -> 12, of which waited for: 4 -> 5; matrix products, arithmetic and copies ran while one was open for 12% -> 12% of each run, Pallas kernels for 18% -> 17%
where the time goes in v12:
time: 53.8 us; the launch traced here: 53.5 us
  waiting for transfers between devices  16.3 us (30%)
  starting transfers between devices  13.9 us (26%)
  Pallas kernels  9.25 us (17%)
  other arithmetic  5.88 us (11%)
  local copies, waits for them, and re-layouts  4.58 us (9%)
  between operations  2.77 us (5%)
  matrix products  0.74 us (1%)
    ppermute x6, waiting for transfers between devices, local(): lax.ppermute(blk, 'chan', perm=[(i, (i + d) % peers) for i in range(peers)])  12.1 us
    pallas_call x2, Pallas kernels, spectra(): pl.pallas_call(spectra_kernel, grid_spec=grid_spec, cost_estimate=pl.Cost...  9.25 us
    ppermute x6, starting transfers between devices, local(): lax.ppermute(piece, 'tm', perm=[(i, (i + d) % ntm) for i in range(ntm)])  7.29 us
    ppermute x6, starting transfers between devices, local(): lax.ppermute(blk, 'chan', perm=[(i, (i + d) % peers) for i in range(peers)])  6.63 us
    ppermute x6, waiting for transfers between devices, local(): lax.ppermute(piece, 'tm', perm=[(i, (i + d) % ntm) for i in range(ntm)])  4.27 us
    slice x2, local copies, waits for them, and re-layouts, local(): parts[:, :, bounds[h]:bounds[h + 1]].reshape(ntm, blocks * rows, width)  2.2 us
    another operation x2, other arithmetic, local(): picked_parts.append(jnp.stack(recv))  1.97 us
    another operation x2, other arithmetic, local(): prev_slots = jnp.stack(slots)  1.71 us
  transfers between devices with their start and end apart: 12, of which 5 were waited for; matrix products, arithmetic and copies ran while one was open for 12% of the time, Pallas kernels for 17%

profile of v12, /device:TPU:0, one launch (start us, length us, event | category | flops | bytes accessed | tf_op | source)
XLA Modules:
  0.0 53.5 jit_solution(1351684432713709041)
XLA Ops:
  0.0 0.0 copy-start.1
  0.0 0.0 copy-start.2
  0.0 1.2 %slice.50 = bf16[4,2,96,512]{3,2,1,0:T(8,128)(2,1)S(1)} slice(bf16[4,2,128,512]{3,2,1,0:T(8,128)(2,1)} %bitcast.77), slice={[0:4], [0:2], [0:96], [0:512]} | slice | bytes 1572864 | tf_op jit(solution)/shard_map/slice | solution.py:147
  1.3 0.1 constant_dynamic-slice_fusion.4
  1.3 2.4 %collective-permute-start.2 = (bf16[192,512]{1,0:T(8,128)(2,1)S(1)}, bf16[192,512]{1,0:T(8,128)(2,1)S(1)}, u32[]{:S(2)}, u32[]{:S(2)}) collective-permute-start(bf16[192,512]{1,0:T(8,128)(2,1)S(1)} %get-tuple-element.8), channel_id=1, source_target_pairs={{0,3},{1,0},{2,1},{3,2},{4,7},{5,4},{6,5},{7,6},{8,11},{9,8},{10,9... | collective-permute-start | bytes 589832 | tf_op jit(solution)/shard_map/ppermute | solution.py:153
  3.8 0.0 collective-permute-start
  3.8 1.1 %collective-permute-start.1 = (bf16[192,512]{1,0:T(8,128)(2,1)S(1)}, bf16[192,512]{1,0:T(8,128)(2,1)S(1)}, u32[]{:S(2)}, u32[]{:S(2)}) collective-permute-start(bf16[192,512]{1,0:T(8,128)(2,1)S(1)} %get-tuple-element.9), channel_id=1, source_target_pairs={{0,2},{1,3},{2,0},{3,1},{4,6},{5,7},{6,4},{7,5},{8,10},{9,11},{10,... | collective-permute-start | bytes 589832 | tf_op jit(solution)/shard_map/ppermute | solution.py:153
  4.8 1.0 %slice.53 = bf16[4,2,32,512]{3,2,1,0:T(8,128)(2,1)S(1)} slice(bf16[4,2,128,512]{3,2,1,0:T(8,128)(2,1)} %bitcast.78), slice={[0:4], [0:2], [96:128], [0:512]} | slice | bytes 524288 | tf_op jit(solution)/shard_map/slice | solution.py:147
  5.9 0.0 copy-done.1
  5.9 0.7 %constant_dynamic-slice_fusion.5 = (s32[1,1,1,1]{2,3,1,0:T(1,128)}, s32[1,1,1,1]{2,3,1,0:T(1,128)}, s32[1,1,1,1]{2,3,1,0:T(1,128)}, s32[1,1,1,1]{2,3,1,0:T(1,128)}) fusion(s32[1,1,4,1]{2,3,1,0:T(1,128)S(1)} %copy-done.1, s32[]{:T(128)S(6)} %select_n.194, s32[]{:T(128)S(6)} %select_n.205, s32[]{:T(128)S(6)} %select_n.213, s32[]{:T(128)S(6)} %select_n.209), kind=kLoop, calls=%fused_computation.56 | loop fusion | bytes 48 | tf_op jit(solution)/shard_map/jit(dynamic_index_in_dim)/dynamic_slice | solution.py:162
  9.1 0.0 copy-done.2
  9.2 0.0 collective-permute-done.2
  9.2 1.8 %collective-permute-done = bf16[192,512]{1,0:T(8,128)(2,1)S(1)} collective-permute-done((bf16[192,512]{1,0:T(8,128)(2,1)S(1)}, bf16[192,512]{1,0:T(8,128)(2,1)S(1)}, u32[]{:S(2)}, u32[]{:S(2)}) %collective-permute-start) | collective-permute-done | bytes 196640 | tf_op jit(solution)/shard_map/ppermute | solution.py:153
  10.9 2.5 %collective-permute-done.1 = bf16[192,512]{1,0:T(8,128)(2,1)S(1)} collective-permute-done((bf16[192,512]{1,0:T(8,128)(2,1)S(1)}, bf16[192,512]{1,0:T(8,128)(2,1)S(1)}, u32[]{:S(2)}, u32[]{:S(2)}) %collective-permute-start.1) | collective-permute-done | bytes 196640 | tf_op jit(solution)/shard_map/ppermute | solution.py:153
  13.4 1.0 %pad_maximum_fusion.1.x_ref = bf16[4,192,512]{2,1,0:T(8,128)(2,1)} fusion(bf16[1,192,512]{2,1,0:T(8,128)(2,1)S(1)} %bitcast.80, bf16[1,192,512]{2,1,0:T(8,128)(2,1)S(1)} %bitcast.82, bf16[1,192,512]{2,1,0:T(8,128)(2,1)S(1)} %bitcast.81, bf16[1,192,512]{2,1,0:T(8,128)(2,1)S(1)} %get-tuple-element.7), kind=kLoop, calls=%fused_computation.27 | loop fusion | flops 1179648 | bytes 1572864 | tf_op jit(solution)/shard_map/stack | solution.py:154
  14.4 0.7 %collective-permute-start.6 = (bf16[64,512]{1,0:T(8,128)(2,1)S(1)}, bf16[64,512]{1,0:T(8,128)(2,1)S(1)}, u32[]{:S(2)}, u32[]{:S(2)}) collective-permute-start(bf16[64,512]{1,0:T(8,128)(2,1)S(1)} %get-tuple-element.20), channel_id=1, source_target_pairs={{0,1},{1,2},{2,3},{3,0},{4,5},{5,6},{6,7},{7,4},{8,9},{9,10},{10,1... | collective-permute-start | bytes 196616 | tf_op jit(solution)/shard_map/ppermute | solution.py:153
  15.2 1.7 %collective-permute-start.7 = (bf16[64,512]{1,0:T(8,128)(2,1)S(1)}, bf16[64,512]{1,0:T(8,128)(2,1)S(1)}, u32[]{:S(2)}, u32[]{:S(2)}) collective-permute-start(bf16[64,512]{1,0:T(8,128)(2,1)S(1)} %get-tuple-element.19), channel_id=1, source_target_pairs={{0,2},{1,3},{2,0},{3,1},{4,6},{5,7},{6,4},{7,5},{8,10},{9,11},{10,... | collective-permute-start | bytes 196616 | tf_op jit(solution)/shard_map/ppermute | solution.py:153
  16.9 1.4 %collective-permute-start.8 = (bf16[64,512]{1,0:T(8,128)(2,1)S(1)}, bf16[64,512]{1,0:T(8,128)(2,1)S(1)}, u32[]{:S(2)}, u32[]{:S(2)}) collective-permute-start(bf16[64,512]{1,0:T(8,128)(2,1)S(1)} %get-tuple-element.18), channel_id=1, source_target_pairs={{0,3},{1,0},{2,1},{3,2},{4,7},{5,4},{6,5},{7,6},{8,11},{9,8},{10,9... | collective-permute-start | bytes 196616 | tf_op jit(solution)/shard_map/ppermute | solution.py:153
  18.2 5.0 %shard_map.91 = bf16[192,1024]{1,0:T(8,128)(2,1)} custom-call(s32[1]{0:T(128)} %bitcast.2.pos_ref, bf16[4,192,512]{2,1,0:T(8,128)(2,1)} %pad_maximum_fusion.1.x_ref, bf16[384,256]{1,0:T(8,128)(2,1)} %constant.144.clone.band_ref, bf16[1024,1024]{1,0:T(8,128)(2,1)} %constant.145.clone.tab_ref, bf16[512,512]{1,0:T(8,128)(2,1)} %constant.146.clone.grp_ref), custom_call_target="tpu_custom_call" | custom-call | flops 1610612736 | bytes 3276800 | tf_op jit(solution)/shard_map/pallas_call | solution.py:121
  23.2 1.1 %select_bitcast_fusion = (bf16[1,1,96,1024]{3,2,1,0:T(8,128)(2,1)S(1)}, bf16[96,1024]{1,0:T(8,128)(2,1)S(1)}, bf16[96,1024]{1,0:T(8,128)(2,1)S(1)}, bf16[96,1024]{1,0:T(8,128)(2,1)S(1)}) fusion(pred[]{:T(512)} %bitcast.1, bf16[192,1024]{1,0:T(8,128)(2,1)} %shard_map.91, pred[]{:T(512)} %bitcast.14, pred[]{:T(512)} %bitcast.16, pred[]{:T(512)} %bitcast.12), kind=kLoop, calls=%fused_computation.36 | loop fusion | flops 393216 | bytes 1179652 | tf_op jit(solution)/shard_map/stack;stack | solution.py:170
  24.3 0.0 copy-start
  24.3 1.6 %collective-permute-start.3 = (bf16[96,1024]{1,0:T(8,128)(2,1)S(1)}, bf16[96,1024]{1,0:T(8,128)(2,1)S(1)}, u32[]{:S(2)}, u32[]{:S(2)}) collective-permute-start(bf16[96,1024]{1,0:T(8,128)(2,1)S(1)} %get-tuple-element.16), channel_id=1, source_target_pairs={{0,4},{4,8},{8,12},{12,0},{1,5},{5,9},{9,13},{13,1},{2,6},{6,10},{... | collective-permute-start | bytes 589832 | tf_op jit(solution)/shard_map/ppermute | solution.py:167
  26.0 2.6 %collective-permute-start.4 = (bf16[96,1024]{1,0:T(8,128)(2,1)S(1)}, bf16[96,1024]{1,0:T(8,128)(2,1)S(1)}, u32[]{:S(2)}, u32[]{:S(2)}) collective-permute-start(bf16[96,1024]{1,0:T(8,128)(2,1)S(1)} %get-tuple-element.14), channel_id=1, source_target_pairs={{0,8},{4,12},{8,0},{12,4},{1,9},{5,13},{9,1},{13,5},{2,10},{6,14},... | collective-permute-start | bytes 589832 | tf_op jit(solution)/shard_map/ppermute | solution.py:167
  28.6 0.0 collective-permute-done.6
  28.6 1.3 %collective-permute-start.5 = (bf16[96,1024]{1,0:T(8,128)(2,1)S(1)}, bf16[96,1024]{1,0:T(8,128)(2,1)S(1)}, u32[]{:S(2)}, u32[]{:S(2)}) collective-permute-start(bf16[96,1024]{1,0:T(8,128)(2,1)S(1)} %get-tuple-element.15), channel_id=1, source_target_pairs={{0,12},{4,0},{8,4},{12,8},{1,13},{5,1},{9,5},{13,9},{2,14},{6,2},{... | collective-permute-start | bytes 589832 | tf_op jit(solution)/shard_map/ppermute | solution.py:167
  29.9 0.0 collective-permute-done.7
  29.9 0.0 collective-permute-done.8
  29.9 0.7 %pad_maximum_fusion.2.x_ref = bf16[4,64,512]{2,1,0:T(8,128)(2,1)} fusion(bf16[1,64,512]{2,1,0:T(8,128)(2,1)S(1)} %bitcast.85, bf16[1,64,512]{2,1,0:T(8,128)(2,1)S(1)} %bitcast.84, bf16[1,64,512]{2,1,0:T(8,128)(2,1)S(1)} %bitcast.83, bf16[1,64,512]{2,1,0:T(8,128)(2,1)S(1)} %get-tuple-element.17), kind=kLoop, calls=%fused_computation.35 | loop fusion | flops 393216 | bytes 524288 | tf_op jit(solution)/shard_map/stack | solution.py:154
  30.6 4.2 %shard_map.92 = bf16[64,1024]{1,0:T(8,128)(2,1)} custom-call(s32[1]{0:T(128)} %bitcast.2.pos_ref, bf16[4,64,512]{2,1,0:T(8,128)(2,1)} %pad_maximum_fusion.2.x_ref, bf16[384,256]{1,0:T(8,128)(2,1)} %constant.144.clone.band_ref, bf16[1024,1024]{1,0:T(8,128)(2,1)} %constant.145.clone.tab_ref, bf16[512,512]{1,0:T(8,128)(2,1)} %constant.146.clone.grp_ref), custom_call_target="tpu_custom_call" | custom-call | flops 536870912 | bytes 2490368 | tf_op jit(solution)/shard_map/pallas_call | solution.py:121
  34.9 0.9 %select_bitcast_fusion.1 = (bf16[1,1,32,1024]{3,2,1,0:T(8,128)(2,1)S(1)}, bf16[32,1024]{1,0:T(8,128)(2,1)S(1)}, bf16[32,1024]{1,0:T(8,128)(2,1)S(1)}, bf16[32,1024]{1,0:T(8,128)(2,1)S(1)}) fusion(pred[]{:T(512)} %bitcast.1, bf16[64,1024]{1,0:T(8,128)(2,1)} %shard_map.92, pred[]{:T(512)} %bitcast.14, pred[]{:T(512)} %bitcast.16, pred[]{:T(512)} %bitcast.12), kind=kLoop, calls=%fused_computation.43 | loop fusion | flops 131072 | bytes 393220 | tf_op jit(solution)/shard_map/stack;stack | solution.py:170
  35.8 0.7 %collective-permute-start.9 = (bf16[32,1024]{1,0:T(8,128)(2,1)S(1)}, bf16[32,1024]{1,0:T(8,128)(2,1)S(1)}, u32[]{:S(2)}, u32[]{:S(2)}) collective-permute-start(bf16[32,1024]{1,0:T(8,128)(2,1)S(1)} %get-tuple-element.24), channel_id=1, source_target_pairs={{0,4},{4,8},{8,12},{12,0},{1,5},{5,9},{9,13},{13,1},{2,6},{6,10},{... | collective-permute-start | bytes 196616 | tf_op jit(solution)/shard_map/ppermute | solution.py:167
  36.5 0.3 collective-permute-start.10
  36.8 0.0 copy-done
  36.8 0.9 %fusion.20 = (bf16[2,128,512]{2,1,0:T(8,128)(2,1)S(1)}, bf16[2,128,512]{2,1,0:T(8,128)(2,1)S(1)}) fusion(bf16[2,96,1024]{2,1,0:T(8,128)(2,1)S(1)} %bitcast.72, bf16[2,32,1024]{2,1,0:T(8,128)(2,1)} %bitcast.75), kind=kLoop, calls=%fused_computation.32 | loop fusion | flops 1179648 | bytes 1048576 | tf_op jit(solution)/shard_map/concatenate | solution.py:171
  37.8 5.1 %collective-permute-done.9 = bf16[32,1024]{1,0:T(8,128)(2,1)S(1)} collective-permute-done((bf16[32,1024]{1,0:T(8,128)(2,1)S(1)}, bf16[32,1024]{1,0:T(8,128)(2,1)S(1)}, u32[]{:S(2)}, u32[]{:S(2)}) %collective-permute-start.9) | collective-permute-done | bytes 65568 | tf_op jit(solution)/shard_map/ppermute | solution.py:167
  42.9 0.0 collective-permute-start.11
  42.9 1.0 %fusion.19 = (bf16[2,1,128,1024]{3,2,1,0:T(8,128)(2,1)S(1)}, bf16[2,1,128,1024]{3,2,1,0:T(8,128)(2,1)S(1)}) fusion(bf16[2,32,1024]{2,1,0:T(8,128)(2,1)} %bitcast.76, bf16[2,96,1024]{2,1,0:T(8,128)(2,1)S(1)} %bitcast.73, bf16[2,128,512]{2,1,0:T(8,128)(2,1)S(1)} %get-tuple-element.12, bf16[2,128,512]{2,1,0:T(8,128)(2,1)S(1)} %get-tuple-element.11), kind=kLoop, calls=%fused_computation.30 | loop fusion | flops 2097152 | bytes 2097152 | tf_op jit(solution)/shard_map/stack | solution.py:174
  43.9 5.3 %collective-permute-done.10 = bf16[32,1024]{1,0:T(8,128)(2,1)S(1)} collective-permute-done((bf16[32,1024]{1,0:T(8,128)(2,1)S(1)}, bf16[32,1024]{1,0:T(8,128)(2,1)S(1)}, u32[]{:S(2)}, u32[]{:S(2)}) %collective-permute-start.10) | collective-permute-done | bytes 65568 | tf_op jit(solution)/shard_map/ppermute | solution.py:167
  49.2 1.7 %collective-permute-done.11 = bf16[32,1024]{1,0:T(8,128)(2,1)S(1)} collective-permute-done((bf16[32,1024]{1,0:T(8,128)(2,1)S(1)}, bf16[32,1024]{1,0:T(8,128)(2,1)S(1)}, u32[]{:S(2)}, u32[]{:S(2)}) %collective-permute-start.11) | collective-permute-done | bytes 65568 | tf_op jit(solution)/shard_map/ppermute | solution.py:167
  50.8 0.0 collective-permute-done.3
  50.8 0.0 collective-permute-done.4
  50.8 0.0 collective-permute-done.5
  50.8 0.7 %convolution_bitcast_fusion = f32[4,2,2,128,128]{3,4,2,1,0:T(8,128)S(1)} fusion(bf16[1,1,32,1024]{3,2,1,0:T(8,128)(2,1)S(1)} %bitcast.91, bf16[1,1,32,1024]{3,2,1,0:T(8,128)(2,1)S(1)} %bitcast.90, bf16[1,1,32,1024]{3,2,1,0:T(8,128)(2,1)S(1)} %bitcast.89, bf16[1,1,32,1024]{3,2,1,0:T(8,128)(2,1)S(1)} %get-tuple-element.21, ...), kind=kOutput, calls=%fused_computation.1 | convolution fusion | flops 547356672 | bytes 3145728 | tf_op jit(solution)/shard_map/lrif,dkjf->dklrij/dot_general | solution.py:175
  51.6 0.6 %gather_fusion = f32[4,2,2,128,128]{3,4,2,1,0:T(8,128)S(1)} fusion(f32[4,2,2,128,128]{3,4,2,1,0:T(8,128)S(1)} %convolution_bitcast_fusion, s32[1024]{0:T(1024)S(1)} %pad_clamp_fusion), kind=kCustom, calls=%fused_computation | custom fusion | bytes 2097168 | tf_op jit(solution)/shard_map/jit(_take)/gather | solution.py:177
  52.2 0.2 fusion.18
  52.5 1.0 %copy.11 = bf16[1,1,4,1,2,2,128,128]{7,6,5,4,3,2,1,0:T(8,128)(2,1)} copy(bf16[1,1,4,1,2,2,128,128]{6,7,5,4,2,3,1,0:T(8,128)(2,1)S(1)} %fusion.18) | data formatting | bytes 1048576 | tf_op jit(solution)/shard_map/convert_element_type | solution.py:181
  (5 shorter events, 0.1 us)
Async XLA Ops:
  0.0 5.9 %copy-start.1 = (s32[1,1,4,1]{2,3,1,0:T(1,128)S(1)}, s32[1,1,4,1]{2,3,1,0:T(1,128)}, u32[]{:S(2)}) copy-start(s32[1,1,4,1]{2,3,1,0:T(1,128)} %param.10) | copy-start | bytes 52
  0.0 9.1 %copy-start.2 = (s32[1,1,4]{2,1,0:T(1,128)S(1)}, s32[1,1,4]{2,1,0:T(1,128)}, u32[]{:S(2)}) copy-start(s32[1,1,4]{2,1,0:T(1,128)} %param.11) | copy-start | bytes 52
  1.3 7.8 %collective-permute-start.2 = (bf16[192,512]{1,0:T(8,128)(2,1)S(1)}, bf16[192,512]{1,0:T(8,128)(2,1)S(1)}, u32[]{:S(2)}, u32[]{:S(2)}) collective-permute-start(bf16[192,512]{1,0:T(8,128)(2,1)S(1)} %get-tuple-element.8), channel_id=1, source_target_pairs={{0,3},{1,0},{2,1},{3,2},{4,7},{5,4},{6,5},{7,6},{8,11},{9,8},{10,9... | collective-permute-start | bytes 589832 | tf_op jit(solution)/shard_map/ppermute | solution.py:153
  3.8 7.2 %collective-permute-start = (bf16[192,512]{1,0:T(8,128)(2,1)S(1)}, bf16[192,512]{1,0:T(8,128)(2,1)S(1)}, u32[]{:S(2)}, u32[]{:S(2)}) collective-permute-start(bf16[192,512]{1,0:T(8,128)(2,1)S(1)} %get-tuple-element.10), channel_id=1, source_target_pairs={{0,1},{1,2},{2,3},{3,0},{4,5},{5,6},{6,7},{7,4},{8,9},{9,10},{10,1... | collective-permute-start | bytes 589832 | tf_op jit(solution)/shard_map/ppermute | solution.py:153
  3.8 9.7 %collective-permute-start.1 = (bf16[192,512]{1,0:T(8,128)(2,1)S(1)}, bf16[192,512]{1,0:T(8,128)(2,1)S(1)}, u32[]{:S(2)}, u32[]{:S(2)}) collective-permute-start(bf16[192,512]{1,0:T(8,128)(2,1)S(1)} %get-tuple-element.9), channel_id=1, source_target_pairs={{0,2},{1,3},{2,0},{3,1},{4,6},{5,7},{6,4},{7,5},{8,10},{9,11},{10,... | collective-permute-start | bytes 589832 | tf_op jit(solution)/shard_map/ppermute | solution.py:153
  14.4 14.1 %collective-permute-start.6 = (bf16[64,512]{1,0:T(8,128)(2,1)S(1)}, bf16[64,512]{1,0:T(8,128)(2,1)S(1)}, u32[]{:S(2)}, u32[]{:S(2)}) collective-permute-start(bf16[64,512]{1,0:T(8,128)(2,1)S(1)} %get-tuple-element.20), channel_id=1, source_target_pairs={{0,1},{1,2},{2,3},{3,0},{4,5},{5,6},{6,7},{7,4},{8,9},{9,10},{10,1... | collective-permute-start | bytes 196616 | tf_op jit(solution)/shard_map/ppermute | solution.py:153
  15.2 14.7 %collective-permute-start.7 = (bf16[64,512]{1,0:T(8,128)(2,1)S(1)}, bf16[64,512]{1,0:T(8,128)(2,1)S(1)}, u32[]{:S(2)}, u32[]{:S(2)}) collective-permute-start(bf16[64,512]{1,0:T(8,128)(2,1)S(1)} %get-tuple-element.19), channel_id=1, source_target_pairs={{0,2},{1,3},{2,0},{3,1},{4,6},{5,7},{6,4},{7,5},{8,10},{9,11},{10,... | collective-permute-start | bytes 196616 | tf_op jit(solution)/shard_map/ppermute | solution.py:153
  16.9 13.0 %collective-permute-start.8 = (bf16[64,512]{1,0:T(8,128)(2,1)S(1)}, bf16[64,512]{1,0:T(8,128)(2,1)S(1)}, u32[]{:S(2)}, u32[]{:S(2)}) collective-permute-start(bf16[64,512]{1,0:T(8,128)(2,1)S(1)} %get-tuple-element.18), channel_id=1, source_target_pairs={{0,3},{1,0},{2,1},{3,2},{4,7},{5,4},{6,5},{7,6},{8,11},{9,8},{10,9... | collective-permute-start | bytes 196616 | tf_op jit(solution)/shard_map/ppermute | solution.py:153
  24.3 12.5 %copy-start = (bf16[192,1024]{1,0:T(8,128)(2,1)S(1)}, bf16[192,1024]{1,0:T(8,128)(2,1)}, u32[]{:S(2)}) copy-start(bf16[192,1024]{1,0:T(8,128)(2,1)} %shard_map.91) | copy-start | bytes 1179652
  24.3 26.5 %collective-permute-start.3 = (bf16[96,1024]{1,0:T(8,128)(2,1)S(1)}, bf16[96,1024]{1,0:T(8,128)(2,1)S(1)}, u32[]{:S(2)}, u32[]{:S(2)}) collective-permute-start(bf16[96,1024]{1,0:T(8,128)(2,1)S(1)} %get-tuple-element.16), channel_id=1, source_target_pairs={{0,4},{4,8},{8,12},{12,0},{1,5},{5,9},{9,13},{13,1},{2,6},{6,10},{... | collective-permute-start | bytes 589832 | tf_op jit(solution)/shard_map/ppermute | solution.py:167
  26.0 24.9 %collective-permute-start.4 = (bf16[96,1024]{1,0:T(8,128)(2,1)S(1)}, bf16[96,1024]{1,0:T(8,128)(2,1)S(1)}, u32[]{:S(2)}, u32[]{:S(2)}) collective-permute-start(bf16[96,1024]{1,0:T(8,128)(2,1)S(1)} %get-tuple-element.14), channel_id=1, source_target_pairs={{0,8},{4,12},{8,0},{12,4},{1,9},{5,13},{9,1},{13,5},{2,10},{6,14},... | collective-permute-start | bytes 589832 | tf_op jit(solution)/shard_map/ppermute | solution.py:167
  28.6 22.3 %collective-permute-start.5 = (bf16[96,1024]{1,0:T(8,128)(2,1)S(1)}, bf16[96,1024]{1,0:T(8,128)(2,1)S(1)}, u32[]{:S(2)}, u32[]{:S(2)}) collective-permute-start(bf16[96,1024]{1,0:T(8,128)(2,1)S(1)} %get-tuple-element.15), channel_id=1, source_target_pairs={{0,12},{4,0},{8,4},{12,8},{1,13},{5,1},{9,5},{13,9},{2,14},{6,2},{... | collective-permute-start | bytes 589832 | tf_op jit(solution)/shard_map/ppermute | solution.py:167
  35.8 7.1 %collective-permute-start.9 = (bf16[32,1024]{1,0:T(8,128)(2,1)S(1)}, bf16[32,1024]{1,0:T(8,128)(2,1)S(1)}, u32[]{:S(2)}, u32[]{:S(2)}) collective-permute-start(bf16[32,1024]{1,0:T(8,128)(2,1)S(1)} %get-tuple-element.24), channel_id=1, source_target_pairs={{0,4},{4,8},{8,12},{12,0},{1,5},{5,9},{9,13},{13,1},{2,6},{6,10},{... | collective-permute-start | bytes 196616 | tf_op jit(solution)/shard_map/ppermute | solution.py:167
  36.5 12.7 %collective-permute-start.10 = (bf16[32,1024]{1,0:T(8,128)(2,1)S(1)}, bf16[32,1024]{1,0:T(8,128)(2,1)S(1)}, u32[]{:S(2)}, u32[]{:S(2)}) collective-permute-start(bf16[32,1024]{1,0:T(8,128)(2,1)S(1)} %get-tuple-element.22), channel_id=1, source_target_pairs={{0,8},{4,12},{8,0},{12,4},{1,9},{5,13},{9,1},{13,5},{2,10},{6,14},... | collective-permute-start | bytes 196616 | tf_op jit(solution)/shard_map/ppermute | solution.py:167
  42.9 7.9 %collective-permute-start.11 = (bf16[32,1024]{1,0:T(8,128)(2,1)S(1)}, bf16[32,1024]{1,0:T(8,128)(2,1)S(1)}, u32[]{:S(2)}, u32[]{:S(2)}) collective-permute-start(bf16[32,1024]{1,0:T(8,128)(2,1)S(1)} %get-tuple-element.23), channel_id=1, source_target_pairs={{0,12},{4,0},{8,4},{12,8},{1,13},{5,1},{9,5},{13,9},{2,14},{6,2},{... | collective-permute-start | bytes 196616 | tf_op jit(solution)/shard_map/ppermute | solution.py:167

commit v13 on v7

--- a/solution.py
+++ b/solution.py
@@ -170,7 +170,8 @@
     picked = jnp.concatenate(picked_parts, axis=2)
     turned = jnp.concatenate([whitened[..., NBAND:], -whitened[..., :NBAND]], axis=-1)
     paired = jnp.stack([whitened, turned], axis=1)
-    result = jnp.einsum("lrif,dkjf->dklrij", paired, picked, preferred_element_type=jnp.float32)
+    result = lax.dot_general(paired, picked, (((3,), (3,)), ((), ())), preferred_element_type=jnp.float32)
+    result = jnp.transpose(result, (3, 4, 0, 1, 2, 5))
     order = (mine - jnp.arange(peers, dtype=jnp.int32)) % peers
     result = jnp.take(result, order, axis=0)
     result = result * (1.0 / math.sqrt(NBAND))

time: 47.4 us -> 49.3 us (1.040)
  waiting for transfers between devices: 8.07 us -> 13.4 us
  starting transfers between devices: 16.8 us -> 13.9 us
  local copies, waits for them, and re-layouts: 3.7 us -> 2.68 us
  other arithmetic: 6.08 us -> 6.89 us
    ppermute x6, waiting for transfers between devices: 5.61 us -> 10 us  [local(): lax.ppermute(blk, 'chan', perm=[(i, (i + d) % peers) for i in range(peers)])]
    ppermute x6, starting transfers between devices: 7.29 us -> 5.16 us  [local(): lax.ppermute(piece, 'tm', perm=[(i, (i + d) % ntm) for i in range(ntm)])]
    convert_element_type x1 -> x0, local copies, waits for them, and re-layouts: 1.01 us -> none  [local(): return result.astype(jnp.bfloat16)[None, None]]
    ppermute x6, waiting for transfers between devices: 2.45 us -> 3.41 us  [local(): lax.ppermute(piece, 'tm', perm=[(i, (i + d) % ntm) for i in range(ntm)])]
    convert_element_type x1, other arithmetic: 0.24 us -> 1.04 us  [local(): return result.astype(jnp.bfloat16)[None, None]]
    ppermute x6, starting transfers between devices: 9.49 us -> 8.72 us  [local(): lax.ppermute(blk, 'chan', perm=[(i, (i + d) % peers) for i in range(peers)])]
  transfers between devices with their start and end apart: 12 -> 12, of which waited for: 4 -> 3; matrix products, arithmetic and copies ran while one was open for 12% -> 12% of each run, Pallas kernels for 18% -> 18%
where the time goes in v13:
time: 49.3 us; the launch traced here: 49 us
  starting transfers between devices  13.9 us (28%)
  waiting for transfers between devices  13.4 us (27%)
  Pallas kernels  8.58 us (17%)
  other arithmetic  6.89 us (14%)
  between operations  2.75 us (6%)
  local copies, waits for them, and re-layouts  2.68 us (5%)
  matrix products  0.76 us (2%)
    ppermute x6, waiting for transfers between devices, local(): lax.ppermute(blk, 'chan', perm=[(i, (i + d) % peers) for i in range(peers)])  10 us
    ppermute x6, starting transfers between devices, local(): lax.ppermute(blk, 'chan', perm=[(i, (i + d) % peers) for i in range(peers)])  8.72 us
    pallas_call x2, Pallas kernels, spectra(): pl.pallas_call(spectra_kernel, grid_spec=grid_spec, cost_estimate=pl.Cost...  8.58 us
    ppermute x6, starting transfers between devices, local(): lax.ppermute(piece, 'tm', perm=[(i, (i + d) % ntm) for i in range(ntm)])  5.16 us
    ppermute x6, waiting for transfers between devices, local(): lax.ppermute(piece, 'tm', perm=[(i, (i + d) % ntm) for i in range(ntm)])  3.41 us
    another operation x2, other arithmetic, local(): picked_parts.append(jnp.stack(recv))  2.01 us
    another operation x2, other arithmetic, local(): prev_slots = jnp.stack(slots)  1.72 us
    slice x1, local copies, waits for them, and re-layouts, local(): part = parts[:, :, h].reshape(ntm, blocks * rows, width)  1.32 us
  transfers between devices with their start and end apart: 12, of which 3 were waited for; matrix products, arithmetic and copies ran while one was open for 12% of the time, Pallas kernels for 18%

profile of v13, /device:TPU:0, one launch (start us, length us, event | category | flops | bytes accessed | tf_op | source)
XLA Modules:
  0.0 49.0 jit_solution(7995454268563612901)
XLA Ops:
  0.0 0.0 copy-start.2
  0.0 0.0 copy-start.1
  0.0 1.3 %fusion.28 = (bf16[4,2,1,64,512]{4,3,2,1,0:T(8,128)(2,1)S(1)}, bf16[4,2,1,64,512]{4,3,2,1,0:T(8,128)(2,1)S(1)}) fusion(bf16[4,2,2,64,512]{4,3,2,1,0:T(8,128)(2,1)} %bitcast.88), kind=kLoop, calls=%fused_computation.72 | loop fusion | bytes 2097152 | tf_op jit(solution)/shard_map/slice | solution.py:145
  1.4 2.4 %collective-permute-start.2 = (bf16[128,512]{1,0:T(8,128)(2,1)S(1)}, bf16[128,512]{1,0:T(8,128)(2,1)S(1)}, u32[]{:S(2)}, u32[]{:S(2)}) collective-permute-start(bf16[128,512]{1,0:T(8,128)(2,1)S(1)} %get-tuple-element.16), channel_id=1, source_target_pairs={{0,3},{1,0},{2,1},{3,2},{4,7},{5,4},{6,5},{7,6},{8,11},{9,8},{10,9... | collective-permute-start | bytes 393224 | tf_op jit(solution)/shard_map/ppermute | solution.py:151
  3.8 0.6 %collective-permute-start.1 = (bf16[128,512]{1,0:T(8,128)(2,1)S(1)}, bf16[128,512]{1,0:T(8,128)(2,1)S(1)}, u32[]{:S(2)}, u32[]{:S(2)}) collective-permute-start(bf16[128,512]{1,0:T(8,128)(2,1)S(1)} %get-tuple-element.17), channel_id=1, source_target_pairs={{0,2},{1,3},{2,0},{3,1},{4,6},{5,7},{6,4},{7,5},{8,10},{9,11},{10,... | collective-permute-start | bytes 393224 | tf_op jit(solution)/shard_map/ppermute | solution.py:151
  4.5 0.2 collective-permute-start
  4.6 0.0 copy-done.2
  4.7 0.0 copy-done.1
  4.8 0.7 %constant_dynamic-slice_fusion.3 = (s32[1,1,1,1]{2,3,1,0:T(1,128)}, s32[1,1,1,1]{2,3,1,0:T(1,128)}, s32[1,1,1,1]{2,3,1,0:T(1,128)}, s32[1,1,1,1]{2,3,1,0:T(1,128)}) fusion(s32[1,1,4,1]{2,3,1,0:T(1,128)S(1)} %copy-done.1, s32[]{:T(128)S(6)} %select_n.190, s32[]{:T(128)S(6)} %select_n.194, s32[]{:T(128)S(6)} %select_n.202, s32[]{:T(128)S(6)} %select_n.198), kind=kLoop, calls=%fused_computation.55 | loop fusion | bytes 48 | tf_op jit(solution)/shard_map/jit(dynamic_index_in_dim)/dynamic_slice | solution.py:160
  8.0 0.0 collective-permute-done.2
  8.0 3.4 %collective-permute-done.1 = bf16[128,512]{1,0:T(8,128)(2,1)S(1)} collective-permute-done((bf16[128,512]{1,0:T(8,128)(2,1)S(1)}, bf16[128,512]{1,0:T(8,128)(2,1)S(1)}, u32[]{:S(2)}, u32[]{:S(2)}) %collective-permute-start.1) | collective-permute-done | bytes 131104 | tf_op jit(solution)/shard_map/ppermute | solution.py:151
  11.4 0.0 collective-permute-done
  11.4 0.9 %pad_maximum_fusion.1.x_ref = bf16[4,128,512]{2,1,0:T(8,128)(2,1)} fusion(bf16[1,128,512]{2,1,0:T(8,128)(2,1)S(1)} %bitcast.89, bf16[1,128,512]{2,1,0:T(8,128)(2,1)S(1)} %bitcast.90, bf16[1,128,512]{2,1,0:T(8,128)(2,1)S(1)} %bitcast.91, bf16[1,128,512]{2,1,0:T(8,128)(2,1)S(1)} %get-tuple-element.15), kind=kLoop, calls=%fused_computation.31 | loop fusion | flops 786432 | bytes 1048576 | tf_op jit(solution)/shard_map/stack | solution.py:152
  12.3 0.1 collective-permute-start.5
  12.3 1.7 %collective-permute-start.4 = (bf16[128,512]{1,0:T(8,128)(2,1)S(1)}, bf16[128,512]{1,0:T(8,128)(2,1)S(1)}, u32[]{:S(2)}, u32[]{:S(2)}) collective-permute-start(bf16[128,512]{1,0:T(8,128)(2,1)S(1)} %get-tuple-element.13), channel_id=1, source_target_pairs={{0,2},{1,3},{2,0},{3,1},{4,6},{5,7},{6,4},{7,5},{8,10},{9,11},{10,... | collective-permute-start | bytes 393224 | tf_op jit(solution)/shard_map/ppermute | solution.py:151
  14.0 0.2 collective-permute-start.3
  14.2 4.3 %shard_map.91 = bf16[128,1024]{1,0:T(8,128)(2,1)} custom-call(s32[1]{0:T(128)} %bitcast.1.pos_ref, bf16[4,128,512]{2,1,0:T(8,128)(2,1)} %pad_maximum_fusion.1.x_ref, bf16[384,256]{1,0:T(8,128)(2,1)} %constant.142.clone.band_ref, bf16[1024,1024]{1,0:T(8,128)(2,1)} %constant.143.clone.tab_ref, bf16[512,512]{1,0:T(8,128)(2,1)} %constant.144.clone.grp_ref), custom_call_target="tpu_custom_call" | custom-call | flops 1073741824 | bytes 2883584 | tf_op jit(solution)/shard_map/pallas_call | solution.py:121
  18.5 1.0 %select_bitcast_fusion.1 = (bf16[1,1,64,1024]{3,2,1,0:T(8,128)(2,1)S(1)}, bf16[64,1024]{1,0:T(8,128)(2,1)S(1)}, bf16[64,1024]{1,0:T(8,128)(2,1)S(1)}, bf16[64,1024]{1,0:T(8,128)(2,1)S(1)}) fusion(pred[]{:T(512)} %bitcast.24, bf16[128,1024]{1,0:T(8,128)(2,1)} %shard_map.91, pred[]{:T(512)} %bitcast.28, pred[]{:T(512)} %bitcast.30, pred[]{:T(512)} %bitcast.26), kind=kLoop, calls=%fused_computation.38 | loop fusion | flops 262144 | bytes 786436 | tf_op jit(solution)/shard_map/stack;stack | solution.py:168
  19.5 3.7 %collective-permute-start.8 = (bf16[64,1024]{1,0:T(8,128)(2,1)S(1)}, bf16[64,1024]{1,0:T(8,128)(2,1)S(1)}, u32[]{:S(2)}, u32[]{:S(2)}) collective-permute-start(bf16[64,1024]{1,0:T(8,128)(2,1)S(1)} %get-tuple-element.21), channel_id=1, source_target_pairs={{0,12},{4,0},{8,4},{12,8},{1,13},{5,1},{9,5},{13,9},{2,14},{6,2},{... | collective-permute-start | bytes 393224 | tf_op jit(solution)/shard_map/ppermute | solution.py:165
  23.2 0.0 collective-permute-start.7
  23.2 0.0 collective-permute-done.5
  23.2 1.0 %collective-permute-start.6 = (bf16[64,1024]{1,0:T(8,128)(2,1)S(1)}, bf16[64,1024]{1,0:T(8,128)(2,1)S(1)}, u32[]{:S(2)}, u32[]{:S(2)}) collective-permute-start(bf16[64,1024]{1,0:T(8,128)(2,1)S(1)} %get-tuple-element.22), channel_id=1, source_target_pairs={{0,4},{4,8},{8,12},{12,0},{1,5},{5,9},{9,13},{13,1},{2,6},{6,10},{... | collective-permute-start | bytes 393224 | tf_op jit(solution)/shard_map/ppermute | solution.py:165
  24.2 0.0 collective-permute-done.4
  24.2 0.0 collective-permute-done.3
  24.2 0.9 %pad_maximum_fusion.2.x_ref = bf16[4,128,512]{2,1,0:T(8,128)(2,1)} fusion(bf16[1,128,512]{2,1,0:T(8,128)(2,1)S(1)} %bitcast.92, bf16[1,128,512]{2,1,0:T(8,128)(2,1)S(1)} %bitcast.93, bf16[1,128,512]{2,1,0:T(8,128)(2,1)S(1)} %bitcast.94, bf16[1,128,512]{2,1,0:T(8,128)(2,1)S(1)} %get-tuple-element.11), kind=kLoop, calls=%fused_computation.32 | loop fusion | flops 786432 | bytes 1048576 | tf_op jit(solution)/shard_map/stack | solution.py:152
  25.0 0.0 copy-start
  25.0 4.3 %shard_map.92 = bf16[128,1024]{1,0:T(8,128)(2,1)} custom-call(s32[1]{0:T(128)} %bitcast.1.pos_ref, bf16[4,128,512]{2,1,0:T(8,128)(2,1)} %pad_maximum_fusion.2.x_ref, bf16[384,256]{1,0:T(8,128)(2,1)} %constant.142.clone.band_ref, bf16[1024,1024]{1,0:T(8,128)(2,1)} %constant.143.clone.tab_ref, bf16[512,512]{1,0:T(8,128)(2,1)} %constant.144.clone.grp_ref), custom_call_target="tpu_custom_call" | custom-call | flops 1073741824 | bytes 2883584 | tf_op jit(solution)/shard_map/pallas_call | solution.py:121
  29.3 1.0 %select_bitcast_fusion = (bf16[1,1,64,1024]{3,2,1,0:T(8,128)(2,1)S(1)}, bf16[64,1024]{1,0:T(8,128)(2,1)S(1)}, bf16[64,1024]{1,0:T(8,128)(2,1)S(1)}, bf16[64,1024]{1,0:T(8,128)(2,1)S(1)}) fusion(pred[]{:T(512)} %bitcast.24, bf16[128,1024]{1,0:T(8,128)(2,1)} %shard_map.92, pred[]{:T(512)} %bitcast.28, pred[]{:T(512)} %bitcast.30, pred[]{:T(512)} %bitcast.26), kind=kLoop, calls=%fused_computation.37 | loop fusion | flops 262144 | bytes 786436 | tf_op jit(solution)/shard_map/stack;stack | solution.py:168
  30.4 2.9 %collective-permute-start.11 = (bf16[64,1024]{1,0:T(8,128)(2,1)S(1)}, bf16[64,1024]{1,0:T(8,128)(2,1)S(1)}, u32[]{:S(2)}, u32[]{:S(2)}) collective-permute-start(bf16[64,1024]{1,0:T(8,128)(2,1)S(1)} %get-tuple-element.25), channel_id=1, source_target_pairs={{0,12},{4,0},{8,4},{12,8},{1,13},{5,1},{9,5},{13,9},{2,14},{6,2},{... | collective-permute-start | bytes 393224 | tf_op jit(solution)/shard_map/ppermute | solution.py:165
  33.2 1.1 %collective-permute-start.10 = (bf16[64,1024]{1,0:T(8,128)(2,1)S(1)}, bf16[64,1024]{1,0:T(8,128)(2,1)S(1)}, u32[]{:S(2)}, u32[]{:S(2)}) collective-permute-start(bf16[64,1024]{1,0:T(8,128)(2,1)S(1)} %get-tuple-element.24), channel_id=1, source_target_pairs={{0,8},{4,12},{8,0},{12,4},{1,9},{5,13},{9,1},{13,5},{2,10},{6,14},... | collective-permute-start | bytes 393224 | tf_op jit(solution)/shard_map/ppermute | solution.py:165
  34.3 0.0 copy-done
  34.3 1.0 %fusion.21 = (bf16[2,128,512]{2,1,0:T(8,128)(2,1)S(1)}, bf16[2,128,512]{2,1,0:T(8,128)(2,1)S(1)}) fusion(bf16[2,64,1024]{2,1,0:T(8,128)(2,1)S(1)} %bitcast.82, bf16[2,64,1024]{2,1,0:T(8,128)(2,1)} %bitcast.84), kind=kLoop, calls=%fused_computation.34 | loop fusion | flops 1179648 | bytes 1048576 | tf_op jit(solution)/shard_map/concatenate | solution.py:169
  35.4 0.0 collective-permute-done.8
  35.4 0.1 collective-permute-start.9
  35.5 1.1 %fusion.19 = (bf16[2,1,128,1024]{3,2,1,0:T(8,128)(2,1)S(1)}, bf16[2,1,128,1024]{3,2,1,0:T(8,128)(2,1)S(1)}) fusion(bf16[2,64,1024]{2,1,0:T(8,128)(2,1)} %bitcast.85, bf16[2,64,1024]{2,1,0:T(8,128)(2,1)S(1)} %bitcast.83, bf16[2,128,512]{2,1,0:T(8,128)(2,1)S(1)} %get-tuple-element.10, bf16[2,128,512]{2,1,0:T(8,128)(2,1)S(1)} %get-tuple-element.9), kind=kLoop, calls=%fused_computation.29 | loop fusion | flops 2097152 | bytes 2097152 | tf_op jit(solution)/shard_map/stack | solution.py:172
  36.5 0.0 collective-permute-done.7
  36.5 0.0 collective-permute-done.6
  36.5 1.6 %collective-permute-done.11 = bf16[64,1024]{1,0:T(8,128)(2,1)S(1)} collective-permute-done((bf16[64,1024]{1,0:T(8,128)(2,1)S(1)}, bf16[64,1024]{1,0:T(8,128)(2,1)S(1)}, u32[]{:S(2)}, u32[]{:S(2)}) %collective-permute-start.11) | collective-permute-done | bytes 131104 | tf_op jit(solution)/shard_map/ppermute | solution.py:165
  38.1 8.4 %collective-permute-done.10 = bf16[64,1024]{1,0:T(8,128)(2,1)S(1)} collective-permute-done((bf16[64,1024]{1,0:T(8,128)(2,1)S(1)}, bf16[64,1024]{1,0:T(8,128)(2,1)S(1)}, u32[]{:S(2)}, u32[]{:S(2)}) %collective-permute-start.10) | collective-permute-done | bytes 131104 | tf_op jit(solution)/shard_map/ppermute | solution.py:165
  46.5 0.0 collective-permute-done.9
  46.5 0.8 %convolution_bitcast_fusion = f32[4,2,2,128,128]{4,3,0,2,1:T(8,128)S(1)} fusion(bf16[2,1,128,1024]{3,2,1,0:T(8,128)(2,1)S(1)} %get-tuple-element.32, bf16[2,1,128,1024]{3,2,1,0:T(8,128)(2,1)S(1)} %get-tuple-element.31, bf16[1,1,64,1024]{3,2,1,0:T(8,128)(2,1)S(1)} %bitcast.98, bf16[1,1,64,1024]{3,2,1,0:T(8,128)(2,1)S(1)} %bitcast.99, ...), kind=kOutput, calls=%fused_computation.1 | convolution fusion | flops 547356672 | bytes 3145728 | tf_op jit(solution)/shard_map/dot_general | solution.py:173
  47.3 0.6 %gather_fusion = f32[4,2,2,128,128]{4,3,2,1,0:T(8,128)S(1)} fusion(f32[4,2,2,128,128]{4,3,0,2,1:T(8,128)S(1)} %convolution_bitcast_fusion, s32[1024]{0:T(1024)S(1)} %pad_clamp_fusion), kind=kCustom, calls=%fused_computation | custom fusion | bytes 2097168 | tf_op jit(solution)/shard_map/jit(_take)/gather | solution.py:176
  47.9 1.0 %fusion.20 = bf16[1,1,4,1,2,2,128,128]{7,6,5,4,3,2,1,0:T(8,128)(2,1)} fusion(f32[4,2,2,128,128]{4,3,2,1,0:T(8,128)S(1)} %gather_fusion, pred[4]{0:T(512)(128)(4,1)S(1)} %compare_and_fusion, pred[4]{0:T(512)(128)(4,1)S(1)} %compare_bitcast_fusion), kind=kLoop, calls=%fused_computation.30 | loop fusion | flops 1048576 | bytes 1572872 | tf_op jit(solution)/shard_map/convert_element_type | solution.py:180
  (6 shorter events, 0.1 us)
Async XLA Ops:
  0.0 4.7 %copy-start.2 = (s32[1,1,4]{2,1,0:T(1,128)S(1)}, s32[1,1,4]{2,1,0:T(1,128)}, u32[]{:S(2)}) copy-start(s32[1,1,4]{2,1,0:T(1,128)} %param.11) | copy-start | bytes 52
  0.0 4.7 %copy-start.1 = (s32[1,1,4,1]{2,3,1,0:T(1,128)S(1)}, s32[1,1,4,1]{2,3,1,0:T(1,128)}, u32[]{:S(2)}) copy-start(s32[1,1,4,1]{2,3,1,0:T(1,128)} %param.10) | copy-start | bytes 52
  1.4 6.6 %collective-permute-start.2 = (bf16[128,512]{1,0:T(8,128)(2,1)S(1)}, bf16[128,512]{1,0:T(8,128)(2,1)S(1)}, u32[]{:S(2)}, u32[]{:S(2)}) collective-permute-start(bf16[128,512]{1,0:T(8,128)(2,1)S(1)} %get-tuple-element.16), channel_id=1, source_target_pairs={{0,3},{1,0},{2,1},{3,2},{4,7},{5,4},{6,5},{7,6},{8,11},{9,8},{10,9... | collective-permute-start | bytes 393224 | tf_op jit(solution)/shard_map/ppermute | solution.py:151
  3.8 7.5 %collective-permute-start.1 = (bf16[128,512]{1,0:T(8,128)(2,1)S(1)}, bf16[128,512]{1,0:T(8,128)(2,1)S(1)}, u32[]{:S(2)}, u32[]{:S(2)}) collective-permute-start(bf16[128,512]{1,0:T(8,128)(2,1)S(1)} %get-tuple-element.17), channel_id=1, source_target_pairs={{0,2},{1,3},{2,0},{3,1},{4,6},{5,7},{6,4},{7,5},{8,10},{9,11},{10,... | collective-permute-start | bytes 393224 | tf_op jit(solution)/shard_map/ppermute | solution.py:151
  4.5 6.9 %collective-permute-start = (bf16[128,512]{1,0:T(8,128)(2,1)S(1)}, bf16[128,512]{1,0:T(8,128)(2,1)S(1)}, u32[]{:S(2)}, u32[]{:S(2)}) collective-permute-start(bf16[128,512]{1,0:T(8,128)(2,1)S(1)} %get-tuple-element.18), channel_id=1, source_target_pairs={{0,1},{1,2},{2,3},{3,0},{4,5},{5,6},{6,7},{7,4},{8,9},{9,10},{10,1... | collective-permute-start | bytes 393224 | tf_op jit(solution)/shard_map/ppermute | solution.py:151
  12.3 10.9 %collective-permute-start.5 = (bf16[128,512]{1,0:T(8,128)(2,1)S(1)}, bf16[128,512]{1,0:T(8,128)(2,1)S(1)}, u32[]{:S(2)}, u32[]{:S(2)}) collective-permute-start(bf16[128,512]{1,0:T(8,128)(2,1)S(1)} %get-tuple-element.12), channel_id=1, source_target_pairs={{0,3},{1,0},{2,1},{3,2},{4,7},{5,4},{6,5},{7,6},{8,11},{9,8},{10,9... | collective-permute-start | bytes 393224 | tf_op jit(solution)/shard_map/ppermute | solution.py:151
  12.3 11.8 %collective-permute-start.4 = (bf16[128,512]{1,0:T(8,128)(2,1)S(1)}, bf16[128,512]{1,0:T(8,128)(2,1)S(1)}, u32[]{:S(2)}, u32[]{:S(2)}) collective-permute-start(bf16[128,512]{1,0:T(8,128)(2,1)S(1)} %get-tuple-element.13), channel_id=1, source_target_pairs={{0,2},{1,3},{2,0},{3,1},{4,6},{5,7},{6,4},{7,5},{8,10},{9,11},{10,... | collective-permute-start | bytes 393224 | tf_op jit(solution)/shard_map/ppermute | solution.py:151
  14.0 10.1 %collective-permute-start.3 = (bf16[128,512]{1,0:T(8,128)(2,1)S(1)}, bf16[128,512]{1,0:T(8,128)(2,1)S(1)}, u32[]{:S(2)}, u32[]{:S(2)}) collective-permute-start(bf16[128,512]{1,0:T(8,128)(2,1)S(1)} %get-tuple-element.14), channel_id=1, source_target_pairs={{0,1},{1,2},{2,3},{3,0},{4,5},{5,6},{6,7},{7,4},{8,9},{9,10},{10,1... | collective-permute-start | bytes 393224 | tf_op jit(solution)/shard_map/ppermute | solution.py:151
  19.5 15.9 %collective-permute-start.8 = (bf16[64,1024]{1,0:T(8,128)(2,1)S(1)}, bf16[64,1024]{1,0:T(8,128)(2,1)S(1)}, u32[]{:S(2)}, u32[]{:S(2)}) collective-permute-start(bf16[64,1024]{1,0:T(8,128)(2,1)S(1)} %get-tuple-element.21), channel_id=1, source_target_pairs={{0,12},{4,0},{8,4},{12,8},{1,13},{5,1},{9,5},{13,9},{2,14},{6,2},{... | collective-permute-start | bytes 393224 | tf_op jit(solution)/shard_map/ppermute | solution.py:165
  23.2 13.4 %collective-permute-start.7 = (bf16[64,1024]{1,0:T(8,128)(2,1)S(1)}, bf16[64,1024]{1,0:T(8,128)(2,1)S(1)}, u32[]{:S(2)}, u32[]{:S(2)}) collective-permute-start(bf16[64,1024]{1,0:T(8,128)(2,1)S(1)} %get-tuple-element.20), channel_id=1, source_target_pairs={{0,8},{4,12},{8,0},{12,4},{1,9},{5,13},{9,1},{13,5},{2,10},{6,14},... | collective-permute-start | bytes 393224 | tf_op jit(solution)/shard_map/ppermute | solution.py:165
  23.2 13.4 %collective-permute-start.6 = (bf16[64,1024]{1,0:T(8,128)(2,1)S(1)}, bf16[64,1024]{1,0:T(8,128)(2,1)S(1)}, u32[]{:S(2)}, u32[]{:S(2)}) collective-permute-start(bf16[64,1024]{1,0:T(8,128)(2,1)S(1)} %get-tuple-element.22), channel_id=1, source_target_pairs={{0,4},{4,8},{8,12},{12,0},{1,5},{5,9},{9,13},{13,1},{2,6},{6,10},{... | collective-permute-start | bytes 393224 | tf_op jit(solution)/shard_map/ppermute | solution.py:165
  25.0 9.3 %copy-start = (bf16[128,1024]{1,0:T(8,128)(2,1)S(1)}, bf16[128,1024]{1,0:T(8,128)(2,1)}, u32[]{:S(2)}) copy-start(bf16[128,1024]{1,0:T(8,128)(2,1)} %shard_map.91) | copy-start | bytes 786436
  30.4 7.8 %collective-permute-start.11 = (bf16[64,1024]{1,0:T(8,128)(2,1)S(1)}, bf16[64,1024]{1,0:T(8,128)(2,1)S(1)}, u32[]{:S(2)}, u32[]{:S(2)}) collective-permute-start(bf16[64,1024]{1,0:T(8,128)(2,1)S(1)} %get-tuple-element.25), channel_id=1, source_target_pairs={{0,12},{4,0},{8,4},{12,8},{1,13},{5,1},{9,5},{13,9},{2,14},{6,2},{... | collective-permute-start | bytes 393224 | tf_op jit(solution)/shard_map/ppermute | solution.py:165
  33.2 13.3 %collective-permute-start.10 = (bf16[64,1024]{1,0:T(8,128)(2,1)S(1)}, bf16[64,1024]{1,0:T(8,128)(2,1)S(1)}, u32[]{:S(2)}, u32[]{:S(2)}) collective-permute-start(bf16[64,1024]{1,0:T(8,128)(2,1)S(1)} %get-tuple-element.24), channel_id=1, source_target_pairs={{0,8},{4,12},{8,0},{12,4},{1,9},{5,13},{9,1},{13,5},{2,10},{6,14},... | collective-permute-start | bytes 393224 | tf_op jit(solution)/shard_map/ppermute | solution.py:165
  35.4 11.2 %collective-permute-start.9 = (bf16[64,1024]{1,0:T(8,128)(2,1)S(1)}, bf16[64,1024]{1,0:T(8,128)(2,1)S(1)}, u32[]{:S(2)}, u32[]{:S(2)}) collective-permute-start(bf16[64,1024]{1,0:T(8,128)(2,1)S(1)} %get-tuple-element.26), channel_id=1, source_target_pairs={{0,4},{4,8},{8,12},{12,0},{1,5},{5,9},{9,13},{13,1},{2,6},{6,10},{... | collective-permute-start | bytes 393224 | tf_op jit(solution)/shard_map/ppermute | solution.py:165

commit v14 on v7

--- a/solution.py
+++ b/solution.py
@@ -75,14 +75,18 @@
         chunk, off = divmod((j % ntile) * TILE, width)
         return x_ref[(pos - chunk + nslot) % nslot, :, off:off + TILE]
 
+    nrows = x_ref.shape[1]
     band = band_ref[...]
     for j in range(ntile):
         win = jnp.concatenate([tile(j - 1), tile(j), tile(j + 1)], axis=1)
         acc = jnp.dot(win, band, preferred_element_type=jnp.float32)
-        filt_ref[:, j * TILE:(j + 1) * TILE] = (acc[:, :TILE] + acc[:, TILE:]).astype(jnp.bfloat16)
-    tab = tab_ref[...]
-    first = jnp.dot(filt_ref[:, :HALF], tab, preferred_element_type=jnp.float32)
-    second = jnp.dot(filt_ref[:, HALF:], tab, preferred_element_type=jnp.float32)
+        half, col = divmod(j * TILE, HALF)
+        filt_ref[half * nrows:(half + 1) * nrows, col:col + TILE] = (acc[:, :TILE] + acc[:, TILE:]).astype(
+            jnp.bfloat16
+        )
+    both = jnp.dot(filt_ref[...], tab_ref[...], preferred_element_type=jnp.float32)
+    first = both[:nrows]
+    second = both[nrows:]
     lane = lax.broadcasted_iota(jnp.int32, first.shape, 1)
     spec = jnp.where(lane % 2 == 0, first + second, first - second)
     re = spec[:, :NBAND]
@@ -90,10 +94,8 @@
     power = re * re + im * im
     p_hi = power.astype(jnp.bfloat16)
     p_lo = (power - p_hi.astype(jnp.float32)).astype(jnp.bfloat16)
-    grp = grp_ref[...]
-    mean = jnp.dot(p_hi, grp, preferred_element_type=jnp.float32) + jnp.dot(
-        p_lo, grp, preferred_element_type=jnp.float32
-    )
+    sums = jnp.dot(jnp.concatenate([p_hi, p_lo], axis=0), grp_ref[...], preferred_element_type=jnp.float32)
+    mean = sums[:nrows] + sums[nrows:]
     level = 1.0 / jnp.sqrt(mean + 1e-06)
     o_ref[:, :NBAND] = (re * level).astype(jnp.bfloat16)
     o_ref[:, NBAND:] = (im * level).astype(jnp.bfloat16)
@@ -114,7 +116,7 @@
             pl.BlockSpec(grp.shape, lambda r, p: (0, 0)),
         ],
         out_specs=pl.BlockSpec((BLOCK, 2 * NBAND), lambda r, p: (r, 0)),
-        scratch_shapes=[pltpu.VMEM((BLOCK, NT), jnp.bfloat16)],
+        scratch_shapes=[pltpu.VMEM((2 * BLOCK, HALF), jnp.bfloat16)],
     )
     flops = 2 * nrows * (3 * TILE * 2 * TILE * (NT // TILE) + NT * 2 * NBAND + 2 * NBAND * NBAND)
     nbytes = rows3.size * 2 + tab.size * 2 + nrows * 2 * NBAND * 2

time: 47.4 us -> 47.4 us (level)
  no operation moved by 1% of the time
where the time goes in v14:
time: 47.4 us; the launch traced here: 46.7 us
  starting transfers between devices  16.8 us (35%)
  Pallas kernels  8.53 us (18%)
  waiting for transfers between devices  8.1 us (17%)
  other arithmetic  6.08 us (13%)
  local copies, waits for them, and re-layouts  3.7 us (8%)
  between operations  2.75 us (6%)
  matrix products  0.74 us (2%)
    ppermute x6, starting transfers between devices, local(): lax.ppermute(blk, 'chan', perm=[(i, (i + d) % peers) for i in range(peers)])  9.49 us
    pallas_call x2, Pallas kernels, spectra(): pl.pallas_call(spectra_kernel, grid_spec=grid_spec, cost_estimate=pl.Cost...  8.53 us
    ppermute x6, starting transfers between devices, local(): lax.ppermute(piece, 'tm', perm=[(i, (i + d) % ntm) for i in range(ntm)])  7.29 us
    ppermute x6, waiting for transfers between devices, local(): lax.ppermute(blk, 'chan', perm=[(i, (i + d) % peers) for i in range(peers)])  5.65 us
    ppermute x6, waiting for transfers between devices, local(): lax.ppermute(piece, 'tm', perm=[(i, (i + d) % ntm) for i in range(ntm)])  2.45 us
    another operation x2, other arithmetic, local(): picked_parts.append(jnp.stack(recv))  2.01 us
    another operation x2, other arithmetic, local(): prev_slots = jnp.stack(slots)  1.72 us
    slice x1, local copies, waits for them, and re-layouts, local(): part = parts[:, :, h].reshape(ntm, blocks * rows, width)  1.32 us
  transfers between devices with their start and end apart: 12, of which 4 were waited for; matrix products, arithmetic and copies ran while one was open for 12% of the time, Pallas kernels for 18%

profile of v14, /device:TPU:0, one launch (start us, length us, event | category | flops | bytes accessed | tf_op | source)
XLA Modules:
  0.0 46.7 jit_solution(9254970012541592979)
XLA Ops:
  0.0 0.0 copy-start.2
  0.0 0.0 copy-start.1
  0.0 1.3 %fusion.27 = (bf16[4,2,1,64,512]{4,3,2,1,0:T(8,128)(2,1)S(1)}, bf16[4,2,1,64,512]{4,3,2,1,0:T(8,128)(2,1)S(1)}) fusion(bf16[4,2,2,64,512]{4,3,2,1,0:T(8,128)(2,1)} %bitcast.82), kind=kLoop, calls=%fused_computation.71 | loop fusion | bytes 2097152 | tf_op jit(solution)/shard_map/slice | solution.py:147
  1.4 2.4 %collective-permute-start.2 = (bf16[128,512]{1,0:T(8,128)(2,1)S(1)}, bf16[128,512]{1,0:T(8,128)(2,1)S(1)}, u32[]{:S(2)}, u32[]{:S(2)}) collective-permute-start(bf16[128,512]{1,0:T(8,128)(2,1)S(1)} %get-tuple-element.16), channel_id=1, source_target_pairs={{0,3},{1,0},{2,1},{3,2},{4,7},{5,4},{6,5},{7,6},{8,11},{9,8},{10,9... | collective-permute-start | bytes 393224 | tf_op jit(solution)/shard_map/ppermute | solution.py:153
  3.8 0.0 collective-permute-start
  3.8 1.1 %collective-permute-start.1 = (bf16[128,512]{1,0:T(8,128)(2,1)S(1)}, bf16[128,512]{1,0:T(8,128)(2,1)S(1)}, u32[]{:S(2)}, u32[]{:S(2)}) collective-permute-start(bf16[128,512]{1,0:T(8,128)(2,1)S(1)} %get-tuple-element.17), channel_id=1, source_target_pairs={{0,2},{1,3},{2,0},{3,1},{4,6},{5,7},{6,4},{7,5},{8,10},{9,11},{10,... | collective-permute-start | bytes 393224 | tf_op jit(solution)/shard_map/ppermute | solution.py:153
  4.9 0.0 copy-done.2
  5.0 0.0 copy-done.1
  5.0 0.7 %constant_dynamic-slice_fusion.5 = (s32[1,1,1,1]{2,3,1,0:T(1,128)}, s32[1,1,1,1]{2,3,1,0:T(1,128)}, s32[1,1,1,1]{2,3,1,0:T(1,128)}, s32[1,1,1,1]{2,3,1,0:T(1,128)}) fusion(s32[1,1,4,1]{2,3,1,0:T(1,128)S(1)} %copy-done.1, s32[]{:T(128)S(6)} %select_n.183, s32[]{:T(128)S(6)} %select_n.194, s32[]{:T(128)S(6)} %select_n.202, s32[]{:T(128)S(6)} %select_n.198), kind=kLoop, calls=%fused_computation.56 | loop fusion | bytes 48 | tf_op jit(solution)/shard_map/jit(dynamic_index_in_dim)/dynamic_slice | solution.py:162
  8.2 0.0 collective-permute-done.2
  8.2 1.4 %collective-permute-done = bf16[128,512]{1,0:T(8,128)(2,1)S(1)} collective-permute-done((bf16[128,512]{1,0:T(8,128)(2,1)S(1)}, bf16[128,512]{1,0:T(8,128)(2,1)S(1)}, u32[]{:S(2)}, u32[]{:S(2)}) %collective-permute-start) | collective-permute-done | bytes 131104 | tf_op jit(solution)/shard_map/ppermute | solution.py:153
  9.6 1.1 %collective-permute-done.1 = bf16[128,512]{1,0:T(8,128)(2,1)S(1)} collective-permute-done((bf16[128,512]{1,0:T(8,128)(2,1)S(1)}, bf16[128,512]{1,0:T(8,128)(2,1)S(1)}, u32[]{:S(2)}, u32[]{:S(2)}) %collective-permute-start.1) | collective-permute-done | bytes 131104 | tf_op jit(solution)/shard_map/ppermute | solution.py:153
  10.7 0.9 %pad_maximum_fusion.1.x_ref = bf16[4,128,512]{2,1,0:T(8,128)(2,1)} fusion(bf16[1,128,512]{2,1,0:T(8,128)(2,1)S(1)} %bitcast.83, bf16[1,128,512]{2,1,0:T(8,128)(2,1)S(1)} %bitcast.85, bf16[1,128,512]{2,1,0:T(8,128)(2,1)S(1)} %bitcast.84, bf16[1,128,512]{2,1,0:T(8,128)(2,1)S(1)} %get-tuple-element.15), kind=kLoop, calls=%fused_computation.30 | loop fusion | flops 786432 | bytes 1048576 | tf_op jit(solution)/shard_map/stack | solution.py:154
  11.6 0.7 %collective-permute-start.6 = (bf16[128,512]{1,0:T(8,128)(2,1)S(1)}, bf16[128,512]{1,0:T(8,128)(2,1)S(1)}, u32[]{:S(2)}, u32[]{:S(2)}) collective-permute-start(bf16[128,512]{1,0:T(8,128)(2,1)S(1)} %get-tuple-element.14), channel_id=1, source_target_pairs={{0,1},{1,2},{2,3},{3,0},{4,5},{5,6},{6,7},{7,4},{8,9},{9,10},{10,1... | collective-permute-start | bytes 393224 | tf_op jit(solution)/shard_map/ppermute | solution.py:153
  12.3 1.7 %collective-permute-start.7 = (bf16[128,512]{1,0:T(8,128)(2,1)S(1)}, bf16[128,512]{1,0:T(8,128)(2,1)S(1)}, u32[]{:S(2)}, u32[]{:S(2)}) collective-permute-start(bf16[128,512]{1,0:T(8,128)(2,1)S(1)} %get-tuple-element.13), channel_id=1, source_target_pairs={{0,2},{1,3},{2,0},{3,1},{4,6},{5,7},{6,4},{7,5},{8,10},{9,11},{10,... | collective-permute-start | bytes 393224 | tf_op jit(solution)/shard_map/ppermute | solution.py:153
  14.0 1.4 %collective-permute-start.8 = (bf16[128,512]{1,0:T(8,128)(2,1)S(1)}, bf16[128,512]{1,0:T(8,128)(2,1)S(1)}, u32[]{:S(2)}, u32[]{:S(2)}) collective-permute-start(bf16[128,512]{1,0:T(8,128)(2,1)S(1)} %get-tuple-element.12), channel_id=1, source_target_pairs={{0,3},{1,0},{2,1},{3,2},{4,7},{5,4},{6,5},{7,6},{8,11},{9,8},{10,9... | collective-permute-start | bytes 393224 | tf_op jit(solution)/shard_map/ppermute | solution.py:153
  15.4 4.3 %shard_map.91 = bf16[128,1024]{1,0:T(8,128)(2,1)} custom-call(s32[1]{0:T(128)} %bitcast.2.pos_ref, bf16[4,128,512]{2,1,0:T(8,128)(2,1)} %pad_maximum_fusion.1.x_ref, bf16[384,256]{1,0:T(8,128)(2,1)} %constant.142.clone.band_ref, bf16[1024,1024]{1,0:T(8,128)(2,1)} %constant.143.clone.tab_ref, bf16[512,512]{1,0:T(8,128)(2,1)} %constant.144.clone.grp_ref), custom_call_target="tpu_custom_call" | custom-call | flops 1073741824 | bytes 2883584 | tf_op jit(solution)/shard_map/pallas_call | solution.py:123
  19.6 1.0 %select_bitcast_fusion.1 = (bf16[1,1,64,1024]{3,2,1,0:T(8,128)(2,1)S(1)}, bf16[64,1024]{1,0:T(8,128)(2,1)S(1)}, bf16[64,1024]{1,0:T(8,128)(2,1)S(1)}, bf16[64,1024]{1,0:T(8,128)(2,1)S(1)}) fusion(pred[]{:T(512)} %bitcast.1, bf16[128,1024]{1,0:T(8,128)(2,1)} %shard_map.91, pred[]{:T(512)} %bitcast.14, pred[]{:T(512)} %bitcast.16, pred[]{:T(512)} %bitcast.12), kind=kLoop, calls=%fused_computation.40 | loop fusion | flops 262144 | bytes 786436 | tf_op jit(solution)/shard_map/stack;stack | solution.py:170
  20.6 1.6 %collective-permute-start.3 = (bf16[64,1024]{1,0:T(8,128)(2,1)S(1)}, bf16[64,1024]{1,0:T(8,128)(2,1)S(1)}, u32[]{:S(2)}, u32[]{:S(2)}) collective-permute-start(bf16[64,1024]{1,0:T(8,128)(2,1)S(1)} %get-tuple-element.22), channel_id=1, source_target_pairs={{0,4},{4,8},{8,12},{12,0},{1,5},{5,9},{9,13},{13,1},{2,6},{6,10},{... | collective-permute-start | bytes 393224 | tf_op jit(solution)/shard_map/ppermute | solution.py:167
  22.3 2.6 %collective-permute-start.4 = (bf16[64,1024]{1,0:T(8,128)(2,1)S(1)}, bf16[64,1024]{1,0:T(8,128)(2,1)S(1)}, u32[]{:S(2)}, u32[]{:S(2)}) collective-permute-start(bf16[64,1024]{1,0:T(8,128)(2,1)S(1)} %get-tuple-element.20), channel_id=1, source_target_pairs={{0,8},{4,12},{8,0},{12,4},{1,9},{5,13},{9,1},{13,5},{2,10},{6,14},... | collective-permute-start | bytes 393224 | tf_op jit(solution)/shard_map/ppermute | solution.py:167
  24.9 0.0 collective-permute-done.6
  24.9 1.3 %collective-permute-start.5 = (bf16[64,1024]{1,0:T(8,128)(2,1)S(1)}, bf16[64,1024]{1,0:T(8,128)(2,1)S(1)}, u32[]{:S(2)}, u32[]{:S(2)}) collective-permute-start(bf16[64,1024]{1,0:T(8,128)(2,1)S(1)} %get-tuple-element.21), channel_id=1, source_target_pairs={{0,12},{4,0},{8,4},{12,8},{1,13},{5,1},{9,5},{13,9},{2,14},{6,2},{... | collective-permute-start | bytes 393224 | tf_op jit(solution)/shard_map/ppermute | solution.py:167
  26.2 0.0 collective-permute-done.7
  26.2 0.0 collective-permute-done.8
  26.2 0.9 %pad_maximum_fusion.2.x_ref = bf16[4,128,512]{2,1,0:T(8,128)(2,1)} fusion(bf16[1,128,512]{2,1,0:T(8,128)(2,1)S(1)} %bitcast.88, bf16[1,128,512]{2,1,0:T(8,128)(2,1)S(1)} %bitcast.87, bf16[1,128,512]{2,1,0:T(8,128)(2,1)S(1)} %bitcast.86, bf16[1,128,512]{2,1,0:T(8,128)(2,1)S(1)} %get-tuple-element.11), kind=kLoop, calls=%fused_computation.31 | loop fusion | flops 786432 | bytes 1048576 | tf_op jit(solution)/shard_map/stack | solution.py:154
  27.1 0.0 copy-start
  27.1 4.3 %shard_map.92 = bf16[128,1024]{1,0:T(8,128)(2,1)} custom-call(s32[1]{0:T(128)} %bitcast.2.pos_ref, bf16[4,128,512]{2,1,0:T(8,128)(2,1)} %pad_maximum_fusion.2.x_ref, bf16[384,256]{1,0:T(8,128)(2,1)} %constant.142.clone.band_ref, bf16[1024,1024]{1,0:T(8,128)(2,1)} %constant.143.clone.tab_ref, bf16[512,512]{1,0:T(8,128)(2,1)} %constant.144.clone.grp_ref), custom_call_target="tpu_custom_call" | custom-call | flops 1073741824 | bytes 2883584 | tf_op jit(solution)/shard_map/pallas_call | solution.py:123
  31.4 1.0 %select_bitcast_fusion = (bf16[1,1,64,1024]{3,2,1,0:T(8,128)(2,1)S(1)}, bf16[64,1024]{1,0:T(8,128)(2,1)S(1)}, bf16[64,1024]{1,0:T(8,128)(2,1)S(1)}, bf16[64,1024]{1,0:T(8,128)(2,1)S(1)}) fusion(pred[]{:T(512)} %bitcast.1, bf16[128,1024]{1,0:T(8,128)(2,1)} %shard_map.92, pred[]{:T(512)} %bitcast.14, pred[]{:T(512)} %bitcast.16, pred[]{:T(512)} %bitcast.12), kind=kLoop, calls=%fused_computation.36 | loop fusion | flops 262144 | bytes 786436 | tf_op jit(solution)/shard_map/stack;stack | solution.py:170
  32.4 0.7 %collective-permute-start.9 = (bf16[64,1024]{1,0:T(8,128)(2,1)S(1)}, bf16[64,1024]{1,0:T(8,128)(2,1)S(1)}, u32[]{:S(2)}, u32[]{:S(2)}) collective-permute-start(bf16[64,1024]{1,0:T(8,128)(2,1)S(1)} %get-tuple-element.26), channel_id=1, source_target_pairs={{0,4},{4,8},{8,12},{12,0},{1,5},{5,9},{9,13},{13,1},{2,6},{6,10},{... | collective-permute-start | bytes 393224 | tf_op jit(solution)/shard_map/ppermute | solution.py:167
  33.1 0.3 collective-permute-start.10
  33.4 0.0 copy-done
  33.4 1.0 %fusion.20 = (bf16[2,128,512]{2,1,0:T(8,128)(2,1)S(1)}, bf16[2,128,512]{2,1,0:T(8,128)(2,1)S(1)}) fusion(bf16[2,64,1024]{2,1,0:T(8,128)(2,1)S(1)} %bitcast.76, bf16[2,64,1024]{2,1,0:T(8,128)(2,1)} %bitcast.78), kind=kLoop, calls=%fused_computation.33 | loop fusion | flops 1179648 | bytes 1048576 | tf_op jit(solution)/shard_map/concatenate | solution.py:171
  34.5 0.0 collective-permute-done.3
  34.5 2.9 %collective-permute-start.11 = (bf16[64,1024]{1,0:T(8,128)(2,1)S(1)}, bf16[64,1024]{1,0:T(8,128)(2,1)S(1)}, u32[]{:S(2)}, u32[]{:S(2)}) collective-permute-start(bf16[64,1024]{1,0:T(8,128)(2,1)S(1)} %get-tuple-element.25), channel_id=1, source_target_pairs={{0,12},{4,0},{8,4},{12,8},{1,13},{5,1},{9,5},{13,9},{2,14},{6,2},{... | collective-permute-start | bytes 393224 | tf_op jit(solution)/shard_map/ppermute | solution.py:167
  37.3 1.0 %fusion.19 = (bf16[2,1,128,1024]{3,2,1,0:T(8,128)(2,1)S(1)}, bf16[2,1,128,1024]{3,2,1,0:T(8,128)(2,1)S(1)}) fusion(bf16[2,64,1024]{2,1,0:T(8,128)(2,1)} %bitcast.79, bf16[2,64,1024]{2,1,0:T(8,128)(2,1)S(1)} %bitcast.77, bf16[2,128,512]{2,1,0:T(8,128)(2,1)S(1)} %get-tuple-element.10, bf16[2,128,512]{2,1,0:T(8,128)(2,1)S(1)} %get-tuple-element.9), kind=kLoop, calls=%fused_computation.29 | loop fusion | flops 2097152 | bytes 2097152 | tf_op jit(solution)/shard_map/stack | solution.py:174
  38.4 0.0 collective-permute-done.4
  38.4 0.0 collective-permute-done.5
  38.4 2.3 %collective-permute-done.9 = bf16[64,1024]{1,0:T(8,128)(2,1)S(1)} collective-permute-done((bf16[64,1024]{1,0:T(8,128)(2,1)S(1)}, bf16[64,1024]{1,0:T(8,128)(2,1)S(1)}, u32[]{:S(2)}, u32[]{:S(2)}) %collective-permute-start.9) | collective-permute-done | bytes 131104 | tf_op jit(solution)/shard_map/ppermute | solution.py:167
  40.7 3.3 %collective-permute-done.10 = bf16[64,1024]{1,0:T(8,128)(2,1)S(1)} collective-permute-done((bf16[64,1024]{1,0:T(8,128)(2,1)S(1)}, bf16[64,1024]{1,0:T(8,128)(2,1)S(1)}, u32[]{:S(2)}, u32[]{:S(2)}) %collective-permute-start.10) | collective-permute-done | bytes 131104 | tf_op jit(solution)/shard_map/ppermute | solution.py:167
  44.1 0.0 collective-permute-done.11
  44.1 0.7 %convolution_bitcast_fusion = f32[4,2,2,128,128]{3,4,2,1,0:T(8,128)S(1)} fusion(bf16[1,1,64,1024]{3,2,1,0:T(8,128)(2,1)S(1)} %bitcast.94, bf16[1,1,64,1024]{3,2,1,0:T(8,128)(2,1)S(1)} %bitcast.93, bf16[1,1,64,1024]{3,2,1,0:T(8,128)(2,1)S(1)} %bitcast.92, bf16[1,1,64,1024]{3,2,1,0:T(8,128)(2,1)S(1)} %get-tuple-element.23, ...), kind=kOutput, calls=%fused_computation.1 | convolution fusion | flops 547356672 | bytes 3145728 | tf_op jit(solution)/shard_map/lrif,dkjf->dklrij/dot_general | solution.py:175
  44.8 0.6 %gather_fusion = f32[4,2,2,128,128]{3,4,2,1,0:T(8,128)S(1)} fusion(f32[4,2,2,128,128]{3,4,2,1,0:T(8,128)S(1)} %convolution_bitcast_fusion, s32[1024]{0:T(1024)S(1)} %pad_clamp_fusion), kind=kCustom, calls=%fused_computation | custom fusion | bytes 2097168 | tf_op jit(solution)/shard_map/jit(_take)/gather | solution.py:177
  45.4 0.2 fusion.18
  45.7 1.0 %copy.13 = bf16[1,1,4,1,2,2,128,128]{7,6,5,4,3,2,1,0:T(8,128)(2,1)} copy(bf16[1,1,4,1,2,2,128,128]{6,7,5,4,2,3,1,0:T(8,128)(2,1)S(1)} %fusion.18) | data formatting | bytes 1048576 | tf_op jit(solution)/shard_map/convert_element_type | solution.py:181
  (6 shorter events, 0.1 us)
Async XLA Ops:
  0.0 4.9 %copy-start.2 = (s32[1,1,4]{2,1,0:T(1,128)S(1)}, s32[1,1,4]{2,1,0:T(1,128)}, u32[]{:S(2)}) copy-start(s32[1,1,4]{2,1,0:T(1,128)} %param.11) | copy-start | bytes 52
  0.0 5.0 %copy-start.1 = (s32[1,1,4,1]{2,3,1,0:T(1,128)S(1)}, s32[1,1,4,1]{2,3,1,0:T(1,128)}, u32[]{:S(2)}) copy-start(s32[1,1,4,1]{2,3,1,0:T(1,128)} %param.10) | copy-start | bytes 52
  1.4 6.8 %collective-permute-start.2 = (bf16[128,512]{1,0:T(8,128)(2,1)S(1)}, bf16[128,512]{1,0:T(8,128)(2,1)S(1)}, u32[]{:S(2)}, u32[]{:S(2)}) collective-permute-start(bf16[128,512]{1,0:T(8,128)(2,1)S(1)} %get-tuple-element.16), channel_id=1, source_target_pairs={{0,3},{1,0},{2,1},{3,2},{4,7},{5,4},{6,5},{7,6},{8,11},{9,8},{10,9... | collective-permute-start | bytes 393224 | tf_op jit(solution)/shard_map/ppermute | solution.py:153
  3.8 5.8 %collective-permute-start = (bf16[128,512]{1,0:T(8,128)(2,1)S(1)}, bf16[128,512]{1,0:T(8,128)(2,1)S(1)}, u32[]{:S(2)}, u32[]{:S(2)}) collective-permute-start(bf16[128,512]{1,0:T(8,128)(2,1)S(1)} %get-tuple-element.18), channel_id=1, source_target_pairs={{0,1},{1,2},{2,3},{3,0},{4,5},{5,6},{6,7},{7,4},{8,9},{9,10},{10,1... | collective-permute-start | bytes 393224 | tf_op jit(solution)/shard_map/ppermute | solution.py:153
  3.8 6.8 %collective-permute-start.1 = (bf16[128,512]{1,0:T(8,128)(2,1)S(1)}, bf16[128,512]{1,0:T(8,128)(2,1)S(1)}, u32[]{:S(2)}, u32[]{:S(2)}) collective-permute-start(bf16[128,512]{1,0:T(8,128)(2,1)S(1)} %get-tuple-element.17), channel_id=1, source_target_pairs={{0,2},{1,3},{2,0},{3,1},{4,6},{5,7},{6,4},{7,5},{8,10},{9,11},{10,... | collective-permute-start | bytes 393224 | tf_op jit(solution)/shard_map/ppermute | solution.py:153
  11.6 13.3 %collective-permute-start.6 = (bf16[128,512]{1,0:T(8,128)(2,1)S(1)}, bf16[128,512]{1,0:T(8,128)(2,1)S(1)}, u32[]{:S(2)}, u32[]{:S(2)}) collective-permute-start(bf16[128,512]{1,0:T(8,128)(2,1)S(1)} %get-tuple-element.14), channel_id=1, source_target_pairs={{0,1},{1,2},{2,3},{3,0},{4,5},{5,6},{6,7},{7,4},{8,9},{9,10},{10,1... | collective-permute-start | bytes 393224 | tf_op jit(solution)/shard_map/ppermute | solution.py:153
  12.3 13.9 %collective-permute-start.7 = (bf16[128,512]{1,0:T(8,128)(2,1)S(1)}, bf16[128,512]{1,0:T(8,128)(2,1)S(1)}, u32[]{:S(2)}, u32[]{:S(2)}) collective-permute-start(bf16[128,512]{1,0:T(8,128)(2,1)S(1)} %get-tuple-element.13), channel_id=1, source_target_pairs={{0,2},{1,3},{2,0},{3,1},{4,6},{5,7},{6,4},{7,5},{8,10},{9,11},{10,... | collective-permute-start | bytes 393224 | tf_op jit(solution)/shard_map/ppermute | solution.py:153
  14.0 12.2 %collective-permute-start.8 = (bf16[128,512]{1,0:T(8,128)(2,1)S(1)}, bf16[128,512]{1,0:T(8,128)(2,1)S(1)}, u32[]{:S(2)}, u32[]{:S(2)}) collective-permute-start(bf16[128,512]{1,0:T(8,128)(2,1)S(1)} %get-tuple-element.12), channel_id=1, source_target_pairs={{0,3},{1,0},{2,1},{3,2},{4,7},{5,4},{6,5},{7,6},{8,11},{9,8},{10,9... | collective-permute-start | bytes 393224 | tf_op jit(solution)/shard_map/ppermute | solution.py:153
  20.6 13.8 %collective-permute-start.3 = (bf16[64,1024]{1,0:T(8,128)(2,1)S(1)}, bf16[64,1024]{1,0:T(8,128)(2,1)S(1)}, u32[]{:S(2)}, u32[]{:S(2)}) collective-permute-start(bf16[64,1024]{1,0:T(8,128)(2,1)S(1)} %get-tuple-element.22), channel_id=1, source_target_pairs={{0,4},{4,8},{8,12},{12,0},{1,5},{5,9},{9,13},{13,1},{2,6},{6,10},{... | collective-permute-start | bytes 393224 | tf_op jit(solution)/shard_map/ppermute | solution.py:167
  22.3 16.1 %collective-permute-start.4 = (bf16[64,1024]{1,0:T(8,128)(2,1)S(1)}, bf16[64,1024]{1,0:T(8,128)(2,1)S(1)}, u32[]{:S(2)}, u32[]{:S(2)}) collective-permute-start(bf16[64,1024]{1,0:T(8,128)(2,1)S(1)} %get-tuple-element.20), channel_id=1, source_target_pairs={{0,8},{4,12},{8,0},{12,4},{1,9},{5,13},{9,1},{13,5},{2,10},{6,14},... | collective-permute-start | bytes 393224 | tf_op jit(solution)/shard_map/ppermute | solution.py:167
  24.9 13.5 %collective-permute-start.5 = (bf16[64,1024]{1,0:T(8,128)(2,1)S(1)}, bf16[64,1024]{1,0:T(8,128)(2,1)S(1)}, u32[]{:S(2)}, u32[]{:S(2)}) collective-permute-start(bf16[64,1024]{1,0:T(8,128)(2,1)S(1)} %get-tuple-element.21), channel_id=1, source_target_pairs={{0,12},{4,0},{8,4},{12,8},{1,13},{5,1},{9,5},{13,9},{2,14},{6,2},{... | collective-permute-start | bytes 393224 | tf_op jit(solution)/shard_map/ppermute | solution.py:167
  27.1 6.4 %copy-start = (bf16[128,1024]{1,0:T(8,128)(2,1)S(1)}, bf16[128,1024]{1,0:T(8,128)(2,1)}, u32[]{:S(2)}) copy-start(bf16[128,1024]{1,0:T(8,128)(2,1)} %shard_map.91) | copy-start | bytes 786436
  32.4 8.4 %collective-permute-start.9 = (bf16[64,1024]{1,0:T(8,128)(2,1)S(1)}, bf16[64,1024]{1,0:T(8,128)(2,1)S(1)}, u32[]{:S(2)}, u32[]{:S(2)}) collective-permute-start(bf16[64,1024]{1,0:T(8,128)(2,1)S(1)} %get-tuple-element.26), channel_id=1, source_target_pairs={{0,4},{4,8},{8,12},{12,0},{1,5},{5,9},{9,13},{13,1},{2,6},{6,10},{... | collective-permute-start | bytes 393224 | tf_op jit(solution)/shard_map/ppermute | solution.py:167
  33.1 11.0 %collective-permute-start.10 = (bf16[64,1024]{1,0:T(8,128)(2,1)S(1)}, bf16[64,1024]{1,0:T(8,128)(2,1)S(1)}, u32[]{:S(2)}, u32[]{:S(2)}) collective-permute-start(bf16[64,1024]{1,0:T(8,128)(2,1)S(1)} %get-tuple-element.24), channel_id=1, source_target_pairs={{0,8},{4,12},{8,0},{12,4},{1,9},{5,13},{9,1},{13,5},{2,10},{6,14},... | collective-permute-start | bytes 393224 | tf_op jit(solution)/shard_map/ppermute | solution.py:167
  34.5 9.6 %collective-permute-start.11 = (bf16[64,1024]{1,0:T(8,128)(2,1)S(1)}, bf16[64,1024]{1,0:T(8,128)(2,1)S(1)}, u32[]{:S(2)}, u32[]{:S(2)}) collective-permute-start(bf16[64,1024]{1,0:T(8,128)(2,1)S(1)} %get-tuple-element.25), channel_id=1, source_target_pairs={{0,12},{4,0},{8,4},{12,8},{1,13},{5,1},{9,5},{13,9},{2,14},{6,2},{... | collective-permute-start | bytes 393224 | tf_op jit(solution)/shard_map/ppermute | solution.py:167

commit v15 on v14

--- a/solution.py
+++ b/solution.py
@@ -1,3 +1,4 @@
+import functools
 import math
 
 import jax
@@ -66,24 +67,29 @@
     return ((g[:, None] == g[None, :]).astype(np.float32) / SUBW).astype(BF16)
 
 
-def spectra_kernel(pos_ref, x_ref, band_ref, tab_ref, grp_ref, o_ref, filt_ref):
-    nslot, _, width = x_ref.shape
+def spectra_kernel(pos_ref, *refs):
+    nslot = len(refs) - 5
+    x_refs = refs[:nslot]
+    band_ref, tab_ref, grp_ref, o_ref, filt_ref = refs[nslot:]
+    nrows, width = x_refs[0].shape
     ntile = NT // TILE
-    pos = pos_ref[0]
 
-    def tile(j):
-        chunk, off = divmod((j % ntile) * TILE, width)
-        return x_ref[(pos - chunk + nslot) % nslot, :, off:off + TILE]
+    def filter_at(here):
+        def tile(j):
+            chunk, off = divmod((j % ntile) * TILE, width)
+            return x_refs[(here - chunk) % nslot][:, off:off + TILE]
 
-    nrows = x_ref.shape[1]
-    band = band_ref[...]
-    for j in range(ntile):
-        win = jnp.concatenate([tile(j - 1), tile(j), tile(j + 1)], axis=1)
-        acc = jnp.dot(win, band, preferred_element_type=jnp.float32)
-        half, col = divmod(j * TILE, HALF)
-        filt_ref[half * nrows:(half + 1) * nrows, col:col + TILE] = (acc[:, :TILE] + acc[:, TILE:]).astype(
-            jnp.bfloat16
-        )
+        band = band_ref[...]
+        for j in range(ntile):
+            win = jnp.concatenate([tile(j - 1), tile(j), tile(j + 1)], axis=1)
+            acc = jnp.dot(win, band, preferred_element_type=jnp.float32)
+            half, col = divmod(j * TILE, HALF)
+            filt_ref[half * nrows:(half + 1) * nrows, col:col + TILE] = (acc[:, :TILE] + acc[:, TILE:]).astype(
+                jnp.bfloat16
+            )
+
+    for here in range(nslot):
+        pl.when(pos_ref[0] == here)(functools.partial(filter_at, here))
     both = jnp.dot(filt_ref[...], tab_ref[...], preferred_element_type=jnp.float32)
     first = both[:nrows]
     second = both[nrows:]
@@ -101,31 +107,32 @@
     o_ref[:, NBAND:] = (im * level).astype(jnp.bfloat16)
 
 
-def spectra(pos, rows3):
-    ntm, nrows, width = rows3.shape
+def spectra(pos, slots):
+    ntm = len(slots)
+    nrows, width = slots[0].shape
     band = jnp.asarray(band_matrix())
     tab = jnp.asarray(dft_top())
     grp = jnp.asarray(group_matrix())
     grid_spec = pltpu.PrefetchScalarGridSpec(
         num_scalar_prefetch=1,
-        grid=(nrows // BLOCK,),
-        in_specs=[
-            pl.BlockSpec((ntm, BLOCK, width), lambda r, p: (0, r, 0)),
+        grid=(1,),
+        in_specs=[pl.BlockSpec((nrows, width), lambda r, p: (0, 0))] * ntm
+        + [
             pl.BlockSpec(band.shape, lambda r, p: (0, 0)),
             pl.BlockSpec(tab.shape, lambda r, p: (0, 0)),
             pl.BlockSpec(grp.shape, lambda r, p: (0, 0)),
         ],
-        out_specs=pl.BlockSpec((BLOCK, 2 * NBAND), lambda r, p: (r, 0)),
-        scratch_shapes=[pltpu.VMEM((2 * BLOCK, HALF), jnp.bfloat16)],
+        out_specs=pl.BlockSpec((nrows, 2 * NBAND), lambda r, p: (0, 0)),
+        scratch_shapes=[pltpu.VMEM((2 * nrows, HALF), jnp.bfloat16)],
     )
     flops = 2 * nrows * (3 * TILE * 2 * TILE * (NT // TILE) + NT * 2 * NBAND + 2 * NBAND * NBAND)
-    nbytes = rows3.size * 2 + tab.size * 2 + nrows * 2 * NBAND * 2
+    nbytes = ntm * nrows * width * 2 + tab.size * 2 + nrows * 2 * NBAND * 2
     return pl.pallas_call(
         spectra_kernel,
         grid_spec=grid_spec,
         cost_estimate=pl.CostEstimate(flops=flops, transcendentals=nrows * NBAND, bytes_accessed=nbytes),
         out_shape=jax.ShapeDtypeStruct((nrows, 2 * NBAND), jnp.bfloat16),
-    )(pos, rows3, band, tab, grp)
+    )(pos, *slots, band, tab, grp)
 
 
 def local(raw, send_blocks, pair_count):
@@ -151,8 +158,8 @@
         for d in range(1, ntm):
             piece = lax.dynamic_index_in_dim(part, (here + d) % ntm, axis=0, keepdims=False)
             slots.append(lax.ppermute(piece, "tm", perm=[(i, (i + d) % ntm) for i in range(ntm)]))
-        prev_slots = jnp.stack(slots)
-        whitened = spectra(pos, prev_slots).reshape(blocks, rows, 2 * NBAND)
+        prev_slots = tuple(slots)
+        whitened = spectra(pos, slots).reshape(blocks, rows, 2 * NBAND)
         own_parts.append(whitened)
         recv = []
         for d in range(peers):

time: 47.4 us -> 47.7 us (level)
  local copies, waits for them, and re-layouts: 3.7 us -> 5.75 us
  other arithmetic: 6.08 us -> 4.36 us
  starting transfers between devices: 16.8 us -> 16.2 us
    another operation x2 -> x0, other arithmetic: 1.72 us -> none  [local(): prev_slots = jnp.stack(slots)]
    squeeze x0 -> x2, local copies, waits for them, and re-layouts: none -> 1.41 us  [local(): lax.dynamic_index_in_dim(part, (here + d) % ntm, axis=0, keepdims=False)]
    ppermute x6, waiting for transfers between devices: 2.45 us -> 1.18 us  [local(): lax.ppermute(piece, 'tm', perm=[(i, (i + d) % ntm) for i in range(ntm)])]
    ppermute x6, waiting for transfers between devices: 5.65 us -> 6.9 us  [local(): lax.ppermute(blk, 'chan', perm=[(i, (i + d) % peers) for i in range(peers)])]
    unnamed x6 -> x18, local copies, waits for them, and re-layouts: 0.01 us -> 0.72 us
    ppermute x6, starting transfers between devices: 7.29 us -> 6.71 us  [local(): lax.ppermute(piece, 'tm', perm=[(i, (i + d) % ntm) for i in range(ntm)])]
  transfers between devices with their start and end apart: 12 -> 12, of which waited for: 4 -> 3; matrix products, arithmetic and copies ran while one was open for 12% -> 10% of each run, Pallas kernels for 18% -> 19%
where the time goes in v15:
time: 47.7 us; the launch traced here: 47 us
  starting transfers between devices  16.2 us (34%)
  Pallas kernels  8.94 us (19%)
  waiting for transfers between devices  8.08 us (17%)
  local copies, waits for them, and re-layouts  5.75 us (12%)
  other arithmetic  4.36 us (9%)
  between operations  2.89 us (6%)
  matrix products  0.74 us (2%)
    ppermute x6, starting transfers between devices, local(): lax.ppermute(blk, 'chan', perm=[(i, (i + d) % peers) for i in range(peers)])  9.49 us
    pallas_call x2, Pallas kernels, spectra(): pl.pallas_call(spectra_kernel, grid_spec=grid_spec, cost_estimate=pl.Cost...  8.94 us
    ppermute x6, waiting for transfers between devices, local(): lax.ppermute(blk, 'chan', perm=[(i, (i + d) % peers) for i in range(peers)])  6.9 us
    ppermute x6, starting transfers between devices, local(): lax.ppermute(piece, 'tm', perm=[(i, (i + d) % ntm) for i in range(ntm)])  6.71 us
    another operation x2, other arithmetic, local(): picked_parts.append(jnp.stack(recv))  2.01 us
    squeeze x2, local copies, waits for them, and re-layouts, local(): lax.dynamic_index_in_dim(part, (here + d) % ntm, axis=0, keepdims=False)  1.41 us
    slice x1, local copies, waits for them, and re-layouts, local(): part = parts[:, :, h].reshape(ntm, blocks * rows, width)  1.32 us
    ppermute x6, waiting for transfers between devices, local(): lax.ppermute(piece, 'tm', perm=[(i, (i + d) % ntm) for i in range(ntm)])  1.18 us
  transfers between devices with their start and end apart: 12, of which 3 were waited for; matrix products, arithmetic and copies ran while one was open for 10% of the time, Pallas kernels for 19%

profile of v15, /device:TPU:0, one launch (start us, length us, event | category | flops | bytes accessed | tf_op | source)
XLA Modules:
  0.0 47.0 jit_solution(7098398376304369902)
XLA Ops:
  0.0 1.3 %fusion.27 = (bf16[4,2,1,64,512]{4,3,2,1,0:T(8,128)(2,1)S(1)}, bf16[4,2,1,64,512]{4,3,2,1,0:T(8,128)(2,1)S(1)}) fusion(bf16[4,2,2,64,512]{4,3,2,1,0:T(8,128)(2,1)} %bitcast.76), kind=kLoop, calls=%fused_computation.69 | loop fusion | bytes 2097152 | tf_op jit(solution)/shard_map/slice | solution.py:154
  1.3 0.7 %dynamic-slice_bitcast_fusion.4 = (bf16[128,512]{1,0:T(8,128)(2,1)S(1)}, bf16[128,512]{1,0:T(8,128)(2,1)S(1)}, bf16[128,512]{1,0:T(8,128)(2,1)S(1)}, bf16[128,512]{1,0:T(8,128)(2,1)}) fusion(bf16[4,128,512]{2,1,0:T(8,128)(2,1)S(1)} %bitcast.75, s32[]{:T(128)S(6)} %select_n.191, s32[]{:T(128)S(6)} %select_n.189, s32[]{:T(128)S(6)} %select_n.187, s32[]{:T(128)S(6)} %select_n.185), kind=kLoop, calls=%fused_computation.40 | loop fusion | bytes 1048592 | tf_op jit(solution)/shard_map/jit(dynamic_index_in_dim)/squeeze | solution.py:159
  2.1 0.5 collective-permute-start
  2.5 2.5 %collective-permute-start.1 = (bf16[128,512]{1,0:T(8,128)(2,1)S(1)}, bf16[128,512]{1,0:T(8,128)(2,1)S(1)}, u32[]{:S(2)}, u32[]{:S(2)}) collective-permute-start(bf16[128,512]{1,0:T(8,128)(2,1)S(1)} %get-tuple-element.16), channel_id=1, source_target_pairs={{0,2},{1,3},{2,0},{3,1},{4,6},{5,7},{6,4},{7,5},{8,10},{9,11},{10,... | collective-permute-start | bytes 393224 | tf_op jit(solution)/shard_map/ppermute | solution.py:160
  5.0 1.4 %collective-permute-start.2 = (bf16[128,512]{1,0:T(8,128)(2,1)S(1)}, bf16[128,512]{1,0:T(8,128)(2,1)S(1)}, u32[]{:S(2)}, u32[]{:S(2)}) collective-permute-start(bf16[128,512]{1,0:T(8,128)(2,1)S(1)} %get-tuple-element.15), channel_id=1, source_target_pairs={{0,3},{1,0},{2,1},{3,2},{4,7},{5,4},{6,5},{7,6},{8,11},{9,8},{10,9... | collective-permute-start | bytes 393224 | tf_op jit(solution)/shard_map/ppermute | solution.py:160
  6.5 0.0 copy-done.8
  6.6 0.0 copy-done.1
  6.6 0.7 %constant_dynamic-slice_fusion.3 = (s32[1,1,1,1]{2,3,1,0:T(1,128)}, s32[1,1,1,1]{2,3,1,0:T(1,128)}, s32[1,1,1,1]{2,3,1,0:T(1,128)}, s32[1,1,1,1]{2,3,1,0:T(1,128)}) fusion(s32[1,1,4,1]{2,3,1,0:T(1,128)S(1)} %copy-done.1, s32[]{:T(128)S(6)} %select_n.183, s32[]{:T(128)S(6)} %select_n.194, s32[]{:T(128)S(6)} %select_n.202, s32[]{:T(128)S(6)} %select_n.198), kind=kLoop, calls=%fused_computation.54 | loop fusion | bytes 48 | tf_op jit(solution)/shard_map/jit(dynamic_index_in_dim)/dynamic_slice | solution.py:169
  9.9 0.0 collective-permute-done.refs_1_
  9.9 0.0 copy-start.2
  9.9 0.0 collective-permute-done.1.refs_2_
  9.9 0.0 copy-start.3
  9.9 1.2 %collective-permute-done.2.refs_3_ = bf16[128,512]{1,0:T(8,128)(2,1)S(1)} collective-permute-done((bf16[128,512]{1,0:T(8,128)(2,1)S(1)}, bf16[128,512]{1,0:T(8,128)(2,1)S(1)}, u32[]{:S(2)}, u32[]{:S(2)}) %collective-permute-start.2) | collective-permute-done | bytes 131104 | tf_op jit(solution)/shard_map/ppermute | solution.py:160
  11.1 0.7 %dynamic-slice_bitcast_fusion = (bf16[128,512]{1,0:T(8,128)(2,1)S(1)}, bf16[128,512]{1,0:T(8,128)(2,1)S(1)}, bf16[128,512]{1,0:T(8,128)(2,1)S(1)}, bf16[128,512]{1,0:T(8,128)(2,1)}) fusion(bf16[4,128,512]{2,1,0:T(8,128)(2,1)S(1)} %bitcast.74, s32[]{:T(128)S(6)} %select_n.191, s32[]{:T(128)S(6)} %select_n.189, s32[]{:T(128)S(6)} %select_n.187, s32[]{:T(128)S(6)} %select_n.185), kind=kLoop, calls=%fused_computation.35 | loop fusion | bytes 1048592 | tf_op jit(solution)/shard_map/jit(dynamic_index_in_dim)/squeeze | solution.py:159
  11.8 0.0 collective-permute-start.6
  11.8 2.3 %collective-permute-start.7 = (bf16[128,512]{1,0:T(8,128)(2,1)S(1)}, bf16[128,512]{1,0:T(8,128)(2,1)S(1)}, u32[]{:S(2)}, u32[]{:S(2)}) collective-permute-start(bf16[128,512]{1,0:T(8,128)(2,1)S(1)} %get-tuple-element.12), channel_id=1, source_target_pairs={{0,2},{1,3},{2,0},{3,1},{4,6},{5,7},{6,4},{7,5},{8,10},{9,11},{10,... | collective-permute-start | bytes 393224 | tf_op jit(solution)/shard_map/ppermute | solution.py:160
  14.1 0.0 collective-permute-start.8
  14.1 0.0 copy-done.2
  14.1 0.0 copy-done.3
  14.1 0.0 copy-done.4
  14.1 4.5 %shard_map.91 = bf16[128,1024]{1,0:T(8,128)(2,1)} custom-call(s32[1]{0:T(128)} %bitcast.2.pos_ref, bf16[128,512]{1,0:T(8,128)(2,1)} %get-tuple-element.18.refs_0_, bf16[128,512]{1,0:T(8,128)(2,1)} %copy-done.2, bf16[128,512]{1,0:T(8,128)(2,1)} %copy-done.3, bf16[128,512]{1,0:T(8,128)(2,1)} %copy-done.4, bf16[384,256]{1,0:T(8,128)(2,1)} %constant.142.clone.refs_4_, ...), custom_call_target="tpu_custom_call" | custom-call | flops 1073741824 | bytes 2883584 | tf_op jit(solution)/shard_map/pallas_call | solution.py:130
  18.6 1.0 %select_bitcast_fusion.1 = (bf16[1,1,64,1024]{3,2,1,0:T(8,128)(2,1)S(1)}, bf16[64,1024]{1,0:T(8,128)(2,1)S(1)}, bf16[64,1024]{1,0:T(8,128)(2,1)S(1)}, bf16[64,1024]{1,0:T(8,128)(2,1)S(1)}) fusion(pred[]{:T(512)} %bitcast.1, bf16[128,1024]{1,0:T(8,128)(2,1)} %shard_map.91, pred[]{:T(512)} %bitcast.12, pred[]{:T(512)} %bitcast.14, pred[]{:T(512)} %bitcast.10), kind=kLoop, calls=%fused_computation.39 | loop fusion | flops 262144 | bytes 786436 | tf_op jit(solution)/shard_map/stack;stack | solution.py:177
  19.6 1.6 %collective-permute-start.3 = (bf16[64,1024]{1,0:T(8,128)(2,1)S(1)}, bf16[64,1024]{1,0:T(8,128)(2,1)S(1)}, u32[]{:S(2)}, u32[]{:S(2)}) collective-permute-start(bf16[64,1024]{1,0:T(8,128)(2,1)S(1)} %get-tuple-element.22), channel_id=1, source_target_pairs={{0,4},{4,8},{8,12},{12,0},{1,5},{5,9},{9,13},{13,1},{2,6},{6,10},{... | collective-permute-start | bytes 393224 | tf_op jit(solution)/shard_map/ppermute | solution.py:174
  21.2 2.6 %collective-permute-start.4 = (bf16[64,1024]{1,0:T(8,128)(2,1)S(1)}, bf16[64,1024]{1,0:T(8,128)(2,1)S(1)}, u32[]{:S(2)}, u32[]{:S(2)}) collective-permute-start(bf16[64,1024]{1,0:T(8,128)(2,1)S(1)} %get-tuple-element.20), channel_id=1, source_target_pairs={{0,8},{4,12},{8,0},{12,4},{1,9},{5,13},{9,1},{13,5},{2,10},{6,14},... | collective-permute-start | bytes 393224 | tf_op jit(solution)/shard_map/ppermute | solution.py:174
  23.8 0.0 collective-permute-done.6.refs_1_
  23.8 1.3 %collective-permute-start.5 = (bf16[64,1024]{1,0:T(8,128)(2,1)S(1)}, bf16[64,1024]{1,0:T(8,128)(2,1)S(1)}, u32[]{:S(2)}, u32[]{:S(2)}) collective-permute-start(bf16[64,1024]{1,0:T(8,128)(2,1)S(1)} %get-tuple-element.21), channel_id=1, source_target_pairs={{0,12},{4,0},{8,4},{12,8},{1,13},{5,1},{9,5},{13,9},{2,14},{6,2},{... | collective-permute-start | bytes 393224 | tf_op jit(solution)/shard_map/ppermute | solution.py:174
  25.2 0.0 collective-permute-done.7.refs_2_
  25.2 0.0 collective-permute-done.8.refs_3_
  25.2 0.0 copy-start.7
  25.2 0.6 %copy-done.6 = bf16[128,512]{1,0:T(8,128)(2,1)} copy-done((bf16[128,512]{1,0:T(8,128)(2,1)}, bf16[128,512]{1,0:T(8,128)(2,1)S(1)}, u32[]{:S(2)}) %copy-start.6) | copy-done | bytes 131096
  25.8 0.1 copy-done.7
  25.9 4.5 %shard_map.92 = bf16[128,1024]{1,0:T(8,128)(2,1)} custom-call(s32[1]{0:T(128)} %bitcast.2.pos_ref, bf16[128,512]{1,0:T(8,128)(2,1)} %get-tuple-element.14.refs_0_, bf16[128,512]{1,0:T(8,128)(2,1)} %copy-done.5, bf16[128,512]{1,0:T(8,128)(2,1)} %copy-done.6, bf16[128,512]{1,0:T(8,128)(2,1)} %copy-done.7, bf16[384,256]{1,0:T(8,128)(2,1)} %constant.142.clone.refs_4_, ...), custom_call_target="tpu_custom_call" | custom-call | flops 1073741824 | bytes 2883584 | tf_op jit(solution)/shard_map/pallas_call | solution.py:130
  30.4 1.0 %select_bitcast_fusion = (bf16[1,1,64,1024]{3,2,1,0:T(8,128)(2,1)S(1)}, bf16[64,1024]{1,0:T(8,128)(2,1)S(1)}, bf16[64,1024]{1,0:T(8,128)(2,1)S(1)}, bf16[64,1024]{1,0:T(8,128)(2,1)S(1)}) fusion(pred[]{:T(512)} %bitcast.1, bf16[128,1024]{1,0:T(8,128)(2,1)} %shard_map.92, pred[]{:T(512)} %bitcast.12, pred[]{:T(512)} %bitcast.14, pred[]{:T(512)} %bitcast.10), kind=kLoop, calls=%fused_computation.34 | loop fusion | flops 262144 | bytes 786436 | tf_op jit(solution)/shard_map/stack;stack | solution.py:177
  31.4 0.7 %collective-permute-start.9 = (bf16[64,1024]{1,0:T(8,128)(2,1)S(1)}, bf16[64,1024]{1,0:T(8,128)(2,1)S(1)}, u32[]{:S(2)}, u32[]{:S(2)}) collective-permute-start(bf16[64,1024]{1,0:T(8,128)(2,1)S(1)} %get-tuple-element.26), channel_id=1, source_target_pairs={{0,4},{4,8},{8,12},{12,0},{1,5},{5,9},{9,13},{13,1},{2,6},{6,10},{... | collective-permute-start | bytes 393224 | tf_op jit(solution)/shard_map/ppermute | solution.py:174
  32.1 0.3 collective-permute-start.10
  32.5 1.0 %fusion.20 = (bf16[2,128,512]{2,1,0:T(8,128)(2,1)S(1)}, bf16[2,128,512]{2,1,0:T(8,128)(2,1)S(1)}) fusion(bf16[2,64,1024]{2,1,0:T(8,128)(2,1)S(1)} %bitcast.70, bf16[2,64,1024]{2,1,0:T(8,128)(2,1)} %bitcast.72), kind=kLoop, calls=%fused_computation.31 | loop fusion | flops 1179648 | bytes 1048576 | tf_op jit(solution)/shard_map/concatenate | solution.py:178
  33.5 0.0 collective-permute-done.3
  33.5 2.9 %collective-permute-start.11 = (bf16[64,1024]{1,0:T(8,128)(2,1)S(1)}, bf16[64,1024]{1,0:T(8,128)(2,1)S(1)}, u32[]{:S(2)}, u32[]{:S(2)}) collective-permute-start(bf16[64,1024]{1,0:T(8,128)(2,1)S(1)} %get-tuple-element.25), channel_id=1, source_target_pairs={{0,12},{4,0},{8,4},{12,8},{1,13},{5,1},{9,5},{13,9},{2,14},{6,2},{... | collective-permute-start | bytes 393224 | tf_op jit(solution)/shard_map/ppermute | solution.py:174
  36.4 1.0 %fusion.19 = (bf16[2,1,128,1024]{3,2,1,0:T(8,128)(2,1)S(1)}, bf16[2,1,128,1024]{3,2,1,0:T(8,128)(2,1)S(1)}) fusion(bf16[2,64,1024]{2,1,0:T(8,128)(2,1)} %bitcast.73, bf16[2,64,1024]{2,1,0:T(8,128)(2,1)S(1)} %bitcast.71, bf16[2,128,512]{2,1,0:T(8,128)(2,1)S(1)} %get-tuple-element.10, bf16[2,128,512]{2,1,0:T(8,128)(2,1)S(1)} %get-tuple-element.9), kind=kLoop, calls=%fused_computation.29 | loop fusion | flops 2097152 | bytes 2097152 | tf_op jit(solution)/shard_map/stack | solution.py:181
  37.4 0.0 collective-permute-done.4
  37.4 0.0 collective-permute-done.5
  37.4 2.3 %collective-permute-done.9 = bf16[64,1024]{1,0:T(8,128)(2,1)S(1)} collective-permute-done((bf16[64,1024]{1,0:T(8,128)(2,1)S(1)}, bf16[64,1024]{1,0:T(8,128)(2,1)S(1)}, u32[]{:S(2)}, u32[]{:S(2)}) %collective-permute-start.9) | collective-permute-done | bytes 131104 | tf_op jit(solution)/shard_map/ppermute | solution.py:174
  39.7 4.6 %collective-permute-done.10 = bf16[64,1024]{1,0:T(8,128)(2,1)S(1)} collective-permute-done((bf16[64,1024]{1,0:T(8,128)(2,1)S(1)}, bf16[64,1024]{1,0:T(8,128)(2,1)S(1)}, u32[]{:S(2)}, u32[]{:S(2)}) %collective-permute-start.10) | collective-permute-done | bytes 131104 | tf_op jit(solution)/shard_map/ppermute | solution.py:174
  44.3 0.0 collective-permute-done.11
  44.3 0.7 %convolution_bitcast_fusion = f32[4,2,2,128,128]{3,4,2,1,0:T(8,128)S(1)} fusion(bf16[1,1,64,1024]{3,2,1,0:T(8,128)(2,1)S(1)} %bitcast.82, bf16[1,1,64,1024]{3,2,1,0:T(8,128)(2,1)S(1)} %bitcast.81, bf16[1,1,64,1024]{3,2,1,0:T(8,128)(2,1)S(1)} %bitcast.80, bf16[1,1,64,1024]{3,2,1,0:T(8,128)(2,1)S(1)} %get-tuple-element.23, ...), kind=kOutput, calls=%fused_computation.1 | convolution fusion | flops 547356672 | bytes 3145728 | tf_op jit(solution)/shard_map/lrif,dkjf->dklrij/dot_general | solution.py:182
  45.1 0.6 %gather_fusion = f32[4,2,2,128,128]{3,4,2,1,0:T(8,128)S(1)} fusion(f32[4,2,2,128,128]{3,4,2,1,0:T(8,128)S(1)} %convolution_bitcast_fusion, s32[1024]{0:T(1024)S(1)} %pad_clamp_fusion), kind=kCustom, calls=%fused_computation | custom fusion | bytes 2097168 | tf_op jit(solution)/shard_map/jit(_take)/gather | solution.py:184
  45.7 0.2 fusion.18
  45.9 1.0 %copy.11 = bf16[1,1,4,1,2,2,128,128]{7,6,5,4,3,2,1,0:T(8,128)(2,1)} copy(bf16[1,1,4,1,2,2,128,128]{6,7,5,4,2,3,1,0:T(8,128)(2,1)S(1)} %fusion.18) | data formatting | bytes 1048576 | tf_op jit(solution)/shard_map/convert_element_type | solution.py:188
  (12 shorter events, 0.1 us)
Async XLA Ops:
  0.0 6.5 %copy-start.8 = (s32[1,1,4]{2,1,0:T(1,128)S(1)}, s32[1,1,4]{2,1,0:T(1,128)}, u32[]{:S(2)}) copy-start(s32[1,1,4]{2,1,0:T(1,128)} %param.11) | copy-start | bytes 52
  0.0 6.6 %copy-start.1 = (s32[1,1,4,1]{2,3,1,0:T(1,128)S(1)}, s32[1,1,4,1]{2,3,1,0:T(1,128)}, u32[]{:S(2)}) copy-start(s32[1,1,4,1]{2,3,1,0:T(1,128)} %param.10) | copy-start | bytes 52
  2.1 7.9 %collective-permute-start = (bf16[128,512]{1,0:T(8,128)(2,1)S(1)}, bf16[128,512]{1,0:T(8,128)(2,1)S(1)}, u32[]{:S(2)}, u32[]{:S(2)}) collective-permute-start(bf16[128,512]{1,0:T(8,128)(2,1)S(1)} %get-tuple-element.17), channel_id=1, source_target_pairs={{0,1},{1,2},{2,3},{3,0},{4,5},{5,6},{6,7},{7,4},{8,9},{9,10},{10,1... | collective-permute-start | bytes 393224 | tf_op jit(solution)/shard_map/ppermute | solution.py:160
  2.5 7.4 %collective-permute-start.1 = (bf16[128,512]{1,0:T(8,128)(2,1)S(1)}, bf16[128,512]{1,0:T(8,128)(2,1)S(1)}, u32[]{:S(2)}, u32[]{:S(2)}) collective-permute-start(bf16[128,512]{1,0:T(8,128)(2,1)S(1)} %get-tuple-element.16), channel_id=1, source_target_pairs={{0,2},{1,3},{2,0},{3,1},{4,6},{5,7},{6,4},{7,5},{8,10},{9,11},{10,... | collective-permute-start | bytes 393224 | tf_op jit(solution)/shard_map/ppermute | solution.py:160
  5.0 6.1 %collective-permute-start.2 = (bf16[128,512]{1,0:T(8,128)(2,1)S(1)}, bf16[128,512]{1,0:T(8,128)(2,1)S(1)}, u32[]{:S(2)}, u32[]{:S(2)}) collective-permute-start(bf16[128,512]{1,0:T(8,128)(2,1)S(1)} %get-tuple-element.15), channel_id=1, source_target_pairs={{0,3},{1,0},{2,1},{3,2},{4,7},{5,4},{6,5},{7,6},{8,11},{9,8},{10,9... | collective-permute-start | bytes 393224 | tf_op jit(solution)/shard_map/ppermute | solution.py:160
  9.9 4.2 %copy-start.2 = (bf16[128,512]{1,0:T(8,128)(2,1)}, bf16[128,512]{1,0:T(8,128)(2,1)S(1)}, u32[]{:S(2)}) copy-start(bf16[128,512]{1,0:T(8,128)(2,1)S(1)} %collective-permute-done.refs_1_) | copy-start | bytes 393220
  9.9 4.2 %copy-start.3 = (bf16[128,512]{1,0:T(8,128)(2,1)}, bf16[128,512]{1,0:T(8,128)(2,1)S(1)}, u32[]{:S(2)}) copy-start(bf16[128,512]{1,0:T(8,128)(2,1)S(1)} %collective-permute-done.1.refs_2_) | copy-start | bytes 393220
  11.1 3.0 %copy-start.4 = (bf16[128,512]{1,0:T(8,128)(2,1)}, bf16[128,512]{1,0:T(8,128)(2,1)S(1)}, u32[]{:S(2)}) copy-start(bf16[128,512]{1,0:T(8,128)(2,1)S(1)} %collective-permute-done.2.refs_3_) | copy-start | bytes 393220
  11.8 12.0 %collective-permute-start.6 = (bf16[128,512]{1,0:T(8,128)(2,1)S(1)}, bf16[128,512]{1,0:T(8,128)(2,1)S(1)}, u32[]{:S(2)}, u32[]{:S(2)}) collective-permute-start(bf16[128,512]{1,0:T(8,128)(2,1)S(1)} %get-tuple-element.13), channel_id=1, source_target_pairs={{0,1},{1,2},{2,3},{3,0},{4,5},{5,6},{6,7},{7,4},{8,9},{9,10},{10,1... | collective-permute-start | bytes 393224 | tf_op jit(solution)/shard_map/ppermute | solution.py:160
  11.8 13.4 %collective-permute-start.7 = (bf16[128,512]{1,0:T(8,128)(2,1)S(1)}, bf16[128,512]{1,0:T(8,128)(2,1)S(1)}, u32[]{:S(2)}, u32[]{:S(2)}) collective-permute-start(bf16[128,512]{1,0:T(8,128)(2,1)S(1)} %get-tuple-element.12), channel_id=1, source_target_pairs={{0,2},{1,3},{2,0},{3,1},{4,6},{5,7},{6,4},{7,5},{8,10},{9,11},{10,... | collective-permute-start | bytes 393224 | tf_op jit(solution)/shard_map/ppermute | solution.py:160
  14.1 11.1 %collective-permute-start.8 = (bf16[128,512]{1,0:T(8,128)(2,1)S(1)}, bf16[128,512]{1,0:T(8,128)(2,1)S(1)}, u32[]{:S(2)}, u32[]{:S(2)}) collective-permute-start(bf16[128,512]{1,0:T(8,128)(2,1)S(1)} %get-tuple-element.11), channel_id=1, source_target_pairs={{0,3},{1,0},{2,1},{3,2},{4,7},{5,4},{6,5},{7,6},{8,11},{9,8},{10,9... | collective-permute-start | bytes 393224 | tf_op jit(solution)/shard_map/ppermute | solution.py:160
  19.6 13.9 %collective-permute-start.3 = (bf16[64,1024]{1,0:T(8,128)(2,1)S(1)}, bf16[64,1024]{1,0:T(8,128)(2,1)S(1)}, u32[]{:S(2)}, u32[]{:S(2)}) collective-permute-start(bf16[64,1024]{1,0:T(8,128)(2,1)S(1)} %get-tuple-element.22), channel_id=1, source_target_pairs={{0,4},{4,8},{8,12},{12,0},{1,5},{5,9},{9,13},{13,1},{2,6},{6,10},{... | collective-permute-start | bytes 393224 | tf_op jit(solution)/shard_map/ppermute | solution.py:174
  21.2 16.2 %collective-permute-start.4 = (bf16[64,1024]{1,0:T(8,128)(2,1)S(1)}, bf16[64,1024]{1,0:T(8,128)(2,1)S(1)}, u32[]{:S(2)}, u32[]{:S(2)}) collective-permute-start(bf16[64,1024]{1,0:T(8,128)(2,1)S(1)} %get-tuple-element.20), channel_id=1, source_target_pairs={{0,8},{4,12},{8,0},{12,4},{1,9},{5,13},{9,1},{13,5},{2,10},{6,14},... | collective-permute-start | bytes 393224 | tf_op jit(solution)/shard_map/ppermute | solution.py:174
  23.8 1.4 %copy-start.5 = (bf16[128,512]{1,0:T(8,128)(2,1)}, bf16[128,512]{1,0:T(8,128)(2,1)S(1)}, u32[]{:S(2)}) copy-start(bf16[128,512]{1,0:T(8,128)(2,1)S(1)} %collective-permute-done.6.refs_1_) | copy-start | bytes 393220
  23.8 13.6 %collective-permute-start.5 = (bf16[64,1024]{1,0:T(8,128)(2,1)S(1)}, bf16[64,1024]{1,0:T(8,128)(2,1)S(1)}, u32[]{:S(2)}, u32[]{:S(2)}) collective-permute-start(bf16[64,1024]{1,0:T(8,128)(2,1)S(1)} %get-tuple-element.21), channel_id=1, source_target_pairs={{0,12},{4,0},{8,4},{12,8},{1,13},{5,1},{9,5},{13,9},{2,14},{6,2},{... | collective-permute-start | bytes 393224 | tf_op jit(solution)/shard_map/ppermute | solution.py:174
  25.2 0.7 %copy-start.6 = (bf16[128,512]{1,0:T(8,128)(2,1)}, bf16[128,512]{1,0:T(8,128)(2,1)S(1)}, u32[]{:S(2)}) copy-start(bf16[128,512]{1,0:T(8,128)(2,1)S(1)} %collective-permute-done.7.refs_2_) | copy-start | bytes 393220
  25.2 0.7 %copy-start.7 = (bf16[128,512]{1,0:T(8,128)(2,1)}, bf16[128,512]{1,0:T(8,128)(2,1)S(1)}, u32[]{:S(2)}) copy-start(bf16[128,512]{1,0:T(8,128)(2,1)S(1)} %collective-permute-done.8.refs_3_) | copy-start | bytes 393220
  25.9 6.5 %copy-start = (bf16[128,1024]{1,0:T(8,128)(2,1)S(1)}, bf16[128,1024]{1,0:T(8,128)(2,1)}, u32[]{:S(2)}) copy-start(bf16[128,1024]{1,0:T(8,128)(2,1)} %shard_map.91) | copy-start | bytes 786436
  31.4 8.3 %collective-permute-start.9 = (bf16[64,1024]{1,0:T(8,128)(2,1)S(1)}, bf16[64,1024]{1,0:T(8,128)(2,1)S(1)}, u32[]{:S(2)}, u32[]{:S(2)}) collective-permute-start(bf16[64,1024]{1,0:T(8,128)(2,1)S(1)} %get-tuple-element.26), channel_id=1, source_target_pairs={{0,4},{4,8},{8,12},{12,0},{1,5},{5,9},{9,13},{13,1},{2,6},{6,10},{... | collective-permute-start | bytes 393224 | tf_op jit(solution)/shard_map/ppermute | solution.py:174
  32.1 12.2 %collective-permute-start.10 = (bf16[64,1024]{1,0:T(8,128)(2,1)S(1)}, bf16[64,1024]{1,0:T(8,128)(2,1)S(1)}, u32[]{:S(2)}, u32[]{:S(2)}) collective-permute-start(bf16[64,1024]{1,0:T(8,128)(2,1)S(1)} %get-tuple-element.24), channel_id=1, source_target_pairs={{0,8},{4,12},{8,0},{12,4},{1,9},{5,13},{9,1},{13,5},{2,10},{6,14},... | collective-permute-start | bytes 393224 | tf_op jit(solution)/shard_map/ppermute | solution.py:174
  33.5 10.8 %collective-permute-start.11 = (bf16[64,1024]{1,0:T(8,128)(2,1)S(1)}, bf16[64,1024]{1,0:T(8,128)(2,1)S(1)}, u32[]{:S(2)}, u32[]{:S(2)}) collective-permute-start(bf16[64,1024]{1,0:T(8,128)(2,1)S(1)} %get-tuple-element.25), channel_id=1, source_target_pairs={{0,12},{4,0},{8,4},{12,8},{1,13},{5,1},{9,5},{13,9},{2,14},{6,2},{... | collective-permute-start | bytes 393224 | tf_op jit(solution)/shard_map/ppermute | solution.py:174

commit v16 on v14

--- a/solution.py
+++ b/solution.py
@@ -170,9 +170,10 @@
         picked_parts.append(jnp.stack(recv))
     whitened = jnp.concatenate(own_parts, axis=1)
     picked = jnp.concatenate(picked_parts, axis=2)
-    turned = jnp.concatenate([whitened[..., NBAND:], -whitened[..., :NBAND]], axis=-1)
-    paired = jnp.stack([whitened, turned], axis=1)
-    result = jnp.einsum("lrif,dkjf->dklrij", paired, picked, preferred_element_type=jnp.float32)
+    pair = lambda x, y: jnp.einsum("lif,dkjf->dklij", x, y, preferred_element_type=jnp.float32)
+    real = pair(whitened, picked)
+    imag = pair(whitened[..., NBAND:], picked[..., :NBAND]) - pair(whitened[..., :NBAND], picked[..., NBAND:])
+    result = jnp.stack([real, imag], axis=3)
     order = (mine - jnp.arange(peers, dtype=jnp.int32)) % peers
     result = jnp.take(result, order, axis=0)
     result = result * (1.0 / math.sqrt(NBAND))

time: 47.4 us -> 47.9 us (1.011)
  waiting for transfers between devices: 8.1 us -> 10.3 us
  other arithmetic: 6.08 us -> 4.22 us
    ppermute x6, waiting for transfers between devices: 5.65 us -> 7.74 us  [local(): lax.ppermute(blk, 'chan', perm=[(i, (i + d) % peers) for i in range(peers)])]
    another operation x1, other arithmetic: 1.05 us -> 0.07 us  [local(): result = jnp.stack([real, imag], axis=3)]
    concatenate x1, other arithmetic: 1.02 us -> 0.08 us  [local(): picked = jnp.concatenate(picked_parts, axis=2)]
    dot_general x1 -> x3, matrix products: 0.74 us -> 1.14 us  [local(): jnp.einsum('lif,dkjf->dklij', x, y, preferred_element_type=jnp.float32)]
  transfers between devices with their start and end apart: 12 -> 12, of which waited for: 4 -> 4; matrix products, arithmetic and copies ran while one was open for 12% -> 8% of each run, Pallas kernels for 18% -> 18%
where the time goes in v16:
time: 47.9 us; the launch traced here: 47.3 us
  starting transfers between devices  16.7 us (35%)
  waiting for transfers between devices  10.3 us (22%)
  Pallas kernels  8.49 us (18%)
  other arithmetic  4.22 us (9%)
  local copies, waits for them, and re-layouts  3.69 us (8%)
  between operations  2.7 us (6%)
  matrix products  1.14 us (2%)
    ppermute x6, starting transfers between devices, local(): lax.ppermute(blk, 'chan', perm=[(i, (i + d) % peers) for i in range(peers)])  9.44 us
    pallas_call x2, Pallas kernels, spectra(): pl.pallas_call(spectra_kernel, grid_spec=grid_spec, cost_estimate=pl.Cost...  8.49 us
    ppermute x6, waiting for transfers between devices, local(): lax.ppermute(blk, 'chan', perm=[(i, (i + d) % peers) for i in range(peers)])  7.74 us
    ppermute x6, starting transfers between devices, local(): lax.ppermute(piece, 'tm', perm=[(i, (i + d) % ntm) for i in range(ntm)])  7.29 us
    ppermute x6, waiting for transfers between devices, local(): lax.ppermute(piece, 'tm', perm=[(i, (i + d) % ntm) for i in range(ntm)])  2.56 us
    another operation x2, other arithmetic, local(): picked_parts.append(jnp.stack(recv))  2.07 us
    another operation x2, other arithmetic, local(): prev_slots = jnp.stack(slots)  1.72 us
    slice x1, local copies, waits for them, and re-layouts, local(): part = parts[:, :, h].reshape(ntm, blocks * rows, width)  1.32 us
  transfers between devices with their start and end apart: 12, of which 4 were waited for; matrix products, arithmetic and copies ran while one was open for 8% of the time, Pallas kernels for 18%

profile of v16, /device:TPU:0, one launch (start us, length us, event | category | flops | bytes accessed | tf_op | source)
XLA Modules:
  0.0 47.3 jit_solution(8153351764502860109)
XLA Ops:
  0.0 0.0 copy-start.3
  0.0 0.0 copy-start.2
  0.0 1.3 %fusion.20 = (bf16[4,2,1,64,512]{4,3,2,1,0:T(8,128)(2,1)S(1)}, bf16[4,2,1,64,512]{4,3,2,1,0:T(8,128)(2,1)S(1)}) fusion(bf16[4,2,2,64,512]{4,3,2,1,0:T(8,128)(2,1)} %bitcast.97), kind=kLoop, calls=%fused_computation.63 | loop fusion | bytes 2097152 | tf_op jit(solution)/shard_map/slice | solution.py:147
  1.4 2.4 %collective-permute-start.2 = (bf16[128,512]{1,0:T(8,128)(2,1)S(1)}, bf16[128,512]{1,0:T(8,128)(2,1)S(1)}, u32[]{:S(2)}, u32[]{:S(2)}) collective-permute-start(bf16[128,512]{1,0:T(8,128)(2,1)S(1)} %get-tuple-element.14), channel_id=1, source_target_pairs={{0,3},{1,0},{2,1},{3,2},{4,7},{5,4},{6,5},{7,6},{8,11},{9,8},{10,9... | collective-permute-start | bytes 393224 | tf_op jit(solution)/shard_map/ppermute | solution.py:153
  3.8 0.0 collective-permute-start
  3.8 1.1 %collective-permute-start.1 = (bf16[128,512]{1,0:T(8,128)(2,1)S(1)}, bf16[128,512]{1,0:T(8,128)(2,1)S(1)}, u32[]{:S(2)}, u32[]{:S(2)}) collective-permute-start(bf16[128,512]{1,0:T(8,128)(2,1)S(1)} %get-tuple-element.15), channel_id=1, source_target_pairs={{0,2},{1,3},{2,0},{3,1},{4,6},{5,7},{6,4},{7,5},{8,10},{9,11},{10,... | collective-permute-start | bytes 393224 | tf_op jit(solution)/shard_map/ppermute | solution.py:153
  4.9 0.0 copy-done.3
  4.9 0.0 copy-done.2
  4.9 0.7 %constant_dynamic-slice_fusion.5 = (s32[1,1,1,1]{2,3,1,0:T(1,128)}, s32[1,1,1,1]{2,3,1,0:T(1,128)}, s32[1,1,1,1]{2,3,1,0:T(1,128)}, s32[1,1,1,1]{2,3,1,0:T(1,128)}) fusion(s32[1,1,4,1]{2,3,1,0:T(1,128)S(1)} %copy-done.2, s32[]{:T(128)S(6)} %select_n.183, s32[]{:T(128)S(6)} %select_n.194, s32[]{:T(128)S(6)} %select_n.202, s32[]{:T(128)S(6)} %select_n.198), kind=kLoop, calls=%fused_computation.46 | loop fusion | bytes 48 | tf_op jit(solution)/shard_map/jit(dynamic_index_in_dim)/dynamic_slice | solution.py:162
  8.1 0.0 collective-permute-done.2
  8.1 1.5 %collective-permute-done = bf16[128,512]{1,0:T(8,128)(2,1)S(1)} collective-permute-done((bf16[128,512]{1,0:T(8,128)(2,1)S(1)}, bf16[128,512]{1,0:T(8,128)(2,1)S(1)}, u32[]{:S(2)}, u32[]{:S(2)}) %collective-permute-start) | collective-permute-done | bytes 131104 | tf_op jit(solution)/shard_map/ppermute | solution.py:153
  9.6 1.1 %collective-permute-done.1 = bf16[128,512]{1,0:T(8,128)(2,1)S(1)} collective-permute-done((bf16[128,512]{1,0:T(8,128)(2,1)S(1)}, bf16[128,512]{1,0:T(8,128)(2,1)S(1)}, u32[]{:S(2)}, u32[]{:S(2)}) %collective-permute-start.1) | collective-permute-done | bytes 131104 | tf_op jit(solution)/shard_map/ppermute | solution.py:153
  10.7 0.9 %pad_maximum_fusion.1.x_ref = bf16[4,128,512]{2,1,0:T(8,128)(2,1)} fusion(bf16[1,128,512]{2,1,0:T(8,128)(2,1)S(1)} %bitcast.110, bf16[1,128,512]{2,1,0:T(8,128)(2,1)S(1)} %bitcast.112, bf16[1,128,512]{2,1,0:T(8,128)(2,1)S(1)} %bitcast.111, bf16[1,128,512]{2,1,0:T(8,128)(2,1)S(1)} %get-tuple-element.13), kind=kLoop, calls=%fused_computation.20 | loop fusion | flops 786432 | bytes 1048576 | tf_op jit(solution)/shard_map/stack | solution.py:154
  11.6 0.7 %collective-permute-start.6 = (bf16[128,512]{1,0:T(8,128)(2,1)S(1)}, bf16[128,512]{1,0:T(8,128)(2,1)S(1)}, u32[]{:S(2)}, u32[]{:S(2)}) collective-permute-start(bf16[128,512]{1,0:T(8,128)(2,1)S(1)} %get-tuple-element.12), channel_id=1, source_target_pairs={{0,1},{1,2},{2,3},{3,0},{4,5},{5,6},{6,7},{7,4},{8,9},{9,10},{10,1... | collective-permute-start | bytes 393224 | tf_op jit(solution)/shard_map/ppermute | solution.py:153
  12.3 1.7 %collective-permute-start.7 = (bf16[128,512]{1,0:T(8,128)(2,1)S(1)}, bf16[128,512]{1,0:T(8,128)(2,1)S(1)}, u32[]{:S(2)}, u32[]{:S(2)}) collective-permute-start(bf16[128,512]{1,0:T(8,128)(2,1)S(1)} %get-tuple-element.11), channel_id=1, source_target_pairs={{0,2},{1,3},{2,0},{3,1},{4,6},{5,7},{6,4},{7,5},{8,10},{9,11},{10,... | collective-permute-start | bytes 393224 | tf_op jit(solution)/shard_map/ppermute | solution.py:153
  14.0 1.4 %collective-permute-start.8 = (bf16[128,512]{1,0:T(8,128)(2,1)S(1)}, bf16[128,512]{1,0:T(8,128)(2,1)S(1)}, u32[]{:S(2)}, u32[]{:S(2)}) collective-permute-start(bf16[128,512]{1,0:T(8,128)(2,1)S(1)} %get-tuple-element.10), channel_id=1, source_target_pairs={{0,3},{1,0},{2,1},{3,2},{4,7},{5,4},{6,5},{7,6},{8,11},{9,8},{10,9... | collective-permute-start | bytes 393224 | tf_op jit(solution)/shard_map/ppermute | solution.py:153
  15.4 4.2 %shard_map.91 = bf16[128,1024]{1,0:T(8,128)(2,1)} custom-call(s32[1]{0:T(128)} %bitcast.2.pos_ref, bf16[4,128,512]{2,1,0:T(8,128)(2,1)} %pad_maximum_fusion.1.x_ref, bf16[384,256]{1,0:T(8,128)(2,1)} %constant.142.clone.band_ref, bf16[1024,1024]{1,0:T(8,128)(2,1)} %constant.143.clone.tab_ref, bf16[512,512]{1,0:T(8,128)(2,1)} %constant.144.clone.grp_ref), custom_call_target="tpu_custom_call" | custom-call | flops 1073741824 | bytes 2883584 | tf_op jit(solution)/shard_map/pallas_call | solution.py:123
  19.6 1.0 %select_bitcast_fusion.1 = (bf16[1,1,64,1024]{3,2,1,0:T(8,128)(2,1)S(1)}, bf16[64,1024]{1,0:T(8,128)(2,1)S(1)}, bf16[64,1024]{1,0:T(8,128)(2,1)S(1)}, bf16[64,1024]{1,0:T(8,128)(2,1)S(1)}) fusion(pred[]{:T(512)} %bitcast.1, bf16[128,1024]{1,0:T(8,128)(2,1)} %shard_map.91, pred[]{:T(512)} %bitcast.14, pred[]{:T(512)} %bitcast.16, pred[]{:T(512)} %bitcast.12), kind=kLoop, calls=%fused_computation.30 | loop fusion | flops 262144 | bytes 786436 | tf_op jit(solution)/shard_map/stack;stack | solution.py:170
  20.6 1.6 %collective-permute-start.3 = (bf16[64,1024]{1,0:T(8,128)(2,1)S(1)}, bf16[64,1024]{1,0:T(8,128)(2,1)S(1)}, u32[]{:S(2)}, u32[]{:S(2)}) collective-permute-start(bf16[64,1024]{1,0:T(8,128)(2,1)S(1)} %get-tuple-element.20), channel_id=1, source_target_pairs={{0,4},{4,8},{8,12},{12,0},{1,5},{5,9},{9,13},{13,1},{2,6},{6,10},{... | collective-permute-start | bytes 393224 | tf_op jit(solution)/shard_map/ppermute | solution.py:167
  22.3 2.6 %collective-permute-start.4 = (bf16[64,1024]{1,0:T(8,128)(2,1)S(1)}, bf16[64,1024]{1,0:T(8,128)(2,1)S(1)}, u32[]{:S(2)}, u32[]{:S(2)}) collective-permute-start(bf16[64,1024]{1,0:T(8,128)(2,1)S(1)} %get-tuple-element.18), channel_id=1, source_target_pairs={{0,8},{4,12},{8,0},{12,4},{1,9},{5,13},{9,1},{13,5},{2,10},{6,14},... | collective-permute-start | bytes 393224 | tf_op jit(solution)/shard_map/ppermute | solution.py:167
  24.9 0.0 collective-permute-done.6
  24.9 1.3 %collective-permute-start.5 = (bf16[64,1024]{1,0:T(8,128)(2,1)S(1)}, bf16[64,1024]{1,0:T(8,128)(2,1)S(1)}, u32[]{:S(2)}, u32[]{:S(2)}) collective-permute-start(bf16[64,1024]{1,0:T(8,128)(2,1)S(1)} %get-tuple-element.19), channel_id=1, source_target_pairs={{0,12},{4,0},{8,4},{12,8},{1,13},{5,1},{9,5},{13,9},{2,14},{6,2},{... | collective-permute-start | bytes 393224 | tf_op jit(solution)/shard_map/ppermute | solution.py:167
  26.2 0.0 collective-permute-done.7
  26.2 0.0 collective-permute-done.8
  26.2 0.9 %pad_maximum_fusion.2.x_ref = bf16[4,128,512]{2,1,0:T(8,128)(2,1)} fusion(bf16[1,128,512]{2,1,0:T(8,128)(2,1)S(1)} %bitcast.115, bf16[1,128,512]{2,1,0:T(8,128)(2,1)S(1)} %bitcast.114, bf16[1,128,512]{2,1,0:T(8,128)(2,1)S(1)} %bitcast.113, bf16[1,128,512]{2,1,0:T(8,128)(2,1)S(1)} %get-tuple-element.9), kind=kLoop, calls=%fused_computation.21 | loop fusion | flops 786432 | bytes 1048576 | tf_op jit(solution)/shard_map/stack | solution.py:154
  27.1 4.2 %shard_map.92 = bf16[128,1024]{1,0:T(8,128)(2,1)} custom-call(s32[1]{0:T(128)} %bitcast.2.pos_ref, bf16[4,128,512]{2,1,0:T(8,128)(2,1)} %pad_maximum_fusion.2.x_ref, bf16[384,256]{1,0:T(8,128)(2,1)} %constant.142.clone.band_ref, bf16[1024,1024]{1,0:T(8,128)(2,1)} %constant.143.clone.tab_ref, bf16[512,512]{1,0:T(8,128)(2,1)} %constant.144.clone.grp_ref), custom_call_target="tpu_custom_call" | custom-call | flops 1073741824 | bytes 2883584 | tf_op jit(solution)/shard_map/pallas_call | solution.py:123
  31.3 0.0 copy-start
  31.3 0.0 copy-start.1
  31.3 1.1 %select_bitcast_fusion = (bf16[1,1,64,1024]{3,2,1,0:T(8,128)(2,1)S(1)}, bf16[64,1024]{1,0:T(8,128)(2,1)S(1)}, bf16[64,1024]{1,0:T(8,128)(2,1)S(1)}, bf16[64,1024]{1,0:T(8,128)(2,1)S(1)}) fusion(pred[]{:T(512)} %bitcast.1, bf16[128,1024]{1,0:T(8,128)(2,1)} %shard_map.92, pred[]{:T(512)} %bitcast.14, pred[]{:T(512)} %bitcast.16, pred[]{:T(512)} %bitcast.12), kind=kLoop, calls=%fused_computation.26 | loop fusion | flops 262144 | bytes 786436 | tf_op jit(solution)/shard_map/stack;stack | solution.py:170
  32.4 0.7 %collective-permute-start.9 = (bf16[64,1024]{1,0:T(8,128)(2,1)S(1)}, bf16[64,1024]{1,0:T(8,128)(2,1)S(1)}, u32[]{:S(2)}, u32[]{:S(2)}) collective-permute-start(bf16[64,1024]{1,0:T(8,128)(2,1)S(1)} %get-tuple-element.24), channel_id=1, source_target_pairs={{0,4},{4,8},{8,12},{12,0},{1,5},{5,9},{9,13},{13,1},{2,6},{6,10},{... | collective-permute-start | bytes 393224 | tf_op jit(solution)/shard_map/ppermute | solution.py:167
  33.1 0.3 collective-permute-start.10
  33.4 0.0 collective-permute-done.3
  33.4 2.8 %collective-permute-start.11 = (bf16[64,1024]{1,0:T(8,128)(2,1)S(1)}, bf16[64,1024]{1,0:T(8,128)(2,1)S(1)}, u32[]{:S(2)}, u32[]{:S(2)}) collective-permute-start(bf16[64,1024]{1,0:T(8,128)(2,1)S(1)} %get-tuple-element.23), channel_id=1, source_target_pairs={{0,12},{4,0},{8,4},{12,8},{1,13},{5,1},{9,5},{13,9},{2,14},{6,2},{... | collective-permute-start | bytes 393224 | tf_op jit(solution)/shard_map/ppermute | solution.py:167
  36.3 0.0 collective-permute-done.4
  36.3 0.0 collective-permute-done.5
  36.3 4.4 %collective-permute-done.9 = bf16[64,1024]{1,0:T(8,128)(2,1)S(1)} collective-permute-done((bf16[64,1024]{1,0:T(8,128)(2,1)S(1)}, bf16[64,1024]{1,0:T(8,128)(2,1)S(1)}, u32[]{:S(2)}, u32[]{:S(2)}) %collective-permute-start.9) | collective-permute-done | bytes 131104 | tf_op jit(solution)/shard_map/ppermute | solution.py:167
  40.7 3.3 %collective-permute-done.10 = bf16[64,1024]{1,0:T(8,128)(2,1)S(1)} collective-permute-done((bf16[64,1024]{1,0:T(8,128)(2,1)S(1)}, bf16[64,1024]{1,0:T(8,128)(2,1)S(1)}, u32[]{:S(2)}, u32[]{:S(2)}) %collective-permute-start.10) | collective-permute-done | bytes 131104 | tf_op jit(solution)/shard_map/ppermute | solution.py:167
  44.0 0.0 collective-permute-done.11
  44.0 0.1 maximum_maximum_fusion
  44.1 0.0 copy-done
  44.1 0.0 copy-done.1
  44.1 0.5 %convolution_bitcast_fusion = f32[4,1,2,1,128,128]{4,5,2,0,3,1:T(8,128)S(1)} fusion(bf16[4,1,128,1024]{3,2,1,0:T(8,128)(2,1)S(1)} %maximum_maximum_fusion, bf16[2,64,1024]{2,1,0:T(8,128)(2,1)S(1)} %bitcast.101, bf16[2,64,1024]{2,1,0:T(8,128)(2,1)S(1)} %bitcast.98), kind=kOutput, calls=%fused_computation.1 | convolution fusion | flops 269484032 | bytes 2097152 | tf_op jit(solution)/shard_map/lif,dkjf->dklij/dot_general | solution.py:173
  44.6 0.3 fusion.7
  45.0 0.3 fusion
  45.3 0.1 maximum_bitcast_fusion
  45.4 0.6 %gather_fusion = f32[4,2,2,128,128]{3,4,1,2,0:T(8,128)S(1)} fusion(f32[4,2,2,128,128]{3,4,1,0,2:T(8,128)S(1)} %maximum_bitcast_fusion, s32[1024]{0:T(1024)S(1)} %pad_clamp_fusion), kind=kCustom, calls=%fused_computation | custom fusion | bytes 2097168 | tf_op jit(solution)/shard_map/jit(_take)/gather | solution.py:178
  46.0 0.2 fusion.4
  46.3 1.0 %copy.12 = bf16[1,1,4,1,2,2,128,128]{7,6,5,4,3,2,1,0:T(8,128)(2,1)} copy(bf16[1,1,4,1,2,2,128,128]{6,7,4,5,2,3,1,0:T(8,128)(2,1)S(1)} %fusion.4) | data formatting | bytes 1048576 | tf_op jit(solution)/shard_map/convert_element_type | solution.py:182
  (6 shorter events, 0.1 us)
Async XLA Ops:
  0.0 4.9 %copy-start.3 = (s32[1,1,4]{2,1,0:T(1,128)S(1)}, s32[1,1,4]{2,1,0:T(1,128)}, u32[]{:S(2)}) copy-start(s32[1,1,4]{2,1,0:T(1,128)} %param.11) | copy-start | bytes 52
  0.0 4.9 %copy-start.2 = (s32[1,1,4,1]{2,3,1,0:T(1,128)S(1)}, s32[1,1,4,1]{2,3,1,0:T(1,128)}, u32[]{:S(2)}) copy-start(s32[1,1,4,1]{2,3,1,0:T(1,128)} %param.10) | copy-start | bytes 52
  1.4 6.7 %collective-permute-start.2 = (bf16[128,512]{1,0:T(8,128)(2,1)S(1)}, bf16[128,512]{1,0:T(8,128)(2,1)S(1)}, u32[]{:S(2)}, u32[]{:S(2)}) collective-permute-start(bf16[128,512]{1,0:T(8,128)(2,1)S(1)} %get-tuple-element.14), channel_id=1, source_target_pairs={{0,3},{1,0},{2,1},{3,2},{4,7},{5,4},{6,5},{7,6},{8,11},{9,8},{10,9... | collective-permute-start | bytes 393224 | tf_op jit(solution)/shard_map/ppermute | solution.py:153
  3.8 5.8 %collective-permute-start = (bf16[128,512]{1,0:T(8,128)(2,1)S(1)}, bf16[128,512]{1,0:T(8,128)(2,1)S(1)}, u32[]{:S(2)}, u32[]{:S(2)}) collective-permute-start(bf16[128,512]{1,0:T(8,128)(2,1)S(1)} %get-tuple-element.16), channel_id=1, source_target_pairs={{0,1},{1,2},{2,3},{3,0},{4,5},{5,6},{6,7},{7,4},{8,9},{9,10},{10,1... | collective-permute-start | bytes 393224 | tf_op jit(solution)/shard_map/ppermute | solution.py:153
  3.8 6.8 %collective-permute-start.1 = (bf16[128,512]{1,0:T(8,128)(2,1)S(1)}, bf16[128,512]{1,0:T(8,128)(2,1)S(1)}, u32[]{:S(2)}, u32[]{:S(2)}) collective-permute-start(bf16[128,512]{1,0:T(8,128)(2,1)S(1)} %get-tuple-element.15), channel_id=1, source_target_pairs={{0,2},{1,3},{2,0},{3,1},{4,6},{5,7},{6,4},{7,5},{8,10},{9,11},{10,... | collective-permute-start | bytes 393224 | tf_op jit(solution)/shard_map/ppermute | solution.py:153
  11.6 13.3 %collective-permute-start.6 = (bf16[128,512]{1,0:T(8,128)(2,1)S(1)}, bf16[128,512]{1,0:T(8,128)(2,1)S(1)}, u32[]{:S(2)}, u32[]{:S(2)}) collective-permute-start(bf16[128,512]{1,0:T(8,128)(2,1)S(1)} %get-tuple-element.12), channel_id=1, source_target_pairs={{0,1},{1,2},{2,3},{3,0},{4,5},{5,6},{6,7},{7,4},{8,9},{9,10},{10,1... | collective-permute-start | bytes 393224 | tf_op jit(solution)/shard_map/ppermute | solution.py:153
  12.3 13.9 %collective-permute-start.7 = (bf16[128,512]{1,0:T(8,128)(2,1)S(1)}, bf16[128,512]{1,0:T(8,128)(2,1)S(1)}, u32[]{:S(2)}, u32[]{:S(2)}) collective-permute-start(bf16[128,512]{1,0:T(8,128)(2,1)S(1)} %get-tuple-element.11), channel_id=1, source_target_pairs={{0,2},{1,3},{2,0},{3,1},{4,6},{5,7},{6,4},{7,5},{8,10},{9,11},{10,... | collective-permute-start | bytes 393224 | tf_op jit(solution)/shard_map/ppermute | solution.py:153
  14.0 12.2 %collective-permute-start.8 = (bf16[128,512]{1,0:T(8,128)(2,1)S(1)}, bf16[128,512]{1,0:T(8,128)(2,1)S(1)}, u32[]{:S(2)}, u32[]{:S(2)}) collective-permute-start(bf16[128,512]{1,0:T(8,128)(2,1)S(1)} %get-tuple-element.10), channel_id=1, source_target_pairs={{0,3},{1,0},{2,1},{3,2},{4,7},{5,4},{6,5},{7,6},{8,11},{9,8},{10,9... | collective-permute-start | bytes 393224 | tf_op jit(solution)/shard_map/ppermute | solution.py:153
  20.6 12.8 %collective-permute-start.3 = (bf16[64,1024]{1,0:T(8,128)(2,1)S(1)}, bf16[64,1024]{1,0:T(8,128)(2,1)S(1)}, u32[]{:S(2)}, u32[]{:S(2)}) collective-permute-start(bf16[64,1024]{1,0:T(8,128)(2,1)S(1)} %get-tuple-element.20), channel_id=1, source_target_pairs={{0,4},{4,8},{8,12},{12,0},{1,5},{5,9},{9,13},{13,1},{2,6},{6,10},{... | collective-permute-start | bytes 393224 | tf_op jit(solution)/shard_map/ppermute | solution.py:167
  22.3 14.0 %collective-permute-start.4 = (bf16[64,1024]{1,0:T(8,128)(2,1)S(1)}, bf16[64,1024]{1,0:T(8,128)(2,1)S(1)}, u32[]{:S(2)}, u32[]{:S(2)}) collective-permute-start(bf16[64,1024]{1,0:T(8,128)(2,1)S(1)} %get-tuple-element.18), channel_id=1, source_target_pairs={{0,8},{4,12},{8,0},{12,4},{1,9},{5,13},{9,1},{13,5},{2,10},{6,14},... | collective-permute-start | bytes 393224 | tf_op jit(solution)/shard_map/ppermute | solution.py:167
  24.9 11.5 %collective-permute-start.5 = (bf16[64,1024]{1,0:T(8,128)(2,1)S(1)}, bf16[64,1024]{1,0:T(8,128)(2,1)S(1)}, u32[]{:S(2)}, u32[]{:S(2)}) collective-permute-start(bf16[64,1024]{1,0:T(8,128)(2,1)S(1)} %get-tuple-element.19), channel_id=1, source_target_pairs={{0,12},{4,0},{8,4},{12,8},{1,13},{5,1},{9,5},{13,9},{2,14},{6,2},{... | collective-permute-start | bytes 393224 | tf_op jit(solution)/shard_map/ppermute | solution.py:167
  31.3 12.8 %copy-start = (bf16[128,1024]{1,0:T(8,128)(2,1)S(1)}, bf16[128,1024]{1,0:T(8,128)(2,1)}, u32[]{:S(2)}) copy-start(bf16[128,1024]{1,0:T(8,128)(2,1)} %shard_map.91) | copy-start | bytes 786436
  31.3 12.8 %copy-start.1 = (bf16[128,1024]{1,0:T(8,128)(2,1)S(1)}, bf16[128,1024]{1,0:T(8,128)(2,1)}, u32[]{:S(2)}) copy-start(bf16[128,1024]{1,0:T(8,128)(2,1)} %shard_map.92) | copy-start | bytes 786436
  32.4 8.3 %collective-permute-start.9 = (bf16[64,1024]{1,0:T(8,128)(2,1)S(1)}, bf16[64,1024]{1,0:T(8,128)(2,1)S(1)}, u32[]{:S(2)}, u32[]{:S(2)}) collective-permute-start(bf16[64,1024]{1,0:T(8,128)(2,1)S(1)} %get-tuple-element.24), channel_id=1, source_target_pairs={{0,4},{4,8},{8,12},{12,0},{1,5},{5,9},{9,13},{13,1},{2,6},{6,10},{... | collective-permute-start | bytes 393224 | tf_op jit(solution)/shard_map/ppermute | solution.py:167
  33.1 10.9 %collective-permute-start.10 = (bf16[64,1024]{1,0:T(8,128)(2,1)S(1)}, bf16[64,1024]{1,0:T(8,128)(2,1)S(1)}, u32[]{:S(2)}, u32[]{:S(2)}) collective-permute-start(bf16[64,1024]{1,0:T(8,128)(2,1)S(1)} %get-tuple-element.22), channel_id=1, source_target_pairs={{0,8},{4,12},{8,0},{12,4},{1,9},{5,13},{9,1},{13,5},{2,10},{6,14},... | collective-permute-start | bytes 393224 | tf_op jit(solution)/shard_map/ppermute | solution.py:167
  33.4 10.6 %collective-permute-start.11 = (bf16[64,1024]{1,0:T(8,128)(2,1)S(1)}, bf16[64,1024]{1,0:T(8,128)(2,1)S(1)}, u32[]{:S(2)}, u32[]{:S(2)}) collective-permute-start(bf16[64,1024]{1,0:T(8,128)(2,1)S(1)} %get-tuple-element.23), channel_id=1, source_target_pairs={{0,12},{4,0},{8,4},{12,8},{1,13},{5,1},{9,5},{13,9},{2,14},{6,2},{... | collective-permute-start | bytes 393224 | tf_op jit(solution)/shard_map/ppermute | solution.py:167

commit v17 on v14

--- a/solution.py
+++ b/solution.py
@@ -73,7 +73,7 @@
 
     def tile(j):
         chunk, off = divmod((j % ntile) * TILE, width)
-        return x_ref[(pos - chunk + nslot) % nslot, :, off:off + TILE]
+        return x_ref[lax.bitwise_xor(pos, chunk), :, off:off + TILE]
 
     nrows = x_ref.shape[1]
     band = band_ref[...]
@@ -130,6 +130,7 @@
 
 def local(raw, send_blocks, pair_count):
     ntm = lax.axis_size("tm")
+    assert ntm & (ntm - 1) == 0 and lax.axis_size("chan") & (lax.axis_size("chan") - 1) == 0
     nch, width = raw.shape
     here = lax.axis_index("tm")
     blocks = nch // ntm // BLOCK
@@ -148,15 +149,15 @@
         if own_parts:
             part, prev_slots = lax.optimization_barrier((part, prev_slots))
         slots = [lax.dynamic_index_in_dim(part, here, axis=0, keepdims=False)]
-        for d in range(1, ntm):
-            piece = lax.dynamic_index_in_dim(part, (here + d) % ntm, axis=0, keepdims=False)
-            slots.append(lax.ppermute(piece, "tm", perm=[(i, (i + d) % ntm) for i in range(ntm)]))
+        for m in range(1, ntm):
+            piece = lax.dynamic_index_in_dim(part, here ^ m, axis=0, keepdims=False)
+            slots.append(lax.ppermute(piece, "tm", perm=[(i, i ^ m) for i in range(ntm)]))
         prev_slots = jnp.stack(slots)
         whitened = spectra(pos, prev_slots).reshape(blocks, rows, 2 * NBAND)
         own_parts.append(whitened)
         recv = []
         for d in range(peers):
-            dest = (mine + d) % peers
+            dest = mine ^ d
             row = []
             for k in range(cap):
                 want = lax.dynamic_index_in_dim(ids[:, k], dest, keepdims=False)
@@ -164,7 +165,7 @@
                 for b in range(1, blocks):
                     blk = jnp.where(want == b, whitened[b], blk)
                 if d:
-                    blk = lax.ppermute(blk, "chan", perm=[(i, (i + d) % peers) for i in range(peers)])
+                    blk = lax.ppermute(blk, "chan", perm=[(i, i ^ d) for i in range(peers)])
                 row.append(blk)
             recv.append(jnp.stack(row))
         picked_parts.append(jnp.stack(recv))
@@ -173,7 +174,7 @@
     turned = jnp.concatenate([whitened[..., NBAND:], -whitened[..., :NBAND]], axis=-1)
     paired = jnp.stack([whitened, turned], axis=1)
     result = jnp.einsum("lrif,dkjf->dklrij", paired, picked, preferred_element_type=jnp.float32)
-    order = (mine - jnp.arange(peers, dtype=jnp.int32)) % peers
+    order = mine ^ jnp.arange(peers, dtype=jnp.int32)
     result = jnp.take(result, order, axis=0)
     result = result * (1.0 / math.sqrt(NBAND))
     live = jnp.arange(cap, dtype=jnp.int32)[None, :] < pair_count[0, 0][:, None]

time: 47.4 us -> 48.3 us (1.019)
  waiting for transfers between devices: 8.1 us -> 11.6 us
  starting transfers between devices: 16.8 us -> 14.7 us
    ppermute x12, waiting for transfers between devices: 8.1 us -> 11.6 us  [the longest x6 8.76 us: local(): blk = lax.ppermute(blk, 'chan', perm=[(i, i ^ d) for i in range(peers)])]
    ppermute x12, starting transfers between devices: 16.8 us -> 14.7 us  [the longest x6 8.99 us: local(): blk = lax.ppermute(blk, 'chan', perm=[(i, i ^ d) for i in range(peers)])]
  transfers between devices with their start and end apart: 12 -> 12, of which waited for: 4 -> 3; matrix products, arithmetic and copies ran while one was open for 12% -> 12% of each run, Pallas kernels for 18% -> 18%
where the time goes in v17:
time: 48.3 us; the launch traced here: 48.1 us
  starting transfers between devices  14.7 us (30%)
  waiting for transfers between devices  11.6 us (24%)
  Pallas kernels  8.52 us (18%)
  other arithmetic  6.07 us (13%)
  local copies, waits for them, and re-layouts  3.7 us (8%)
  between operations  2.73 us (6%)
  matrix products  0.74 us (2%)
    ppermute x6, starting transfers between devices, local(): blk = lax.ppermute(blk, 'chan', perm=[(i, i ^ d) for i in range(peers)])  8.99 us
    ppermute x6, waiting for transfers between devices, local(): blk = lax.ppermute(blk, 'chan', perm=[(i, i ^ d) for i in range(peers)])  8.76 us
    pallas_call x2, Pallas kernels, spectra(): pl.pallas_call(spectra_kernel, grid_spec=grid_spec, cost_estimate=pl.Cost...  8.52 us
    ppermute x6, starting transfers between devices, local(): lax.ppermute(piece, 'tm', perm=[(i, i ^ m) for i in range(ntm)])  5.67 us
    ppermute x6, waiting for transfers between devices, local(): lax.ppermute(piece, 'tm', perm=[(i, i ^ m) for i in range(ntm)])  2.87 us
    another operation x2, other arithmetic, local(): picked_parts.append(jnp.stack(recv))  2.01 us
    another operation x2, other arithmetic, local(): prev_slots = jnp.stack(slots)  1.72 us
    slice x1, local copies, waits for them, and re-layouts, local(): part = parts[:, :, h].reshape(ntm, blocks * rows, width)  1.32 us
  transfers between devices with their start and end apart: 12, of which 3 were waited for; matrix products, arithmetic and copies ran while one was open for 12% of the time, Pallas kernels for 18%

profile of v17, /device:TPU:0, one launch (start us, length us, event | category | flops | bytes accessed | tf_op | source)
XLA Modules:
  0.0 48.1 jit_solution(1455705460655434682)
XLA Ops:
  0.0 0.0 copy-start.2
  0.0 0.0 copy-start.1
  0.0 1.3 %fusion.25 = (bf16[4,2,1,64,512]{4,3,2,1,0:T(8,128)(2,1)S(1)}, bf16[4,2,1,64,512]{4,3,2,1,0:T(8,128)(2,1)S(1)}) fusion(bf16[4,2,2,64,512]{4,3,2,1,0:T(8,128)(2,1)} %bitcast.82), kind=kLoop, calls=%fused_computation.63 | loop fusion | bytes 2097152 | tf_op jit(solution)/shard_map/slice | solution.py:148
  1.4 2.4 %collective-permute-start.2 = (bf16[128,512]{1,0:T(8,128)(2,1)S(1)}, bf16[128,512]{1,0:T(8,128)(2,1)S(1)}, u32[]{:S(2)}, u32[]{:S(2)}) collective-permute-start(bf16[128,512]{1,0:T(8,128)(2,1)S(1)} %get-tuple-element.16), channel_id=1, source_target_pairs={{0,3},{1,2},{2,1},{3,0},{4,7},{5,6},{6,5},{7,4},{8,11},{9,10},{10,... | collective-permute-start | bytes 393224 | tf_op jit(solution)/shard_map/ppermute | solution.py:154
  3.8 0.7 %collective-permute-start = (bf16[128,512]{1,0:T(8,128)(2,1)S(1)}, bf16[128,512]{1,0:T(8,128)(2,1)S(1)}, u32[]{:S(2)}, u32[]{:S(2)}) collective-permute-start(bf16[128,512]{1,0:T(8,128)(2,1)S(1)} %get-tuple-element.18), channel_id=1, source_target_pairs={{0,1},{1,0},{2,3},{3,2},{4,5},{5,4},{6,7},{7,6},{8,9},{9,8},{10,11... | collective-permute-start | bytes 393224 | tf_op jit(solution)/shard_map/ppermute | solution.py:154
  4.5 0.0 collective-permute-start.1
  4.6 0.0 copy-done.2
  4.6 0.0 copy-done.1
  4.6 0.7 %constant_dynamic-slice_fusion.5 = (s32[1,1,1,1]{2,3,1,0:T(1,128)}, s32[1,1,1,1]{2,3,1,0:T(1,128)}, s32[1,1,1,1]{2,3,1,0:T(1,128)}, s32[1,1,1,1]{2,3,1,0:T(1,128)}) fusion(s32[1,1,4,1]{2,3,1,0:T(1,128)S(1)} %copy-done.1, s32[]{:T(128)S(6)} %select_n.119, s32[]{:T(128)S(6)} %select_n.126, s32[]{:T(128)S(6)} %select_n.132, s32[]{:T(128)S(6)} %select_n.129), kind=kLoop, calls=%fused_computation.56 | loop fusion | bytes 48 | tf_op jit(solution)/shard_map/jit(dynamic_index_in_dim)/dynamic_slice | solution.py:163
  7.8 0.0 collective-permute-done.2
  7.8 0.0 collective-permute-done
  7.8 2.9 %collective-permute-done.1 = bf16[128,512]{1,0:T(8,128)(2,1)S(1)} collective-permute-done((bf16[128,512]{1,0:T(8,128)(2,1)S(1)}, bf16[128,512]{1,0:T(8,128)(2,1)S(1)}, u32[]{:S(2)}, u32[]{:S(2)}) %collective-permute-start.1) | collective-permute-done | bytes 131104 | tf_op jit(solution)/shard_map/ppermute | solution.py:154
  10.7 0.9 %pad_maximum_fusion.1.x_ref = bf16[4,128,512]{2,1,0:T(8,128)(2,1)} fusion(bf16[1,128,512]{2,1,0:T(8,128)(2,1)S(1)} %bitcast.83, bf16[1,128,512]{2,1,0:T(8,128)(2,1)S(1)} %bitcast.85, bf16[1,128,512]{2,1,0:T(8,128)(2,1)S(1)} %bitcast.84, bf16[1,128,512]{2,1,0:T(8,128)(2,1)S(1)} %get-tuple-element.15), kind=kLoop, calls=%fused_computation.30 | loop fusion | flops 786432 | bytes 1048576 | tf_op jit(solution)/shard_map/stack | solution.py:155
  11.6 0.1 collective-permute-start.6
  11.7 2.4 %collective-permute-start.7 = (bf16[128,512]{1,0:T(8,128)(2,1)S(1)}, bf16[128,512]{1,0:T(8,128)(2,1)S(1)}, u32[]{:S(2)}, u32[]{:S(2)}) collective-permute-start(bf16[128,512]{1,0:T(8,128)(2,1)S(1)} %get-tuple-element.13), channel_id=1, source_target_pairs={{0,2},{1,3},{2,0},{3,1},{4,6},{5,7},{6,4},{7,5},{8,10},{9,11},{10,... | collective-permute-start | bytes 393224 | tf_op jit(solution)/shard_map/ppermute | solution.py:154
  14.1 0.1 collective-permute-start.8
  14.1 4.2 %shard_map.91 = bf16[128,1024]{1,0:T(8,128)(2,1)} custom-call(s32[1]{0:T(128)} %bitcast.2.pos_ref, bf16[4,128,512]{2,1,0:T(8,128)(2,1)} %pad_maximum_fusion.1.x_ref, bf16[384,256]{1,0:T(8,128)(2,1)} %constant.84.clone.band_ref, bf16[1024,1024]{1,0:T(8,128)(2,1)} %constant.85.clone.tab_ref, bf16[512,512]{1,0:T(8,128)(2,1)} %constant.86.clone.grp_ref), custom_call_target="tpu_custom_call" | custom-call | flops 1073741824 | bytes 2883584 | tf_op jit(solution)/shard_map/pallas_call | solution.py:123
  18.4 1.0 %select_bitcast_fusion.1 = (bf16[1,1,64,1024]{3,2,1,0:T(8,128)(2,1)S(1)}, bf16[64,1024]{1,0:T(8,128)(2,1)S(1)}, bf16[64,1024]{1,0:T(8,128)(2,1)S(1)}, bf16[64,1024]{1,0:T(8,128)(2,1)S(1)}) fusion(pred[]{:T(512)} %bitcast.1, bf16[128,1024]{1,0:T(8,128)(2,1)} %shard_map.91, pred[]{:T(512)} %bitcast.14, pred[]{:T(512)} %bitcast.16, pred[]{:T(512)} %bitcast.12), kind=kLoop, calls=%fused_computation.40 | loop fusion | flops 262144 | bytes 786436 | tf_op jit(solution)/shard_map/stack;stack | solution.py:171
  19.4 1.9 %collective-permute-start.3 = (bf16[64,1024]{1,0:T(8,128)(2,1)S(1)}, bf16[64,1024]{1,0:T(8,128)(2,1)S(1)}, u32[]{:S(2)}, u32[]{:S(2)}) collective-permute-start(bf16[64,1024]{1,0:T(8,128)(2,1)S(1)} %get-tuple-element.22), channel_id=1, source_target_pairs={{0,4},{4,0},{8,12},{12,8},{1,5},{5,1},{9,13},{13,9},{2,6},{6,2},{1... | collective-permute-start | bytes 393224 | tf_op jit(solution)/shard_map/ppermute | solution.py:168
  21.3 2.6 %collective-permute-start.4 = (bf16[64,1024]{1,0:T(8,128)(2,1)S(1)}, bf16[64,1024]{1,0:T(8,128)(2,1)S(1)}, u32[]{:S(2)}, u32[]{:S(2)}) collective-permute-start(bf16[64,1024]{1,0:T(8,128)(2,1)S(1)} %get-tuple-element.20), channel_id=1, source_target_pairs={{0,8},{4,12},{8,0},{12,4},{1,9},{5,13},{9,1},{13,5},{2,10},{6,14},... | collective-permute-start | bytes 393224 | tf_op jit(solution)/shard_map/ppermute | solution.py:168
  23.8 0.0 collective-permute-done.6
  23.9 0.0 collective-permute-start.5
  23.9 0.0 collective-permute-done.7
  23.9 0.0 collective-permute-done.8
  23.9 0.9 %pad_maximum_fusion.2.x_ref = bf16[4,128,512]{2,1,0:T(8,128)(2,1)} fusion(bf16[1,128,512]{2,1,0:T(8,128)(2,1)S(1)} %bitcast.88, bf16[1,128,512]{2,1,0:T(8,128)(2,1)S(1)} %bitcast.87, bf16[1,128,512]{2,1,0:T(8,128)(2,1)S(1)} %bitcast.86, bf16[1,128,512]{2,1,0:T(8,128)(2,1)S(1)} %get-tuple-element.11), kind=kLoop, calls=%fused_computation.31 | loop fusion | flops 786432 | bytes 1048576 | tf_op jit(solution)/shard_map/stack | solution.py:155
  24.7 0.0 copy-start
  24.7 4.3 %shard_map.92 = bf16[128,1024]{1,0:T(8,128)(2,1)} custom-call(s32[1]{0:T(128)} %bitcast.2.pos_ref, bf16[4,128,512]{2,1,0:T(8,128)(2,1)} %pad_maximum_fusion.2.x_ref, bf16[384,256]{1,0:T(8,128)(2,1)} %constant.84.clone.band_ref, bf16[1024,1024]{1,0:T(8,128)(2,1)} %constant.85.clone.tab_ref, bf16[512,512]{1,0:T(8,128)(2,1)} %constant.86.clone.grp_ref), custom_call_target="tpu_custom_call" | custom-call | flops 1073741824 | bytes 2883584 | tf_op jit(solution)/shard_map/pallas_call | solution.py:123
  29.0 1.0 %select_bitcast_fusion = (bf16[1,1,64,1024]{3,2,1,0:T(8,128)(2,1)S(1)}, bf16[64,1024]{1,0:T(8,128)(2,1)S(1)}, bf16[64,1024]{1,0:T(8,128)(2,1)S(1)}, bf16[64,1024]{1,0:T(8,128)(2,1)S(1)}) fusion(pred[]{:T(512)} %bitcast.1, bf16[128,1024]{1,0:T(8,128)(2,1)} %shard_map.92, pred[]{:T(512)} %bitcast.14, pred[]{:T(512)} %bitcast.16, pred[]{:T(512)} %bitcast.12), kind=kLoop, calls=%fused_computation.36 | loop fusion | flops 262144 | bytes 786436 | tf_op jit(solution)/shard_map/stack;stack | solution.py:171
  30.0 1.0 %collective-permute-start.9 = (bf16[64,1024]{1,0:T(8,128)(2,1)S(1)}, bf16[64,1024]{1,0:T(8,128)(2,1)S(1)}, u32[]{:S(2)}, u32[]{:S(2)}) collective-permute-start(bf16[64,1024]{1,0:T(8,128)(2,1)S(1)} %get-tuple-element.26), channel_id=1, source_target_pairs={{0,4},{4,0},{8,12},{12,8},{1,5},{5,1},{9,13},{13,9},{2,6},{6,2},{1... | collective-permute-start | bytes 393224 | tf_op jit(solution)/shard_map/ppermute | solution.py:168
  31.0 3.5 %collective-permute-start.10 = (bf16[64,1024]{1,0:T(8,128)(2,1)S(1)}, bf16[64,1024]{1,0:T(8,128)(2,1)S(1)}, u32[]{:S(2)}, u32[]{:S(2)}) collective-permute-start(bf16[64,1024]{1,0:T(8,128)(2,1)S(1)} %get-tuple-element.24), channel_id=1, source_target_pairs={{0,8},{4,12},{8,0},{12,4},{1,9},{5,13},{9,1},{13,5},{2,10},{6,14},... | collective-permute-start | bytes 393224 | tf_op jit(solution)/shard_map/ppermute | solution.py:168
  34.5 0.0 copy-done
  34.5 1.0 %fusion.20 = (bf16[2,128,512]{2,1,0:T(8,128)(2,1)S(1)}, bf16[2,128,512]{2,1,0:T(8,128)(2,1)S(1)}) fusion(bf16[2,64,1024]{2,1,0:T(8,128)(2,1)S(1)} %bitcast.76, bf16[2,64,1024]{2,1,0:T(8,128)(2,1)} %bitcast.78), kind=kLoop, calls=%fused_computation.33 | loop fusion | flops 1179648 | bytes 1048576 | tf_op jit(solution)/shard_map/concatenate | solution.py:172
  35.5 0.0 collective-permute-done.3
  35.5 0.1 collective-permute-start.11
  35.6 1.1 %fusion.19 = (bf16[2,1,128,1024]{3,2,1,0:T(8,128)(2,1)S(1)}, bf16[2,1,128,1024]{3,2,1,0:T(8,128)(2,1)S(1)}) fusion(bf16[2,64,1024]{2,1,0:T(8,128)(2,1)} %bitcast.79, bf16[2,64,1024]{2,1,0:T(8,128)(2,1)S(1)} %bitcast.77, bf16[2,128,512]{2,1,0:T(8,128)(2,1)S(1)} %get-tuple-element.10, bf16[2,128,512]{2,1,0:T(8,128)(2,1)S(1)} %get-tuple-element.9), kind=kLoop, calls=%fused_computation.29 | loop fusion | flops 2097152 | bytes 2097152 | tf_op jit(solution)/shard_map/stack | solution.py:175
  36.7 0.0 collective-permute-done.4
  36.7 0.0 collective-permute-done.5
  36.7 0.4 collective-permute-done.9
  37.1 8.3 %collective-permute-done.10 = bf16[64,1024]{1,0:T(8,128)(2,1)S(1)} collective-permute-done((bf16[64,1024]{1,0:T(8,128)(2,1)S(1)}, bf16[64,1024]{1,0:T(8,128)(2,1)S(1)}, u32[]{:S(2)}, u32[]{:S(2)}) %collective-permute-start.10) | collective-permute-done | bytes 131104 | tf_op jit(solution)/shard_map/ppermute | solution.py:168
  45.4 0.0 collective-permute-done.11
  45.4 0.7 %convolution_bitcast_fusion = f32[4,2,2,128,128]{3,4,2,1,0:T(8,128)S(1)} fusion(bf16[1,1,64,1024]{3,2,1,0:T(8,128)(2,1)S(1)} %bitcast.94, bf16[1,1,64,1024]{3,2,1,0:T(8,128)(2,1)S(1)} %bitcast.93, bf16[1,1,64,1024]{3,2,1,0:T(8,128)(2,1)S(1)} %bitcast.92, bf16[1,1,64,1024]{3,2,1,0:T(8,128)(2,1)S(1)} %get-tuple-element.23, ...), kind=kOutput, calls=%fused_computation.1 | convolution fusion | flops 547356672 | bytes 3145728 | tf_op jit(solution)/shard_map/lrif,dkjf->dklrij/dot_general | solution.py:176
  46.2 0.6 %gather_fusion = f32[4,2,2,128,128]{3,4,2,1,0:T(8,128)S(1)} fusion(f32[4,2,2,128,128]{3,4,2,1,0:T(8,128)S(1)} %convolution_bitcast_fusion, s32[1024]{0:T(1024)S(1)} %pad_clamp_fusion), kind=kCustom, calls=%fused_computation | custom fusion | bytes 2097168 | tf_op jit(solution)/shard_map/jit(_take)/gather | solution.py:178
  46.8 0.2 fusion.18
  47.0 1.0 %copy.13 = bf16[1,1,4,1,2,2,128,128]{7,6,5,4,3,2,1,0:T(8,128)(2,1)} copy(bf16[1,1,4,1,2,2,128,128]{6,7,5,4,2,3,1,0:T(8,128)(2,1)S(1)} %fusion.18) | data formatting | bytes 1048576 | tf_op jit(solution)/shard_map/convert_element_type | solution.py:182
  (6 shorter events, 0.1 us)
Async XLA Ops:
  0.0 4.6 %copy-start.2 = (s32[1,1,4]{2,1,0:T(1,128)S(1)}, s32[1,1,4]{2,1,0:T(1,128)}, u32[]{:S(2)}) copy-start(s32[1,1,4]{2,1,0:T(1,128)} %param.11) | copy-start | bytes 52
  0.0 4.6 %copy-start.1 = (s32[1,1,4,1]{2,3,1,0:T(1,128)S(1)}, s32[1,1,4,1]{2,3,1,0:T(1,128)}, u32[]{:S(2)}) copy-start(s32[1,1,4,1]{2,3,1,0:T(1,128)} %param.10) | copy-start | bytes 52
  1.4 6.4 %collective-permute-start.2 = (bf16[128,512]{1,0:T(8,128)(2,1)S(1)}, bf16[128,512]{1,0:T(8,128)(2,1)S(1)}, u32[]{:S(2)}, u32[]{:S(2)}) collective-permute-start(bf16[128,512]{1,0:T(8,128)(2,1)S(1)} %get-tuple-element.16), channel_id=1, source_target_pairs={{0,3},{1,2},{2,1},{3,0},{4,7},{5,6},{6,5},{7,4},{8,11},{9,10},{10,... | collective-permute-start | bytes 393224 | tf_op jit(solution)/shard_map/ppermute | solution.py:154
  3.8 4.0 %collective-permute-start = (bf16[128,512]{1,0:T(8,128)(2,1)S(1)}, bf16[128,512]{1,0:T(8,128)(2,1)S(1)}, u32[]{:S(2)}, u32[]{:S(2)}) collective-permute-start(bf16[128,512]{1,0:T(8,128)(2,1)S(1)} %get-tuple-element.18), channel_id=1, source_target_pairs={{0,1},{1,0},{2,3},{3,2},{4,5},{5,4},{6,7},{7,6},{8,9},{9,8},{10,11... | collective-permute-start | bytes 393224 | tf_op jit(solution)/shard_map/ppermute | solution.py:154
  4.5 6.2 %collective-permute-start.1 = (bf16[128,512]{1,0:T(8,128)(2,1)S(1)}, bf16[128,512]{1,0:T(8,128)(2,1)S(1)}, u32[]{:S(2)}, u32[]{:S(2)}) collective-permute-start(bf16[128,512]{1,0:T(8,128)(2,1)S(1)} %get-tuple-element.17), channel_id=1, source_target_pairs={{0,2},{1,3},{2,0},{3,1},{4,6},{5,7},{6,4},{7,5},{8,10},{9,11},{10,... | collective-permute-start | bytes 393224 | tf_op jit(solution)/shard_map/ppermute | solution.py:154
  11.6 12.2 %collective-permute-start.6 = (bf16[128,512]{1,0:T(8,128)(2,1)S(1)}, bf16[128,512]{1,0:T(8,128)(2,1)S(1)}, u32[]{:S(2)}, u32[]{:S(2)}) collective-permute-start(bf16[128,512]{1,0:T(8,128)(2,1)S(1)} %get-tuple-element.14), channel_id=1, source_target_pairs={{0,1},{1,0},{2,3},{3,2},{4,5},{5,4},{6,7},{7,6},{8,9},{9,8},{10,11... | collective-permute-start | bytes 393224 | tf_op jit(solution)/shard_map/ppermute | solution.py:154
  11.7 12.2 %collective-permute-start.7 = (bf16[128,512]{1,0:T(8,128)(2,1)S(1)}, bf16[128,512]{1,0:T(8,128)(2,1)S(1)}, u32[]{:S(2)}, u32[]{:S(2)}) collective-permute-start(bf16[128,512]{1,0:T(8,128)(2,1)S(1)} %get-tuple-element.13), channel_id=1, source_target_pairs={{0,2},{1,3},{2,0},{3,1},{4,6},{5,7},{6,4},{7,5},{8,10},{9,11},{10,... | collective-permute-start | bytes 393224 | tf_op jit(solution)/shard_map/ppermute | solution.py:154
  14.1 9.8 %collective-permute-start.8 = (bf16[128,512]{1,0:T(8,128)(2,1)S(1)}, bf16[128,512]{1,0:T(8,128)(2,1)S(1)}, u32[]{:S(2)}, u32[]{:S(2)}) collective-permute-start(bf16[128,512]{1,0:T(8,128)(2,1)S(1)} %get-tuple-element.12), channel_id=1, source_target_pairs={{0,3},{1,2},{2,1},{3,0},{4,7},{5,6},{6,5},{7,4},{8,11},{9,10},{10,... | collective-permute-start | bytes 393224 | tf_op jit(solution)/shard_map/ppermute | solution.py:154
  19.4 16.1 %collective-permute-start.3 = (bf16[64,1024]{1,0:T(8,128)(2,1)S(1)}, bf16[64,1024]{1,0:T(8,128)(2,1)S(1)}, u32[]{:S(2)}, u32[]{:S(2)}) collective-permute-start(bf16[64,1024]{1,0:T(8,128)(2,1)S(1)} %get-tuple-element.22), channel_id=1, source_target_pairs={{0,4},{4,0},{8,12},{12,8},{1,5},{5,1},{9,13},{13,9},{2,6},{6,2},{1... | collective-permute-start | bytes 393224 | tf_op jit(solution)/shard_map/ppermute | solution.py:168
  21.3 15.4 %collective-permute-start.4 = (bf16[64,1024]{1,0:T(8,128)(2,1)S(1)}, bf16[64,1024]{1,0:T(8,128)(2,1)S(1)}, u32[]{:S(2)}, u32[]{:S(2)}) collective-permute-start(bf16[64,1024]{1,0:T(8,128)(2,1)S(1)} %get-tuple-element.20), channel_id=1, source_target_pairs={{0,8},{4,12},{8,0},{12,4},{1,9},{5,13},{9,1},{13,5},{2,10},{6,14},... | collective-permute-start | bytes 393224 | tf_op jit(solution)/shard_map/ppermute | solution.py:168
  23.9 12.8 %collective-permute-start.5 = (bf16[64,1024]{1,0:T(8,128)(2,1)S(1)}, bf16[64,1024]{1,0:T(8,128)(2,1)S(1)}, u32[]{:S(2)}, u32[]{:S(2)}) collective-permute-start(bf16[64,1024]{1,0:T(8,128)(2,1)S(1)} %get-tuple-element.21), channel_id=1, source_target_pairs={{0,12},{4,8},{8,4},{12,0},{1,13},{5,9},{9,5},{13,1},{2,14},{6,10},... | collective-permute-start | bytes 393224 | tf_op jit(solution)/shard_map/ppermute | solution.py:168
  24.7 9.7 %copy-start = (bf16[128,1024]{1,0:T(8,128)(2,1)S(1)}, bf16[128,1024]{1,0:T(8,128)(2,1)}, u32[]{:S(2)}) copy-start(bf16[128,1024]{1,0:T(8,128)(2,1)} %shard_map.91) | copy-start | bytes 786436
  30.0 7.1 %collective-permute-start.9 = (bf16[64,1024]{1,0:T(8,128)(2,1)S(1)}, bf16[64,1024]{1,0:T(8,128)(2,1)S(1)}, u32[]{:S(2)}, u32[]{:S(2)}) collective-permute-start(bf16[64,1024]{1,0:T(8,128)(2,1)S(1)} %get-tuple-element.26), channel_id=1, source_target_pairs={{0,4},{4,0},{8,12},{12,8},{1,5},{5,1},{9,13},{13,9},{2,6},{6,2},{1... | collective-permute-start | bytes 393224 | tf_op jit(solution)/shard_map/ppermute | solution.py:168
  31.0 14.4 %collective-permute-start.10 = (bf16[64,1024]{1,0:T(8,128)(2,1)S(1)}, bf16[64,1024]{1,0:T(8,128)(2,1)S(1)}, u32[]{:S(2)}, u32[]{:S(2)}) collective-permute-start(bf16[64,1024]{1,0:T(8,128)(2,1)S(1)} %get-tuple-element.24), channel_id=1, source_target_pairs={{0,8},{4,12},{8,0},{12,4},{1,9},{5,13},{9,1},{13,5},{2,10},{6,14},... | collective-permute-start | bytes 393224 | tf_op jit(solution)/shard_map/ppermute | solution.py:168
  35.5 9.9 %collective-permute-start.11 = (bf16[64,1024]{1,0:T(8,128)(2,1)S(1)}, bf16[64,1024]{1,0:T(8,128)(2,1)S(1)}, u32[]{:S(2)}, u32[]{:S(2)}) collective-permute-start(bf16[64,1024]{1,0:T(8,128)(2,1)S(1)} %get-tuple-element.25), channel_id=1, source_target_pairs={{0,12},{4,8},{8,4},{12,0},{1,13},{5,9},{9,5},{13,1},{2,14},{6,10},... | collective-permute-start | bytes 393224 | tf_op jit(solution)/shard_map/ppermute | solution.py:168

commit v18 on v14

--- a/solution.py
+++ b/solution.py
@@ -155,7 +155,7 @@
         whitened = spectra(pos, prev_slots).reshape(blocks, rows, 2 * NBAND)
         own_parts.append(whitened)
         recv = []
-        for d in range(peers):
+        for d in range(1, peers):
             dest = (mine + d) % peers
             row = []
             for k in range(cap):
@@ -169,7 +169,15 @@
             recv.append(jnp.stack(row))
         picked_parts.append(jnp.stack(recv))
     whitened = jnp.concatenate(own_parts, axis=1)
+    self_blocks = []
+    for k in range(cap):
+        want = lax.dynamic_index_in_dim(ids[:, k], mine, keepdims=False)
+        blk = whitened[0]
+        for b in range(1, blocks):
+            blk = jnp.where(want == b, whitened[b], blk)
+        self_blocks.append(blk)
     picked = jnp.concatenate(picked_parts, axis=2)
+    picked = jnp.concatenate([jnp.stack(self_blocks)[None], picked], axis=0)
     turned = jnp.concatenate([whitened[..., NBAND:], -whitened[..., :NBAND]], axis=-1)
     paired = jnp.stack([whitened, turned], axis=1)
     result = jnp.einsum("lrif,dkjf->dklrij", paired, picked, preferred_element_type=jnp.float32)

time: 47.4 us -> 47.5 us (level)
    select_n x0 -> x3, other arithmetic: none -> 3.07 us  [local(): blk = jnp.where(want == b, whitened[b], blk)]
    another operation x2 -> x0, other arithmetic: 2.01 us -> none  [local(): picked_parts.append(jnp.stack(recv))]
    another operation x1, other arithmetic: 1.05 us -> 0.09 us  [local(): paired = jnp.stack([whitened, turned], axis=1)]
  transfers between devices with their start and end apart: 12 -> 12, of which waited for: 4 -> 5; matrix products, arithmetic and copies ran while one was open for 12% -> 12% of each run, Pallas kernels for 18% -> 18%
where the time goes in v18:
time: 47.5 us; the launch traced here: 47.2 us
  starting transfers between devices  16.8 us (35%)
  Pallas kernels  8.53 us (18%)
  waiting for transfers between devices  8.46 us (18%)
  other arithmetic  6.19 us (13%)
  local copies, waits for them, and re-layouts  3.71 us (8%)
  between operations  2.8 us (6%)
  matrix products  0.74 us (2%)
    ppermute x6, starting transfers between devices, local(): lax.ppermute(blk, 'chan', perm=[(i, (i + d) % peers) for i in range(peers)])  9.49 us
    pallas_call x2, Pallas kernels, spectra(): pl.pallas_call(spectra_kernel, grid_spec=grid_spec, cost_estimate=pl.Cost...  8.53 us
    ppermute x6, starting transfers between devices, local(): lax.ppermute(piece, 'tm', perm=[(i, (i + d) % ntm) for i in range(ntm)])  7.29 us
    ppermute x6, waiting for transfers between devices, local(): lax.ppermute(blk, 'chan', perm=[(i, (i + d) % peers) for i in range(peers)])  6.06 us
    select_n x3, other arithmetic, local(): blk = jnp.where(want == b, whitened[b], blk)  3.07 us
    ppermute x6, waiting for transfers between devices, local(): lax.ppermute(piece, 'tm', perm=[(i, (i + d) % ntm) for i in range(ntm)])  2.39 us
    another operation x2, other arithmetic, local(): prev_slots = jnp.stack(slots)  1.72 us
    slice x1, local copies, waits for them, and re-layouts, local(): part = parts[:, :, h].reshape(ntm, blocks * rows, width)  1.32 us
  transfers between devices with their start and end apart: 12, of which 5 were waited for; matrix products, arithmetic and copies ran while one was open for 12% of the time, Pallas kernels for 18%

profile of v18, /device:TPU:0, one launch (start us, length us, event | category | flops | bytes accessed | tf_op | source)
XLA Modules:
  0.0 47.2 jit_solution(11596845664022412814)
XLA Ops:
  0.0 0.0 copy-start.3
  0.0 0.0 copy-start.2
  0.0 1.3 %fusion.29 = (bf16[4,2,1,64,512]{4,3,2,1,0:T(8,128)(2,1)S(1)}, bf16[4,2,1,64,512]{4,3,2,1,0:T(8,128)(2,1)S(1)}) fusion(bf16[4,2,2,64,512]{4,3,2,1,0:T(8,128)(2,1)} %bitcast.80), kind=kLoop, calls=%fused_computation.75 | loop fusion | bytes 2097152 | tf_op jit(solution)/shard_map/slice | solution.py:147
  1.4 2.4 %collective-permute-start.2 = (bf16[128,512]{1,0:T(8,128)(2,1)S(1)}, bf16[128,512]{1,0:T(8,128)(2,1)S(1)}, u32[]{:S(2)}, u32[]{:S(2)}) collective-permute-start(bf16[128,512]{1,0:T(8,128)(2,1)S(1)} %get-tuple-element.16), channel_id=1, source_target_pairs={{0,3},{1,0},{2,1},{3,2},{4,7},{5,4},{6,5},{7,6},{8,11},{9,8},{10,9... | collective-permute-start | bytes 393224 | tf_op jit(solution)/shard_map/ppermute | solution.py:153
  3.8 0.0 collective-permute-start
  3.8 1.1 %collective-permute-start.1 = (bf16[128,512]{1,0:T(8,128)(2,1)S(1)}, bf16[128,512]{1,0:T(8,128)(2,1)S(1)}, u32[]{:S(2)}, u32[]{:S(2)}) collective-permute-start(bf16[128,512]{1,0:T(8,128)(2,1)S(1)} %get-tuple-element.17), channel_id=1, source_target_pairs={{0,2},{1,3},{2,0},{3,1},{4,6},{5,7},{6,4},{7,5},{8,10},{9,11},{10,... | collective-permute-start | bytes 393224 | tf_op jit(solution)/shard_map/ppermute | solution.py:153
  4.9 0.0 copy-done.3
  5.0 0.0 copy-done.2
  5.0 0.7 %constant_dynamic-slice_fusion.5 = (s32[1,1,1,1]{2,3,1,0:T(1,128)}, s32[1,1,1,1]{2,3,1,0:T(1,128)}, s32[1,1,1,1]{2,3,1,0:T(1,128)}, s32[1,1,1,1]{2,3,1,0:T(1,128)}) fusion(s32[1,1,4,1]{2,3,1,0:T(1,128)S(1)} %copy-done.2, s32[]{:T(128)S(6)} %select_n.183, s32[]{:T(128)S(6)} %select_n.195, s32[]{:T(128)S(6)} %select_n.203, s32[]{:T(128)S(6)} %select_n.199), kind=kLoop, calls=%fused_computation.60 | loop fusion | bytes 48 | tf_op jit(solution)/shard_map/jit(dynamic_index_in_dim)/dynamic_slice | solution.py:174
  8.3 0.0 collective-permute-done.2
  8.3 1.3 %collective-permute-done = bf16[128,512]{1,0:T(8,128)(2,1)S(1)} collective-permute-done((bf16[128,512]{1,0:T(8,128)(2,1)S(1)}, bf16[128,512]{1,0:T(8,128)(2,1)S(1)}, u32[]{:S(2)}, u32[]{:S(2)}) %collective-permute-start) | collective-permute-done | bytes 131104 | tf_op jit(solution)/shard_map/ppermute | solution.py:153
  9.6 1.1 %collective-permute-done.1 = bf16[128,512]{1,0:T(8,128)(2,1)S(1)} collective-permute-done((bf16[128,512]{1,0:T(8,128)(2,1)S(1)}, bf16[128,512]{1,0:T(8,128)(2,1)S(1)}, u32[]{:S(2)}, u32[]{:S(2)}) %collective-permute-start.1) | collective-permute-done | bytes 131104 | tf_op jit(solution)/shard_map/ppermute | solution.py:153
  10.7 0.9 %pad_maximum_fusion.2.x_ref = bf16[4,128,512]{2,1,0:T(8,128)(2,1)} fusion(bf16[1,128,512]{2,1,0:T(8,128)(2,1)S(1)} %bitcast.81, bf16[1,128,512]{2,1,0:T(8,128)(2,1)S(1)} %bitcast.83, bf16[1,128,512]{2,1,0:T(8,128)(2,1)S(1)} %bitcast.82, bf16[1,128,512]{2,1,0:T(8,128)(2,1)S(1)} %get-tuple-element.15), kind=kLoop, calls=%fused_computation.32 | loop fusion | flops 786432 | bytes 1048576 | tf_op jit(solution)/shard_map/stack | solution.py:154
  11.6 0.7 %collective-permute-start.3 = (bf16[128,512]{1,0:T(8,128)(2,1)S(1)}, bf16[128,512]{1,0:T(8,128)(2,1)S(1)}, u32[]{:S(2)}, u32[]{:S(2)}) collective-permute-start(bf16[128,512]{1,0:T(8,128)(2,1)S(1)} %get-tuple-element.14), channel_id=1, source_target_pairs={{0,1},{1,2},{2,3},{3,0},{4,5},{5,6},{6,7},{7,4},{8,9},{9,10},{10,1... | collective-permute-start | bytes 393224 | tf_op jit(solution)/shard_map/ppermute | solution.py:153
  12.3 1.7 %collective-permute-start.4 = (bf16[128,512]{1,0:T(8,128)(2,1)S(1)}, bf16[128,512]{1,0:T(8,128)(2,1)S(1)}, u32[]{:S(2)}, u32[]{:S(2)}) collective-permute-start(bf16[128,512]{1,0:T(8,128)(2,1)S(1)} %get-tuple-element.13), channel_id=1, source_target_pairs={{0,2},{1,3},{2,0},{3,1},{4,6},{5,7},{6,4},{7,5},{8,10},{9,11},{10,... | collective-permute-start | bytes 393224 | tf_op jit(solution)/shard_map/ppermute | solution.py:153
  14.0 1.4 %collective-permute-start.5 = (bf16[128,512]{1,0:T(8,128)(2,1)S(1)}, bf16[128,512]{1,0:T(8,128)(2,1)S(1)}, u32[]{:S(2)}, u32[]{:S(2)}) collective-permute-start(bf16[128,512]{1,0:T(8,128)(2,1)S(1)} %get-tuple-element.12), channel_id=1, source_target_pairs={{0,3},{1,0},{2,1},{3,2},{4,7},{5,4},{6,5},{7,6},{8,11},{9,8},{10,9... | collective-permute-start | bytes 393224 | tf_op jit(solution)/shard_map/ppermute | solution.py:153
  15.4 4.3 %shard_map.91 = bf16[128,1024]{1,0:T(8,128)(2,1)} custom-call(s32[1]{0:T(128)} %bitcast.2.pos_ref, bf16[4,128,512]{2,1,0:T(8,128)(2,1)} %pad_maximum_fusion.2.x_ref, bf16[384,256]{1,0:T(8,128)(2,1)} %constant.134.clone.band_ref, bf16[1024,1024]{1,0:T(8,128)(2,1)} %constant.135.clone.tab_ref, bf16[512,512]{1,0:T(8,128)(2,1)} %constant.136.clone.grp_ref), custom_call_target="tpu_custom_call" | custom-call | flops 1073741824 | bytes 2883584 | tf_op jit(solution)/shard_map/pallas_call | solution.py:123
  19.6 1.0 %broadcast_select_fusion.5 = (bf16[64,1024]{1,0:T(8,128)(2,1)S(1)}, bf16[64,1024]{1,0:T(8,128)(2,1)S(1)}, bf16[64,1024]{1,0:T(8,128)(2,1)S(1)}) fusion(pred[]{:T(512)} %bitcast.21, bf16[128,1024]{1,0:T(8,128)(2,1)} %shard_map.91, pred[]{:T(512)} %bitcast.25, pred[]{:T(512)} %bitcast.23), kind=kLoop, calls=%fused_computation.53 | loop fusion | flops 196608 | bytes 655363 | tf_op jit(solution)/shard_map/jit(_where)/select_n | solution.py:165
  20.6 1.6 %collective-permute-start.6 = (bf16[64,1024]{1,0:T(8,128)(2,1)S(1)}, bf16[64,1024]{1,0:T(8,128)(2,1)S(1)}, u32[]{:S(2)}, u32[]{:S(2)}) collective-permute-start(bf16[64,1024]{1,0:T(8,128)(2,1)S(1)} %get-tuple-element.19), channel_id=1, source_target_pairs={{0,4},{4,8},{8,12},{12,0},{1,5},{5,9},{9,13},{13,1},{2,6},{6,10},{... | collective-permute-start | bytes 393224 | tf_op jit(solution)/shard_map/ppermute | solution.py:167
  22.3 2.6 %collective-permute-start.7 = (bf16[64,1024]{1,0:T(8,128)(2,1)S(1)}, bf16[64,1024]{1,0:T(8,128)(2,1)S(1)}, u32[]{:S(2)}, u32[]{:S(2)}) collective-permute-start(bf16[64,1024]{1,0:T(8,128)(2,1)S(1)} %get-tuple-element.21), channel_id=1, source_target_pairs={{0,8},{4,12},{8,0},{12,4},{1,9},{5,13},{9,1},{13,5},{2,10},{6,14},... | collective-permute-start | bytes 393224 | tf_op jit(solution)/shard_map/ppermute | solution.py:167
  24.9 0.0 collective-permute-done.3
  24.9 1.3 %collective-permute-start.8 = (bf16[64,1024]{1,0:T(8,128)(2,1)S(1)}, bf16[64,1024]{1,0:T(8,128)(2,1)S(1)}, u32[]{:S(2)}, u32[]{:S(2)}) collective-permute-start(bf16[64,1024]{1,0:T(8,128)(2,1)S(1)} %get-tuple-element.20), channel_id=1, source_target_pairs={{0,12},{4,0},{8,4},{12,8},{1,13},{5,1},{9,5},{13,9},{2,14},{6,2},{... | collective-permute-start | bytes 393224 | tf_op jit(solution)/shard_map/ppermute | solution.py:167
  26.2 0.0 collective-permute-done.4
  26.2 0.0 collective-permute-done.5
  26.2 0.9 %pad_maximum_fusion.3.x_ref = bf16[4,128,512]{2,1,0:T(8,128)(2,1)} fusion(bf16[1,128,512]{2,1,0:T(8,128)(2,1)S(1)} %bitcast.86, bf16[1,128,512]{2,1,0:T(8,128)(2,1)S(1)} %bitcast.85, bf16[1,128,512]{2,1,0:T(8,128)(2,1)S(1)} %bitcast.84, bf16[1,128,512]{2,1,0:T(8,128)(2,1)S(1)} %get-tuple-element.11), kind=kLoop, calls=%fused_computation.33 | loop fusion | flops 786432 | bytes 1048576 | tf_op jit(solution)/shard_map/stack | solution.py:154
  27.1 0.0 copy-start
  27.1 4.3 %shard_map.92 = bf16[128,1024]{1,0:T(8,128)(2,1)} custom-call(s32[1]{0:T(128)} %bitcast.2.pos_ref, bf16[4,128,512]{2,1,0:T(8,128)(2,1)} %pad_maximum_fusion.3.x_ref, bf16[384,256]{1,0:T(8,128)(2,1)} %constant.134.clone.band_ref, bf16[1024,1024]{1,0:T(8,128)(2,1)} %constant.135.clone.tab_ref, bf16[512,512]{1,0:T(8,128)(2,1)} %constant.136.clone.grp_ref), custom_call_target="tpu_custom_call" | custom-call | flops 1073741824 | bytes 2883584 | tf_op jit(solution)/shard_map/pallas_call | solution.py:123
  31.3 0.0 copy-start.1
  31.3 1.0 %broadcast_select_fusion.4 = (bf16[64,1024]{1,0:T(8,128)(2,1)S(1)}, bf16[64,1024]{1,0:T(8,128)(2,1)S(1)}, bf16[64,1024]{1,0:T(8,128)(2,1)S(1)}) fusion(pred[]{:T(512)} %bitcast.21, bf16[128,1024]{1,0:T(8,128)(2,1)} %shard_map.92, pred[]{:T(512)} %bitcast.25, pred[]{:T(512)} %bitcast.23), kind=kLoop, calls=%fused_computation.52 | loop fusion | flops 196608 | bytes 655363 | tf_op jit(solution)/shard_map/jit(_where)/select_n | solution.py:165
  32.4 0.7 %collective-permute-start.9 = (bf16[64,1024]{1,0:T(8,128)(2,1)S(1)}, bf16[64,1024]{1,0:T(8,128)(2,1)S(1)}, u32[]{:S(2)}, u32[]{:S(2)}) collective-permute-start(bf16[64,1024]{1,0:T(8,128)(2,1)S(1)} %get-tuple-element.22), channel_id=1, source_target_pairs={{0,4},{4,8},{8,12},{12,0},{1,5},{5,9},{9,13},{13,1},{2,6},{6,10},{... | collective-permute-start | bytes 393224 | tf_op jit(solution)/shard_map/ppermute | solution.py:167
  33.1 0.3 collective-permute-start.10
  33.5 0.0 copy-done
  33.5 1.0 %fusion.20 = bf16[1,1,128,1024]{3,2,1,0:T(8,128)(2,1)S(1)} fusion(bf16[2,64,1024]{2,1,0:T(8,128)(2,1)S(1)} %bitcast.72, bf16[2,64,1024]{2,1,0:T(8,128)(2,1)} %bitcast.75, pred[]{:T(512)} %bitcast.1), kind=kLoop, calls=%fused_computation.37 | loop fusion | flops 1179648 | bytes 786433 | tf_op jit(solution)/shard_map/jit(_where)/select_n | solution.py:177
  34.5 1.0 %fusion.22 = (bf16[2,128,512]{2,1,0:T(8,128)(2,1)S(1)}, bf16[2,128,512]{2,1,0:T(8,128)(2,1)S(1)}) fusion(bf16[2,64,1024]{2,1,0:T(8,128)(2,1)S(1)} %bitcast.73, bf16[2,64,1024]{2,1,0:T(8,128)(2,1)} %bitcast.76), kind=kLoop, calls=%fused_computation.39 | loop fusion | flops 1179648 | bytes 1048576 | tf_op jit(solution)/shard_map/concatenate | solution.py:171
  35.5 0.0 collective-permute-done.6
  35.5 2.9 %collective-permute-start.11 = (bf16[64,1024]{1,0:T(8,128)(2,1)S(1)}, bf16[64,1024]{1,0:T(8,128)(2,1)S(1)}, u32[]{:S(2)}, u32[]{:S(2)}) collective-permute-start(bf16[64,1024]{1,0:T(8,128)(2,1)S(1)} %get-tuple-element.23), channel_id=1, source_target_pairs={{0,12},{4,0},{8,4},{12,8},{1,13},{5,1},{9,5},{13,9},{2,14},{6,2},{... | collective-permute-start | bytes 393224 | tf_op jit(solution)/shard_map/ppermute | solution.py:167
  38.4 0.0 copy-done.1
  38.4 0.1 fusion.17
  38.5 0.0 collective-permute-done.7
  38.5 0.0 collective-permute-done.8
  38.5 2.2 %collective-permute-done.9 = bf16[64,1024]{1,0:T(8,128)(2,1)S(1)} collective-permute-done((bf16[64,1024]{1,0:T(8,128)(2,1)S(1)}, bf16[64,1024]{1,0:T(8,128)(2,1)S(1)}, u32[]{:S(2)}, u32[]{:S(2)}) %collective-permute-start.9) | collective-permute-done | bytes 131104 | tf_op jit(solution)/shard_map/ppermute | solution.py:167
  40.7 3.4 %collective-permute-done.10 = bf16[64,1024]{1,0:T(8,128)(2,1)S(1)} collective-permute-done((bf16[64,1024]{1,0:T(8,128)(2,1)S(1)}, bf16[64,1024]{1,0:T(8,128)(2,1)S(1)}, u32[]{:S(2)}, u32[]{:S(2)}) %collective-permute-start.10) | collective-permute-done | bytes 131104 | tf_op jit(solution)/shard_map/ppermute | solution.py:167
  44.1 0.5 %collective-permute-done.11 = bf16[64,1024]{1,0:T(8,128)(2,1)S(1)} collective-permute-done((bf16[64,1024]{1,0:T(8,128)(2,1)S(1)}, bf16[64,1024]{1,0:T(8,128)(2,1)S(1)}, u32[]{:S(2)}, u32[]{:S(2)}) %collective-permute-start.11) | collective-permute-done | bytes 131104 | tf_op jit(solution)/shard_map/ppermute | solution.py:167
  44.6 0.7 %convolution_bitcast_fusion = f32[4,2,2,128,128]{3,4,2,1,0:T(8,128)S(1)} fusion(bf16[1,1,64,1024]{3,2,1,0:T(8,128)(2,1)S(1)} %bitcast.92, bf16[1,1,64,1024]{3,2,1,0:T(8,128)(2,1)S(1)} %bitcast.91, bf16[1,1,64,1024]{3,2,1,0:T(8,128)(2,1)S(1)} %bitcast.90, bf16[1,1,64,1024]{3,2,1,0:T(8,128)(2,1)S(1)} %bitcast.89, bf16[1,1,64,1024]{3,2,1,0:T(8,128)(2,1)S(1)} %bitcast.88, ...), kind=kOutput, calls=%fused_computation.1 | convolution fusion | flops 544735232 | bytes 3145728 | tf_op jit(solution)/shard_map/lrif,dkjf->dklrij/dot_general | solution.py:183
  45.3 0.6 %gather_fusion = f32[4,2,2,128,128]{3,4,2,1,0:T(8,128)S(1)} fusion(f32[4,2,2,128,128]{3,4,2,1,0:T(8,128)S(1)} %convolution_bitcast_fusion, s32[1024]{0:T(1024)S(1)} %pad_clamp_fusion), kind=kCustom, calls=%fused_computation | custom fusion | bytes 2097168 | tf_op jit(solution)/shard_map/jit(_take)/gather | solution.py:185
  46.0 0.2 fusion.14
  46.2 1.0 %copy.13 = bf16[1,1,4,1,2,2,128,128]{7,6,5,4,3,2,1,0:T(8,128)(2,1)} copy(bf16[1,1,4,1,2,2,128,128]{6,7,5,4,2,3,1,0:T(8,128)(2,1)S(1)} %fusion.14) | data formatting | bytes 1048576 | tf_op jit(solution)/shard_map/convert_element_type | solution.py:189
  (6 shorter events, 0.1 us)
Async XLA Ops:
  0.0 4.9 %copy-start.3 = (s32[1,1,4]{2,1,0:T(1,128)S(1)}, s32[1,1,4]{2,1,0:T(1,128)}, u32[]{:S(2)}) copy-start(s32[1,1,4]{2,1,0:T(1,128)} %param.11) | copy-start | bytes 52
  0.0 5.0 %copy-start.2 = (s32[1,1,4,1]{2,3,1,0:T(1,128)S(1)}, s32[1,1,4,1]{2,3,1,0:T(1,128)}, u32[]{:S(2)}) copy-start(s32[1,1,4,1]{2,3,1,0:T(1,128)} %param.10) | copy-start | bytes 52
  1.4 6.9 %collective-permute-start.2 = (bf16[128,512]{1,0:T(8,128)(2,1)S(1)}, bf16[128,512]{1,0:T(8,128)(2,1)S(1)}, u32[]{:S(2)}, u32[]{:S(2)}) collective-permute-start(bf16[128,512]{1,0:T(8,128)(2,1)S(1)} %get-tuple-element.16), channel_id=1, source_target_pairs={{0,3},{1,0},{2,1},{3,2},{4,7},{5,4},{6,5},{7,6},{8,11},{9,8},{10,9... | collective-permute-start | bytes 393224 | tf_op jit(solution)/shard_map/ppermute | solution.py:153
  3.8 5.8 %collective-permute-start = (bf16[128,512]{1,0:T(8,128)(2,1)S(1)}, bf16[128,512]{1,0:T(8,128)(2,1)S(1)}, u32[]{:S(2)}, u32[]{:S(2)}) collective-permute-start(bf16[128,512]{1,0:T(8,128)(2,1)S(1)} %get-tuple-element.18), channel_id=1, source_target_pairs={{0,1},{1,2},{2,3},{3,0},{4,5},{5,6},{6,7},{7,4},{8,9},{9,10},{10,1... | collective-permute-start | bytes 393224 | tf_op jit(solution)/shard_map/ppermute | solution.py:153
  3.8 6.8 %collective-permute-start.1 = (bf16[128,512]{1,0:T(8,128)(2,1)S(1)}, bf16[128,512]{1,0:T(8,128)(2,1)S(1)}, u32[]{:S(2)}, u32[]{:S(2)}) collective-permute-start(bf16[128,512]{1,0:T(8,128)(2,1)S(1)} %get-tuple-element.17), channel_id=1, source_target_pairs={{0,2},{1,3},{2,0},{3,1},{4,6},{5,7},{6,4},{7,5},{8,10},{9,11},{10,... | collective-permute-start | bytes 393224 | tf_op jit(solution)/shard_map/ppermute | solution.py:153
  11.6 13.3 %collective-permute-start.3 = (bf16[128,512]{1,0:T(8,128)(2,1)S(1)}, bf16[128,512]{1,0:T(8,128)(2,1)S(1)}, u32[]{:S(2)}, u32[]{:S(2)}) collective-permute-start(bf16[128,512]{1,0:T(8,128)(2,1)S(1)} %get-tuple-element.14), channel_id=1, source_target_pairs={{0,1},{1,2},{2,3},{3,0},{4,5},{5,6},{6,7},{7,4},{8,9},{9,10},{10,1... | collective-permute-start | bytes 393224 | tf_op jit(solution)/shard_map/ppermute | solution.py:153
  12.3 13.9 %collective-permute-start.4 = (bf16[128,512]{1,0:T(8,128)(2,1)S(1)}, bf16[128,512]{1,0:T(8,128)(2,1)S(1)}, u32[]{:S(2)}, u32[]{:S(2)}) collective-permute-start(bf16[128,512]{1,0:T(8,128)(2,1)S(1)} %get-tuple-element.13), channel_id=1, source_target_pairs={{0,2},{1,3},{2,0},{3,1},{4,6},{5,7},{6,4},{7,5},{8,10},{9,11},{10,... | collective-permute-start | bytes 393224 | tf_op jit(solution)/shard_map/ppermute | solution.py:153
  14.0 12.2 %collective-permute-start.5 = (bf16[128,512]{1,0:T(8,128)(2,1)S(1)}, bf16[128,512]{1,0:T(8,128)(2,1)S(1)}, u32[]{:S(2)}, u32[]{:S(2)}) collective-permute-start(bf16[128,512]{1,0:T(8,128)(2,1)S(1)} %get-tuple-element.12), channel_id=1, source_target_pairs={{0,3},{1,0},{2,1},{3,2},{4,7},{5,4},{6,5},{7,6},{8,11},{9,8},{10,9... | collective-permute-start | bytes 393224 | tf_op jit(solution)/shard_map/ppermute | solution.py:153
  20.6 14.9 %collective-permute-start.6 = (bf16[64,1024]{1,0:T(8,128)(2,1)S(1)}, bf16[64,1024]{1,0:T(8,128)(2,1)S(1)}, u32[]{:S(2)}, u32[]{:S(2)}) collective-permute-start(bf16[64,1024]{1,0:T(8,128)(2,1)S(1)} %get-tuple-element.19), channel_id=1, source_target_pairs={{0,4},{4,8},{8,12},{12,0},{1,5},{5,9},{9,13},{13,1},{2,6},{6,10},{... | collective-permute-start | bytes 393224 | tf_op jit(solution)/shard_map/ppermute | solution.py:167
  22.3 16.3 %collective-permute-start.7 = (bf16[64,1024]{1,0:T(8,128)(2,1)S(1)}, bf16[64,1024]{1,0:T(8,128)(2,1)S(1)}, u32[]{:S(2)}, u32[]{:S(2)}) collective-permute-start(bf16[64,1024]{1,0:T(8,128)(2,1)S(1)} %get-tuple-element.21), channel_id=1, source_target_pairs={{0,8},{4,12},{8,0},{12,4},{1,9},{5,13},{9,1},{13,5},{2,10},{6,14},... | collective-permute-start | bytes 393224 | tf_op jit(solution)/shard_map/ppermute | solution.py:167
  24.9 13.7 %collective-permute-start.8 = (bf16[64,1024]{1,0:T(8,128)(2,1)S(1)}, bf16[64,1024]{1,0:T(8,128)(2,1)S(1)}, u32[]{:S(2)}, u32[]{:S(2)}) collective-permute-start(bf16[64,1024]{1,0:T(8,128)(2,1)S(1)} %get-tuple-element.20), channel_id=1, source_target_pairs={{0,12},{4,0},{8,4},{12,8},{1,13},{5,1},{9,5},{13,9},{2,14},{6,2},{... | collective-permute-start | bytes 393224 | tf_op jit(solution)/shard_map/ppermute | solution.py:167
  27.1 6.4 %copy-start = (bf16[128,1024]{1,0:T(8,128)(2,1)S(1)}, bf16[128,1024]{1,0:T(8,128)(2,1)}, u32[]{:S(2)}) copy-start(bf16[128,1024]{1,0:T(8,128)(2,1)} %shard_map.91) | copy-start | bytes 786436
  31.3 7.1 %copy-start.1 = (bf16[128,1024]{1,0:T(8,128)(2,1)S(1)}, bf16[128,1024]{1,0:T(8,128)(2,1)}, u32[]{:S(2)}) copy-start(bf16[128,1024]{1,0:T(8,128)(2,1)} %shard_map.92) | copy-start | bytes 786436
  32.4 8.3 %collective-permute-start.9 = (bf16[64,1024]{1,0:T(8,128)(2,1)S(1)}, bf16[64,1024]{1,0:T(8,128)(2,1)S(1)}, u32[]{:S(2)}, u32[]{:S(2)}) collective-permute-start(bf16[64,1024]{1,0:T(8,128)(2,1)S(1)} %get-tuple-element.22), channel_id=1, source_target_pairs={{0,4},{4,8},{8,12},{12,0},{1,5},{5,9},{9,13},{13,1},{2,6},{6,10},{... | collective-permute-start | bytes 393224 | tf_op jit(solution)/shard_map/ppermute | solution.py:167
  33.1 11.0 %collective-permute-start.10 = (bf16[64,1024]{1,0:T(8,128)(2,1)S(1)}, bf16[64,1024]{1,0:T(8,128)(2,1)S(1)}, u32[]{:S(2)}, u32[]{:S(2)}) collective-permute-start(bf16[64,1024]{1,0:T(8,128)(2,1)S(1)} %get-tuple-element.24), channel_id=1, source_target_pairs={{0,8},{4,12},{8,0},{12,4},{1,9},{5,13},{9,1},{13,5},{2,10},{6,14},... | collective-permute-start | bytes 393224 | tf_op jit(solution)/shard_map/ppermute | solution.py:167
  35.5 9.1 %collective-permute-start.11 = (bf16[64,1024]{1,0:T(8,128)(2,1)S(1)}, bf16[64,1024]{1,0:T(8,128)(2,1)S(1)}, u32[]{:S(2)}, u32[]{:S(2)}) collective-permute-start(bf16[64,1024]{1,0:T(8,128)(2,1)S(1)} %get-tuple-element.23), channel_id=1, source_target_pairs={{0,12},{4,0},{8,4},{12,8},{1,13},{5,1},{9,5},{13,9},{2,14},{6,2},{... | collective-permute-start | bytes 393224 | tf_op jit(solution)/shard_map/ppermute | solution.py:167
